TPU v7x, 256 devices: a whole 4x4x8 slice. The times are simulated.
256 devices in a mesh: dp: 32 (over y, z_hi, core), tensor: 8 (over z_lo, x).
Axes of the slice: x: 4, y: 4, z: 8 (z_hi: 4, z_lo: 2; z = z_hi * 2 + z_lo), core: 2. Of those that a mesh axis runs over, the one named last changes fastest.
Arguments:
- inputs: bfloat16 [32768, 2048], P(('dp', 'tensor')), may hold values from -6 to 6
- norm_gain: float32 [2048], replicated, may hold values from 0.1 to 1.9
- proj_weight: bfloat16 [2048, 3, 2048], P('dp', None, 'tensor'), may hold values from -0.125 to 0.125
- filters: float32 [3, 7, 2048], P(None, None, 'tensor'), may hold values from -2.4 to 2.4
- cotangent: bfloat16 [32768, 2048], P('dp', 'tensor'), may hold values from -18 to 18
Outputs:
- mixed: bfloat16 [32768, 2048], P('dp', 'tensor')
- grad_inputs: bfloat16 [32768, 2048], P(('dp', 'tensor'))
- grad_proj: bfloat16 [2048, 3, 2048], P('dp', None, 'tensor')
- grad_filters: float32 [3, 7, 2048], P(None, None, 'tensor')
- grad_gain: float32 [2048], replicated
All inputs are finite; a program needn't handle non-finite values.
Results may differ from a plain program's by a relative error of at most 0.02.
Values may be sent and summed in bfloat16 or wider, within the bound.
No kernel may reach another device: no remote copies, remote signals or barrier semaphores. Data moves between devices by JAX's collectives and lax.ppermute only.
A program may use at most 64 MiB of HBM per device.

v0:
```python
import jax
import jax.numpy as jnp
from jax import lax
from jax.sharding import PartitionSpec as P

TENSOR_SPLIT = (2, 4)
DP_SPLIT = (4, 4, 2)


def passed_along(shard, axis, by):
    size = lax.axis_size(axis)
    pairs = [(i, i + by) for i in range(size) if 0 <= i + by < size]
    return lax.ppermute(shard, axis, pairs)


def butterfly_sum(value, axis):
    size = lax.axis_size(axis)
    step = 1
    while step < size:
        pairs = [(i, i ^ step) for i in range(size)]
        value = value + lax.ppermute(value, axis, pairs)
        step *= 2
    return value


def digits(index, split):
    out = []
    for size in reversed(split):
        out.append(index % size)
        index = index // size
    return out[::-1]


def number(parts, split):
    index = 0
    for part, size in zip(parts, split):
        index = index * size + part
    return index


def mover(axis, split, field):
    def move(value, by):
        pairs = []
        for i in range(lax.axis_size(axis)):
            parts = digits(i, split)
            parts[field] = (parts[field] + by) % split[field]
            pairs.append((i, number(parts, split)))
        return lax.ppermute(value, axis, pairs)

    return move


def halves(value, axis):
    cut = value.shape[axis] // 2
    return (
        lax.slice_in_dim(value, 0, cut, axis=axis),
        lax.slice_in_dim(value, cut, value.shape[axis], axis=axis),
    )


def ring_gather(own, move, axis):
    from_left = move(own, 1)
    from_right = move(own, -1)
    far = jnp.concatenate(
        [move(halves(from_left, axis)[0], 1), move(halves(from_right, axis)[1], -1)], axis=axis
    )
    return [own, from_right, far, from_left]


def ring_scatter(shard, move, axis):
    first_far, second_far = halves(shard[2], axis)
    got_left = move(first_far.astype(jnp.bfloat16), 1).astype(jnp.float32)
    got_right = move(second_far.astype(jnp.bfloat16), -1).astype(jnp.float32)
    first, second = halves(shard[1], axis)
    send_right = jnp.concatenate([first + got_left, second], axis=axis)
    first, second = halves(shard[3], axis)
    send_left = jnp.concatenate([first, second + got_right], axis=axis)
    return (
        shard[0]
        + move(send_right.astype(jnp.bfloat16), 1).astype(jnp.float32)
        + move(send_left.astype(jnp.bfloat16), -1).astype(jnp.float32)
    )


def slot_tables(axis, split):
    me = digits(lax.axis_index(axis), split)
    total = 1
    for size in split:
        total *= size
    r = digits(jnp.arange(total, dtype=jnp.int32), split)
    absolute = number([(m + d) % s for m, d, s in zip(me, r, split)], split)
    relative = number([(d - m) % s for m, d, s in zip(me, r, split)], split)
    return absolute, relative


def gather_tensor(own):
    along_x = mover("tensor", TENSOR_SPLIT, 1)
    across_z = mover("tensor", TENSOR_SPLIT, 0)
    partner = across_z(own, 1)
    return jnp.stack(ring_gather(own, along_x, 0) + ring_gather(partner, along_x, 0))


def scatter_dp(blocks):
    along_y = mover("dp", DP_SPLIT, 0)
    along_h = mover("dp", DP_SPLIT, 1)
    across_core = mover("dp", DP_SPLIT, 2)
    grid = blocks.reshape(DP_SPLIT + blocks.shape[1:])
    summed = grid[:, :, 0].astype(jnp.float32) + across_core(grid[:, :, 1], 1).astype(jnp.float32)
    column = ring_scatter([summed[k] for k in range(DP_SPLIT[0])], along_y, 1)
    return ring_scatter([column[k] for k in range(DP_SPLIT[1])], along_h, 0)


def body(inputs, norm_gain, proj_weight, filters, cotangent):
    taps = filters.shape[1]
    width = taps - 1
    rows = inputs.shape[0]
    _, t_relative = slot_tables("tensor", TENSOR_SPLIT)
    d_absolute, _ = slot_tables("dp", DP_SPLIT)
    wide = inputs.astype(jnp.float32)
    inv_rms = lax.rsqrt(jnp.mean(wide * wide, axis=1, keepdims=True) + 1e-05)
    weights = lax.all_gather(proj_weight, "dp", axis=0, tiled=True)
    gathered = jnp.take(gather_tensor(inputs), t_relative, axis=0).reshape(-1, inputs.shape[1])
    wide_all = gathered.astype(jnp.float32)
    inv_all = lax.rsqrt(jnp.mean(wide_all * wide_all, axis=1, keepdims=True) + 1e-05)
    unit_all = wide_all * inv_all
    positions = (unit_all * norm_gain).astype(jnp.bfloat16)
    length = positions.shape[0]
    streams = jnp.einsum(
        "td,dsc->tsc", positions, weights, preferred_element_type=jnp.float32
    ).astype(jnp.bfloat16)
    before = passed_along(streams[length - width :], "dp", 1)
    extended = jnp.concatenate([before, streams], axis=0).astype(jnp.float32)
    conv = jnp.zeros(streams.shape, jnp.float32)
    for tap in range(taps):
        conv = conv + filters[:, tap, :] * extended[width - tap : width - tap + length]
    mixed = (conv[:, 0] * conv[:, 1] * conv[:, 2]).astype(jnp.bfloat16)
    grad_out = cotangent.astype(jnp.float32)
    grad_conv = jnp.stack(
        [
            grad_out * conv[:, 1] * conv[:, 2],
            grad_out * conv[:, 0] * conv[:, 2],
            grad_out * conv[:, 0] * conv[:, 1],
        ],
        axis=1,
    )
    after = passed_along(grad_conv[:width], "dp", -1)
    grad_extended = jnp.concatenate([grad_conv, after], axis=0)
    grad_acc = jnp.zeros(streams.shape, jnp.float32)
    for tap in range(taps):
        grad_acc = grad_acc + filters[:, tap, :] * grad_extended[tap : tap + length]
    grad_streams = grad_acc.astype(jnp.bfloat16)
    filter_local = jnp.stack(
        [
            jnp.sum(grad_conv * extended[width - tap : width - tap + length], axis=0)
            for tap in range(taps)
        ],
        axis=1,
    )
    normed_terms = jnp.einsum(
        "tsc,dsc->td", grad_streams, weights, preferred_element_type=jnp.float32
    ).astype(jnp.bfloat16)
    gain_local = jnp.sum(normed_terms.astype(jnp.float32) * unit_all, axis=0)
    grad_normed = lax.psum_scatter(
        normed_terms, "tensor", scatter_dimension=0, tiled=True
    ).astype(jnp.float32)
    weight_terms = jnp.einsum(
        "td,tsc->dsc", positions, grad_streams, preferred_element_type=jnp.float32
    ).astype(jnp.bfloat16)
    block = proj_weight.shape[0]
    weight_blocks = jnp.take(
        weight_terms.reshape((-1, block) + weight_terms.shape[1:]), d_absolute, axis=0
    )
    grad_proj = scatter_dp(weight_blocks).astype(jnp.bfloat16)
    joined = butterfly_sum(jnp.concatenate([filter_local.reshape(-1), gain_local]), "dp")
    grad_filters = joined[: filter_local.size].reshape(filter_local.shape)
    grad_gain = butterfly_sum(joined[filter_local.size :], "tensor")
    scaled = norm_gain * grad_normed
    grad_inputs = inv_rms * (
        scaled - wide * inv_rms * inv_rms * jnp.mean(scaled * wide, axis=1, keepdims=True)
    )
    return (mixed, grad_inputs.astype(jnp.bfloat16), grad_proj, grad_filters, grad_gain)


def solution(mesh):
    return jax.shard_map(
        body,
        mesh=mesh,
        in_specs=(
            P(("dp", "tensor"), None),
            P(),
            P("dp", None, "tensor"),
            P(None, None, "tensor"),
            P("dp", "tensor"),
        ),
        out_specs=(
            P("dp", "tensor"),
            P(("dp", "tensor"), None),
            P("dp", None, "tensor"),
            P(None, None, "tensor"),
            P(),
        ),
        check_vma=False,
    )
```

profile of v0, /device:TPU:10, one launch (start us, length us, event | category | flops | bytes accessed | tf_op | source)
XLA Modules:
  0.0 184.2 jit_solution(8312909048299547596)
XLA Ops:
  8.6 1.5 collective-permute-start.1
  10.1 1.9 %collective-permute-start.4 = (bf16[128,2048]{1,0:T(8,128)(2,1)}, bf16[128,2048]{1,0:T(8,128)(2,1)S(1)}, u32[]{:S(2)}, u32[]{:S(2)}) collective-permute-start(bf16[128,2048]{1,0:T(8,128)(2,1)} %param.5), channel_id=1, source_target_pairs={{0,4},{1,5},{2,6},{3,7},{4,0},{5,1},{6,2},{7,3},{8,12},{9,13},{10,... | collective-permute-start | bytes 1572872 | tf_op jit(solution)/shard_map/ppermute | solution.py:48
  12.1 1.0 fusion.81
  13.1 1.9 %bitcast_dynamic-update-slice_fusion.5 = bf16[8,128,2048]{2,1,0:T(8,128)(2,1)} fusion(bf16[128,2048]{1,0:T(8,128)(2,1)} %param.5), kind=kLoop, calls=%fused_computation.76 | loop fusion | bytes 1048576
  15.0 6.9 %collective-permute-done = bf16[128,2048]{1,0:T(8,128)(2,1)S(1)} collective-permute-done((bf16[128,2048]{1,0:T(8,128)(2,1)}, bf16[128,2048]{1,0:T(8,128)(2,1)S(1)}, u32[]{:S(2)}, u32[]{:S(2)}) %collective-permute-start) | collective-permute-done | bytes 524320 | tf_op jit(solution)/shard_map/ppermute | solution.py:48
  21.9 1.0 collective-permute-start.3
  23.2 0.9 collective-permute-start.2
  24.1 2.6 %collective-permute-start.5 = (bf16[128,2048]{1,0:T(8,128)(2,1)S(1)}, bf16[128,2048]{1,0:T(8,128)(2,1)S(1)}, u32[]{:S(2)}, u32[]{:S(2)}) collective-permute-start(bf16[128,2048]{1,0:T(8,128)(2,1)S(1)} %collective-permute-done.4), channel_id=1, source_target_pairs={{0,3},{1,0},{2,1},{3,2},{4,7},{5,4},{6,5},{7,6},{8,11},{9,8},{10,9... | collective-permute-start | bytes 1572872 | tf_op jit(solution)/shard_map/ppermute | solution.py:48
  26.7 0.8 bitcast_dynamic-update-slice_fusion.4
  27.5 3.7 %collective-permute-done.3 = bf16[64,2048]{1,0:T(8,128)(2,1)S(1)} collective-permute-done((bf16[64,2048]{1,0:T(8,128)(2,1)S(1)}, bf16[64,2048]{1,0:T(8,128)(2,1)S(1)}, u32[]{:S(2)}, u32[]{:S(2)}) %collective-permute-start.3) | collective-permute-done | bytes 262176 | tf_op jit(solution)/shard_map/ppermute | solution.py:48
  31.2 2.6 %collective-permute-done.2 = bf16[64,2048]{1,0:T(8,128)(2,1)S(1)} collective-permute-done((bf16[64,2048]{1,0:T(8,128)(2,1)S(1)}, bf16[64,2048]{1,0:T(8,128)(2,1)S(1)}, u32[]{:S(2)}, u32[]{:S(2)}) %collective-permute-start.2) | collective-permute-done | bytes 262176 | tf_op jit(solution)/shard_map/ppermute | solution.py:48
  33.8 0.9 fusion.25
  34.7 0.9 bitcast_dynamic-update-slice_fusion.3
  35.5 0.8 bitcast_dynamic-update-slice_fusion.2
  36.4 4.0 %collective-permute-done.5 = bf16[128,2048]{1,0:T(8,128)(2,1)S(1)} collective-permute-done((bf16[128,2048]{1,0:T(8,128)(2,1)S(1)}, bf16[128,2048]{1,0:T(8,128)(2,1)S(1)}, u32[]{:S(2)}, u32[]{:S(2)}) %collective-permute-start.5) | collective-permute-done | bytes 524320 | tf_op jit(solution)/shard_map/ppermute | solution.py:48
  40.4 2.1 %collective-permute-start.8 = (bf16[64,2048]{1,0:T(8,128)(2,1)S(1)}, bf16[64,2048]{1,0:T(8,128)(2,1)S(1)}, u32[]{:S(2)}, u32[]{:S(2)}) collective-permute-start(bf16[64,2048]{1,0:T(8,128)(2,1)S(1)} %slice.262), channel_id=1, source_target_pairs={{0,3},{1,0},{2,1},{3,2},{4,7},{5,4},{6,5},{7,6},{8,11},{9,8},{10,9... | collective-permute-start | bytes 786440 | tf_op jit(solution)/shard_map/ppermute | solution.py:48
  43.1 0.8 bitcast_dynamic-update-slice_fusion.1
  44.0 3.6 %collective-permute-done.8 = bf16[64,2048]{1,0:T(8,128)(2,1)S(1)} collective-permute-done((bf16[64,2048]{1,0:T(8,128)(2,1)S(1)}, bf16[64,2048]{1,0:T(8,128)(2,1)S(1)}, u32[]{:S(2)}, u32[]{:S(2)}) %collective-permute-start.8) | collective-permute-done | bytes 262176 | tf_op jit(solution)/shard_map/ppermute | solution.py:48
  47.6 3.1 %collective-permute-done.7 = bf16[64,2048]{1,0:T(8,128)(2,1)S(1)} collective-permute-done((bf16[64,2048]{1,0:T(8,128)(2,1)S(1)}, bf16[64,2048]{1,0:T(8,128)(2,1)S(1)}, u32[]{:S(2)}, u32[]{:S(2)}) %collective-permute-start.7) | collective-permute-done | bytes 262176 | tf_op jit(solution)/shard_map/ppermute | solution.py:48
  50.7 0.8 fusion.26
  51.5 0.8 bitcast_dynamic-update-slice_fusion
  52.4 5.0 %gather_fusion = bf16[8,128,2048]{2,1,0:T(8,128)(2,1)} fusion(bf16[8,128,2048]{2,1,0:T(8,128)(2,1)} %bitcast_dynamic-update-slice_fusion, s32[1024]{0:T(1024)S(1)} %pad_clamp_fusion.1), kind=kCustom, calls=%fused_computation | custom fusion | bytes 8388640 | tf_op jit(solution)/shard_map/jit(_take)/gather | solution.py:122
  57.4 3.7 %multiply_reduce_fusion.1 = f32[8,128]{1,0:T(8,128)S(1)} fusion(bf16[8,128,2048]{2,1,0:T(8,128)(2,1)} %gather_fusion, pred[8]{0:T(512)(128)(4,1)S(1)} %compare_and_fusion.1), kind=kLoop, calls=%fused_computation.5 | loop fusion | flops 8387584 | bytes 4198408 | tf_op jit(solution)/shard_map/reduce_sum | solution.py:124
  61.1 2.7 %bitcast_select_fusion = bf16[1024,2048]{1,0:T(8,128)(2,1)} fusion(bf16[8,128,2048]{2,1,0:T(8,128)(2,1)S(1)} %copy-done, pred[1024]{0:T(1024)(128)(4,1)S(1)} %broadcast_bitcast_fusion), kind=kLoop, calls=%fused_computation.8 | loop fusion | flops 2097152 | bytes 8389632 | tf_op jit(solution)/shard_map/jit(_take)/select_n | solution.py:122
  63.8 5.8 %all-gather.2.cloned.1.call-done = bf16[2048,3,256]{2,0,1:T(8,128)(2,1)} async-done(((bf16[64,3,256]{2,0,1:T(8,128)(2,1)}), bf16[2048,3,256]{2,0,1:T(8,128)(2,1)}) %all-gather.2.cloned.1.call-update) | async-done | bytes 3145744 | tf_op jit(solution)/shard_map/all_gather | solution.py:121
  69.6 6.6 %fusion.11 = bf16[1024,3,256]{2,0,1:T(8,128)(2,1)S(1)} fusion(bf16[2048,3,256]{2,0,1:T(8,128)(2,1)} %all-gather.2.cloned.1.call-done, bf16[1024,2048]{1,0:T(8,128)(2,1)} %bitcast_select_fusion, f32[2048]{0:T(1024)S(1)} %copy-done.5, f32[1024]{0:T(1024)S(1)} %rsqrt_bitcast_fusion), kind=kOutput, calls=%fused_computation.36 | convolution fusion | flops 3230400512 | bytes 8925184 | tf_op jit(solution)/shard_map/td,dsc->tsc/dot_general | solution.py:128
  76.3 2.4 %collective-permute-start.9 = (bf16[6,3,256]{2,0,1:T(8,128)(2,1)S(1)}, bf16[6,3,256]{2,0,1:T(8,128)(2,1)S(1)}, u32[]{:S(2)}, u32[]{:S(2)}) collective-permute-start(bf16[6,3,256]{2,0,1:T(8,128)(2,1)S(1)} %slice.263), channel_id=1, source_target_pairs={{0,8},{8,16},{16,24},{24,32},{32,40},{40,48},{48,56},{56,64},{64,7... | collective-permute-start | bytes 27656 | tf_op jit(solution)/shard_map/ppermute | solution.py:13
  78.7 5.8 %collective-permute-done.9 = bf16[6,3,256]{2,0,1:T(8,128)(2,1)S(1)} collective-permute-done((bf16[6,3,256]{2,0,1:T(8,128)(2,1)S(1)}, bf16[6,3,256]{2,0,1:T(8,128)(2,1)S(1)}, u32[]{:S(2)}, u32[]{:S(2)}) %collective-permute-start.9) | collective-permute-done | bytes 9248 | tf_op jit(solution)/shard_map/ppermute | solution.py:13
  84.8 2.6 %multiply_add_fusion = f32[1024,3,256]{2,0,1:T(8,128)S(1)} fusion(f32[1030,3,256]{2,0,1:T(8,128)S(1)} %maximum_convert_fusion, f32[3,256]{1,0:T(4,128)S(1)} %get-tuple-element.43, f32[3,256]{1,0:T(4,128)S(1)} %get-tuple-element.44, f32[3,256]{1,0:T(4,128)S(1)} %get-tuple-element.45, f32[3,256]{1,0:T(4,128)S(1)} %get-tuple-element.46, ...), kind=kLoop, calls=%fused_computation.33 | loop fusion | flops 10223616 | bytes 25187328 | tf_op jit(solution)/shard_map/add | solution.py:135
  87.4 1.2 fusion.15
  88.5 2.9 %multiply_reduce_fusion.2 = (f32[3,256]{1,0:T(4,128)S(1)}, f32[3,256]{1,0:T(4,128)S(1)}, f32[3,256]{1,0:T(4,128)S(1)}, f32[3,256]{1,0:T(4,128)S(1)}, f32[3,256]{...) fusion(f32[1030,3,256]{2,0,1:T(8,128)S(1)} %maximum_convert_fusion, ...), kind=kLoop, calls=%fused_computation.26 | loop fusion | flops 12577536 | bytes 28333056 | tf_op jit(solution)/shard_map/reduce_sum | solution.py:154
  91.4 1.9 %collective-permute-start.10 = (f32[6,3,256]{2,0,1:T(8,128)S(1)}, f32[6,3,256]{2,0,1:T(8,128)S(1)}, u32[]{:S(2)}, u32[]{:S(2)}) collective-permute-start(f32[6,3,256]{2,0,1:T(8,128)S(1)} %slice.274), channel_id=1, source_target_pairs={{8,0},{16,8},{24,16},{32,24},{40,32},{48,40},{56,48},{64,56},{72,6... | collective-permute-start | bytes 55304 | tf_op jit(solution)/shard_map/ppermute | solution.py:13
  93.3 1.5 collective-permute-done.10
  95.1 2.7 %fusion.2 = bf16[1024,3,256]{2,0,1:T(8,128)(2,1)S(1)} fusion(f32[1030,3,256]{2,0,1:T(8,128)S(1)} %pad_maximum_fusion, f32[3,256]{1,0:T(4,128)S(1)} %get-tuple-element.43, f32[3,256]{1,0:T(4,128)S(1)} %get-tuple-element.44, f32[3,256]{1,0:T(4,128)S(1)} %get-tuple-element.45, f32[3,256]{1,0:T(4,128)S(1)} %get-tuple-element.46, ...), kind=kLoop, calls=%fused_computation.13 | loop fusion | flops 12582912 | bytes 23614464 | tf_op jit(solution)/shard_map/convert_element_type | solution.py:151
  98.2 5.2 %multiply_reduce_fusion = (f32[2048]{0:T(1024)S(1)}, bf16[1024,2048]{1,0:T(8,128)(2,1)}) fusion(bf16[1024,2048]{1,0:T(8,128)(2,1)S(1)} %copy-done.3, f32[1024]{0:T(1024)S(1)} %rsqrt_bitcast_fusion, bf16[1024,3,256]{2,0,1:T(8,128)(2,1)S(1)} %fusion.2, bf16[2048,3,256]{2,0,1:T(8,128)(2,1)S(1)} %copy-done.6), kind=kOutput, calls=%fused_computation.3 | convolution fusion | flops 3233806336 | bytes 13119488 | tf_op jit(solution)/shard_map/tsc,dsc->td/dot_general | solution.py:159
  103.6 7.8 %convolution_convert_fusion = bf16[2048,3,256]{2,0,1:T(8,128)(2,1)} fusion(bf16[1024,3,256]{2,0,1:T(8,128)(2,1)S(1)} %fusion.2, bf16[1024,2048]{1,0:T(8,128)(2,1)} %bitcast_select_fusion, f32[2048]{0:T(1024)S(1)} %copy-done.5, f32[1024]{0:T(1024)S(1)} %rsqrt_bitcast_fusion), kind=kOutput, calls=%fused_computation.9 | convolution fusion | flops 3231186944 | bytes 8925184 | tf_op jit(solution)/shard_map/td,tsc->dsc/dot_general | solution.py:166
  111.4 2.6 %gather_fusion.1 = bf16[32,64,3,256]{3,1,2,0:T(8,128)(2,1)S(1)} fusion(bf16[32,64,3,256]{3,1,0,2:T(8,128)(2,1)} %bitcast.143, s32[1024]{0:T(1024)S(1)} %pad_clamp_fusion), kind=kCustom, calls=%fused_computation.1 | custom fusion | bytes 6291584 | tf_op jit(solution)/shard_map/jit(_take)/gather | solution.py:170
  114.4 1.7 copy-done.1
  116.7 3.2 %collective-permute-done.11 = bf16[4,4,64,3,256]{4,2,3,1,0:T(8,128)(2,1)S(1)} collective-permute-done((bf16[4,4,64,3,256]{4,2,3,1,0:T(8,128)(2,1)S(1)}, bf16[4,4,64,3,256]{4,2,3,1,0:T(8,128)(2,1)S(1)}, u32[]{:S(2)}, u32[]{:S(2)}) %collective-permute-start.11) | collective-permute-done | bytes 1572896 | tf_op jit(solution)/shard_map/ppermute | solution.py:48
  119.9 2.0 %convert_add_fusion = f32[4,4,64,3,256]{4,2,3,1,0:T(8,128)S(1)} fusion(bf16[4,4,64,3,256]{4,2,3,1,0:T(8,128)(2,1)S(1)} %collective-permute-done.11, bf16[4,4,2,64,3,256]{5,3,4,2,1,0:T(8,128)(2,1)} %copy-done.1), kind=kLoop, calls=%fused_computation.25 | loop fusion | flops 2359296 | bytes 6291456 | tf_op jit(solution)/shard_map/add | solution.py:108
  122.0 0.8 collective-permute-start.14
  123.0 1.4 collective-permute-start.12
  124.4 4.6 %collective-permute-done.14 = bf16[4,32,3,256]{3,1,2,0:T(8,128)(2,1)S(1)} collective-permute-done((bf16[4,32,3,256]{3,1,2,0:T(8,128)(2,1)S(1)}, bf16[4,32,3,256]{3,1,2,0:T(8,128)(2,1)S(1)}, u32[]{:S(2)}, u32[]{:S(2)}) %collective-permute-start.14) | collective-permute-done | bytes 196640 | tf_op jit(solution)/shard_map/ppermute | solution.py:48
  129.1 1.0 collective-permute-start.15
  130.6 0.9 collective-permute-start.13
  131.4 1.2 collective-permute-done.20
  132.6 1.6 collective-permute-start.21
  134.3 3.3 %collective-permute-done.21 = f32[7424]{0:T(1024)S(1)} collective-permute-done((f32[7424]{0:T(1024)S(1)}, f32[7424]{0:T(1024)S(1)}, u32[]{:S(2)}, u32[]{:S(2)}) %collective-permute-start.21) | collective-permute-done | bytes 29728 | tf_op jit(solution)/shard_map/ppermute | solution.py:21
  137.5 4.3 %collective-permute-start.22 = (f32[7424]{0:T(1024)S(1)}, f32[7424]{0:T(1024)S(1)}, u32[]{:S(2)}, u32[]{:S(2)}) collective-permute-start(f32[7424]{0:T(1024)S(1)} %add.547), channel_id=1, source_target_pairs={{0,32},{8,40},{16,48},{24,56},{32,0},{40,8},{48,16},{56,24},{64,96... | collective-permute-start | bytes 89096 | tf_op jit(solution)/shard_map/ppermute | solution.py:21
  141.9 3.5 %collective-permute-done.22 = f32[7424]{0:T(1024)S(1)} collective-permute-done((f32[7424]{0:T(1024)S(1)}, f32[7424]{0:T(1024)S(1)}, u32[]{:S(2)}, u32[]{:S(2)}) %collective-permute-start.22) | collective-permute-done | bytes 29728 | tf_op jit(solution)/shard_map/ppermute | solution.py:21
  145.4 2.4 %collective-permute-start.23 = (f32[7424]{0:T(1024)S(1)}, f32[7424]{0:T(1024)S(1)}, u32[]{:S(2)}, u32[]{:S(2)}) collective-permute-start(f32[7424]{0:T(1024)S(1)} %add.548), channel_id=1, source_target_pairs={{0,64},{8,72},{16,80},{24,88},{32,96},{40,104},{48,112},{56,120},{... | collective-permute-start | bytes 89096 | tf_op jit(solution)/shard_map/ppermute | solution.py:21
  148.0 1.5 collective-permute-start.16
  149.6 2.7 %collective-permute-start.18 = (bf16[32,3,256]{2,0,1:T(8,128)(2,1)S(1)}, bf16[32,3,256]{2,0,1:T(8,128)(2,1)S(1)}, u32[]{:S(2)}, u32[]{:S(2)}) collective-permute-start(bf16[32,3,256]{2,0,1:T(8,128)(2,1)S(1)} %get-tuple-element.29), channel_id=1, source_target_pairs={{0,48},{8,56},{16,0},{24,8},{32,16},{40,24},{48,32},{56,40},{64,11... | collective-permute-start | bytes 147464 | tf_op jit(solution)/shard_map/ppermute | solution.py:48
  152.3 2.1 %collective-permute-start.24 = (f32[7424]{0:T(1024)S(1)}, f32[7424]{0:T(1024)S(1)}, u32[]{:S(2)}, u32[]{:S(2)}) collective-permute-start(f32[7424]{0:T(1024)S(1)} %add.549), channel_id=1, source_target_pairs={{0,128},{8,136},{16,144},{24,152},{32,160},{40,168},{48,176},{56,1... | collective-permute-start | bytes 89096 | tf_op jit(solution)/shard_map/ppermute | solution.py:21
  154.3 3.4 %collective-permute-done.24 = f32[7424]{0:T(1024)S(1)} collective-permute-done((f32[7424]{0:T(1024)S(1)}, f32[7424]{0:T(1024)S(1)}, u32[]{:S(2)}, u32[]{:S(2)}) %collective-permute-start.24) | collective-permute-done | bytes 29728 | tf_op jit(solution)/shard_map/ppermute | solution.py:21
  157.8 2.7 %collective-permute-start.25 = (f32[2048]{0:T(1024)S(1)}, f32[2048]{0:T(1024)S(1)}, u32[]{:S(2)}, u32[]{:S(2)}) collective-permute-start(f32[2048]{0:T(1024)S(1)} %slice.301), channel_id=1, source_target_pairs={{0,1},{1,0},{2,3},{3,2},{4,5},{5,4},{6,7},{7,6},{8,9},{9,8},{10,11... | collective-permute-start | bytes 24584 | tf_op jit(solution)/shard_map/ppermute | solution.py:21
  160.6 1.8 collective-permute-start.19
  162.4 1.2 collective-permute-start.17
  163.7 0.8 collective-permute-start.26
  164.5 4.4 %collective-permute-done.26 = f32[2048]{0:T(1024)S(1)} collective-permute-done((f32[2048]{0:T(1024)S(1)}, f32[2048]{0:T(1024)S(1)}, u32[]{:S(2)}, u32[]{:S(2)}) %collective-permute-start.26) | collective-permute-done | bytes 8224 | tf_op jit(solution)/shard_map/ppermute | solution.py:21
  168.9 1.9 %collective-permute-start.27 = (f32[2048]{0:T(1024)S(1)}, f32[2048]{0:T(1024)S(1)}, u32[]{:S(2)}, u32[]{:S(2)}) collective-permute-start(f32[2048]{0:T(1024)S(1)} %add.552), channel_id=1, source_target_pairs={{0,4},{1,5},{2,6},{3,7},{4,0},{5,1},{6,2},{7,3},{8,12},{9,13},{10,... | collective-permute-start | bytes 24584 | tf_op jit(solution)/shard_map/ppermute | solution.py:21
  171.4 1.1 collective-permute-done.27
  173.8 1.4 fusion.16
  175.2 2.2 %fusion.21 = bf16[128,2048]{1,0:T(8,128)(2,1)} fusion(bf16[128,2048]{1,0:T(8,128)(2,1)S(1)} %copy-done.2, bf16[128,2048]{1,0:T(8,128)(2,1)} %reduce-scatter.2.cloned.1.call-done, f32[128]{0:T(128)S(1)} %broadcast_multiply_fusion, f32[2048]{0:T(1024)S(1)} %copy-done.5, f32[128]{0:T(128)S(1)} %add_rsqrt_fusion), kind=kLoop, calls=%fused_computation.52 | loop fusion | flops 2359296 | bytes 1582080 | tf_op jit(solution)/shard_map/convert_element_type | solution.py:181
  (95 shorter events, 7.4 us)
Async XLA Ops:
  7.2 62.5 %all-gather.2.cloned.1.call-start = ((), (), s32[]{:S(2)}) async-start(), calls=%async_computation.1 | async-start | bytes 3244032 | tf_op jit(solution)/shard_map/all_gather | solution.py:121
  7.9 165.9 %reduce-scatter.2.cloned.1.call-start = ((), (), s32[]{:S(2)}) async-start(), calls=%async_computation.2 | async-start | bytes 4718592 | tf_op jit(solution)/shard_map/reduce_scatter | solution.py:163
  7.9 14.0 %collective-permute-start = (bf16[128,2048]{1,0:T(8,128)(2,1)}, bf16[128,2048]{1,0:T(8,128)(2,1)S(1)}, u32[]{:S(2)}, u32[]{:S(2)}) collective-permute-start(bf16[128,2048]{1,0:T(8,128)(2,1)} %param.5), channel_id=1, source_target_pairs={{0,3},{1,0},{2,1},{3,2},{4,7},{5,4},{6,5},{7,6},{8,11},{9,8},{10,9... | collective-permute-start | bytes 1572872 | tf_op jit(solution)/shard_map/ppermute | solution.py:48
  8.6 14.6 %collective-permute-start.1 = (bf16[128,2048]{1,0:T(8,128)(2,1)}, bf16[128,2048]{1,0:T(8,128)(2,1)S(1)}, u32[]{:S(2)}, u32[]{:S(2)}) collective-permute-start(bf16[128,2048]{1,0:T(8,128)(2,1)} %param.5), channel_id=1, source_target_pairs={{0,1},{1,2},{2,3},{3,0},{4,5},{5,6},{6,7},{7,4},{8,9},{9,10},{10,1... | collective-permute-start | bytes 1572872 | tf_op jit(solution)/shard_map/ppermute | solution.py:48
  10.1 14.1 %collective-permute-start.4 = (bf16[128,2048]{1,0:T(8,128)(2,1)}, bf16[128,2048]{1,0:T(8,128)(2,1)S(1)}, u32[]{:S(2)}, u32[]{:S(2)}) collective-permute-start(bf16[128,2048]{1,0:T(8,128)(2,1)} %param.5), channel_id=1, source_target_pairs={{0,4},{1,5},{2,6},{3,7},{4,0},{5,1},{6,2},{7,3},{8,12},{9,13},{10,... | collective-permute-start | bytes 1572872 | tf_op jit(solution)/shard_map/ppermute | solution.py:48
  21.9 9.3 %collective-permute-start.3 = (bf16[64,2048]{1,0:T(8,128)(2,1)S(1)}, bf16[64,2048]{1,0:T(8,128)(2,1)S(1)}, u32[]{:S(2)}, u32[]{:S(2)}) collective-permute-start(bf16[64,2048]{1,0:T(8,128)(2,1)S(1)} %slice.260), channel_id=1, source_target_pairs={{0,3},{1,0},{2,1},{3,2},{4,7},{5,4},{6,5},{7,6},{8,11},{9,8},{10,9... | collective-permute-start | bytes 786440 | tf_op jit(solution)/shard_map/ppermute | solution.py:48
  23.2 10.6 %collective-permute-start.2 = (bf16[64,2048]{1,0:T(8,128)(2,1)S(1)}, bf16[64,2048]{1,0:T(8,128)(2,1)S(1)}, u32[]{:S(2)}, u32[]{:S(2)}) collective-permute-start(bf16[64,2048]{1,0:T(8,128)(2,1)S(1)} %slice.259), channel_id=1, source_target_pairs={{0,1},{1,2},{2,3},{3,0},{4,5},{5,6},{6,7},{7,4},{8,9},{9,10},{10,1... | collective-permute-start | bytes 786440 | tf_op jit(solution)/shard_map/ppermute | solution.py:48
  24.1 16.3 %collective-permute-start.5 = (bf16[128,2048]{1,0:T(8,128)(2,1)S(1)}, bf16[128,2048]{1,0:T(8,128)(2,1)S(1)}, u32[]{:S(2)}, u32[]{:S(2)}) collective-permute-start(bf16[128,2048]{1,0:T(8,128)(2,1)S(1)} %collective-permute-done.4), channel_id=1, source_target_pairs={{0,3},{1,0},{2,1},{3,2},{4,7},{5,4},{6,5},{7,6},{8,11},{9,8},{10,9... | collective-permute-start | bytes 1572872 | tf_op jit(solution)/shard_map/ppermute | solution.py:48
  26.7 16.3 %collective-permute-start.6 = (bf16[128,2048]{1,0:T(8,128)(2,1)S(1)}, bf16[128,2048]{1,0:T(8,128)(2,1)S(1)}, u32[]{:S(2)}, u32[]{:S(2)}) collective-permute-start(bf16[128,2048]{1,0:T(8,128)(2,1)S(1)} %collective-permute-done.4), channel_id=1, source_target_pairs={{0,1},{1,2},{2,3},{3,0},{4,5},{5,6},{6,7},{7,4},{8,9},{9,10},{10,1... | collective-permute-start | bytes 1572872 | tf_op jit(solution)/shard_map/ppermute | solution.py:48
  40.4 7.1 %collective-permute-start.8 = (bf16[64,2048]{1,0:T(8,128)(2,1)S(1)}, bf16[64,2048]{1,0:T(8,128)(2,1)S(1)}, u32[]{:S(2)}, u32[]{:S(2)}) collective-permute-start(bf16[64,2048]{1,0:T(8,128)(2,1)S(1)} %slice.262), channel_id=1, source_target_pairs={{0,3},{1,0},{2,1},{3,2},{4,7},{5,4},{6,5},{7,6},{8,11},{9,8},{10,9... | collective-permute-start | bytes 786440 | tf_op jit(solution)/shard_map/ppermute | solution.py:48
  43.0 7.7 %collective-permute-start.7 = (bf16[64,2048]{1,0:T(8,128)(2,1)S(1)}, bf16[64,2048]{1,0:T(8,128)(2,1)S(1)}, u32[]{:S(2)}, u32[]{:S(2)}) collective-permute-start(bf16[64,2048]{1,0:T(8,128)(2,1)S(1)} %slice.261), channel_id=1, source_target_pairs={{0,1},{1,2},{2,3},{3,0},{4,5},{5,6},{6,7},{7,4},{8,9},{9,10},{10,1... | collective-permute-start | bytes 786440 | tf_op jit(solution)/shard_map/ppermute | solution.py:48
  57.4 3.7 %copy-start = (bf16[8,128,2048]{2,1,0:T(8,128)(2,1)S(1)}, bf16[8,128,2048]{2,1,0:T(8,128)(2,1)}, u32[]{:S(2)}) copy-start(bf16[8,128,2048]{2,1,0:T(8,128)(2,1)} %gather_fusion) | copy-start | bytes 12582916
  61.1 8.6 %copy-start.5 = (f32[2048]{0:T(1024)S(1)}, f32[2048]{0:T(1024)}, u32[]{:S(2)}) copy-start(f32[2048]{0:T(1024)} %param.6) | copy-start | bytes 24580
  76.3 8.2 %collective-permute-start.9 = (bf16[6,3,256]{2,0,1:T(8,128)(2,1)S(1)}, bf16[6,3,256]{2,0,1:T(8,128)(2,1)S(1)}, u32[]{:S(2)}, u32[]{:S(2)}) collective-permute-start(bf16[6,3,256]{2,0,1:T(8,128)(2,1)S(1)} %slice.263), channel_id=1, source_target_pairs={{0,8},{8,16},{16,24},{24,32},{32,40},{40,48},{48,56},{56,64},{64,7... | collective-permute-start | bytes 27656 | tf_op jit(solution)/shard_map/ppermute | solution.py:13
  84.8 2.6 %copy-start.4 = (bf16[1024,256]{1,0:T(8,128)(2,1)S(1)}, bf16[1024,256]{1,0:T(8,128)(2,1)}, u32[]{:S(2)}) copy-start(bf16[1024,256]{1,0:T(8,128)(2,1)} %param.9) | copy-start | bytes 1572868
  91.4 3.4 %collective-permute-start.10 = (f32[6,3,256]{2,0,1:T(8,128)S(1)}, f32[6,3,256]{2,0,1:T(8,128)S(1)}, u32[]{:S(2)}, u32[]{:S(2)}) collective-permute-start(f32[6,3,256]{2,0,1:T(8,128)S(1)} %slice.274), channel_id=1, source_target_pairs={{8,0},{16,8},{24,16},{32,24},{40,32},{48,40},{56,48},{64,56},{72,6... | collective-permute-start | bytes 55304 | tf_op jit(solution)/shard_map/ppermute | solution.py:13
  95.0 2.7 %copy-start.3 = (bf16[1024,2048]{1,0:T(8,128)(2,1)S(1)}, bf16[1024,2048]{1,0:T(8,128)(2,1)}, u32[]{:S(2)}) copy-start(bf16[1024,2048]{1,0:T(8,128)(2,1)} %bitcast_select_fusion) | copy-start | bytes 12582916
  95.1 3.2 %copy-start.6 = (bf16[2048,3,256]{2,0,1:T(8,128)(2,1)S(1)}, bf16[2048,3,256]{2,0,1:T(8,128)(2,1)}, u32[]{:S(2)}) copy-start(bf16[2048,3,256]{2,0,1:T(8,128)(2,1)} %all-gather.2.cloned.1.call-done) | copy-start | bytes 9437188
  114.4 1.7 copy-start.1
  116.2 3.7 %collective-permute-start.11 = (bf16[4,4,64,3,256]{4,2,3,1,0:T(8,128)(2,1)S(1)}, bf16[4,4,64,3,256]{4,2,3,1,0:T(8,128)(2,1)S(1)}, u32[]{:S(2)}, u32[]{:S(2)}) collective-permute-start(bf16[4,4,64,3,256]{4,2,3,1,0:T(8,128)(2,1)S(1)} %slice_bitcast_fusion), channel_id=1, source_target_pairs={{0,8},{8,0},{16,24},{24,16},{32,40},{40,32},{48,56},{56,48},{64,72... | collective-permute-start | bytes 4718600 | tf_op jit(solution)/shard_map/ppermute | solution.py:48
  122.0 7.0 %collective-permute-start.14 = (bf16[4,32,3,256]{3,1,2,0:T(8,128)(2,1)S(1)}, bf16[4,32,3,256]{3,1,2,0:T(8,128)(2,1)S(1)}, u32[]{:S(2)}, u32[]{:S(2)}) collective-permute-start(bf16[4,32,3,256]{3,1,2,0:T(8,128)(2,1)S(1)} %get-tuple-element.33), channel_id=1, source_target_pairs={{0,192},{8,200},{16,208},{24,216},{32,224},{40,232},{48,240},{56,2... | collective-permute-start | bytes 589832 | tf_op jit(solution)/shard_map/ppermute | solution.py:48
  123.0 7.5 %collective-permute-start.12 = (bf16[4,32,3,256]{3,1,2,0:T(8,128)(2,1)S(1)}, bf16[4,32,3,256]{3,1,2,0:T(8,128)(2,1)S(1)}, u32[]{:S(2)}, u32[]{:S(2)}) collective-permute-start(bf16[4,32,3,256]{3,1,2,0:T(8,128)(2,1)S(1)} %get-tuple-element.32), channel_id=1, source_target_pairs={{0,64},{8,72},{16,80},{24,88},{32,96},{40,104},{48,112},{56,120},{... | collective-permute-start | bytes 589832 | tf_op jit(solution)/shard_map/ppermute | solution.py:48
  129.1 18.7 %collective-permute-start.15 = (bf16[4,64,3,256]{3,1,2,0:T(8,128)(2,1)S(1)}, bf16[4,64,3,256]{3,1,2,0:T(8,128)(2,1)S(1)}, u32[]{:S(2)}, u32[]{:S(2)}) collective-permute-start(bf16[4,64,3,256]{3,1,2,0:T(8,128)(2,1)S(1)} %pad_maximum_fusion.3), channel_id=1, source_target_pairs={{0,192},{8,200},{16,208},{24,216},{32,224},{40,232},{48,240},{56,2... | collective-permute-start | bytes 1179656 | tf_op jit(solution)/shard_map/ppermute | solution.py:48
  130.5 43.3 %copy-start.2 = (bf16[128,2048]{1,0:T(8,128)(2,1)S(1)}, bf16[128,2048]{1,0:T(8,128)(2,1)}, u32[]{:S(2)}) copy-start(bf16[128,2048]{1,0:T(8,128)(2,1)} %param.5) | copy-start | bytes 1572868
  130.6 17.3 %collective-permute-start.13 = (bf16[4,64,3,256]{3,1,2,0:T(8,128)(2,1)S(1)}, bf16[4,64,3,256]{3,1,2,0:T(8,128)(2,1)S(1)}, u32[]{:S(2)}, u32[]{:S(2)}) collective-permute-start(bf16[4,64,3,256]{3,1,2,0:T(8,128)(2,1)S(1)} %pad_maximum_fusion.2), channel_id=1, source_target_pairs={{0,64},{8,72},{16,80},{24,88},{32,96},{40,104},{48,112},{56,120},{... | collective-permute-start | bytes 1179656 | tf_op jit(solution)/shard_map/ppermute | solution.py:48
  131.4 1.2 collective-permute-start.20
  132.6 4.9 %collective-permute-start.21 = (f32[7424]{0:T(1024)S(1)}, f32[7424]{0:T(1024)S(1)}, u32[]{:S(2)}, u32[]{:S(2)}) collective-permute-start(f32[7424]{0:T(1024)S(1)} %fusion.77), channel_id=1, source_target_pairs={{0,16},{8,24},{16,0},{24,8},{32,48},{40,56},{48,32},{56,40},{64,80... | collective-permute-start | bytes 89096 | tf_op jit(solution)/shard_map/ppermute | solution.py:21
  137.5 7.8 %collective-permute-start.22 = (f32[7424]{0:T(1024)S(1)}, f32[7424]{0:T(1024)S(1)}, u32[]{:S(2)}, u32[]{:S(2)}) collective-permute-start(f32[7424]{0:T(1024)S(1)} %add.547), channel_id=1, source_target_pairs={{0,32},{8,40},{16,48},{24,56},{32,0},{40,8},{48,16},{56,24},{64,96... | collective-permute-start | bytes 89096 | tf_op jit(solution)/shard_map/ppermute | solution.py:21
  145.4 6.9 %collective-permute-start.23 = (f32[7424]{0:T(1024)S(1)}, f32[7424]{0:T(1024)S(1)}, u32[]{:S(2)}, u32[]{:S(2)}) collective-permute-start(f32[7424]{0:T(1024)S(1)} %add.548), channel_id=1, source_target_pairs={{0,64},{8,72},{16,80},{24,88},{32,96},{40,104},{48,112},{56,120},{... | collective-permute-start | bytes 89096 | tf_op jit(solution)/shard_map/ppermute | solution.py:21
  148.0 12.5 %collective-permute-start.16 = (bf16[32,3,256]{2,0,1:T(8,128)(2,1)S(1)}, bf16[32,3,256]{2,0,1:T(8,128)(2,1)S(1)}, u32[]{:S(2)}, u32[]{:S(2)}) collective-permute-start(bf16[32,3,256]{2,0,1:T(8,128)(2,1)S(1)} %get-tuple-element.28), channel_id=1, source_target_pairs={{0,16},{8,24},{16,32},{24,40},{32,48},{40,56},{48,0},{56,8},{64,80... | collective-permute-start | bytes 147464 | tf_op jit(solution)/shard_map/ppermute | solution.py:48
  149.6 10.9 %collective-permute-start.18 = (bf16[32,3,256]{2,0,1:T(8,128)(2,1)S(1)}, bf16[32,3,256]{2,0,1:T(8,128)(2,1)S(1)}, u32[]{:S(2)}, u32[]{:S(2)}) collective-permute-start(bf16[32,3,256]{2,0,1:T(8,128)(2,1)S(1)} %get-tuple-element.29), channel_id=1, source_target_pairs={{0,48},{8,56},{16,0},{24,8},{32,16},{40,24},{48,32},{56,40},{64,11... | collective-permute-start | bytes 147464 | tf_op jit(solution)/shard_map/ppermute | solution.py:48
  152.3 5.5 %collective-permute-start.24 = (f32[7424]{0:T(1024)S(1)}, f32[7424]{0:T(1024)S(1)}, u32[]{:S(2)}, u32[]{:S(2)}) collective-permute-start(f32[7424]{0:T(1024)S(1)} %add.549), channel_id=1, source_target_pairs={{0,128},{8,136},{16,144},{24,152},{32,160},{40,168},{48,176},{56,1... | collective-permute-start | bytes 89096 | tf_op jit(solution)/shard_map/ppermute | solution.py:21
  157.8 5.9 %collective-permute-start.25 = (f32[2048]{0:T(1024)S(1)}, f32[2048]{0:T(1024)S(1)}, u32[]{:S(2)}, u32[]{:S(2)}) collective-permute-start(f32[2048]{0:T(1024)S(1)} %slice.301), channel_id=1, source_target_pairs={{0,1},{1,0},{2,3},{3,2},{4,5},{5,4},{6,7},{7,6},{8,9},{9,8},{10,11... | collective-permute-start | bytes 24584 | tf_op jit(solution)/shard_map/ppermute | solution.py:21
  160.6 12.6 %collective-permute-start.19 = (bf16[64,3,256]{2,0,1:T(8,128)(2,1)S(1)}, bf16[64,3,256]{2,0,1:T(8,128)(2,1)S(1)}, u32[]{:S(2)}, u32[]{:S(2)}) collective-permute-start(bf16[64,3,256]{2,0,1:T(8,128)(2,1)S(1)} %pad_maximum_fusion.5), channel_id=1, source_target_pairs={{0,48},{8,56},{16,0},{24,8},{32,16},{40,24},{48,32},{56,40},{64,11... | collective-permute-start | bytes 294920 | tf_op jit(solution)/shard_map/ppermute | solution.py:48
  162.4 10.8 %collective-permute-start.17 = (bf16[64,3,256]{2,0,1:T(8,128)(2,1)S(1)}, bf16[64,3,256]{2,0,1:T(8,128)(2,1)S(1)}, u32[]{:S(2)}, u32[]{:S(2)}) collective-permute-start(bf16[64,3,256]{2,0,1:T(8,128)(2,1)S(1)} %pad_maximum_fusion.4), channel_id=1, source_target_pairs={{0,16},{8,24},{16,32},{24,40},{32,48},{40,56},{48,0},{56,8},{64,80... | collective-permute-start | bytes 294920 | tf_op jit(solution)/shard_map/ppermute | solution.py:48
  163.7 5.2 %collective-permute-start.26 = (f32[2048]{0:T(1024)S(1)}, f32[2048]{0:T(1024)S(1)}, u32[]{:S(2)}, u32[]{:S(2)}) collective-permute-start(f32[2048]{0:T(1024)S(1)} %slice_add_fusion.2), channel_id=1, source_target_pairs={{0,2},{1,3},{2,0},{3,1},{4,6},{5,7},{6,4},{7,5},{8,10},{9,11},{10,... | collective-permute-start | bytes 24584 | tf_op jit(solution)/shard_map/ppermute | solution.py:21
  168.9 3.7 %collective-permute-start.27 = (f32[2048]{0:T(1024)S(1)}, f32[2048]{0:T(1024)S(1)}, u32[]{:S(2)}, u32[]{:S(2)}) collective-permute-start(f32[2048]{0:T(1024)S(1)} %add.552), channel_id=1, source_target_pairs={{0,4},{1,5},{2,6},{3,7},{4,0},{5,1},{6,2},{7,3},{8,12},{9,13},{10,... | collective-permute-start | bytes 24584 | tf_op jit(solution)/shard_map/ppermute | solution.py:21
Sparse Core Ops, SparseCore 0:
  10.7 58.9 all-gather.1
  103.5 55.9 reduce-scatter.1
where the time goes:
time: 186 us; the launch traced here: 184 us
  waiting for transfers between devices  63.6 us (34%)
  starting transfers between devices  42.6 us (23%)
  other arithmetic  25.7 us (14%)
  matrix products  19.6 us (11%)
  local copies, waits for them, and re-layouts  18.2 us (10%)
  between operations  14.6 us (8%)
    ppermute x18, waiting for transfers between devices, move(): return lax.ppermute(value, axis, pairs)  32.8 us
    ppermute x18, starting transfers between devices, move(): return lax.ppermute(value, axis, pairs)  22.3 us
    ppermute x8, waiting for transfers between devices, butterfly_sum(): value = value + lax.ppermute(value, axis, pairs)  16.9 us
    ppermute x8, starting transfers between devices, butterfly_sum(): value = value + lax.ppermute(value, axis, pairs)  15.9 us
    dot_general x1, matrix products, body(): jnp.einsum('td,tsc->dsc', positions, grad_streams, preferred_element_type...  7.78 us
    unnamed x23, local copies, waits for them, and re-layouts  7.43 us
    ppermute x2, waiting for transfers between devices, passed_along(): return lax.ppermute(shard, axis, pairs)  7.26 us
    dot_general x1, matrix products, body(): jnp.einsum('td,dsc->tsc', positions, weights, preferred_element_type=jnp....  6.63 us
  transfers between devices with their start and end apart: 30, of which 20 were waited for; matrix products, arithmetic and copies ran while one was open for 20% of the time, Pallas kernels for 0%

commit v1 on v0

--- a/solution.py
+++ b/solution.py
@@ -82,6 +82,13 @@
     )
 
 
+def ring_scatter_direct(shard, move):
+    total = shard[0]
+    for k, by in ((1, 1), (2, 2), (3, -1)):
+        total = total + move(shard[k].astype(jnp.bfloat16), by).astype(jnp.float32)
+    return total
+
+
 def slot_tables(axis, split):
     me = digits(lax.axis_index(axis), split)
     total = 1
@@ -106,8 +113,8 @@
     across_core = mover("dp", DP_SPLIT, 2)
     grid = blocks.reshape(DP_SPLIT + blocks.shape[1:])
     summed = grid[:, :, 0].astype(jnp.float32) + across_core(grid[:, :, 1], 1).astype(jnp.float32)
-    column = ring_scatter([summed[k] for k in range(DP_SPLIT[0])], along_y, 1)
-    return ring_scatter([column[k] for k in range(DP_SPLIT[1])], along_h, 0)
+    column = ring_scatter_direct([summed[k] for k in range(DP_SPLIT[0])], along_y)
+    return ring_scatter_direct([column[k] for k in range(DP_SPLIT[1])], along_h)
 
 
 def body(inputs, norm_gain, proj_weight, filters, cotangent):

time: 186 us -> 182 us (0.978)
  starting transfers between devices: 42.6 us -> 37.5 us
    ppermute x8, waiting for transfers between devices: 16.9 us -> 23.5 us  [butterfly_sum(): value = value + lax.ppermute(value, axis, pairs)]
    ppermute x8, starting transfers between devices: 15.9 us -> 10.5 us  [butterfly_sum(): value = value + lax.ppermute(value, axis, pairs)]
    ppermute x18 -> x16, waiting for transfers between devices: 32.8 us -> 27.9 us  [move(): return lax.ppermute(value, axis, pairs)]
    ppermute x18 -> x16, starting transfers between devices: 22.3 us -> 22.6 us  [move(): return lax.ppermute(value, axis, pairs)]
  transfers between devices with their start and end apart: 30 -> 28, of which waited for: 20 -> 19; matrix products, arithmetic and copies ran while one was open for 20% -> 20% of each run, Pallas kernels for 0% -> 0%
where the time goes in v1:
time: 182 us; the launch traced here: 181 us
  waiting for transfers between devices  65.3 us (36%)
  starting transfers between devices  37.5 us (21%)
  other arithmetic  25.7 us (14%)
  matrix products  19.6 us (11%)
  local copies, waits for them, and re-layouts  17.9 us (10%)
  between operations  14.5 us (8%)
    ppermute x16, waiting for transfers between devices, move(): return lax.ppermute(value, axis, pairs)  27.9 us
    ppermute x8, waiting for transfers between devices, butterfly_sum(): value = value + lax.ppermute(value, axis, pairs)  23.5 us
    ppermute x16, starting transfers between devices, move(): return lax.ppermute(value, axis, pairs)  22.6 us
    ppermute x8, starting transfers between devices, butterfly_sum(): value = value + lax.ppermute(value, axis, pairs)  10.5 us
    dot_general x1, matrix products, body(): jnp.einsum('td,tsc->dsc', positions, grad_streams, preferred_element_type...  7.78 us
    unnamed x23, local copies, waits for them, and re-layouts  7.42 us
    ppermute x2, waiting for transfers between devices, passed_along(): return lax.ppermute(shard, axis, pairs)  7.26 us
    dot_general x1, matrix products, body(): jnp.einsum('td,dsc->tsc', positions, weights, preferred_element_type=jnp....  6.63 us
  transfers between devices with their start and end apart: 28, of which 19 were waited for; matrix products, arithmetic and copies ran while one was open for 20% of the time, Pallas kernels for 0%

profile of v1, /device:TPU:10, one launch (start us, length us, event | category | flops | bytes accessed | tf_op | source)
XLA Modules:
  0.0 180.5 jit_solution(15234957696047091869)
XLA Ops:
  7.2 0.7 all-gather.2.cloned.1.call-update
  7.9 0.6 collective-permute-start
  8.6 1.5 collective-permute-start.1
  10.1 1.9 %collective-permute-start.4 = (bf16[128,2048]{1,0:T(8,128)(2,1)}, bf16[128,2048]{1,0:T(8,128)(2,1)S(1)}, u32[]{:S(2)}, u32[]{:S(2)}) collective-permute-start(bf16[128,2048]{1,0:T(8,128)(2,1)} %param.5), channel_id=1, source_target_pairs={{0,4},{1,5},{2,6},{3,7},{4,0},{5,1},{6,2},{7,3},{8,12},{9,13},{10,... | collective-permute-start | bytes 1572872 | tf_op jit(solution)/shard_map/ppermute | solution.py:48
  12.1 1.0 fusion.76
  13.1 1.9 %bitcast_dynamic-update-slice_fusion.5 = bf16[8,128,2048]{2,1,0:T(8,128)(2,1)} fusion(bf16[128,2048]{1,0:T(8,128)(2,1)} %param.5), kind=kLoop, calls=%fused_computation.74 | loop fusion | bytes 1048576
  15.0 6.9 %collective-permute-done = bf16[128,2048]{1,0:T(8,128)(2,1)S(1)} collective-permute-done((bf16[128,2048]{1,0:T(8,128)(2,1)}, bf16[128,2048]{1,0:T(8,128)(2,1)S(1)}, u32[]{:S(2)}, u32[]{:S(2)}) %collective-permute-start) | collective-permute-done | bytes 524320 | tf_op jit(solution)/shard_map/ppermute | solution.py:48
  21.9 1.0 collective-permute-start.3
  23.2 0.9 collective-permute-start.2
  24.1 2.6 %collective-permute-start.5 = (bf16[128,2048]{1,0:T(8,128)(2,1)S(1)}, bf16[128,2048]{1,0:T(8,128)(2,1)S(1)}, u32[]{:S(2)}, u32[]{:S(2)}) collective-permute-start(bf16[128,2048]{1,0:T(8,128)(2,1)S(1)} %collective-permute-done.4), channel_id=1, source_target_pairs={{0,3},{1,0},{2,1},{3,2},{4,7},{5,4},{6,5},{7,6},{8,11},{9,8},{10,9... | collective-permute-start | bytes 1572872 | tf_op jit(solution)/shard_map/ppermute | solution.py:48
  26.7 0.8 bitcast_dynamic-update-slice_fusion.4
  27.5 3.7 %collective-permute-done.3 = bf16[64,2048]{1,0:T(8,128)(2,1)S(1)} collective-permute-done((bf16[64,2048]{1,0:T(8,128)(2,1)S(1)}, bf16[64,2048]{1,0:T(8,128)(2,1)S(1)}, u32[]{:S(2)}, u32[]{:S(2)}) %collective-permute-start.3) | collective-permute-done | bytes 262176 | tf_op jit(solution)/shard_map/ppermute | solution.py:48
  31.2 2.6 %collective-permute-done.2 = bf16[64,2048]{1,0:T(8,128)(2,1)S(1)} collective-permute-done((bf16[64,2048]{1,0:T(8,128)(2,1)S(1)}, bf16[64,2048]{1,0:T(8,128)(2,1)S(1)}, u32[]{:S(2)}, u32[]{:S(2)}) %collective-permute-start.2) | collective-permute-done | bytes 262176 | tf_op jit(solution)/shard_map/ppermute | solution.py:48
  33.8 0.9 fusion.26
  34.7 0.8 bitcast_dynamic-update-slice_fusion.3
  35.6 0.8 bitcast_dynamic-update-slice_fusion.2
  36.4 4.0 %collective-permute-done.5 = bf16[128,2048]{1,0:T(8,128)(2,1)S(1)} collective-permute-done((bf16[128,2048]{1,0:T(8,128)(2,1)S(1)}, bf16[128,2048]{1,0:T(8,128)(2,1)S(1)}, u32[]{:S(2)}, u32[]{:S(2)}) %collective-permute-start.5) | collective-permute-done | bytes 524320 | tf_op jit(solution)/shard_map/ppermute | solution.py:48
  40.4 2.1 %collective-permute-start.8 = (bf16[64,2048]{1,0:T(8,128)(2,1)S(1)}, bf16[64,2048]{1,0:T(8,128)(2,1)S(1)}, u32[]{:S(2)}, u32[]{:S(2)}) collective-permute-start(bf16[64,2048]{1,0:T(8,128)(2,1)S(1)} %slice.197), channel_id=1, source_target_pairs={{0,3},{1,0},{2,1},{3,2},{4,7},{5,4},{6,5},{7,6},{8,11},{9,8},{10,9... | collective-permute-start | bytes 786440 | tf_op jit(solution)/shard_map/ppermute | solution.py:48
  43.1 0.9 bitcast_dynamic-update-slice_fusion.1
  44.0 3.6 %collective-permute-done.8 = bf16[64,2048]{1,0:T(8,128)(2,1)S(1)} collective-permute-done((bf16[64,2048]{1,0:T(8,128)(2,1)S(1)}, bf16[64,2048]{1,0:T(8,128)(2,1)S(1)}, u32[]{:S(2)}, u32[]{:S(2)}) %collective-permute-start.8) | collective-permute-done | bytes 262176 | tf_op jit(solution)/shard_map/ppermute | solution.py:48
  47.6 3.1 %collective-permute-done.7 = bf16[64,2048]{1,0:T(8,128)(2,1)S(1)} collective-permute-done((bf16[64,2048]{1,0:T(8,128)(2,1)S(1)}, bf16[64,2048]{1,0:T(8,128)(2,1)S(1)}, u32[]{:S(2)}, u32[]{:S(2)}) %collective-permute-start.7) | collective-permute-done | bytes 262176 | tf_op jit(solution)/shard_map/ppermute | solution.py:48
  50.7 0.8 fusion.27
  51.5 0.8 bitcast_dynamic-update-slice_fusion
  52.4 5.0 %gather_fusion = bf16[8,128,2048]{2,1,0:T(8,128)(2,1)} fusion(bf16[8,128,2048]{2,1,0:T(8,128)(2,1)} %bitcast_dynamic-update-slice_fusion, s32[1024]{0:T(1024)S(1)} %pad_clamp_fusion.1), kind=kCustom, calls=%fused_computation | custom fusion | bytes 8388640 | tf_op jit(solution)/shard_map/jit(_take)/gather | solution.py:129
  57.3 3.7 %multiply_reduce_fusion.1 = f32[8,128]{1,0:T(8,128)S(1)} fusion(bf16[8,128,2048]{2,1,0:T(8,128)(2,1)} %gather_fusion, pred[8]{0:T(512)(128)(4,1)S(1)} %compare_and_fusion.1), kind=kLoop, calls=%fused_computation.5 | loop fusion | flops 8387584 | bytes 4198408 | tf_op jit(solution)/shard_map/reduce_sum | solution.py:131
  61.1 2.7 %bitcast_select_fusion = bf16[1024,2048]{1,0:T(8,128)(2,1)} fusion(bf16[8,128,2048]{2,1,0:T(8,128)(2,1)S(1)} %copy-done, pred[1024]{0:T(1024)(128)(4,1)S(1)} %broadcast_bitcast_fusion), kind=kLoop, calls=%fused_computation.8 | loop fusion | flops 2097152 | bytes 8389632 | tf_op jit(solution)/shard_map/jit(_take)/select_n | solution.py:129
  63.8 5.9 %all-gather.2.cloned.1.call-done = bf16[2048,3,256]{2,0,1:T(8,128)(2,1)} async-done(((bf16[64,3,256]{2,0,1:T(8,128)(2,1)}), bf16[2048,3,256]{2,0,1:T(8,128)(2,1)}) %all-gather.2.cloned.1.call-update) | async-done | bytes 3145744 | tf_op jit(solution)/shard_map/all_gather | solution.py:128
  69.6 6.6 %fusion.11 = bf16[1024,3,256]{2,0,1:T(8,128)(2,1)S(1)} fusion(bf16[2048,3,256]{2,0,1:T(8,128)(2,1)} %all-gather.2.cloned.1.call-done, bf16[1024,2048]{1,0:T(8,128)(2,1)} %bitcast_select_fusion, f32[2048]{0:T(1024)S(1)} %copy-done.5, f32[1024]{0:T(1024)S(1)} %rsqrt_bitcast_fusion), kind=kOutput, calls=%fused_computation.36 | convolution fusion | flops 3230400512 | bytes 8925184 | tf_op jit(solution)/shard_map/td,dsc->tsc/dot_general | solution.py:135
  76.3 2.4 %collective-permute-start.9 = (bf16[6,3,256]{2,0,1:T(8,128)(2,1)S(1)}, bf16[6,3,256]{2,0,1:T(8,128)(2,1)S(1)}, u32[]{:S(2)}, u32[]{:S(2)}) collective-permute-start(bf16[6,3,256]{2,0,1:T(8,128)(2,1)S(1)} %slice.198), channel_id=1, source_target_pairs={{0,8},{8,16},{16,24},{24,32},{32,40},{40,48},{48,56},{56,64},{64,7... | collective-permute-start | bytes 27656 | tf_op jit(solution)/shard_map/ppermute | solution.py:13
  78.7 5.8 %collective-permute-done.9 = bf16[6,3,256]{2,0,1:T(8,128)(2,1)S(1)} collective-permute-done((bf16[6,3,256]{2,0,1:T(8,128)(2,1)S(1)}, bf16[6,3,256]{2,0,1:T(8,128)(2,1)S(1)}, u32[]{:S(2)}, u32[]{:S(2)}) %collective-permute-start.9) | collective-permute-done | bytes 9248 | tf_op jit(solution)/shard_map/ppermute | solution.py:13
  84.8 2.6 %multiply_add_fusion = f32[1024,3,256]{2,0,1:T(8,128)S(1)} fusion(f32[1030,3,256]{2,0,1:T(8,128)S(1)} %maximum_convert_fusion, f32[3,256]{1,0:T(4,128)S(1)} %get-tuple-element.41, f32[3,256]{1,0:T(4,128)S(1)} %get-tuple-element.42, f32[3,256]{1,0:T(4,128)S(1)} %get-tuple-element.43, f32[3,256]{1,0:T(4,128)S(1)} %get-tuple-element.44, ...), kind=kLoop, calls=%fused_computation.33 | loop fusion | flops 10223616 | bytes 25187328 | tf_op jit(solution)/shard_map/add | solution.py:142
  87.4 1.2 fusion.15
  88.5 2.9 %multiply_reduce_fusion.2 = (f32[3,256]{1,0:T(4,128)S(1)}, f32[3,256]{1,0:T(4,128)S(1)}, f32[3,256]{1,0:T(4,128)S(1)}, f32[3,256]{1,0:T(4,128)S(1)}, f32[3,256]{...) fusion(f32[1030,3,256]{2,0,1:T(8,128)S(1)} %maximum_convert_fusion, ...), kind=kLoop, calls=%fused_computation.26 | loop fusion | flops 12577536 | bytes 28333056 | tf_op jit(solution)/shard_map/reduce_sum | solution.py:161
  91.4 1.9 %collective-permute-start.10 = (f32[6,3,256]{2,0,1:T(8,128)S(1)}, f32[6,3,256]{2,0,1:T(8,128)S(1)}, u32[]{:S(2)}, u32[]{:S(2)}) collective-permute-start(f32[6,3,256]{2,0,1:T(8,128)S(1)} %slice.209), channel_id=1, source_target_pairs={{8,0},{16,8},{24,16},{32,24},{40,32},{48,40},{56,48},{64,56},{72,6... | collective-permute-start | bytes 55304 | tf_op jit(solution)/shard_map/ppermute | solution.py:13
  93.3 1.5 collective-permute-done.10
  95.1 2.7 %fusion.2 = bf16[1024,3,256]{2,0,1:T(8,128)(2,1)S(1)} fusion(f32[1030,3,256]{2,0,1:T(8,128)S(1)} %pad_maximum_fusion, f32[3,256]{1,0:T(4,128)S(1)} %get-tuple-element.41, f32[3,256]{1,0:T(4,128)S(1)} %get-tuple-element.42, f32[3,256]{1,0:T(4,128)S(1)} %get-tuple-element.43, f32[3,256]{1,0:T(4,128)S(1)} %get-tuple-element.44, ...), kind=kLoop, calls=%fused_computation.13 | loop fusion | flops 12582912 | bytes 23614464 | tf_op jit(solution)/shard_map/convert_element_type | solution.py:158
  98.2 5.2 %multiply_reduce_fusion = (f32[2048]{0:T(1024)S(1)}, bf16[1024,2048]{1,0:T(8,128)(2,1)}) fusion(bf16[1024,2048]{1,0:T(8,128)(2,1)S(1)} %copy-done.3, f32[1024]{0:T(1024)S(1)} %rsqrt_bitcast_fusion, bf16[1024,3,256]{2,0,1:T(8,128)(2,1)S(1)} %fusion.2, bf16[2048,3,256]{2,0,1:T(8,128)(2,1)S(1)} %copy-done.6), kind=kOutput, calls=%fused_computation.3 | convolution fusion | flops 3233806336 | bytes 13119488 | tf_op jit(solution)/shard_map/tsc,dsc->td/dot_general | solution.py:166
  103.6 7.8 %convolution_convert_fusion = bf16[2048,3,256]{2,0,1:T(8,128)(2,1)} fusion(bf16[1024,3,256]{2,0,1:T(8,128)(2,1)S(1)} %fusion.2, bf16[1024,2048]{1,0:T(8,128)(2,1)} %bitcast_select_fusion, f32[2048]{0:T(1024)S(1)} %copy-done.5, f32[1024]{0:T(1024)S(1)} %rsqrt_bitcast_fusion), kind=kOutput, calls=%fused_computation.9 | convolution fusion | flops 3231186944 | bytes 8925184 | tf_op jit(solution)/shard_map/td,tsc->dsc/dot_general | solution.py:173
  111.4 2.6 %gather_fusion.1 = bf16[32,64,3,256]{3,1,2,0:T(8,128)(2,1)S(1)} fusion(bf16[32,64,3,256]{3,1,0,2:T(8,128)(2,1)} %bitcast.135, s32[1024]{0:T(1024)S(1)} %pad_clamp_fusion), kind=kCustom, calls=%fused_computation.1 | custom fusion | bytes 6291584 | tf_op jit(solution)/shard_map/jit(_take)/gather | solution.py:177
  114.4 1.7 copy-done.1
  116.7 3.2 %collective-permute-done.11 = bf16[4,4,64,3,256]{4,2,3,1,0:T(8,128)(2,1)S(1)} collective-permute-done((bf16[4,4,64,3,256]{4,2,3,1,0:T(8,128)(2,1)S(1)}, bf16[4,4,64,3,256]{4,2,3,1,0:T(8,128)(2,1)S(1)}, u32[]{:S(2)}, u32[]{:S(2)}) %collective-permute-start.11) | collective-permute-done | bytes 1572896 | tf_op jit(solution)/shard_map/ppermute | solution.py:48
  119.9 2.1 %convert_add_fusion = (f32[4,4,64,3,256]{4,2,3,1,0:T(8,128)S(1)}, bf16[4,4,64,3,256]{4,2,3,1,0:T(8,128)(2,1)S(1)}) fusion(bf16[4,4,64,3,256]{4,2,3,1,0:T(8,128)(2,1)S(1)} %collective-permute-done.11, bf16[4,4,2,64,3,256]{5,3,4,2,1,0:T(8,128)(2,1)} %copy-done.1), kind=kLoop, calls=%fused_computation.25 | loop fusion | flops 3145728 | bytes 7864320 | tf_op jit(solution)/shard_map/add | solution.py:115
  122.1 0.8 collective-permute-start.14
  122.9 2.2 %collective-permute-start.13 = (bf16[4,64,3,256]{3,1,2,0:T(8,128)(2,1)S(1)}, bf16[4,64,3,256]{3,1,2,0:T(8,128)(2,1)S(1)}, u32[]{:S(2)}, u32[]{:S(2)}) collective-permute-start(bf16[4,64,3,256]{3,1,2,0:T(8,128)(2,1)S(1)} %get-tuple-element.28), channel_id=1, source_target_pairs={{0,128},{8,136},{16,144},{24,152},{32,160},{40,168},{48,176},{56,1... | collective-permute-start | bytes 1179656 | tf_op jit(solution)/shard_map/ppermute | solution.py:48
  125.0 1.8 collective-permute-start.12
  126.8 1.2 collective-permute-done.18
  128.1 1.2 collective-permute-start.19
  129.2 3.7 %collective-permute-done.19 = f32[7424]{0:T(1024)S(1)} collective-permute-done((f32[7424]{0:T(1024)S(1)}, f32[7424]{0:T(1024)S(1)}, u32[]{:S(2)}, u32[]{:S(2)}) %collective-permute-start.19) | collective-permute-done | bytes 29728 | tf_op jit(solution)/shard_map/ppermute | solution.py:21
  133.0 3.7 %collective-permute-start.20 = (f32[7424]{0:T(1024)S(1)}, f32[7424]{0:T(1024)S(1)}, u32[]{:S(2)}, u32[]{:S(2)}) collective-permute-start(f32[7424]{0:T(1024)S(1)} %add.539), channel_id=1, source_target_pairs={{0,32},{8,40},{16,48},{24,56},{32,0},{40,8},{48,16},{56,24},{64,96... | collective-permute-start | bytes 89096 | tf_op jit(solution)/shard_map/ppermute | solution.py:21
  136.7 4.1 %collective-permute-done.20 = f32[7424]{0:T(1024)S(1)} collective-permute-done((f32[7424]{0:T(1024)S(1)}, f32[7424]{0:T(1024)S(1)}, u32[]{:S(2)}, u32[]{:S(2)}) %collective-permute-start.20) | collective-permute-done | bytes 29728 | tf_op jit(solution)/shard_map/ppermute | solution.py:21
  141.0 3.7 %collective-permute-done.21 = f32[7424]{0:T(1024)S(1)} collective-permute-done((f32[7424]{0:T(1024)S(1)}, f32[7424]{0:T(1024)S(1)}, u32[]{:S(2)}, u32[]{:S(2)}) %collective-permute-start.21) | collective-permute-done | bytes 29728 | tf_op jit(solution)/shard_map/ppermute | solution.py:21
  144.7 1.6 collective-permute-start.22
  146.3 3.8 %collective-permute-done.22 = f32[7424]{0:T(1024)S(1)} collective-permute-done((f32[7424]{0:T(1024)S(1)}, f32[7424]{0:T(1024)S(1)}, u32[]{:S(2)}, u32[]{:S(2)}) %collective-permute-start.22) | collective-permute-done | bytes 29728 | tf_op jit(solution)/shard_map/ppermute | solution.py:21
  150.2 2.5 %collective-permute-start.23 = (f32[2048]{0:T(1024)S(1)}, f32[2048]{0:T(1024)S(1)}, u32[]{:S(2)}, u32[]{:S(2)}) collective-permute-start(f32[2048]{0:T(1024)S(1)} %slice.227), channel_id=1, source_target_pairs={{0,1},{1,0},{2,3},{3,2},{4,5},{5,4},{6,7},{7,6},{8,9},{9,8},{10,11... | collective-permute-start | bytes 24584 | tf_op jit(solution)/shard_map/ppermute | solution.py:21
  153.0 2.9 %collective-permute-start.17 = (bf16[64,3,256]{2,0,1:T(8,128)(2,1)S(1)}, bf16[64,3,256]{2,0,1:T(8,128)(2,1)S(1)}, u32[]{:S(2)}, u32[]{:S(2)}) collective-permute-start(bf16[64,3,256]{2,0,1:T(8,128)(2,1)S(1)} %get-tuple-element.30), channel_id=1, source_target_pairs={{0,48},{8,56},{16,0},{24,8},{32,16},{40,24},{48,32},{56,40},{64,11... | collective-permute-start | bytes 294920 | tf_op jit(solution)/shard_map/ppermute | solution.py:48
  155.9 4.1 %collective-permute-start.16 = (bf16[64,3,256]{2,0,1:T(8,128)(2,1)S(1)}, bf16[64,3,256]{2,0,1:T(8,128)(2,1)S(1)}, u32[]{:S(2)}, u32[]{:S(2)}) collective-permute-start(bf16[64,3,256]{2,0,1:T(8,128)(2,1)S(1)} %get-tuple-element.31), channel_id=1, source_target_pairs={{0,32},{8,40},{16,48},{24,56},{32,0},{40,8},{48,16},{56,24},{64,96... | collective-permute-start | bytes 294920 | tf_op jit(solution)/shard_map/ppermute | solution.py:48
  159.9 0.6 collective-permute-start.24
  160.6 4.6 %collective-permute-done.24 = f32[2048]{0:T(1024)S(1)} collective-permute-done((f32[2048]{0:T(1024)S(1)}, f32[2048]{0:T(1024)S(1)}, u32[]{:S(2)}, u32[]{:S(2)}) %collective-permute-start.24) | collective-permute-done | bytes 8224 | tf_op jit(solution)/shard_map/ppermute | solution.py:21
  165.2 0.6 collective-permute-start.25
  165.8 0.6 reshape.535
  166.4 2.4 %collective-permute-done.25 = f32[2048]{0:T(1024)S(1)} collective-permute-done((f32[2048]{0:T(1024)S(1)}, f32[2048]{0:T(1024)S(1)}, u32[]{:S(2)}, u32[]{:S(2)}) %collective-permute-start.25) | collective-permute-done | bytes 8224 | tf_op jit(solution)/shard_map/ppermute | solution.py:21
  169.5 0.7 fusion.31
  170.1 1.4 fusion.16
  171.5 2.2 %fusion.21 = bf16[128,2048]{1,0:T(8,128)(2,1)} fusion(bf16[128,2048]{1,0:T(8,128)(2,1)S(1)} %copy-done.2, bf16[128,2048]{1,0:T(8,128)(2,1)} %reduce-scatter.2.cloned.1.call-done, f32[128]{0:T(128)S(1)} %broadcast_multiply_fusion, f32[2048]{0:T(1024)S(1)} %copy-done.5, f32[128]{0:T(128)S(1)} %add_rsqrt_fusion), kind=kLoop, calls=%fused_computation.52 | loop fusion | flops 2359296 | bytes 1582080 | tf_op jit(solution)/shard_map/convert_element_type | solution.py:188
  (80 shorter events, 4.4 us)
Async XLA Ops:
  7.2 62.5 %all-gather.2.cloned.1.call-start = ((), (), s32[]{:S(2)}) async-start(), calls=%async_computation.1 | async-start | bytes 3244032 | tf_op jit(solution)/shard_map/all_gather | solution.py:128
  7.9 162.2 %reduce-scatter.2.cloned.1.call-start = ((), (), s32[]{:S(2)}) async-start(), calls=%async_computation.2 | async-start | bytes 4718592 | tf_op jit(solution)/shard_map/reduce_scatter | solution.py:170
  7.9 14.0 %collective-permute-start = (bf16[128,2048]{1,0:T(8,128)(2,1)}, bf16[128,2048]{1,0:T(8,128)(2,1)S(1)}, u32[]{:S(2)}, u32[]{:S(2)}) collective-permute-start(bf16[128,2048]{1,0:T(8,128)(2,1)} %param.5), channel_id=1, source_target_pairs={{0,3},{1,0},{2,1},{3,2},{4,7},{5,4},{6,5},{7,6},{8,11},{9,8},{10,9... | collective-permute-start | bytes 1572872 | tf_op jit(solution)/shard_map/ppermute | solution.py:48
  8.6 14.6 %collective-permute-start.1 = (bf16[128,2048]{1,0:T(8,128)(2,1)}, bf16[128,2048]{1,0:T(8,128)(2,1)S(1)}, u32[]{:S(2)}, u32[]{:S(2)}) collective-permute-start(bf16[128,2048]{1,0:T(8,128)(2,1)} %param.5), channel_id=1, source_target_pairs={{0,1},{1,2},{2,3},{3,0},{4,5},{5,6},{6,7},{7,4},{8,9},{9,10},{10,1... | collective-permute-start | bytes 1572872 | tf_op jit(solution)/shard_map/ppermute | solution.py:48
  10.1 14.1 %collective-permute-start.4 = (bf16[128,2048]{1,0:T(8,128)(2,1)}, bf16[128,2048]{1,0:T(8,128)(2,1)S(1)}, u32[]{:S(2)}, u32[]{:S(2)}) collective-permute-start(bf16[128,2048]{1,0:T(8,128)(2,1)} %param.5), channel_id=1, source_target_pairs={{0,4},{1,5},{2,6},{3,7},{4,0},{5,1},{6,2},{7,3},{8,12},{9,13},{10,... | collective-permute-start | bytes 1572872 | tf_op jit(solution)/shard_map/ppermute | solution.py:48
  21.9 9.3 %collective-permute-start.3 = (bf16[64,2048]{1,0:T(8,128)(2,1)S(1)}, bf16[64,2048]{1,0:T(8,128)(2,1)S(1)}, u32[]{:S(2)}, u32[]{:S(2)}) collective-permute-start(bf16[64,2048]{1,0:T(8,128)(2,1)S(1)} %slice.195), channel_id=1, source_target_pairs={{0,3},{1,0},{2,1},{3,2},{4,7},{5,4},{6,5},{7,6},{8,11},{9,8},{10,9... | collective-permute-start | bytes 786440 | tf_op jit(solution)/shard_map/ppermute | solution.py:48
  23.2 10.6 %collective-permute-start.2 = (bf16[64,2048]{1,0:T(8,128)(2,1)S(1)}, bf16[64,2048]{1,0:T(8,128)(2,1)S(1)}, u32[]{:S(2)}, u32[]{:S(2)}) collective-permute-start(bf16[64,2048]{1,0:T(8,128)(2,1)S(1)} %slice.194), channel_id=1, source_target_pairs={{0,1},{1,2},{2,3},{3,0},{4,5},{5,6},{6,7},{7,4},{8,9},{9,10},{10,1... | collective-permute-start | bytes 786440 | tf_op jit(solution)/shard_map/ppermute | solution.py:48
  24.1 16.3 %collective-permute-start.5 = (bf16[128,2048]{1,0:T(8,128)(2,1)S(1)}, bf16[128,2048]{1,0:T(8,128)(2,1)S(1)}, u32[]{:S(2)}, u32[]{:S(2)}) collective-permute-start(bf16[128,2048]{1,0:T(8,128)(2,1)S(1)} %collective-permute-done.4), channel_id=1, source_target_pairs={{0,3},{1,0},{2,1},{3,2},{4,7},{5,4},{6,5},{7,6},{8,11},{9,8},{10,9... | collective-permute-start | bytes 1572872 | tf_op jit(solution)/shard_map/ppermute | solution.py:48
  26.7 16.3 %collective-permute-start.6 = (bf16[128,2048]{1,0:T(8,128)(2,1)S(1)}, bf16[128,2048]{1,0:T(8,128)(2,1)S(1)}, u32[]{:S(2)}, u32[]{:S(2)}) collective-permute-start(bf16[128,2048]{1,0:T(8,128)(2,1)S(1)} %collective-permute-done.4), channel_id=1, source_target_pairs={{0,1},{1,2},{2,3},{3,0},{4,5},{5,6},{6,7},{7,4},{8,9},{9,10},{10,1... | collective-permute-start | bytes 1572872 | tf_op jit(solution)/shard_map/ppermute | solution.py:48
  40.4 7.1 %collective-permute-start.8 = (bf16[64,2048]{1,0:T(8,128)(2,1)S(1)}, bf16[64,2048]{1,0:T(8,128)(2,1)S(1)}, u32[]{:S(2)}, u32[]{:S(2)}) collective-permute-start(bf16[64,2048]{1,0:T(8,128)(2,1)S(1)} %slice.197), channel_id=1, source_target_pairs={{0,3},{1,0},{2,1},{3,2},{4,7},{5,4},{6,5},{7,6},{8,11},{9,8},{10,9... | collective-permute-start | bytes 786440 | tf_op jit(solution)/shard_map/ppermute | solution.py:48
  43.0 7.7 %collective-permute-start.7 = (bf16[64,2048]{1,0:T(8,128)(2,1)S(1)}, bf16[64,2048]{1,0:T(8,128)(2,1)S(1)}, u32[]{:S(2)}, u32[]{:S(2)}) collective-permute-start(bf16[64,2048]{1,0:T(8,128)(2,1)S(1)} %slice.196), channel_id=1, source_target_pairs={{0,1},{1,2},{2,3},{3,0},{4,5},{5,6},{6,7},{7,4},{8,9},{9,10},{10,1... | collective-permute-start | bytes 786440 | tf_op jit(solution)/shard_map/ppermute | solution.py:48
  57.3 3.7 %copy-start = (bf16[8,128,2048]{2,1,0:T(8,128)(2,1)S(1)}, bf16[8,128,2048]{2,1,0:T(8,128)(2,1)}, u32[]{:S(2)}) copy-start(bf16[8,128,2048]{2,1,0:T(8,128)(2,1)} %gather_fusion) | copy-start | bytes 12582916
  61.1 8.6 %copy-start.5 = (f32[2048]{0:T(1024)S(1)}, f32[2048]{0:T(1024)}, u32[]{:S(2)}) copy-start(f32[2048]{0:T(1024)} %param.6) | copy-start | bytes 24580
  76.3 8.2 %collective-permute-start.9 = (bf16[6,3,256]{2,0,1:T(8,128)(2,1)S(1)}, bf16[6,3,256]{2,0,1:T(8,128)(2,1)S(1)}, u32[]{:S(2)}, u32[]{:S(2)}) collective-permute-start(bf16[6,3,256]{2,0,1:T(8,128)(2,1)S(1)} %slice.198), channel_id=1, source_target_pairs={{0,8},{8,16},{16,24},{24,32},{32,40},{40,48},{48,56},{56,64},{64,7... | collective-permute-start | bytes 27656 | tf_op jit(solution)/shard_map/ppermute | solution.py:13
  84.8 2.6 %copy-start.4 = (bf16[1024,256]{1,0:T(8,128)(2,1)S(1)}, bf16[1024,256]{1,0:T(8,128)(2,1)}, u32[]{:S(2)}) copy-start(bf16[1024,256]{1,0:T(8,128)(2,1)} %param.9) | copy-start | bytes 1572868
  91.4 3.4 %collective-permute-start.10 = (f32[6,3,256]{2,0,1:T(8,128)S(1)}, f32[6,3,256]{2,0,1:T(8,128)S(1)}, u32[]{:S(2)}, u32[]{:S(2)}) collective-permute-start(f32[6,3,256]{2,0,1:T(8,128)S(1)} %slice.209), channel_id=1, source_target_pairs={{8,0},{16,8},{24,16},{32,24},{40,32},{48,40},{56,48},{64,56},{72,6... | collective-permute-start | bytes 55304 | tf_op jit(solution)/shard_map/ppermute | solution.py:13
  95.0 2.7 %copy-start.3 = (bf16[1024,2048]{1,0:T(8,128)(2,1)S(1)}, bf16[1024,2048]{1,0:T(8,128)(2,1)}, u32[]{:S(2)}) copy-start(bf16[1024,2048]{1,0:T(8,128)(2,1)} %bitcast_select_fusion) | copy-start | bytes 12582916
  95.1 3.2 %copy-start.6 = (bf16[2048,3,256]{2,0,1:T(8,128)(2,1)S(1)}, bf16[2048,3,256]{2,0,1:T(8,128)(2,1)}, u32[]{:S(2)}) copy-start(bf16[2048,3,256]{2,0,1:T(8,128)(2,1)} %all-gather.2.cloned.1.call-done) | copy-start | bytes 9437188
  114.4 1.7 copy-start.1
  116.2 3.7 %collective-permute-start.11 = (bf16[4,4,64,3,256]{4,2,3,1,0:T(8,128)(2,1)S(1)}, bf16[4,4,64,3,256]{4,2,3,1,0:T(8,128)(2,1)S(1)}, u32[]{:S(2)}, u32[]{:S(2)}) collective-permute-start(bf16[4,4,64,3,256]{4,2,3,1,0:T(8,128)(2,1)S(1)} %slice_bitcast_fusion), channel_id=1, source_target_pairs={{0,8},{8,0},{16,24},{24,16},{32,40},{40,32},{48,56},{56,48},{64,72... | collective-permute-start | bytes 4718600 | tf_op jit(solution)/shard_map/ppermute | solution.py:48
  122.0 48.1 %copy-start.2 = (bf16[128,2048]{1,0:T(8,128)(2,1)S(1)}, bf16[128,2048]{1,0:T(8,128)(2,1)}, u32[]{:S(2)}) copy-start(bf16[128,2048]{1,0:T(8,128)(2,1)} %param.5) | copy-start | bytes 1572868
  122.1 30.6 %collective-permute-start.14 = (bf16[4,64,3,256]{3,1,2,0:T(8,128)(2,1)S(1)}, bf16[4,64,3,256]{3,1,2,0:T(8,128)(2,1)S(1)}, u32[]{:S(2)}, u32[]{:S(2)}) collective-permute-start(bf16[4,64,3,256]{3,1,2,0:T(8,128)(2,1)S(1)} %get-tuple-element.27), channel_id=1, source_target_pairs={{0,192},{8,200},{16,208},{24,216},{32,224},{40,232},{48,240},{56,2... | collective-permute-start | bytes 1179656 | tf_op jit(solution)/shard_map/ppermute | solution.py:48
  122.9 29.8 %collective-permute-start.13 = (bf16[4,64,3,256]{3,1,2,0:T(8,128)(2,1)S(1)}, bf16[4,64,3,256]{3,1,2,0:T(8,128)(2,1)S(1)}, u32[]{:S(2)}, u32[]{:S(2)}) collective-permute-start(bf16[4,64,3,256]{3,1,2,0:T(8,128)(2,1)S(1)} %get-tuple-element.28), channel_id=1, source_target_pairs={{0,128},{8,136},{16,144},{24,152},{32,160},{40,168},{48,176},{56,1... | collective-permute-start | bytes 1179656 | tf_op jit(solution)/shard_map/ppermute | solution.py:48
  125.0 27.7 %collective-permute-start.12 = (bf16[4,64,3,256]{3,1,2,0:T(8,128)(2,1)S(1)}, bf16[4,64,3,256]{3,1,2,0:T(8,128)(2,1)S(1)}, u32[]{:S(2)}, u32[]{:S(2)}) collective-permute-start(bf16[4,64,3,256]{3,1,2,0:T(8,128)(2,1)S(1)} %get-tuple-element.26), channel_id=1, source_target_pairs={{0,64},{8,72},{16,80},{24,88},{32,96},{40,104},{48,112},{56,120},{... | collective-permute-start | bytes 1179656 | tf_op jit(solution)/shard_map/ppermute | solution.py:48
  126.8 1.2 collective-permute-start.18
  128.1 4.9 %collective-permute-start.19 = (f32[7424]{0:T(1024)S(1)}, f32[7424]{0:T(1024)S(1)}, u32[]{:S(2)}, u32[]{:S(2)}) collective-permute-start(f32[7424]{0:T(1024)S(1)} %fusion.72), channel_id=1, source_target_pairs={{0,16},{8,24},{16,0},{24,8},{32,48},{40,56},{48,32},{56,40},{64,80... | collective-permute-start | bytes 89096 | tf_op jit(solution)/shard_map/ppermute | solution.py:21
  133.0 7.8 %collective-permute-start.20 = (f32[7424]{0:T(1024)S(1)}, f32[7424]{0:T(1024)S(1)}, u32[]{:S(2)}, u32[]{:S(2)}) collective-permute-start(f32[7424]{0:T(1024)S(1)} %add.539), channel_id=1, source_target_pairs={{0,32},{8,40},{16,48},{24,56},{32,0},{40,8},{48,16},{56,24},{64,96... | collective-permute-start | bytes 89096 | tf_op jit(solution)/shard_map/ppermute | solution.py:21
  140.8 3.9 %collective-permute-start.21 = (f32[7424]{0:T(1024)S(1)}, f32[7424]{0:T(1024)S(1)}, u32[]{:S(2)}, u32[]{:S(2)}) collective-permute-start(f32[7424]{0:T(1024)S(1)} %add.540), channel_id=1, source_target_pairs={{0,64},{8,72},{16,80},{24,88},{32,96},{40,104},{48,112},{56,120},{... | collective-permute-start | bytes 89096 | tf_op jit(solution)/shard_map/ppermute | solution.py:21
  144.7 5.4 %collective-permute-start.22 = (f32[7424]{0:T(1024)S(1)}, f32[7424]{0:T(1024)S(1)}, u32[]{:S(2)}, u32[]{:S(2)}) collective-permute-start(f32[7424]{0:T(1024)S(1)} %add.541), channel_id=1, source_target_pairs={{0,128},{8,136},{16,144},{24,152},{32,160},{40,168},{48,176},{56,1... | collective-permute-start | bytes 89096 | tf_op jit(solution)/shard_map/ppermute | solution.py:21
  150.2 9.8 %collective-permute-start.23 = (f32[2048]{0:T(1024)S(1)}, f32[2048]{0:T(1024)S(1)}, u32[]{:S(2)}, u32[]{:S(2)}) collective-permute-start(f32[2048]{0:T(1024)S(1)} %slice.227), channel_id=1, source_target_pairs={{0,1},{1,0},{2,3},{3,2},{4,5},{5,4},{6,7},{7,6},{8,9},{9,8},{10,11... | collective-permute-start | bytes 24584 | tf_op jit(solution)/shard_map/ppermute | solution.py:21
  153.0 16.5 %collective-permute-start.17 = (bf16[64,3,256]{2,0,1:T(8,128)(2,1)S(1)}, bf16[64,3,256]{2,0,1:T(8,128)(2,1)S(1)}, u32[]{:S(2)}, u32[]{:S(2)}) collective-permute-start(bf16[64,3,256]{2,0,1:T(8,128)(2,1)S(1)} %get-tuple-element.30), channel_id=1, source_target_pairs={{0,48},{8,56},{16,0},{24,8},{32,16},{40,24},{48,32},{56,40},{64,11... | collective-permute-start | bytes 294920 | tf_op jit(solution)/shard_map/ppermute | solution.py:48
  155.9 13.6 %collective-permute-start.16 = (bf16[64,3,256]{2,0,1:T(8,128)(2,1)S(1)}, bf16[64,3,256]{2,0,1:T(8,128)(2,1)S(1)}, u32[]{:S(2)}, u32[]{:S(2)}) collective-permute-start(bf16[64,3,256]{2,0,1:T(8,128)(2,1)S(1)} %get-tuple-element.31), channel_id=1, source_target_pairs={{0,32},{8,40},{16,48},{24,56},{32,0},{40,8},{48,16},{56,24},{64,96... | collective-permute-start | bytes 294920 | tf_op jit(solution)/shard_map/ppermute | solution.py:48
  159.9 9.5 %collective-permute-start.15 = (bf16[64,3,256]{2,0,1:T(8,128)(2,1)S(1)}, bf16[64,3,256]{2,0,1:T(8,128)(2,1)S(1)}, u32[]{:S(2)}, u32[]{:S(2)}) collective-permute-start(bf16[64,3,256]{2,0,1:T(8,128)(2,1)S(1)} %get-tuple-element.29), channel_id=1, source_target_pairs={{0,16},{8,24},{16,32},{24,40},{32,48},{40,56},{48,0},{56,8},{64,80... | collective-permute-start | bytes 294920 | tf_op jit(solution)/shard_map/ppermute | solution.py:48
  159.9 5.2 %collective-permute-start.24 = (f32[2048]{0:T(1024)S(1)}, f32[2048]{0:T(1024)S(1)}, u32[]{:S(2)}, u32[]{:S(2)}) collective-permute-start(f32[2048]{0:T(1024)S(1)} %slice_add_fusion), channel_id=1, source_target_pairs={{0,2},{1,3},{2,0},{3,1},{4,6},{5,7},{6,4},{7,5},{8,10},{9,11},{10,... | collective-permute-start | bytes 24584 | tf_op jit(solution)/shard_map/ppermute | solution.py:21
  165.2 3.7 %collective-permute-start.25 = (f32[2048]{0:T(1024)S(1)}, f32[2048]{0:T(1024)S(1)}, u32[]{:S(2)}, u32[]{:S(2)}) collective-permute-start(f32[2048]{0:T(1024)S(1)} %add.544), channel_id=1, source_target_pairs={{0,4},{1,5},{2,6},{3,7},{4,0},{5,1},{6,2},{7,3},{8,12},{9,13},{10,... | collective-permute-start | bytes 24584 | tf_op jit(solution)/shard_map/ppermute | solution.py:21
Sparse Core Ops, SparseCore 0:
  10.7 58.9 all-gather.1
  103.5 56.8 reduce-scatter.1

commit v2 on v1

--- a/solution.py
+++ b/solution.py
@@ -132,11 +132,23 @@
     unit_all = wide_all * inv_all
     positions = (unit_all * norm_gain).astype(jnp.bfloat16)
     length = positions.shape[0]
+    edge_rows = jnp.concatenate(
+        [
+            passed_along(gathered[length - width :], "dp", 1),
+            passed_along(gathered[:width], "dp", -1),
+        ],
+        axis=0,
+    ).astype(jnp.float32)
+    edge_inv = lax.rsqrt(jnp.mean(edge_rows * edge_rows, axis=1, keepdims=True) + 1e-05)
+    edge_positions = (edge_rows * edge_inv * norm_gain).astype(jnp.bfloat16)
+    next_grad_out = passed_along(cotangent[:width], "dp", -1).astype(jnp.float32)
     streams = jnp.einsum(
         "td,dsc->tsc", positions, weights, preferred_element_type=jnp.float32
     ).astype(jnp.bfloat16)
-    before = passed_along(streams[length - width :], "dp", 1)
-    extended = jnp.concatenate([before, streams], axis=0).astype(jnp.float32)
+    edge_streams = jnp.einsum(
+        "td,dsc->tsc", edge_positions, weights, preferred_element_type=jnp.float32
+    ).astype(jnp.bfloat16)
+    extended = jnp.concatenate([edge_streams[:width], streams], axis=0).astype(jnp.float32)
     conv = jnp.zeros(streams.shape, jnp.float32)
     for tap in range(taps):
         conv = conv + filters[:, tap, :] * extended[width - tap : width - tap + length]
@@ -150,22 +162,36 @@
         ],
         axis=1,
     )
-    after = passed_along(grad_conv[:width], "dp", -1)
+    next_window = jnp.concatenate(
+        [streams[length - width :], edge_streams[width:]], axis=0
+    ).astype(jnp.float32)
+    next_conv = jnp.zeros((width,) + streams.shape[1:], jnp.float32)
+    for tap in range(taps):
+        next_conv = next_conv + filters[:, tap, :] * next_window[width - tap : 2 * width - tap]
+    after = jnp.stack(
+        [
+            next_grad_out * next_conv[:, 1] * next_conv[:, 2],
+            next_grad_out * next_conv[:, 0] * next_conv[:, 2],
+            next_grad_out * next_conv[:, 0] * next_conv[:, 1],
+        ],
+        axis=1,
+    )
     grad_extended = jnp.concatenate([grad_conv, after], axis=0)
     grad_acc = jnp.zeros(streams.shape, jnp.float32)
     for tap in range(taps):
         grad_acc = grad_acc + filters[:, tap, :] * grad_extended[tap : tap + length]
     grad_streams = grad_acc.astype(jnp.bfloat16)
-    filter_local = jnp.stack(
-        [
-            jnp.sum(grad_conv * extended[width - tap : width - tap + length], axis=0)
-            for tap in range(taps)
-        ],
-        axis=1,
-    )
     normed_terms = jnp.einsum(
         "tsc,dsc->td", grad_streams, weights, preferred_element_type=jnp.float32
     ).astype(jnp.bfloat16)
+    late_conv, late_extended, _ = lax.optimization_barrier((grad_conv, extended, normed_terms))
+    filter_local = jnp.stack(
+        [
+            jnp.sum(late_conv * late_extended[width - tap : width - tap + length], axis=0)
+            for tap in range(taps)
+        ],
+        axis=1,
+    )
     gain_local = jnp.sum(normed_terms.astype(jnp.float32) * unit_all, axis=0)
     grad_normed = lax.psum_scatter(
         normed_terms, "tensor", scatter_dimension=0, tiled=True

time: 182 us -> 181 us (level)
  waiting for transfers between devices: 65.3 us -> 47 us
  starting transfers between devices: 37.5 us -> 47.3 us
  local copies, waits for them, and re-layouts: 17.9 us -> 22.5 us
  matrix products: 19.6 us -> 21.7 us
    ppermute x16, waiting for transfers between devices: 27.9 us -> 17.8 us  [move(): return lax.ppermute(value, axis, pairs)]
    ppermute x2 -> x3, starting transfers between devices: 4.28 us -> 12.5 us  [passed_along(): return lax.ppermute(shard, axis, pairs)]
    all_gather x1, waiting for transfers between devices: 5.88 us -> 0.02 us  [body(): weights = lax.all_gather(proj_weight, 'dp', axis=0, tiled=True)]
    another operation x1 -> x2, other arithmetic: 1.16 us -> 5 us  [body(): jnp.stack([grad_out * conv[:, 1] * conv[:, 2], grad_out * conv[:, 0] * co...]
    convert_element_type x2, other arithmetic: 3.02 us -> 0.32 us  [the longest x1 0.31 us: body(): jnp.concatenate([edge_streams[:width], streams], axis=0).astype(jnp.float32)]
    dot_general x0 -> x1, matrix products: none -> 2.6 us  [body(): jnp.einsum('td,dsc->tsc', edge_positions, weights, preferred_element_type...]
    reduce_sum x1, other arithmetic: 3.69 us -> 1.22 us  [body(): jnp.mean(wide_all * wide_all, axis=1, keepdims=True) + 1e-05]
    ppermute x2 -> x3, waiting for transfers between devices: 7.26 us -> 4.87 us  [passed_along(): return lax.ppermute(shard, axis, pairs)]
  transfers between devices with their start and end apart: 28 -> 29, of which waited for: 19 -> 15; matrix products, arithmetic and copies ran while one was open for 20% -> 31% of each run, Pallas kernels for 0% -> 0%
where the time goes in v2:
time: 181 us; the launch traced here: 180 us
  starting transfers between devices  47.3 us (26%)
  waiting for transfers between devices  47 us (26%)
  other arithmetic  27.1 us (15%)
  local copies, waits for them, and re-layouts  22.5 us (12%)
  matrix products  21.7 us (12%)
  between operations  14.6 us (8%)
    ppermute x8, waiting for transfers between devices, butterfly_sum(): value = value + lax.ppermute(value, axis, pairs)  24.3 us
    ppermute x16, starting transfers between devices, move(): return lax.ppermute(value, axis, pairs)  22.6 us
    ppermute x16, waiting for transfers between devices, move(): return lax.ppermute(value, axis, pairs)  17.8 us
    ppermute x3, starting transfers between devices, passed_along(): return lax.ppermute(shard, axis, pairs)  12.5 us
    ppermute x8, starting transfers between devices, butterfly_sum(): value = value + lax.ppermute(value, axis, pairs)  12.1 us
    unnamed x29, local copies, waits for them, and re-layouts  8.36 us
    dot_general x1, matrix products, body(): jnp.einsum('td,tsc->dsc', positions, grad_streams, preferred_element_type...  8.31 us
    dot_general x1, matrix products, body(): jnp.einsum('td,dsc->tsc', positions, weights, preferred_element_type=jnp....  5.68 us
  transfers between devices with their start and end apart: 29, of which 15 were waited for; matrix products, arithmetic and copies ran while one was open for 31% of the time, Pallas kernels for 0%

profile of v2, /device:TPU:10, one launch (start us, length us, event | category | flops | bytes accessed | tf_op | source)
XLA Modules:
  0.0 180.2 jit_solution(16114480627210795321)
XLA Ops:
  7.2 0.6 collective-permute-start
  7.8 1.5 collective-permute-start.1
  9.3 1.9 %collective-permute-start.4 = (bf16[128,2048]{1,0:T(8,128)(2,1)}, bf16[128,2048]{1,0:T(8,128)(2,1)S(1)}, u32[]{:S(2)}, u32[]{:S(2)}) collective-permute-start(bf16[128,2048]{1,0:T(8,128)(2,1)} %param.5), channel_id=1, source_target_pairs={{0,4},{1,5},{2,6},{3,7},{4,0},{5,1},{6,2},{7,3},{8,12},{9,13},{10,... | collective-permute-start | bytes 1572872 | tf_op jit(solution)/shard_map/ppermute | solution.py:48
  11.3 0.7 slice.239
  12.0 5.8 %collective-permute-start.11 = (bf16[6,256]{1,0:T(8,128)(2,1)S(1)}, bf16[6,256]{1,0:T(8,128)(2,1)S(1)}, u32[]{:S(2)}, u32[]{:S(2)}) collective-permute-start(bf16[6,256]{1,0:T(8,128)(2,1)S(1)} %slice.239), channel_id=1, source_target_pairs={{8,0},{16,8},{24,16},{32,24},{40,32},{48,40},{56,48},{64,56},{72,6... | collective-permute-start | bytes 9224 | tf_op jit(solution)/shard_map/ppermute | solution.py:13
  17.9 1.0 fusion.100
  19.0 1.9 %bitcast_dynamic-update-slice_fusion.5 = bf16[8,128,2048]{2,1,0:T(8,128)(2,1)} fusion(bf16[128,2048]{1,0:T(8,128)(2,1)} %param.5), kind=kLoop, calls=%fused_computation.87 | loop fusion | bytes 1048576
  21.2 1.4 collective-permute-start.3
  22.6 0.8 collective-permute-start.2
  23.4 2.6 %collective-permute-start.5 = (bf16[128,2048]{1,0:T(8,128)(2,1)S(1)}, bf16[128,2048]{1,0:T(8,128)(2,1)S(1)}, u32[]{:S(2)}, u32[]{:S(2)}) collective-permute-start(bf16[128,2048]{1,0:T(8,128)(2,1)S(1)} %collective-permute-done.4), channel_id=1, source_target_pairs={{0,3},{1,0},{2,1},{3,2},{4,7},{5,4},{6,5},{7,6},{8,11},{9,8},{10,9... | collective-permute-start | bytes 1572872 | tf_op jit(solution)/shard_map/ppermute | solution.py:48
  26.0 0.8 bitcast_dynamic-update-slice_fusion.4
  26.8 3.7 %collective-permute-done.3 = bf16[64,2048]{1,0:T(8,128)(2,1)S(1)} collective-permute-done((bf16[64,2048]{1,0:T(8,128)(2,1)S(1)}, bf16[64,2048]{1,0:T(8,128)(2,1)S(1)}, u32[]{:S(2)}, u32[]{:S(2)}) %collective-permute-start.3) | collective-permute-done | bytes 262176 | tf_op jit(solution)/shard_map/ppermute | solution.py:48
  30.5 2.6 %collective-permute-done.2 = bf16[64,2048]{1,0:T(8,128)(2,1)S(1)} collective-permute-done((bf16[64,2048]{1,0:T(8,128)(2,1)S(1)}, bf16[64,2048]{1,0:T(8,128)(2,1)S(1)}, u32[]{:S(2)}, u32[]{:S(2)}) %collective-permute-start.2) | collective-permute-done | bytes 262176 | tf_op jit(solution)/shard_map/ppermute | solution.py:48
  33.1 0.9 fusion.32
  34.0 0.8 bitcast_dynamic-update-slice_fusion.3
  34.8 0.8 bitcast_dynamic-update-slice_fusion.2
  35.6 4.0 %collective-permute-done.5 = bf16[128,2048]{1,0:T(8,128)(2,1)S(1)} collective-permute-done((bf16[128,2048]{1,0:T(8,128)(2,1)S(1)}, bf16[128,2048]{1,0:T(8,128)(2,1)S(1)}, u32[]{:S(2)}, u32[]{:S(2)}) %collective-permute-start.5) | collective-permute-done | bytes 524320 | tf_op jit(solution)/shard_map/ppermute | solution.py:48
  39.7 2.1 %collective-permute-start.8 = (bf16[64,2048]{1,0:T(8,128)(2,1)S(1)}, bf16[64,2048]{1,0:T(8,128)(2,1)S(1)}, u32[]{:S(2)}, u32[]{:S(2)}) collective-permute-start(bf16[64,2048]{1,0:T(8,128)(2,1)S(1)} %slice.284), channel_id=1, source_target_pairs={{0,3},{1,0},{2,1},{3,2},{4,7},{5,4},{6,5},{7,6},{8,11},{9,8},{10,9... | collective-permute-start | bytes 786440 | tf_op jit(solution)/shard_map/ppermute | solution.py:48
  42.4 0.9 bitcast_dynamic-update-slice_fusion.1
  43.2 3.5 %collective-permute-done.8 = bf16[64,2048]{1,0:T(8,128)(2,1)S(1)} collective-permute-done((bf16[64,2048]{1,0:T(8,128)(2,1)S(1)}, bf16[64,2048]{1,0:T(8,128)(2,1)S(1)}, u32[]{:S(2)}, u32[]{:S(2)}) %collective-permute-start.8) | collective-permute-done | bytes 262176 | tf_op jit(solution)/shard_map/ppermute | solution.py:48
  46.7 3.2 %collective-permute-done.7 = bf16[64,2048]{1,0:T(8,128)(2,1)S(1)} collective-permute-done((bf16[64,2048]{1,0:T(8,128)(2,1)S(1)}, bf16[64,2048]{1,0:T(8,128)(2,1)S(1)}, u32[]{:S(2)}, u32[]{:S(2)}) %collective-permute-start.7) | collective-permute-done | bytes 262176 | tf_op jit(solution)/shard_map/ppermute | solution.py:48
  49.9 0.9 fusion.33
  50.8 0.9 bitcast_dynamic-update-slice_fusion
  51.7 4.9 %gather_fusion = bf16[8,128,2048]{2,1,0:T(8,128)(2,1)} fusion(bf16[8,128,2048]{2,1,0:T(8,128)(2,1)} %bitcast_dynamic-update-slice_fusion, s32[1024]{0:T(1024)S(1)} %pad_clamp_fusion.1), kind=kCustom, calls=%fused_computation | custom fusion | bytes 8388640 | tf_op jit(solution)/shard_map/jit(_take)/gather | solution.py:129
  56.6 2.8 %bitcast_select_fusion = bf16[1024,2048]{1,0:T(8,128)(2,1)S(1)} fusion(bf16[8,128,2048]{2,1,0:T(8,128)(2,1)} %gather_fusion, pred[1024]{0:T(1024)(128)(4,1)S(1)} %broadcast_bitcast_fusion), kind=kLoop, calls=%fused_computation.8 | loop fusion | flops 2097152 | bytes 8389632 | tf_op jit(solution)/shard_map/jit(_take)/select_n | solution.py:129
  59.5 4.6 %collective-permute-start.10 = (bf16[6,2048]{1,0:T(8,128)(2,1)S(1)}, bf16[6,2048]{1,0:T(8,128)(2,1)S(1)}, u32[]{:S(2)}, u32[]{:S(2)}) collective-permute-start(bf16[6,2048]{1,0:T(8,128)(2,1)S(1)} %get-tuple-element.23), channel_id=1, source_target_pairs={{8,0},{16,8},{24,16},{32,24},{40,32},{48,40},{56,48},{64,56},{72,6... | collective-permute-start | bytes 73736 | tf_op jit(solution)/shard_map/ppermute | solution.py:13
  64.1 2.1 %collective-permute-start.9 = (bf16[6,2048]{1,0:T(8,128)(2,1)S(1)}, bf16[6,2048]{1,0:T(8,128)(2,1)S(1)}, u32[]{:S(2)}, u32[]{:S(2)}) collective-permute-start(bf16[6,2048]{1,0:T(8,128)(2,1)S(1)} %get-tuple-element.22), channel_id=1, source_target_pairs={{0,8},{8,16},{16,24},{24,32},{32,40},{40,48},{48,56},{56,64},{64,7... | collective-permute-start | bytes 73736 | tf_op jit(solution)/shard_map/ppermute | solution.py:13
  66.3 1.2 multiply_reduce_fusion.1
  67.5 4.9 %collective-permute-done.9 = bf16[6,2048]{1,0:T(8,128)(2,1)S(1)} collective-permute-done((bf16[6,2048]{1,0:T(8,128)(2,1)S(1)}, bf16[6,2048]{1,0:T(8,128)(2,1)S(1)}, u32[]{:S(2)}, u32[]{:S(2)}) %collective-permute-start.9) | collective-permute-done | bytes 24608 | tf_op jit(solution)/shard_map/ppermute | solution.py:13
  72.6 2.6 %convolution_convert_fusion.1 = bf16[12,3,256]{2,0,1:T(8,128)(2,1)S(1)} fusion(bf16[2048,3,256]{2,0,1:T(8,128)(2,1)} %all-gather.2.cloned.1.call-done, f32[2048]{0:T(1024)S(1)} %copy-done.9, f32[12]{0:T(128)S(1)} %add_rsqrt_fusion.1, bf16[6,2048]{1,0:T(8,128)(2,1)S(1)} %collective-permute-done.10, bf16[6,2048]{1,0:T(8,128)(2,1)S(1)} %collective-permute-done.9), kind=kOutput, calls=%fused_computation.57 | convolution fusion | flops 37929984 | bytes 3221552 | tf_op jit(solution)/shard_map/td,dsc->tsc/dot_general | solution.py:148
  75.4 5.7 %fusion.17 = bf16[1024,3,256]{2,0,1:T(8,128)(2,1)S(1)} fusion(bf16[2048,3,256]{2,0,1:T(8,128)(2,1)S(1)} %copy-done.6, bf16[1024,2048]{1,0:T(8,128)(2,1)} %copy-done.4, f32[2048]{0:T(1024)S(1)} %copy-done.9, f32[1024]{0:T(1024)S(1)} %rsqrt_bitcast_fusion), kind=kOutput, calls=%fused_computation.48 | convolution fusion | flops 3230400512 | bytes 8925184 | tf_op jit(solution)/shard_map/td,dsc->tsc/dot_general | solution.py:145
  81.5 2.6 %fusion.8 = f32[1024,3,256]{2,0,1:T(8,128)S(1)} fusion(f32[1030,3,256]{2,0,1:T(8,128)S(1)} %maximum_convert_fusion, f32[3,256]{1,0:T(4,128)S(1)} %get-tuple-element.50, f32[3,256]{1,0:T(4,128)S(1)} %get-tuple-element.51, f32[3,256]{1,0:T(4,128)S(1)} %get-tuple-element.52, f32[3,256]{1,0:T(4,128)S(1)} %get-tuple-element.53, ...), kind=kLoop, calls=%fused_computation.25 | loop fusion | flops 10223616 | bytes 25187328 | tf_op jit(solution)/shard_map/add | solution.py:154
  84.1 1.2 fusion.21
  85.6 3.8 %pad_maximum_fusion = (f32[1024,3,256]{2,0,1:T(8,128)}, bf16[1024,3,256]{2,0,1:T(8,128)(2,1)S(1)}) fusion(f32[1024,1,256]{2,0,1:T(8,128)S(1)} %get-tuple-element.25, f32[1024,1,256]{2,0,1:T(8,128)S(1)} %get-tuple-element.26, f32[1024,1,256]{2,0,1:T(8,128)S(1)} %get-tuple-element.24, f32[1030,3,256]{2,0,1:T(8,128)S(1)} %maximum_maximum_fusion, ...), kind=kLoop, calls=%fused_computation.37 | loop fusion | flops 12582912 | bytes 26760192 | tf_op jit(solution)/shard_map/stack | solution.py:157
  89.4 5.1 %multiply_reduce_fusion = (f32[2048]{0:T(1024)S(1)}, bf16[1024,2048]{1,0:T(8,128)(2,1)}) fusion(bf16[1024,2048]{1,0:T(8,128)(2,1)S(1)} %copy-done.5, f32[1024]{0:T(1024)S(1)} %rsqrt_bitcast_fusion, bf16[1024,3,256]{2,0,1:T(8,128)(2,1)S(1)} %get-tuple-element.28, bf16[2048,3,256]{2,0,1:T(8,128)(2,1)S(1)} %copy-done.6), kind=kOutput, calls=%fused_computation.3 | convolution fusion | flops 3233806336 | bytes 13119488 | tf_op jit(solution)/shard_map/tsc,dsc->td/dot_general | solution.py:184
  94.7 8.3 %convolution_convert_fusion = bf16[2048,3,256]{2,0,1:T(8,128)(2,1)} fusion(bf16[1024,3,256]{2,0,1:T(8,128)(2,1)} %copy-done.7, bf16[1024,2048]{1,0:T(8,128)(2,1)} %copy-done.4, f32[2048]{0:T(1024)S(1)} %copy-done.9, f32[1024]{0:T(1024)S(1)} %rsqrt_bitcast_fusion), kind=kOutput, calls=%fused_computation.9 | convolution fusion | flops 3231186944 | bytes 8925184 | tf_op jit(solution)/shard_map/td,tsc->dsc/dot_general | solution.py:199
  103.0 4.3 %gather_fusion.1 = bf16[32,64,3,256]{3,1,2,0:T(8,128)(2,1)} fusion(bf16[32,64,3,256]{3,1,0,2:T(8,128)(2,1)} %bitcast.165, s32[1024]{0:T(1024)S(1)} %pad_clamp_fusion), kind=kCustom, calls=%fused_computation.1 | custom fusion | bytes 6291584 | tf_op jit(solution)/shard_map/jit(_take)/gather | solution.py:203
  107.3 2.2 %broadcast_select_fusion = bf16[4,4,2,64,3,256]{5,3,4,2,1,0:T(8,128)(2,1)S(1)} fusion(bf16[4,4,2,64,3,256]{5,3,4,2,1,0:T(8,128)(2,1)} %bitcast.164, pred[4,4,2]{2,1,0:T(4,128)(4,1)S(1)} %compare_and_fusion), kind=kLoop, calls=%fused_computation.46 | loop fusion | flops 1572864 | bytes 6291488 | tf_op jit(solution)/shard_map/jit(_take)/select_n | solution.py:203
  109.6 1.7 copy-done.2
  111.3 1.3 slice_bitcast_fusion
  112.6 1.2 copy-done.1
  113.8 2.7 %multiply_reduce_fusion.2 = (f32[3,256]{1,0:T(4,128)S(1)}, f32[3,256]{1,0:T(4,128)S(1)}, f32[3,256]{1,0:T(4,128)S(1)}, f32[3,256]{1,0:T(4,128)S(1)}, f32[3,256]{...) fusion(f32[1024,3,256]{2,0,1:T(8,128)S(1)} %copy-done.1, f32[1030,3,256]{2,0,1:T(8,128)S(1)} %maximum_convert_fusion), kind=kLoop, calls=%fused_computation.39 | loop fusion | flops 11004672 | bytes 25187328 | tf_op jit(solution)/shard_map/reduce_sum | solution.py:190
  116.6 2.7 %convert_add_fusion = (f32[4,4,64,3,256]{4,2,3,1,0:T(8,128)S(1)}, bf16[4,4,64,3,256]{4,2,3,1,0:T(8,128)(2,1)S(1)}) fusion(bf16[4,4,64,3,256]{4,2,3,1,0:T(8,128)(2,1)} %collective-permute-done.12, bf16[4,4,2,64,3,256]{5,3,4,2,1,0:T(8,128)(2,1)} %copy-done.2), kind=kLoop, calls=%fused_computation.38 | loop fusion | flops 3145728 | bytes 7864320 | tf_op jit(solution)/shard_map/add | solution.py:115
  119.5 3.0 %collective-permute-start.14 = (bf16[4,64,3,256]{3,1,2,0:T(8,128)(2,1)S(1)}, bf16[4,64,3,256]{3,1,2,0:T(8,128)(2,1)S(1)}, u32[]{:S(2)}, u32[]{:S(2)}) collective-permute-start(bf16[4,64,3,256]{3,1,2,0:T(8,128)(2,1)S(1)} %get-tuple-element.32), channel_id=1, source_target_pairs={{0,128},{8,136},{16,144},{24,152},{32,160},{40,168},{48,176},{56,1... | collective-permute-start | bytes 1179656 | tf_op jit(solution)/shard_map/ppermute | solution.py:48
  122.6 2.2 %collective-permute-start.13 = (bf16[4,64,3,256]{3,1,2,0:T(8,128)(2,1)S(1)}, bf16[4,64,3,256]{3,1,2,0:T(8,128)(2,1)S(1)}, u32[]{:S(2)}, u32[]{:S(2)}) collective-permute-start(bf16[4,64,3,256]{3,1,2,0:T(8,128)(2,1)S(1)} %get-tuple-element.30), channel_id=1, source_target_pairs={{0,64},{8,72},{16,80},{24,88},{32,96},{40,104},{48,112},{56,120},{... | collective-permute-start | bytes 1179656 | tf_op jit(solution)/shard_map/ppermute | solution.py:48
  124.8 1.2 collective-permute-done.19
  126.1 4.8 %collective-permute-done.20 = f32[7424]{0:T(1024)S(1)} collective-permute-done((f32[7424]{0:T(1024)S(1)}, f32[7424]{0:T(1024)S(1)}, u32[]{:S(2)}, u32[]{:S(2)}) %collective-permute-start.20) | collective-permute-done | bytes 29728 | tf_op jit(solution)/shard_map/ppermute | solution.py:21
  130.9 3.8 %collective-permute-start.21 = (f32[7424]{0:T(1024)S(1)}, f32[7424]{0:T(1024)S(1)}, u32[]{:S(2)}, u32[]{:S(2)}) collective-permute-start(f32[7424]{0:T(1024)S(1)} %add.572), channel_id=1, source_target_pairs={{0,32},{8,40},{16,48},{24,56},{32,0},{40,8},{48,16},{56,24},{64,96... | collective-permute-start | bytes 89096 | tf_op jit(solution)/shard_map/ppermute | solution.py:21
  134.7 4.0 %collective-permute-done.21 = f32[7424]{0:T(1024)S(1)} collective-permute-done((f32[7424]{0:T(1024)S(1)}, f32[7424]{0:T(1024)S(1)}, u32[]{:S(2)}, u32[]{:S(2)}) %collective-permute-start.21) | collective-permute-done | bytes 29728 | tf_op jit(solution)/shard_map/ppermute | solution.py:21
  138.7 3.9 %collective-permute-done.22 = f32[7424]{0:T(1024)S(1)} collective-permute-done((f32[7424]{0:T(1024)S(1)}, f32[7424]{0:T(1024)S(1)}, u32[]{:S(2)}, u32[]{:S(2)}) %collective-permute-start.22) | collective-permute-done | bytes 29728 | tf_op jit(solution)/shard_map/ppermute | solution.py:21
  142.6 1.7 collective-permute-start.23
  144.4 3.7 %collective-permute-done.23 = f32[7424]{0:T(1024)S(1)} collective-permute-done((f32[7424]{0:T(1024)S(1)}, f32[7424]{0:T(1024)S(1)}, u32[]{:S(2)}, u32[]{:S(2)}) %collective-permute-start.23) | collective-permute-done | bytes 29728 | tf_op jit(solution)/shard_map/ppermute | solution.py:21
  148.1 4.9 %collective-permute-start.24 = (f32[2048]{0:T(1024)S(1)}, f32[2048]{0:T(1024)S(1)}, u32[]{:S(2)}, u32[]{:S(2)}) collective-permute-start(f32[2048]{0:T(1024)S(1)} %slice.327), channel_id=1, source_target_pairs={{0,1},{1,0},{2,3},{3,2},{4,5},{5,4},{6,7},{7,6},{8,9},{9,8},{10,11... | collective-permute-start | bytes 24584 | tf_op jit(solution)/shard_map/ppermute | solution.py:21
  153.3 1.8 %collective-permute-start.18 = (bf16[64,3,256]{2,0,1:T(8,128)(2,1)S(1)}, bf16[64,3,256]{2,0,1:T(8,128)(2,1)S(1)}, u32[]{:S(2)}, u32[]{:S(2)}) collective-permute-start(bf16[64,3,256]{2,0,1:T(8,128)(2,1)S(1)} %get-tuple-element.34), channel_id=1, source_target_pairs={{0,48},{8,56},{16,0},{24,8},{32,16},{40,24},{48,32},{56,40},{64,11... | collective-permute-start | bytes 294920 | tf_op jit(solution)/shard_map/ppermute | solution.py:48
  155.1 2.2 %collective-permute-start.17 = (bf16[64,3,256]{2,0,1:T(8,128)(2,1)S(1)}, bf16[64,3,256]{2,0,1:T(8,128)(2,1)S(1)}, u32[]{:S(2)}, u32[]{:S(2)}) collective-permute-start(bf16[64,3,256]{2,0,1:T(8,128)(2,1)S(1)} %get-tuple-element.35), channel_id=1, source_target_pairs={{0,32},{8,40},{16,48},{24,56},{32,0},{40,8},{48,16},{56,24},{64,96... | collective-permute-start | bytes 294920 | tf_op jit(solution)/shard_map/ppermute | solution.py:48
  157.3 2.3 %collective-permute-start.16 = (bf16[64,3,256]{2,0,1:T(8,128)(2,1)S(1)}, bf16[64,3,256]{2,0,1:T(8,128)(2,1)S(1)}, u32[]{:S(2)}, u32[]{:S(2)}) collective-permute-start(bf16[64,3,256]{2,0,1:T(8,128)(2,1)S(1)} %get-tuple-element.33), channel_id=1, source_target_pairs={{0,16},{8,24},{16,32},{24,40},{32,48},{40,56},{48,0},{56,8},{64,80... | collective-permute-start | bytes 294920 | tf_op jit(solution)/shard_map/ppermute | solution.py:48
  159.7 5.1 %collective-permute-done.25 = f32[2048]{0:T(1024)S(1)} collective-permute-done((f32[2048]{0:T(1024)S(1)}, f32[2048]{0:T(1024)S(1)}, u32[]{:S(2)}, u32[]{:S(2)}) %collective-permute-start.25) | collective-permute-done | bytes 8224 | tf_op jit(solution)/shard_map/ppermute | solution.py:21
  164.8 1.5 collective-permute-start.26
  166.3 0.6 reshape.543
  166.9 1.5 collective-permute-done.26
  168.5 0.6 add.578
  169.1 0.7 fusion.37
  169.8 1.4 fusion.22
  171.1 2.2 %fusion.27 = bf16[128,2048]{1,0:T(8,128)(2,1)} fusion(bf16[128,2048]{1,0:T(8,128)(2,1)S(1)} %copy-done.3, bf16[128,2048]{1,0:T(8,128)(2,1)} %reduce-scatter.2.cloned.1.call-done, f32[128]{0:T(128)S(1)} %broadcast_multiply_fusion, f32[2048]{0:T(1024)S(1)} %copy-done.9, f32[128]{0:T(128)S(1)} %add_rsqrt_fusion), kind=kLoop, calls=%fused_computation.65 | loop fusion | flops 2359296 | bytes 1582080 | tf_op jit(solution)/shard_map/convert_element_type | solution.py:214
  (96 shorter events, 3.1 us)
Async XLA Ops:
  7.2 65.4 %all-gather.2.cloned.1.call-start = ((), (), s32[]{:S(2)}) async-start(), calls=%async_computation.1 | async-start | bytes 3244032 | tf_op jit(solution)/shard_map/all_gather | solution.py:128
  7.2 14.0 %collective-permute-start = (bf16[128,2048]{1,0:T(8,128)(2,1)}, bf16[128,2048]{1,0:T(8,128)(2,1)S(1)}, u32[]{:S(2)}, u32[]{:S(2)}) collective-permute-start(bf16[128,2048]{1,0:T(8,128)(2,1)} %param.5), channel_id=1, source_target_pairs={{0,3},{1,0},{2,1},{3,2},{4,7},{5,4},{6,5},{7,6},{8,11},{9,8},{10,9... | collective-permute-start | bytes 1572872 | tf_op jit(solution)/shard_map/ppermute | solution.py:48
  7.8 14.7 %collective-permute-start.1 = (bf16[128,2048]{1,0:T(8,128)(2,1)}, bf16[128,2048]{1,0:T(8,128)(2,1)S(1)}, u32[]{:S(2)}, u32[]{:S(2)}) collective-permute-start(bf16[128,2048]{1,0:T(8,128)(2,1)} %param.5), channel_id=1, source_target_pairs={{0,1},{1,2},{2,3},{3,0},{4,5},{5,6},{6,7},{7,4},{8,9},{9,10},{10,1... | collective-permute-start | bytes 1572872 | tf_op jit(solution)/shard_map/ppermute | solution.py:48
  9.3 14.1 %collective-permute-start.4 = (bf16[128,2048]{1,0:T(8,128)(2,1)}, bf16[128,2048]{1,0:T(8,128)(2,1)S(1)}, u32[]{:S(2)}, u32[]{:S(2)}) collective-permute-start(bf16[128,2048]{1,0:T(8,128)(2,1)} %param.5), channel_id=1, source_target_pairs={{0,4},{1,5},{2,6},{3,7},{4,0},{5,1},{6,2},{7,3},{8,12},{9,13},{10,... | collective-permute-start | bytes 1572872 | tf_op jit(solution)/shard_map/ppermute | solution.py:48
  11.3 158.5 %reduce-scatter.2.cloned.1.call-start = ((), (), s32[]{:S(2)}) async-start(), calls=%async_computation.2 | async-start | bytes 4718592 | tf_op jit(solution)/shard_map/reduce_scatter | solution.py:196
  12.0 73.3 %collective-permute-start.11 = (bf16[6,256]{1,0:T(8,128)(2,1)S(1)}, bf16[6,256]{1,0:T(8,128)(2,1)S(1)}, u32[]{:S(2)}, u32[]{:S(2)}) collective-permute-start(bf16[6,256]{1,0:T(8,128)(2,1)S(1)} %slice.239), channel_id=1, source_target_pairs={{8,0},{16,8},{24,16},{32,24},{40,32},{48,40},{56,48},{64,56},{72,6... | collective-permute-start | bytes 9224 | tf_op jit(solution)/shard_map/ppermute | solution.py:13
  21.2 9.3 %collective-permute-start.3 = (bf16[64,2048]{1,0:T(8,128)(2,1)S(1)}, bf16[64,2048]{1,0:T(8,128)(2,1)S(1)}, u32[]{:S(2)}, u32[]{:S(2)}) collective-permute-start(bf16[64,2048]{1,0:T(8,128)(2,1)S(1)} %slice.282), channel_id=1, source_target_pairs={{0,3},{1,0},{2,1},{3,2},{4,7},{5,4},{6,5},{7,6},{8,11},{9,8},{10,9... | collective-permute-start | bytes 786440 | tf_op jit(solution)/shard_map/ppermute | solution.py:48
  22.6 10.5 %collective-permute-start.2 = (bf16[64,2048]{1,0:T(8,128)(2,1)S(1)}, bf16[64,2048]{1,0:T(8,128)(2,1)S(1)}, u32[]{:S(2)}, u32[]{:S(2)}) collective-permute-start(bf16[64,2048]{1,0:T(8,128)(2,1)S(1)} %slice.281), channel_id=1, source_target_pairs={{0,1},{1,2},{2,3},{3,0},{4,5},{5,6},{6,7},{7,4},{8,9},{9,10},{10,1... | collective-permute-start | bytes 786440 | tf_op jit(solution)/shard_map/ppermute | solution.py:48
  23.4 16.3 %collective-permute-start.5 = (bf16[128,2048]{1,0:T(8,128)(2,1)S(1)}, bf16[128,2048]{1,0:T(8,128)(2,1)S(1)}, u32[]{:S(2)}, u32[]{:S(2)}) collective-permute-start(bf16[128,2048]{1,0:T(8,128)(2,1)S(1)} %collective-permute-done.4), channel_id=1, source_target_pairs={{0,3},{1,0},{2,1},{3,2},{4,7},{5,4},{6,5},{7,6},{8,11},{9,8},{10,9... | collective-permute-start | bytes 1572872 | tf_op jit(solution)/shard_map/ppermute | solution.py:48
  26.0 16.3 %collective-permute-start.6 = (bf16[128,2048]{1,0:T(8,128)(2,1)S(1)}, bf16[128,2048]{1,0:T(8,128)(2,1)S(1)}, u32[]{:S(2)}, u32[]{:S(2)}) collective-permute-start(bf16[128,2048]{1,0:T(8,128)(2,1)S(1)} %collective-permute-done.4), channel_id=1, source_target_pairs={{0,1},{1,2},{2,3},{3,0},{4,5},{5,6},{6,7},{7,4},{8,9},{9,10},{10,1... | collective-permute-start | bytes 1572872 | tf_op jit(solution)/shard_map/ppermute | solution.py:48
  39.7 7.0 %collective-permute-start.8 = (bf16[64,2048]{1,0:T(8,128)(2,1)S(1)}, bf16[64,2048]{1,0:T(8,128)(2,1)S(1)}, u32[]{:S(2)}, u32[]{:S(2)}) collective-permute-start(bf16[64,2048]{1,0:T(8,128)(2,1)S(1)} %slice.284), channel_id=1, source_target_pairs={{0,3},{1,0},{2,1},{3,2},{4,7},{5,4},{6,5},{7,6},{8,11},{9,8},{10,9... | collective-permute-start | bytes 786440 | tf_op jit(solution)/shard_map/ppermute | solution.py:48
  42.3 7.7 %collective-permute-start.7 = (bf16[64,2048]{1,0:T(8,128)(2,1)S(1)}, bf16[64,2048]{1,0:T(8,128)(2,1)S(1)}, u32[]{:S(2)}, u32[]{:S(2)}) collective-permute-start(bf16[64,2048]{1,0:T(8,128)(2,1)S(1)} %slice.283), channel_id=1, source_target_pairs={{0,1},{1,2},{2,3},{3,0},{4,5},{5,6},{6,7},{7,4},{8,9},{9,10},{10,1... | collective-permute-start | bytes 786440 | tf_op jit(solution)/shard_map/ppermute | solution.py:48
  56.6 9.6 %copy-start = (bf16[8,128,2048]{2,1,0:T(8,128)(2,1)S(1)}, bf16[8,128,2048]{2,1,0:T(8,128)(2,1)}, u32[]{:S(2)}) copy-start(bf16[8,128,2048]{2,1,0:T(8,128)(2,1)} %gather_fusion) | copy-start | bytes 12582916
  59.5 8.0 %copy-start.4 = (bf16[1024,2048]{1,0:T(8,128)(2,1)}, bf16[1024,2048]{1,0:T(8,128)(2,1)S(1)}, u32[]{:S(2)}) copy-start(bf16[1024,2048]{1,0:T(8,128)(2,1)S(1)} %bitcast_select_fusion) | copy-start | bytes 12582916
  59.5 13.1 %copy-start.9 = (f32[2048]{0:T(1024)S(1)}, f32[2048]{0:T(1024)}, u32[]{:S(2)}) copy-start(f32[2048]{0:T(1024)} %param.6) | copy-start | bytes 24580
  59.5 8.0 %collective-permute-start.10 = (bf16[6,2048]{1,0:T(8,128)(2,1)S(1)}, bf16[6,2048]{1,0:T(8,128)(2,1)S(1)}, u32[]{:S(2)}, u32[]{:S(2)}) collective-permute-start(bf16[6,2048]{1,0:T(8,128)(2,1)S(1)} %get-tuple-element.23), channel_id=1, source_target_pairs={{8,0},{16,8},{24,16},{32,24},{40,32},{48,40},{56,48},{64,56},{72,6... | collective-permute-start | bytes 73736 | tf_op jit(solution)/shard_map/ppermute | solution.py:13
  64.1 8.2 %collective-permute-start.9 = (bf16[6,2048]{1,0:T(8,128)(2,1)S(1)}, bf16[6,2048]{1,0:T(8,128)(2,1)S(1)}, u32[]{:S(2)}, u32[]{:S(2)}) collective-permute-start(bf16[6,2048]{1,0:T(8,128)(2,1)S(1)} %get-tuple-element.22), channel_id=1, source_target_pairs={{0,8},{8,16},{16,24},{24,32},{32,40},{40,48},{48,56},{56,64},{64,7... | collective-permute-start | bytes 73736 | tf_op jit(solution)/shard_map/ppermute | solution.py:13
  72.6 2.8 %copy-start.6 = (bf16[2048,3,256]{2,0,1:T(8,128)(2,1)S(1)}, bf16[2048,3,256]{2,0,1:T(8,128)(2,1)}, u32[]{:S(2)}) copy-start(bf16[2048,3,256]{2,0,1:T(8,128)(2,1)} %all-gather.2.cloned.1.call-done) | copy-start | bytes 9437188
  81.4 2.6 %copy-start.8 = (bf16[1024,256]{1,0:T(8,128)(2,1)S(1)}, bf16[1024,256]{1,0:T(8,128)(2,1)}, u32[]{:S(2)}) copy-start(bf16[1024,256]{1,0:T(8,128)(2,1)} %param.9) | copy-start | bytes 1572868
  85.6 3.8 %copy-start.5 = (bf16[1024,2048]{1,0:T(8,128)(2,1)S(1)}, bf16[1024,2048]{1,0:T(8,128)(2,1)}, u32[]{:S(2)}) copy-start(bf16[1024,2048]{1,0:T(8,128)(2,1)} %copy-done.4) | copy-start | bytes 12582916
  89.4 5.1 %copy-start.7 = (bf16[1024,3,256]{2,0,1:T(8,128)(2,1)}, bf16[1024,3,256]{2,0,1:T(8,128)(2,1)S(1)}, u32[]{:S(2)}) copy-start(bf16[1024,3,256]{2,0,1:T(8,128)(2,1)S(1)} %get-tuple-element.28) | copy-start | bytes 4718596
  109.6 1.7 copy-start.2
  111.3 2.5 %copy-start.1 = (f32[1024,3,256]{2,0,1:T(8,128)S(1)}, f32[1024,3,256]{2,0,1:T(8,128)}, u32[]{:S(2)}) copy-start(f32[1024,3,256]{2,0,1:T(8,128)} %get-tuple-element.7) | copy-start | bytes 9437188
  112.6 4.0 %collective-permute-start.12 = (bf16[4,4,64,3,256]{4,2,3,1,0:T(8,128)(2,1)}, bf16[4,4,64,3,256]{4,2,3,1,0:T(8,128)(2,1)}, u32[]{:S(2)}, u32[]{:S(2)}) collective-permute-start(bf16[4,4,64,3,256]{4,2,3,1,0:T(8,128)(2,1)} %slice_bitcast_fusion), channel_id=1, source_target_pairs={{0,8},{8,0},{16,24},{24,16},{32,40},{40,32},{48,56},{56,48},{64,72... | collective-permute-start | bytes 4718600 | tf_op jit(solution)/shard_map/ppermute | solution.py:48
  119.3 50.4 %copy-start.3 = (bf16[128,2048]{1,0:T(8,128)(2,1)S(1)}, bf16[128,2048]{1,0:T(8,128)(2,1)}, u32[]{:S(2)}) copy-start(bf16[128,2048]{1,0:T(8,128)(2,1)} %param.5) | copy-start | bytes 1572868
  119.4 33.5 %collective-permute-start.15 = (bf16[4,64,3,256]{3,1,2,0:T(8,128)(2,1)S(1)}, bf16[4,64,3,256]{3,1,2,0:T(8,128)(2,1)S(1)}, u32[]{:S(2)}, u32[]{:S(2)}) collective-permute-start(bf16[4,64,3,256]{3,1,2,0:T(8,128)(2,1)S(1)} %get-tuple-element.31), channel_id=1, source_target_pairs={{0,192},{8,200},{16,208},{24,216},{32,224},{40,232},{48,240},{56,2... | collective-permute-start | bytes 1179656 | tf_op jit(solution)/shard_map/ppermute | solution.py:48
  119.5 33.5 %collective-permute-start.14 = (bf16[4,64,3,256]{3,1,2,0:T(8,128)(2,1)S(1)}, bf16[4,64,3,256]{3,1,2,0:T(8,128)(2,1)S(1)}, u32[]{:S(2)}, u32[]{:S(2)}) collective-permute-start(bf16[4,64,3,256]{3,1,2,0:T(8,128)(2,1)S(1)} %get-tuple-element.32), channel_id=1, source_target_pairs={{0,128},{8,136},{16,144},{24,152},{32,160},{40,168},{48,176},{56,1... | collective-permute-start | bytes 1179656 | tf_op jit(solution)/shard_map/ppermute | solution.py:48
  122.6 30.4 %collective-permute-start.13 = (bf16[4,64,3,256]{3,1,2,0:T(8,128)(2,1)S(1)}, bf16[4,64,3,256]{3,1,2,0:T(8,128)(2,1)S(1)}, u32[]{:S(2)}, u32[]{:S(2)}) collective-permute-start(bf16[4,64,3,256]{3,1,2,0:T(8,128)(2,1)S(1)} %get-tuple-element.30), channel_id=1, source_target_pairs={{0,64},{8,72},{16,80},{24,88},{32,96},{40,104},{48,112},{56,120},{... | collective-permute-start | bytes 1179656 | tf_op jit(solution)/shard_map/ppermute | solution.py:48
  124.8 1.2 collective-permute-start.19
  126.0 4.9 %collective-permute-start.20 = (f32[7424]{0:T(1024)S(1)}, f32[7424]{0:T(1024)S(1)}, u32[]{:S(2)}, u32[]{:S(2)}) collective-permute-start(f32[7424]{0:T(1024)S(1)} %fusion.94), channel_id=1, source_target_pairs={{0,16},{8,24},{16,0},{24,8},{32,48},{40,56},{48,32},{56,40},{64,80... | collective-permute-start | bytes 89096 | tf_op jit(solution)/shard_map/ppermute | solution.py:21
  130.9 7.8 %collective-permute-start.21 = (f32[7424]{0:T(1024)S(1)}, f32[7424]{0:T(1024)S(1)}, u32[]{:S(2)}, u32[]{:S(2)}) collective-permute-start(f32[7424]{0:T(1024)S(1)} %add.572), channel_id=1, source_target_pairs={{0,32},{8,40},{16,48},{24,56},{32,0},{40,8},{48,16},{56,24},{64,96... | collective-permute-start | bytes 89096 | tf_op jit(solution)/shard_map/ppermute | solution.py:21
  138.7 3.9 %collective-permute-start.22 = (f32[7424]{0:T(1024)S(1)}, f32[7424]{0:T(1024)S(1)}, u32[]{:S(2)}, u32[]{:S(2)}) collective-permute-start(f32[7424]{0:T(1024)S(1)} %add.573), channel_id=1, source_target_pairs={{0,64},{8,72},{16,80},{24,88},{32,96},{40,104},{48,112},{56,120},{... | collective-permute-start | bytes 89096 | tf_op jit(solution)/shard_map/ppermute | solution.py:21
  142.6 5.4 %collective-permute-start.23 = (f32[7424]{0:T(1024)S(1)}, f32[7424]{0:T(1024)S(1)}, u32[]{:S(2)}, u32[]{:S(2)}) collective-permute-start(f32[7424]{0:T(1024)S(1)} %add.574), channel_id=1, source_target_pairs={{0,128},{8,136},{16,144},{24,152},{32,160},{40,168},{48,176},{56,1... | collective-permute-start | bytes 89096 | tf_op jit(solution)/shard_map/ppermute | solution.py:21
  148.1 11.5 %collective-permute-start.24 = (f32[2048]{0:T(1024)S(1)}, f32[2048]{0:T(1024)S(1)}, u32[]{:S(2)}, u32[]{:S(2)}) collective-permute-start(f32[2048]{0:T(1024)S(1)} %slice.327), channel_id=1, source_target_pairs={{0,1},{1,0},{2,3},{3,2},{4,5},{5,4},{6,7},{7,6},{8,9},{9,8},{10,11... | collective-permute-start | bytes 24584 | tf_op jit(solution)/shard_map/ppermute | solution.py:21
  153.3 15.8 %collective-permute-start.18 = (bf16[64,3,256]{2,0,1:T(8,128)(2,1)S(1)}, bf16[64,3,256]{2,0,1:T(8,128)(2,1)S(1)}, u32[]{:S(2)}, u32[]{:S(2)}) collective-permute-start(bf16[64,3,256]{2,0,1:T(8,128)(2,1)S(1)} %get-tuple-element.34), channel_id=1, source_target_pairs={{0,48},{8,56},{16,0},{24,8},{32,16},{40,24},{48,32},{56,40},{64,11... | collective-permute-start | bytes 294920 | tf_op jit(solution)/shard_map/ppermute | solution.py:48
  155.1 14.0 %collective-permute-start.17 = (bf16[64,3,256]{2,0,1:T(8,128)(2,1)S(1)}, bf16[64,3,256]{2,0,1:T(8,128)(2,1)S(1)}, u32[]{:S(2)}, u32[]{:S(2)}) collective-permute-start(bf16[64,3,256]{2,0,1:T(8,128)(2,1)S(1)} %get-tuple-element.35), channel_id=1, source_target_pairs={{0,32},{8,40},{16,48},{24,56},{32,0},{40,8},{48,16},{56,24},{64,96... | collective-permute-start | bytes 294920 | tf_op jit(solution)/shard_map/ppermute | solution.py:48
  157.3 11.8 %collective-permute-start.16 = (bf16[64,3,256]{2,0,1:T(8,128)(2,1)S(1)}, bf16[64,3,256]{2,0,1:T(8,128)(2,1)S(1)}, u32[]{:S(2)}, u32[]{:S(2)}) collective-permute-start(bf16[64,3,256]{2,0,1:T(8,128)(2,1)S(1)} %get-tuple-element.33), channel_id=1, source_target_pairs={{0,16},{8,24},{16,32},{24,40},{32,48},{40,56},{48,0},{56,8},{64,80... | collective-permute-start | bytes 294920 | tf_op jit(solution)/shard_map/ppermute | solution.py:48
  159.6 5.2 %collective-permute-start.25 = (f32[2048]{0:T(1024)S(1)}, f32[2048]{0:T(1024)S(1)}, u32[]{:S(2)}, u32[]{:S(2)}) collective-permute-start(f32[2048]{0:T(1024)S(1)} %slice_add_fusion), channel_id=1, source_target_pairs={{0,2},{1,3},{2,0},{3,1},{4,6},{5,7},{6,4},{7,5},{8,10},{9,11},{10,... | collective-permute-start | bytes 24584 | tf_op jit(solution)/shard_map/ppermute | solution.py:21
  164.8 3.7 %collective-permute-start.26 = (f32[2048]{0:T(1024)S(1)}, f32[2048]{0:T(1024)S(1)}, u32[]{:S(2)}, u32[]{:S(2)}) collective-permute-start(f32[2048]{0:T(1024)S(1)} %add.577), channel_id=1, source_target_pairs={{0,4},{1,5},{2,6},{3,7},{4,0},{5,1},{6,2},{7,3},{8,12},{9,13},{10,... | collective-permute-start | bytes 24584 | tf_op jit(solution)/shard_map/ppermute | solution.py:21
Sparse Core Ops, SparseCore 0:
  11.4 59.0 all-gather.1
  94.6 55.0 reduce-scatter.1

commit v3 on v2

--- a/solution.py
+++ b/solution.py
@@ -107,14 +107,55 @@
     return jnp.stack(ring_gather(own, along_x, 0) + ring_gather(partner, along_x, 0))
 
 
-def scatter_dp(blocks):
+def coded(vec, row):
+    hi = vec.astype(jnp.bfloat16)
+    lo = (vec - hi.astype(jnp.float32)).astype(jnp.bfloat16)
+    width = 1
+    for size in row:
+        width *= size
+    count = -(-2 * vec.shape[0] // width)
+    flat = jnp.pad(jnp.concatenate([hi, lo]), (0, count * width - 2 * vec.shape[0]))
+    return flat.reshape((count,) + row), hi.astype(jnp.float32) + lo.astype(jnp.float32)
+
+
+def decoded(rows, length):
+    flat = rows.reshape(-1)
+    return flat[:length].astype(jnp.float32) + flat[length : 2 * length].astype(jnp.float32)
+
+
+def with_rows(block, rows):
+    flat = block.astype(jnp.bfloat16).reshape((-1,) + rows.shape[1:])
+    return jnp.concatenate([flat, rows], axis=0)
+
+
+def ring_stage(shard, vec, move, place):
+    rows, own = coded(vec, shard[0].shape[-2:])
+    count = rows.shape[0]
+    total = shard[0].astype(jnp.float32)
+    held = {0: own}
+    for k, by in ((1, 1), (2, 2), (3, -1)):
+        got = move(with_rows(shard[k], rows), by)
+        total = total + got[:-count].reshape(shard[k].shape).astype(jnp.float32)
+        held[(-by) % 4] = decoded(got[-count:], vec.shape[0])
+    ordered = jnp.take(jnp.stack([held[r] for r in range(4)]), (jnp.arange(4) - place) % 4, axis=0)
+    return total, (ordered[0] + ordered[1]) + (ordered[2] + ordered[3])
+
+
+def scatter_dp(blocks, vec):
     along_y = mover("dp", DP_SPLIT, 0)
     along_h = mover("dp", DP_SPLIT, 1)
     across_core = mover("dp", DP_SPLIT, 2)
+    place = digits(lax.axis_index("dp"), DP_SPLIT)
     grid = blocks.reshape(DP_SPLIT + blocks.shape[1:])
-    summed = grid[:, :, 0].astype(jnp.float32) + across_core(grid[:, :, 1], 1).astype(jnp.float32)
-    column = ring_scatter_direct([summed[k] for k in range(DP_SPLIT[0])], along_y)
-    return ring_scatter_direct([column[k] for k in range(DP_SPLIT[1])], along_h)
+    rows, own = coded(vec, grid.shape[-2:])
+    count = rows.shape[0]
+    got = across_core(with_rows(grid[:, :, 1], rows), 1)
+    summed = grid[:, :, 0].astype(jnp.float32) + got[:-count].reshape(
+        grid[:, :, 1].shape
+    ).astype(jnp.float32)
+    vec = own + decoded(got[-count:], vec.shape[0])
+    column, vec = ring_stage(summed, vec, along_y, place[0])
+    return ring_stage(column, vec, along_h, place[1])
 
 
 def body(inputs, norm_gain, proj_weight, filters, cotangent):
@@ -203,8 +244,10 @@
     weight_blocks = jnp.take(
         weight_terms.reshape((-1, block) + weight_terms.shape[1:]), d_absolute, axis=0
     )
-    grad_proj = scatter_dp(weight_blocks).astype(jnp.bfloat16)
-    joined = butterfly_sum(jnp.concatenate([filter_local.reshape(-1), gain_local]), "dp")
+    proj_sum, joined = scatter_dp(
+        weight_blocks, jnp.concatenate([filter_local.reshape(-1), gain_local])
+    )
+    grad_proj = proj_sum.astype(jnp.bfloat16)
     grad_filters = joined[: filter_local.size].reshape(filter_local.shape)
     grad_gain = butterfly_sum(joined[filter_local.size :], "tensor")
     scaled = norm_gain * grad_normed

time: 181 us -> 199 us (1.099); the launches traced: 180 us -> 195 us
  waiting for transfers between devices: 47 us -> 57.4 us
  local copies, waits for them, and re-layouts: 22.5 us -> 25.7 us
  matrix products: 21.7 us -> 18.8 us
  other arithmetic: 27.1 us -> 29.6 us
    ppermute x16, waiting for transfers between devices: 17.8 us -> 47.1 us  [move(): return lax.ppermute(value, axis, pairs)]
    ppermute x8 -> x3, waiting for transfers between devices: 24.3 us -> 5.45 us  [butterfly_sum(): value = value + lax.ppermute(value, axis, pairs)]
    slice x0 -> x24, local copies, waits for them, and re-layouts: none -> 7.31 us  [the longest x3 3.09 us: ring_stage(): total = total + got[:-count].reshape(shard[k].shape).astype(jnp.float32)]
    another operation x1 -> x4, other arithmetic: 0.24 us -> 3.24 us
    dot_general x1, matrix products: 8.31 us -> 5.38 us  [body(): jnp.einsum('td,tsc->dsc', positions, grad_streams, preferred_element_type...]
    unnamed x29 -> x23, local copies, waits for them, and re-layouts: 8.36 us -> 5.49 us
    add x1 -> x10, other arithmetic: 2.69 us -> 0.32 us  [the longest x2 0.15 us: ring_stage(): return (total, ordered[0] + ordered[1] + (ordered[2] + ordered[3]))]
    ppermute x8 -> x3, starting transfers between devices: 12.1 us -> 12.1 us  [butterfly_sum(): value = value + lax.ppermute(value, axis, pairs)]
  transfers between devices with their start and end apart: 29 -> 24, of which waited for: 15 -> 16; matrix products, arithmetic and copies ran while one was open for 31% -> 22% of each run, Pallas kernels for 0% -> 0%
where the time goes in v3:
time: 199 us; the launch traced here: 195 us
  waiting for transfers between devices  57.4 us (29%)
  starting transfers between devices  49 us (25%)
  other arithmetic  29.6 us (15%)
  local copies, waits for them, and re-layouts  25.7 us (13%)
  matrix products  18.8 us (9%)
  between operations  14.9 us (7%)
    ppermute x16, waiting for transfers between devices, move(): return lax.ppermute(value, axis, pairs)  47.1 us
    ppermute x16, starting transfers between devices, move(): return lax.ppermute(value, axis, pairs)  24.3 us
    ppermute x3, starting transfers between devices, passed_along(): return lax.ppermute(shard, axis, pairs)  12.5 us
    ppermute x3, starting transfers between devices, butterfly_sum(): value = value + lax.ppermute(value, axis, pairs)  12.1 us
    dot_general x1, matrix products, body(): jnp.einsum('td,dsc->tsc', positions, weights, preferred_element_type=jnp....  5.68 us
    unnamed x23, local copies, waits for them, and re-layouts  5.49 us
    ppermute x3, waiting for transfers between devices, butterfly_sum(): value = value + lax.ppermute(value, axis, pairs)  5.45 us
    dot_general x1, matrix products, body(): jnp.einsum('td,tsc->dsc', positions, grad_streams, preferred_element_type...  5.38 us
  transfers between devices with their start and end apart: 24, of which 16 were waited for; matrix products, arithmetic and copies ran while one was open for 22% of the time, Pallas kernels for 0%

profile of v3, /device:TPU:10, one launch (start us, length us, event | category | flops | bytes accessed | tf_op | source)
XLA Modules:
  0.0 195.5 jit_solution(10802275070323415803)
XLA Ops:
  7.8 1.5 collective-permute-start.1
  9.3 1.9 collective-permute-start.4
  12.0 5.8 %collective-permute-start.11 = (bf16[6,256]{1,0:T(8,128)(2,1)S(1)}, bf16[6,256]{1,0:T(8,128)(2,1)S(1)}, u32[]{:S(2)}, u32[]{:S(2)}) collective-permute-start(bf16[6,256]{1,0:T(8,128)(2,1)S(1)} %slice.351), channel_id=1, source_target_pairs={{8,0},{16,8},{24,16},{32,24},{40,32},{48,40},{56,48},{64,56},{72,6... | collective-permute-start | bytes 9224 | tf_op jit(solution)/shard_map/ppermute | solution.py:13
  17.9 1.1 fusion.122
  19.3 1.9 bitcast_dynamic-update-slice_fusion.5
  21.2 1.6 collective-permute-start.3
  23.4 2.6 %collective-permute-start.5 = (bf16[128,2048]{1,0:T(8,128)(2,1)S(1)}, bf16[128,2048]{1,0:T(8,128)(2,1)S(1)}, u32[]{:S(2)}, u32[]{:S(2)}) collective-permute-start(bf16[128,2048]{1,0:T(8,128)(2,1)S(1)} %collective-permute-done.4), channel_id=1, source_target_pairs={{0,3},{1,0},{2,1},{3,2},{4,7},{5,4},{6,5},{7,6},{8,11},{9,8},{10,9... | collective-permute-start | bytes 1572872 | tf_op jit(solution)/shard_map/ppermute | solution.py:48
  26.0 0.8 bitcast_dynamic-update-slice_fusion.4
  26.8 3.7 %collective-permute-done.3 = bf16[64,2048]{1,0:T(8,128)(2,1)S(1)} collective-permute-done((bf16[64,2048]{1,0:T(8,128)(2,1)S(1)}, bf16[64,2048]{1,0:T(8,128)(2,1)S(1)}, u32[]{:S(2)}, u32[]{:S(2)}) %collective-permute-start.3) | collective-permute-done | bytes 262176 | tf_op jit(solution)/shard_map/ppermute | solution.py:48
  30.5 2.6 %collective-permute-done.2 = bf16[64,2048]{1,0:T(8,128)(2,1)S(1)} collective-permute-done((bf16[64,2048]{1,0:T(8,128)(2,1)S(1)}, bf16[64,2048]{1,0:T(8,128)(2,1)S(1)}, u32[]{:S(2)}, u32[]{:S(2)}) %collective-permute-start.2) | collective-permute-done | bytes 262176 | tf_op jit(solution)/shard_map/ppermute | solution.py:48
  33.1 0.9 fusion.32
  34.0 0.8 bitcast_dynamic-update-slice_fusion.3
  34.8 0.8 bitcast_dynamic-update-slice_fusion.2
  35.7 4.0 %collective-permute-done.5 = bf16[128,2048]{1,0:T(8,128)(2,1)S(1)} collective-permute-done((bf16[128,2048]{1,0:T(8,128)(2,1)S(1)}, bf16[128,2048]{1,0:T(8,128)(2,1)S(1)}, u32[]{:S(2)}, u32[]{:S(2)}) %collective-permute-start.5) | collective-permute-done | bytes 524320 | tf_op jit(solution)/shard_map/ppermute | solution.py:48
  39.7 2.1 %collective-permute-start.8 = (bf16[64,2048]{1,0:T(8,128)(2,1)S(1)}, bf16[64,2048]{1,0:T(8,128)(2,1)S(1)}, u32[]{:S(2)}, u32[]{:S(2)}) collective-permute-start(bf16[64,2048]{1,0:T(8,128)(2,1)S(1)} %slice.437), channel_id=1, source_target_pairs={{0,3},{1,0},{2,1},{3,2},{4,7},{5,4},{6,5},{7,6},{8,11},{9,8},{10,9... | collective-permute-start | bytes 786440 | tf_op jit(solution)/shard_map/ppermute | solution.py:48
  42.4 0.9 bitcast_dynamic-update-slice_fusion.1
  43.2 3.5 %collective-permute-done.8 = bf16[64,2048]{1,0:T(8,128)(2,1)S(1)} collective-permute-done((bf16[64,2048]{1,0:T(8,128)(2,1)S(1)}, bf16[64,2048]{1,0:T(8,128)(2,1)S(1)}, u32[]{:S(2)}, u32[]{:S(2)}) %collective-permute-start.8) | collective-permute-done | bytes 262176 | tf_op jit(solution)/shard_map/ppermute | solution.py:48
  46.7 3.2 %collective-permute-done.7 = bf16[64,2048]{1,0:T(8,128)(2,1)S(1)} collective-permute-done((bf16[64,2048]{1,0:T(8,128)(2,1)S(1)}, bf16[64,2048]{1,0:T(8,128)(2,1)S(1)}, u32[]{:S(2)}, u32[]{:S(2)}) %collective-permute-start.7) | collective-permute-done | bytes 262176 | tf_op jit(solution)/shard_map/ppermute | solution.py:48
  49.9 0.9 fusion.33
  50.8 0.8 bitcast_dynamic-update-slice_fusion
  51.6 5.0 %gather_fusion = bf16[8,128,2048]{2,1,0:T(8,128)(2,1)} fusion(bf16[8,128,2048]{2,1,0:T(8,128)(2,1)} %bitcast_dynamic-update-slice_fusion, s32[1024]{0:T(1024)S(1)} %pad_clamp_fusion.3), kind=kCustom, calls=%fused_computation.2 | custom fusion | bytes 8388640 | tf_op jit(solution)/shard_map/jit(_take)/gather | solution.py:170
  56.6 2.8 %bitcast_select_fusion = bf16[1024,2048]{1,0:T(8,128)(2,1)S(1)} fusion(bf16[8,128,2048]{2,1,0:T(8,128)(2,1)} %gather_fusion, pred[1024]{0:T(1024)(128)(4,1)S(1)} %broadcast_bitcast_fusion), kind=kLoop, calls=%fused_computation.10 | loop fusion | flops 2097152 | bytes 8389632 | tf_op jit(solution)/shard_map/jit(_take)/select_n | solution.py:170
  59.5 4.6 %collective-permute-start.10 = (bf16[6,2048]{1,0:T(8,128)(2,1)S(1)}, bf16[6,2048]{1,0:T(8,128)(2,1)S(1)}, u32[]{:S(2)}, u32[]{:S(2)}) collective-permute-start(bf16[6,2048]{1,0:T(8,128)(2,1)S(1)} %get-tuple-element.33), channel_id=1, source_target_pairs={{8,0},{16,8},{24,16},{32,24},{40,32},{48,40},{56,48},{64,56},{72,6... | collective-permute-start | bytes 73736 | tf_op jit(solution)/shard_map/ppermute | solution.py:13
  64.1 2.1 %collective-permute-start.9 = (bf16[6,2048]{1,0:T(8,128)(2,1)S(1)}, bf16[6,2048]{1,0:T(8,128)(2,1)S(1)}, u32[]{:S(2)}, u32[]{:S(2)}) collective-permute-start(bf16[6,2048]{1,0:T(8,128)(2,1)S(1)} %get-tuple-element.32), channel_id=1, source_target_pairs={{0,8},{8,16},{16,24},{24,32},{32,40},{40,48},{48,56},{56,64},{64,7... | collective-permute-start | bytes 73736 | tf_op jit(solution)/shard_map/ppermute | solution.py:13
  66.3 1.2 multiply_reduce_fusion.1
  67.5 4.9 %collective-permute-done.9 = bf16[6,2048]{1,0:T(8,128)(2,1)S(1)} collective-permute-done((bf16[6,2048]{1,0:T(8,128)(2,1)S(1)}, bf16[6,2048]{1,0:T(8,128)(2,1)S(1)}, u32[]{:S(2)}, u32[]{:S(2)}) %collective-permute-start.9) | collective-permute-done | bytes 24608 | tf_op jit(solution)/shard_map/ppermute | solution.py:13
  72.6 2.6 %convolution_convert_fusion.1 = bf16[12,3,256]{2,0,1:T(8,128)(2,1)S(1)} fusion(bf16[2048,3,256]{2,0,1:T(8,128)(2,1)} %all-gather.2.cloned.1.call-done, f32[2048]{0:T(1024)S(1)} %copy-done.6, f32[12]{0:T(128)S(1)} %add_rsqrt_fusion.1, bf16[6,2048]{1,0:T(8,128)(2,1)S(1)} %collective-permute-done.10, bf16[6,2048]{1,0:T(8,128)(2,1)S(1)} %collective-permute-done.9), kind=kOutput, calls=%fused_computation.59 | convolution fusion | flops 37929984 | bytes 3221552 | tf_op jit(solution)/shard_map/td,dsc->tsc/dot_general | solution.py:189
  75.4 5.7 %fusion.17 = bf16[1024,3,256]{2,0,1:T(8,128)(2,1)S(1)} fusion(bf16[2048,3,256]{2,0,1:T(8,128)(2,1)S(1)} %copy-done.4, bf16[1024,2048]{1,0:T(8,128)(2,1)} %copy-done.2, f32[2048]{0:T(1024)S(1)} %copy-done.6, f32[1024]{0:T(1024)S(1)} %rsqrt_bitcast_fusion), kind=kOutput, calls=%fused_computation.50 | convolution fusion | flops 3230400512 | bytes 8925184 | tf_op jit(solution)/shard_map/td,dsc->tsc/dot_general | solution.py:186
  81.4 2.6 %fusion.8 = f32[1024,3,256]{2,0,1:T(8,128)S(1)} fusion(f32[1030,3,256]{2,0,1:T(8,128)S(1)} %maximum_convert_fusion, f32[3,256]{1,0:T(4,128)S(1)} %get-tuple-element.68, f32[3,256]{1,0:T(4,128)S(1)} %get-tuple-element.69, f32[3,256]{1,0:T(4,128)S(1)} %get-tuple-element.70, f32[3,256]{1,0:T(4,128)S(1)} %get-tuple-element.71, ...), kind=kLoop, calls=%fused_computation.27 | loop fusion | flops 10223616 | bytes 25187328 | tf_op jit(solution)/shard_map/add | solution.py:195
  84.0 1.2 fusion.21
  85.6 3.8 %pad_maximum_fusion = (f32[1024,3,256]{2,0,1:T(8,128)}, bf16[1024,3,256]{2,0,1:T(8,128)(2,1)S(1)}) fusion(f32[1024,1,256]{2,0,1:T(8,128)S(1)} %get-tuple-element.35, f32[1024,1,256]{2,0,1:T(8,128)S(1)} %get-tuple-element.36, f32[1024,1,256]{2,0,1:T(8,128)S(1)} %get-tuple-element.34, f32[1030,3,256]{2,0,1:T(8,128)S(1)} %maximum_maximum_fusion, ...), kind=kLoop, calls=%fused_computation.39 | loop fusion | flops 12582912 | bytes 26760192 | tf_op jit(solution)/shard_map/stack | solution.py:198
  89.4 5.4 %convolution_convert_fusion = bf16[2048,3,256]{2,0,1:T(8,128)(2,1)} fusion(bf16[1024,3,256]{2,0,1:T(8,128)(2,1)S(1)} %get-tuple-element.38, bf16[1024,2048]{1,0:T(8,128)(2,1)S(1)} %copy-done.3, f32[2048]{0:T(1024)S(1)} %copy-done.6, f32[1024]{0:T(1024)S(1)} %rsqrt_bitcast_fusion), kind=kOutput, calls=%fused_computation.11 | convolution fusion | flops 3231186944 | bytes 8925184 | tf_op jit(solution)/shard_map/td,tsc->dsc/dot_general | solution.py:240
  94.7 5.1 %multiply_reduce_fusion = (f32[2048]{0:T(1024)S(1)}, bf16[1024,2048]{1,0:T(8,128)(2,1)}) fusion(bf16[1024,2048]{1,0:T(8,128)(2,1)S(1)} %copy-done.3, f32[1024]{0:T(1024)S(1)} %rsqrt_bitcast_fusion, bf16[1024,3,256]{2,0,1:T(8,128)(2,1)S(1)} %get-tuple-element.38, bf16[2048,3,256]{2,0,1:T(8,128)(2,1)S(1)} %copy-done.4), kind=kOutput, calls=%fused_computation.5 | convolution fusion | flops 3233806336 | bytes 13119488 | tf_op jit(solution)/shard_map/tsc,dsc->td/dot_general | solution.py:225
  99.8 4.1 %multiply_reduce_fusion.2 = (f32[3,256]{1,0:T(4,128)S(1)}, f32[3,256]{1,0:T(4,128)S(1)}, f32[3,256]{1,0:T(4,128)S(1)}, f32[3,256]{1,0:T(4,128)S(1)}, f32[3,256]{...) fusion(f32[1024,3,256]{2,0,1:T(8,128)} %get-tuple-element.8, f32[1030,3,256]{2,0,1:T(8,128)S(1)} %maximum_convert_fusion), kind=kLoop, calls=%fused_computation.41 | loop fusion | flops 11004672 | bytes 25187328 | tf_op jit(solution)/shard_map/reduce_sum | solution.py:231
  104.2 2.6 %gather_fusion.1 = bf16[32,64,3,256]{3,1,2,0:T(8,128)(2,1)S(1)} fusion(bf16[32,64,3,256]{3,1,0,2:T(8,128)(2,1)} %bitcast.169, s32[1024]{0:T(1024)S(1)} %pad_clamp_fusion.2), kind=kCustom, calls=%fused_computation.3 | custom fusion | bytes 6291584 | tf_op jit(solution)/shard_map/jit(_take)/gather | solution.py:244
  107.7 3.4 %collective-permute-done.12 = bf16[1044,3,256]{2,0,1:T(8,128)(2,1)S(1)} collective-permute-done((bf16[1044,3,256]{2,0,1:T(8,128)(2,1)S(1)}, bf16[1044,3,256]{2,0,1:T(8,128)(2,1)S(1)}, u32[]{:S(2)}, u32[]{:S(2)}) %collective-permute-start.12) | collective-permute-done | bytes 1603616 | tf_op jit(solution)/shard_map/ppermute | solution.py:48
  111.3 1.9 fusion.117
  113.3 1.3 fusion.120
  114.7 1.1 pad_maximum_fusion.4
  115.8 1.7 collective-permute-start.13
  117.5 1.3 collective-permute-start.14
  118.9 2.7 %collective-permute-start.15 = (bf16[276,3,256]{2,0,1:T(8,128)(2,1)}, bf16[276,3,256]{2,0,1:T(8,128)(2,1)}, u32[]{:S(2)}, u32[]{:S(2)}) collective-permute-start(bf16[276,3,256]{2,0,1:T(8,128)(2,1)} %get-tuple-element.51), channel_id=1, source_target_pairs={{0,192},{8,200},{16,208},{24,216},{32,224},{40,232},{48,240},{56,2... | collective-permute-start | bytes 1271816 | tf_op jit(solution)/shard_map/ppermute | solution.py:48
  121.6 7.3 %collective-permute-done.13 = bf16[276,3,256]{2,0,1:T(8,128)(2,1)} collective-permute-done((bf16[276,3,256]{2,0,1:T(8,128)(2,1)}, bf16[276,3,256]{2,0,1:T(8,128)(2,1)}, u32[]{:S(2)}, u32[]{:S(2)}) %collective-permute-start.13) | collective-permute-done | bytes 423968 | tf_op jit(solution)/shard_map/ppermute | solution.py:48
  128.9 0.8 slice.490
  129.8 2.7 %collective-permute-done.14 = bf16[276,3,256]{2,0,1:T(8,128)(2,1)} collective-permute-done((bf16[276,3,256]{2,0,1:T(8,128)(2,1)}, bf16[276,3,256]{2,0,1:T(8,128)(2,1)}, u32[]{:S(2)}, u32[]{:S(2)}) %collective-permute-start.14) | collective-permute-done | bytes 423968 | tf_op jit(solution)/shard_map/ppermute | solution.py:48
  132.4 0.8 slice.487
  133.3 6.8 %collective-permute-done.15 = bf16[276,3,256]{2,0,1:T(8,128)(2,1)} collective-permute-done((bf16[276,3,256]{2,0,1:T(8,128)(2,1)}, bf16[276,3,256]{2,0,1:T(8,128)(2,1)}, u32[]{:S(2)}, u32[]{:S(2)}) %collective-permute-start.15) | collective-permute-done | bytes 423968 | tf_op jit(solution)/shard_map/ppermute | solution.py:48
  140.1 0.8 slice.484
  142.1 1.0 slice.477
  143.1 1.0 slice.479
  144.2 1.0 slice.481
  145.2 1.1 fusion.113
  146.8 3.9 %collective-permute-start.18 = (bf16[84,3,256]{2,0,1:T(8,128)(2,1)S(1)}, bf16[84,3,256]{2,0,1:T(8,128)(2,1)S(1)}, u32[]{:S(2)}, u32[]{:S(2)}) collective-permute-start(bf16[84,3,256]{2,0,1:T(8,128)(2,1)S(1)} %get-tuple-element.48), channel_id=1, source_target_pairs={{0,48},{8,56},{16,0},{24,8},{32,16},{40,24},{48,32},{56,40},{64,11... | collective-permute-start | bytes 387080 | tf_op jit(solution)/shard_map/ppermute | solution.py:48
  150.7 3.3 %collective-permute-start.17 = (bf16[84,3,256]{2,0,1:T(8,128)(2,1)S(1)}, bf16[84,3,256]{2,0,1:T(8,128)(2,1)S(1)}, u32[]{:S(2)}, u32[]{:S(2)}) collective-permute-start(bf16[84,3,256]{2,0,1:T(8,128)(2,1)S(1)} %get-tuple-element.47), channel_id=1, source_target_pairs={{0,32},{8,40},{16,48},{24,56},{32,0},{40,8},{48,16},{56,24},{64,96... | collective-permute-start | bytes 387080 | tf_op jit(solution)/shard_map/ppermute | solution.py:48
  154.0 2.8 %collective-permute-done.16 = bf16[84,3,256]{2,0,1:T(8,128)(2,1)S(1)} collective-permute-done((bf16[84,3,256]{2,0,1:T(8,128)(2,1)S(1)}, bf16[84,3,256]{2,0,1:T(8,128)(2,1)S(1)}, u32[]{:S(2)}, u32[]{:S(2)}) %collective-permute-start.16) | collective-permute-done | bytes 129056 | tf_op jit(solution)/shard_map/ppermute | solution.py:48
  156.9 6.5 %collective-permute-done.17 = bf16[84,3,256]{2,0,1:T(8,128)(2,1)S(1)} collective-permute-done((bf16[84,3,256]{2,0,1:T(8,128)(2,1)S(1)}, bf16[84,3,256]{2,0,1:T(8,128)(2,1)S(1)}, u32[]{:S(2)}, u32[]{:S(2)}) %collective-permute-start.17) | collective-permute-done | bytes 129056 | tf_op jit(solution)/shard_map/ppermute | solution.py:48
  164.6 7.5 %collective-permute-start.19 = (f32[2048]{0:T(1024)S(1)}, f32[2048]{0:T(1024)S(1)}, u32[]{:S(2)}, u32[]{:S(2)}) collective-permute-start(f32[2048]{0:T(1024)S(1)} %bitcast.179), channel_id=1, source_target_pairs={{0,1},{1,0},{2,3},{3,2},{4,5},{5,4},{6,7},{7,6},{8,9},{9,8},{10,11... | collective-permute-start | bytes 24584 | tf_op jit(solution)/shard_map/ppermute | solution.py:21
  172.1 1.7 collective-permute-done.19
  174.6 1.6 fusion.37
  176.2 2.8 %collective-permute-done.20 = f32[2048]{0:T(1024)S(1)} collective-permute-done((f32[2048]{0:T(1024)S(1)}, f32[2048]{0:T(1024)S(1)}, u32[]{:S(2)}, u32[]{:S(2)}) %collective-permute-start.20) | collective-permute-done | bytes 8224 | tf_op jit(solution)/shard_map/ppermute | solution.py:21
  179.0 3.8 %collective-permute-start.21 = (f32[2048]{0:T(1024)S(1)}, f32[2048]{0:T(1024)S(1)}, u32[]{:S(2)}, u32[]{:S(2)}) collective-permute-start(f32[2048]{0:T(1024)S(1)} %add.661), channel_id=1, source_target_pairs={{0,4},{1,5},{2,6},{3,7},{4,0},{5,1},{6,2},{7,3},{8,12},{9,13},{10,... | collective-permute-start | bytes 24584 | tf_op jit(solution)/shard_map/ppermute | solution.py:21
  183.5 1.0 collective-permute-done.21
  185.1 1.4 fusion.22
  186.4 2.2 %fusion.27 = bf16[128,2048]{1,0:T(8,128)(2,1)} fusion(bf16[128,2048]{1,0:T(8,128)(2,1)S(1)} %copy-done.1, bf16[128,2048]{1,0:T(8,128)(2,1)} %reduce-scatter.2.cloned.1.call-done, f32[128]{0:T(128)S(1)} %broadcast_multiply_fusion, f32[2048]{0:T(1024)S(1)} %copy-done.6, f32[128]{0:T(128)S(1)} %add_rsqrt_fusion), kind=kLoop, calls=%fused_computation.67 | loop fusion | flops 2359296 | bytes 1582080 | tf_op jit(solution)/shard_map/convert_element_type | solution.py:257
  (145 shorter events, 10.2 us)
Async XLA Ops:
  7.2 65.4 %all-gather.2.cloned.1.call-start = ((), (), s32[]{:S(2)}) async-start(), calls=%async_computation.1 | async-start | bytes 3244032 | tf_op jit(solution)/shard_map/all_gather | solution.py:169
  7.2 14.0 %collective-permute-start = (bf16[128,2048]{1,0:T(8,128)(2,1)}, bf16[128,2048]{1,0:T(8,128)(2,1)S(1)}, u32[]{:S(2)}, u32[]{:S(2)}) collective-permute-start(bf16[128,2048]{1,0:T(8,128)(2,1)} %param.7), channel_id=1, source_target_pairs={{0,3},{1,0},{2,1},{3,2},{4,7},{5,4},{6,5},{7,6},{8,11},{9,8},{10,9... | collective-permute-start | bytes 1572872 | tf_op jit(solution)/shard_map/ppermute | solution.py:48
  7.8 15.0 %collective-permute-start.1 = (bf16[128,2048]{1,0:T(8,128)(2,1)}, bf16[128,2048]{1,0:T(8,128)(2,1)S(1)}, u32[]{:S(2)}, u32[]{:S(2)}) collective-permute-start(bf16[128,2048]{1,0:T(8,128)(2,1)} %param.7), channel_id=1, source_target_pairs={{0,1},{1,2},{2,3},{3,0},{4,5},{5,6},{6,7},{7,4},{8,9},{9,10},{10,1... | collective-permute-start | bytes 1572872 | tf_op jit(solution)/shard_map/ppermute | solution.py:48
  9.3 14.1 %collective-permute-start.4 = (bf16[128,2048]{1,0:T(8,128)(2,1)}, bf16[128,2048]{1,0:T(8,128)(2,1)S(1)}, u32[]{:S(2)}, u32[]{:S(2)}) collective-permute-start(bf16[128,2048]{1,0:T(8,128)(2,1)} %param.7), channel_id=1, source_target_pairs={{0,4},{1,5},{2,6},{3,7},{4,0},{5,1},{6,2},{7,3},{8,12},{9,13},{10,... | collective-permute-start | bytes 1572872 | tf_op jit(solution)/shard_map/ppermute | solution.py:48
  11.3 173.8 %reduce-scatter.2.cloned.1.call-start = ((), (), s32[]{:S(2)}) async-start(), calls=%async_computation.2 | async-start | bytes 4718592 | tf_op jit(solution)/shard_map/reduce_scatter | solution.py:237
  12.0 73.3 %collective-permute-start.11 = (bf16[6,256]{1,0:T(8,128)(2,1)S(1)}, bf16[6,256]{1,0:T(8,128)(2,1)S(1)}, u32[]{:S(2)}, u32[]{:S(2)}) collective-permute-start(bf16[6,256]{1,0:T(8,128)(2,1)S(1)} %slice.351), channel_id=1, source_target_pairs={{8,0},{16,8},{24,16},{32,24},{40,32},{48,40},{56,48},{64,56},{72,6... | collective-permute-start | bytes 9224 | tf_op jit(solution)/shard_map/ppermute | solution.py:13
  21.2 9.3 %collective-permute-start.3 = (bf16[64,2048]{1,0:T(8,128)(2,1)S(1)}, bf16[64,2048]{1,0:T(8,128)(2,1)S(1)}, u32[]{:S(2)}, u32[]{:S(2)}) collective-permute-start(bf16[64,2048]{1,0:T(8,128)(2,1)S(1)} %slice.435), channel_id=1, source_target_pairs={{0,3},{1,0},{2,1},{3,2},{4,7},{5,4},{6,5},{7,6},{8,11},{9,8},{10,9... | collective-permute-start | bytes 786440 | tf_op jit(solution)/shard_map/ppermute | solution.py:48
  22.8 10.3 %collective-permute-start.2 = (bf16[64,2048]{1,0:T(8,128)(2,1)S(1)}, bf16[64,2048]{1,0:T(8,128)(2,1)S(1)}, u32[]{:S(2)}, u32[]{:S(2)}) collective-permute-start(bf16[64,2048]{1,0:T(8,128)(2,1)S(1)} %slice.434), channel_id=1, source_target_pairs={{0,1},{1,2},{2,3},{3,0},{4,5},{5,6},{6,7},{7,4},{8,9},{9,10},{10,1... | collective-permute-start | bytes 786440 | tf_op jit(solution)/shard_map/ppermute | solution.py:48
  23.4 16.3 %collective-permute-start.5 = (bf16[128,2048]{1,0:T(8,128)(2,1)S(1)}, bf16[128,2048]{1,0:T(8,128)(2,1)S(1)}, u32[]{:S(2)}, u32[]{:S(2)}) collective-permute-start(bf16[128,2048]{1,0:T(8,128)(2,1)S(1)} %collective-permute-done.4), channel_id=1, source_target_pairs={{0,3},{1,0},{2,1},{3,2},{4,7},{5,4},{6,5},{7,6},{8,11},{9,8},{10,9... | collective-permute-start | bytes 1572872 | tf_op jit(solution)/shard_map/ppermute | solution.py:48
  26.0 16.3 %collective-permute-start.6 = (bf16[128,2048]{1,0:T(8,128)(2,1)S(1)}, bf16[128,2048]{1,0:T(8,128)(2,1)S(1)}, u32[]{:S(2)}, u32[]{:S(2)}) collective-permute-start(bf16[128,2048]{1,0:T(8,128)(2,1)S(1)} %collective-permute-done.4), channel_id=1, source_target_pairs={{0,1},{1,2},{2,3},{3,0},{4,5},{5,6},{6,7},{7,4},{8,9},{9,10},{10,1... | collective-permute-start | bytes 1572872 | tf_op jit(solution)/shard_map/ppermute | solution.py:48
  39.7 7.0 %collective-permute-start.8 = (bf16[64,2048]{1,0:T(8,128)(2,1)S(1)}, bf16[64,2048]{1,0:T(8,128)(2,1)S(1)}, u32[]{:S(2)}, u32[]{:S(2)}) collective-permute-start(bf16[64,2048]{1,0:T(8,128)(2,1)S(1)} %slice.437), channel_id=1, source_target_pairs={{0,3},{1,0},{2,1},{3,2},{4,7},{5,4},{6,5},{7,6},{8,11},{9,8},{10,9... | collective-permute-start | bytes 786440 | tf_op jit(solution)/shard_map/ppermute | solution.py:48
  42.3 7.7 %collective-permute-start.7 = (bf16[64,2048]{1,0:T(8,128)(2,1)S(1)}, bf16[64,2048]{1,0:T(8,128)(2,1)S(1)}, u32[]{:S(2)}, u32[]{:S(2)}) collective-permute-start(bf16[64,2048]{1,0:T(8,128)(2,1)S(1)} %slice.436), channel_id=1, source_target_pairs={{0,1},{1,2},{2,3},{3,0},{4,5},{5,6},{6,7},{7,4},{8,9},{9,10},{10,1... | collective-permute-start | bytes 786440 | tf_op jit(solution)/shard_map/ppermute | solution.py:48
  56.6 9.6 %copy-start = (bf16[8,128,2048]{2,1,0:T(8,128)(2,1)S(1)}, bf16[8,128,2048]{2,1,0:T(8,128)(2,1)}, u32[]{:S(2)}) copy-start(bf16[8,128,2048]{2,1,0:T(8,128)(2,1)} %gather_fusion) | copy-start | bytes 12582916
  59.5 8.0 %copy-start.2 = (bf16[1024,2048]{1,0:T(8,128)(2,1)}, bf16[1024,2048]{1,0:T(8,128)(2,1)S(1)}, u32[]{:S(2)}) copy-start(bf16[1024,2048]{1,0:T(8,128)(2,1)S(1)} %bitcast_select_fusion) | copy-start | bytes 12582916
  59.5 13.1 %copy-start.6 = (f32[2048]{0:T(1024)S(1)}, f32[2048]{0:T(1024)}, u32[]{:S(2)}) copy-start(f32[2048]{0:T(1024)} %param.8) | copy-start | bytes 24580
  59.5 8.0 %collective-permute-start.10 = (bf16[6,2048]{1,0:T(8,128)(2,1)S(1)}, bf16[6,2048]{1,0:T(8,128)(2,1)S(1)}, u32[]{:S(2)}, u32[]{:S(2)}) collective-permute-start(bf16[6,2048]{1,0:T(8,128)(2,1)S(1)} %get-tuple-element.33), channel_id=1, source_target_pairs={{8,0},{16,8},{24,16},{32,24},{40,32},{48,40},{56,48},{64,56},{72,6... | collective-permute-start | bytes 73736 | tf_op jit(solution)/shard_map/ppermute | solution.py:13
  64.1 8.2 %collective-permute-start.9 = (bf16[6,2048]{1,0:T(8,128)(2,1)S(1)}, bf16[6,2048]{1,0:T(8,128)(2,1)S(1)}, u32[]{:S(2)}, u32[]{:S(2)}) collective-permute-start(bf16[6,2048]{1,0:T(8,128)(2,1)S(1)} %get-tuple-element.32), channel_id=1, source_target_pairs={{0,8},{8,16},{16,24},{24,32},{32,40},{40,48},{48,56},{56,64},{64,7... | collective-permute-start | bytes 73736 | tf_op jit(solution)/shard_map/ppermute | solution.py:13
  72.6 2.8 %copy-start.4 = (bf16[2048,3,256]{2,0,1:T(8,128)(2,1)S(1)}, bf16[2048,3,256]{2,0,1:T(8,128)(2,1)}, u32[]{:S(2)}) copy-start(bf16[2048,3,256]{2,0,1:T(8,128)(2,1)} %all-gather.2.cloned.1.call-done) | copy-start | bytes 9437188
  81.4 2.6 %copy-start.5 = (bf16[1024,256]{1,0:T(8,128)(2,1)S(1)}, bf16[1024,256]{1,0:T(8,128)(2,1)}, u32[]{:S(2)}) copy-start(bf16[1024,256]{1,0:T(8,128)(2,1)} %param.11) | copy-start | bytes 1572868
  85.5 3.8 %copy-start.3 = (bf16[1024,2048]{1,0:T(8,128)(2,1)S(1)}, bf16[1024,2048]{1,0:T(8,128)(2,1)}, u32[]{:S(2)}) copy-start(bf16[1024,2048]{1,0:T(8,128)(2,1)} %copy-done.2) | copy-start | bytes 12582916
  107.6 3.5 %collective-permute-start.12 = (bf16[1044,3,256]{2,0,1:T(8,128)(2,1)S(1)}, bf16[1044,3,256]{2,0,1:T(8,128)(2,1)S(1)}, u32[]{:S(2)}, u32[]{:S(2)}) collective-permute-start(bf16[1044,3,256]{2,0,1:T(8,128)(2,1)S(1)} %pad_maximum_fusion.1), channel_id=1, source_target_pairs={{0,8},{8,0},{16,24},{24,16},{32,40},{40,32},{48,56},{56,48},{64,72... | collective-permute-start | bytes 4810760 | tf_op jit(solution)/shard_map/ppermute | solution.py:48
  115.8 13.1 %collective-permute-start.13 = (bf16[276,3,256]{2,0,1:T(8,128)(2,1)}, bf16[276,3,256]{2,0,1:T(8,128)(2,1)}, u32[]{:S(2)}, u32[]{:S(2)}) collective-permute-start(bf16[276,3,256]{2,0,1:T(8,128)(2,1)} %get-tuple-element.49), channel_id=1, source_target_pairs={{0,64},{8,72},{16,80},{24,88},{32,96},{40,104},{48,112},{56,120},{... | collective-permute-start | bytes 1271816 | tf_op jit(solution)/shard_map/ppermute | solution.py:48
  117.5 14.9 %collective-permute-start.14 = (bf16[276,3,256]{2,0,1:T(8,128)(2,1)}, bf16[276,3,256]{2,0,1:T(8,128)(2,1)}, u32[]{:S(2)}, u32[]{:S(2)}) collective-permute-start(bf16[276,3,256]{2,0,1:T(8,128)(2,1)} %get-tuple-element.50), channel_id=1, source_target_pairs={{0,128},{8,136},{16,144},{24,152},{32,160},{40,168},{48,176},{56,1... | collective-permute-start | bytes 1271816 | tf_op jit(solution)/shard_map/ppermute | solution.py:48
  118.9 21.3 %collective-permute-start.15 = (bf16[276,3,256]{2,0,1:T(8,128)(2,1)}, bf16[276,3,256]{2,0,1:T(8,128)(2,1)}, u32[]{:S(2)}, u32[]{:S(2)}) collective-permute-start(bf16[276,3,256]{2,0,1:T(8,128)(2,1)} %get-tuple-element.51), channel_id=1, source_target_pairs={{0,192},{8,200},{16,208},{24,216},{32,224},{40,232},{48,240},{56,2... | collective-permute-start | bytes 1271816 | tf_op jit(solution)/shard_map/ppermute | solution.py:48
  146.3 38.7 %copy-start.1 = (bf16[128,2048]{1,0:T(8,128)(2,1)S(1)}, bf16[128,2048]{1,0:T(8,128)(2,1)}, u32[]{:S(2)}) copy-start(bf16[128,2048]{1,0:T(8,128)(2,1)} %param.7) | copy-start | bytes 1572868
  146.4 10.4 %collective-permute-start.16 = (bf16[84,3,256]{2,0,1:T(8,128)(2,1)S(1)}, bf16[84,3,256]{2,0,1:T(8,128)(2,1)S(1)}, u32[]{:S(2)}, u32[]{:S(2)}) collective-permute-start(bf16[84,3,256]{2,0,1:T(8,128)(2,1)S(1)} %get-tuple-element.46), channel_id=1, source_target_pairs={{0,16},{8,24},{16,32},{24,40},{32,48},{40,56},{48,0},{56,8},{64,80... | collective-permute-start | bytes 387080 | tf_op jit(solution)/shard_map/ppermute | solution.py:48
  146.8 16.8 %collective-permute-start.18 = (bf16[84,3,256]{2,0,1:T(8,128)(2,1)S(1)}, bf16[84,3,256]{2,0,1:T(8,128)(2,1)S(1)}, u32[]{:S(2)}, u32[]{:S(2)}) collective-permute-start(bf16[84,3,256]{2,0,1:T(8,128)(2,1)S(1)} %get-tuple-element.48), channel_id=1, source_target_pairs={{0,48},{8,56},{16,0},{24,8},{32,16},{40,24},{48,32},{56,40},{64,11... | collective-permute-start | bytes 387080 | tf_op jit(solution)/shard_map/ppermute | solution.py:48
  150.7 12.8 %collective-permute-start.17 = (bf16[84,3,256]{2,0,1:T(8,128)(2,1)S(1)}, bf16[84,3,256]{2,0,1:T(8,128)(2,1)S(1)}, u32[]{:S(2)}, u32[]{:S(2)}) collective-permute-start(bf16[84,3,256]{2,0,1:T(8,128)(2,1)S(1)} %get-tuple-element.47), channel_id=1, source_target_pairs={{0,32},{8,40},{16,48},{24,56},{32,0},{40,8},{48,16},{56,24},{64,96... | collective-permute-start | bytes 387080 | tf_op jit(solution)/shard_map/ppermute | solution.py:48
  164.6 9.2 %collective-permute-start.19 = (f32[2048]{0:T(1024)S(1)}, f32[2048]{0:T(1024)S(1)}, u32[]{:S(2)}, u32[]{:S(2)}) collective-permute-start(f32[2048]{0:T(1024)S(1)} %bitcast.179), channel_id=1, source_target_pairs={{0,1},{1,0},{2,3},{3,2},{4,5},{5,4},{6,7},{7,6},{8,9},{9,8},{10,11... | collective-permute-start | bytes 24584 | tf_op jit(solution)/shard_map/ppermute | solution.py:21
  173.9 5.2 %collective-permute-start.20 = (f32[2048]{0:T(1024)S(1)}, f32[2048]{0:T(1024)S(1)}, u32[]{:S(2)}, u32[]{:S(2)}) collective-permute-start(f32[2048]{0:T(1024)S(1)} %add.660), channel_id=1, source_target_pairs={{0,2},{1,3},{2,0},{3,1},{4,6},{5,7},{6,4},{7,5},{8,10},{9,11},{10,... | collective-permute-start | bytes 24584 | tf_op jit(solution)/shard_map/ppermute | solution.py:21
  179.0 5.4 %collective-permute-start.21 = (f32[2048]{0:T(1024)S(1)}, f32[2048]{0:T(1024)S(1)}, u32[]{:S(2)}, u32[]{:S(2)}) collective-permute-start(f32[2048]{0:T(1024)S(1)} %add.661), channel_id=1, source_target_pairs={{0,4},{1,5},{2,6},{3,7},{4,0},{5,1},{6,2},{7,3},{8,12},{9,13},{10,... | collective-permute-start | bytes 24584 | tf_op jit(solution)/shard_map/ppermute | solution.py:21
Sparse Core Ops, SparseCore 0:
  11.4 59.0 all-gather.1
  119.0 64.8 reduce-scatter.1

commit v4 on v2

--- a/solution.py
+++ b/solution.py
@@ -204,9 +204,10 @@
         weight_terms.reshape((-1, block) + weight_terms.shape[1:]), d_absolute, axis=0
     )
     grad_proj = scatter_dp(weight_blocks).astype(jnp.bfloat16)
-    joined = butterfly_sum(jnp.concatenate([filter_local.reshape(-1), gain_local]), "dp")
+    gain_tensor = butterfly_sum(gain_local, "tensor")
+    joined = butterfly_sum(jnp.concatenate([filter_local.reshape(-1), gain_tensor]), "dp")
     grad_filters = joined[: filter_local.size].reshape(filter_local.shape)
-    grad_gain = butterfly_sum(joined[filter_local.size :], "tensor")
+    grad_gain = joined[filter_local.size :]
     scaled = norm_gain * grad_normed
     grad_inputs = inv_rms * (
         scaled - wide * inv_rms * inv_rms * jnp.mean(scaled * wide, axis=1, keepdims=True)

time: 181 us -> 188 us (1.039); the launches traced: 180 us -> 185 us
  waiting for transfers between devices: 47 us -> 52.1 us
  local copies, waits for them, and re-layouts: 22.5 us -> 20 us
    ppermute x16, waiting for transfers between devices: 17.8 us -> 28.7 us  [move(): return lax.ppermute(value, axis, pairs)]
    ppermute x8, waiting for transfers between devices: 24.3 us -> 18.5 us  [butterfly_sum(): value = value + lax.ppermute(value, axis, pairs)]
    unnamed x29 -> x27, local copies, waits for them, and re-layouts: 8.36 us -> 5.5 us
  transfers between devices with their start and end apart: 29 -> 29, of which waited for: 15 -> 17; matrix products, arithmetic and copies ran while one was open for 31% -> 31% of each run, Pallas kernels for 0% -> 0%
where the time goes in v4:
time: 188 us; the launch traced here: 185 us
  waiting for transfers between devices  52.1 us (28%)
  starting transfers between devices  48.3 us (26%)
  other arithmetic  27.7 us (15%)
  matrix products  21.7 us (12%)
  local copies, waits for them, and re-layouts  20 us (11%)
  between operations  14.6 us (8%)
    ppermute x16, waiting for transfers between devices, move(): return lax.ppermute(value, axis, pairs)  28.7 us
    ppermute x16, starting transfers between devices, move(): return lax.ppermute(value, axis, pairs)  22.5 us
    ppermute x8, waiting for transfers between devices, butterfly_sum(): value = value + lax.ppermute(value, axis, pairs)  18.5 us
    ppermute x8, starting transfers between devices, butterfly_sum(): value = value + lax.ppermute(value, axis, pairs)  13.2 us
    ppermute x3, starting transfers between devices, passed_along(): return lax.ppermute(shard, axis, pairs)  12.5 us
    dot_general x1, matrix products, body(): jnp.einsum('td,tsc->dsc', positions, grad_streams, preferred_element_type...  8.29 us
    dot_general x1, matrix products, body(): jnp.einsum('td,dsc->tsc', positions, weights, preferred_element_type=jnp....  5.68 us
    unnamed x27, local copies, waits for them, and re-layouts  5.5 us
  transfers between devices with their start and end apart: 29, of which 17 were waited for; matrix products, arithmetic and copies ran while one was open for 31% of the time, Pallas kernels for 0%

profile of v4, /device:TPU:10, one launch (start us, length us, event | category | flops | bytes accessed | tf_op | source)
XLA Modules:
  0.0 184.5 jit_solution(2349676504000393046)
XLA Ops:
  7.8 1.5 collective-permute-start.1
  9.3 1.9 %collective-permute-start.4 = (bf16[128,2048]{1,0:T(8,128)(2,1)}, bf16[128,2048]{1,0:T(8,128)(2,1)S(1)}, u32[]{:S(2)}, u32[]{:S(2)}) collective-permute-start(bf16[128,2048]{1,0:T(8,128)(2,1)} %param.5), channel_id=1, source_target_pairs={{0,4},{1,5},{2,6},{3,7},{4,0},{5,1},{6,2},{7,3},{8,12},{9,13},{10,... | collective-permute-start | bytes 1572872 | tf_op jit(solution)/shard_map/ppermute | solution.py:48
  11.3 0.7 slice.239
  12.0 5.8 %collective-permute-start.11 = (bf16[6,256]{1,0:T(8,128)(2,1)S(1)}, bf16[6,256]{1,0:T(8,128)(2,1)S(1)}, u32[]{:S(2)}, u32[]{:S(2)}) collective-permute-start(bf16[6,256]{1,0:T(8,128)(2,1)S(1)} %slice.239), channel_id=1, source_target_pairs={{8,0},{16,8},{24,16},{32,24},{40,32},{48,40},{56,48},{64,56},{72,6... | collective-permute-start | bytes 9224 | tf_op jit(solution)/shard_map/ppermute | solution.py:13
  17.9 1.0 fusion.100
  19.0 1.9 %bitcast_dynamic-update-slice_fusion.5 = bf16[8,128,2048]{2,1,0:T(8,128)(2,1)} fusion(bf16[128,2048]{1,0:T(8,128)(2,1)} %param.5), kind=kLoop, calls=%fused_computation.87 | loop fusion | bytes 1048576
  21.2 1.4 collective-permute-start.3
  22.6 0.8 collective-permute-start.2
  23.4 2.6 %collective-permute-start.5 = (bf16[128,2048]{1,0:T(8,128)(2,1)S(1)}, bf16[128,2048]{1,0:T(8,128)(2,1)S(1)}, u32[]{:S(2)}, u32[]{:S(2)}) collective-permute-start(bf16[128,2048]{1,0:T(8,128)(2,1)S(1)} %collective-permute-done.4), channel_id=1, source_target_pairs={{0,3},{1,0},{2,1},{3,2},{4,7},{5,4},{6,5},{7,6},{8,11},{9,8},{10,9... | collective-permute-start | bytes 1572872 | tf_op jit(solution)/shard_map/ppermute | solution.py:48
  26.0 0.8 bitcast_dynamic-update-slice_fusion.4
  26.8 3.7 %collective-permute-done.3 = bf16[64,2048]{1,0:T(8,128)(2,1)S(1)} collective-permute-done((bf16[64,2048]{1,0:T(8,128)(2,1)S(1)}, bf16[64,2048]{1,0:T(8,128)(2,1)S(1)}, u32[]{:S(2)}, u32[]{:S(2)}) %collective-permute-start.3) | collective-permute-done | bytes 262176 | tf_op jit(solution)/shard_map/ppermute | solution.py:48
  30.5 2.6 %collective-permute-done.2 = bf16[64,2048]{1,0:T(8,128)(2,1)S(1)} collective-permute-done((bf16[64,2048]{1,0:T(8,128)(2,1)S(1)}, bf16[64,2048]{1,0:T(8,128)(2,1)S(1)}, u32[]{:S(2)}, u32[]{:S(2)}) %collective-permute-start.2) | collective-permute-done | bytes 262176 | tf_op jit(solution)/shard_map/ppermute | solution.py:48
  33.1 0.9 fusion.32
  34.0 0.8 bitcast_dynamic-update-slice_fusion.3
  34.8 0.8 bitcast_dynamic-update-slice_fusion.2
  35.7 4.0 %collective-permute-done.5 = bf16[128,2048]{1,0:T(8,128)(2,1)S(1)} collective-permute-done((bf16[128,2048]{1,0:T(8,128)(2,1)S(1)}, bf16[128,2048]{1,0:T(8,128)(2,1)S(1)}, u32[]{:S(2)}, u32[]{:S(2)}) %collective-permute-start.5) | collective-permute-done | bytes 524320 | tf_op jit(solution)/shard_map/ppermute | solution.py:48
  39.7 2.1 %collective-permute-start.8 = (bf16[64,2048]{1,0:T(8,128)(2,1)S(1)}, bf16[64,2048]{1,0:T(8,128)(2,1)S(1)}, u32[]{:S(2)}, u32[]{:S(2)}) collective-permute-start(bf16[64,2048]{1,0:T(8,128)(2,1)S(1)} %slice.284), channel_id=1, source_target_pairs={{0,3},{1,0},{2,1},{3,2},{4,7},{5,4},{6,5},{7,6},{8,11},{9,8},{10,9... | collective-permute-start | bytes 786440 | tf_op jit(solution)/shard_map/ppermute | solution.py:48
  42.4 0.8 bitcast_dynamic-update-slice_fusion.1
  43.2 3.5 %collective-permute-done.8 = bf16[64,2048]{1,0:T(8,128)(2,1)S(1)} collective-permute-done((bf16[64,2048]{1,0:T(8,128)(2,1)S(1)}, bf16[64,2048]{1,0:T(8,128)(2,1)S(1)}, u32[]{:S(2)}, u32[]{:S(2)}) %collective-permute-start.8) | collective-permute-done | bytes 262176 | tf_op jit(solution)/shard_map/ppermute | solution.py:48
  46.7 3.2 %collective-permute-done.7 = bf16[64,2048]{1,0:T(8,128)(2,1)S(1)} collective-permute-done((bf16[64,2048]{1,0:T(8,128)(2,1)S(1)}, bf16[64,2048]{1,0:T(8,128)(2,1)S(1)}, u32[]{:S(2)}, u32[]{:S(2)}) %collective-permute-start.7) | collective-permute-done | bytes 262176 | tf_op jit(solution)/shard_map/ppermute | solution.py:48
  49.9 0.8 fusion.33
  50.8 0.9 bitcast_dynamic-update-slice_fusion
  51.7 5.0 %gather_fusion = bf16[8,128,2048]{2,1,0:T(8,128)(2,1)} fusion(bf16[8,128,2048]{2,1,0:T(8,128)(2,1)} %bitcast_dynamic-update-slice_fusion, s32[1024]{0:T(1024)S(1)} %pad_clamp_fusion.1), kind=kCustom, calls=%fused_computation | custom fusion | bytes 8388640 | tf_op jit(solution)/shard_map/jit(_take)/gather | solution.py:129
  56.6 2.8 %bitcast_select_fusion = bf16[1024,2048]{1,0:T(8,128)(2,1)S(1)} fusion(bf16[8,128,2048]{2,1,0:T(8,128)(2,1)} %gather_fusion, pred[1024]{0:T(1024)(128)(4,1)S(1)} %broadcast_bitcast_fusion), kind=kLoop, calls=%fused_computation.8 | loop fusion | flops 2097152 | bytes 8389632 | tf_op jit(solution)/shard_map/jit(_take)/select_n | solution.py:129
  59.5 4.6 %collective-permute-start.10 = (bf16[6,2048]{1,0:T(8,128)(2,1)S(1)}, bf16[6,2048]{1,0:T(8,128)(2,1)S(1)}, u32[]{:S(2)}, u32[]{:S(2)}) collective-permute-start(bf16[6,2048]{1,0:T(8,128)(2,1)S(1)} %get-tuple-element.23), channel_id=1, source_target_pairs={{8,0},{16,8},{24,16},{32,24},{40,32},{48,40},{56,48},{64,56},{72,6... | collective-permute-start | bytes 73736 | tf_op jit(solution)/shard_map/ppermute | solution.py:13
  64.1 2.1 %collective-permute-start.9 = (bf16[6,2048]{1,0:T(8,128)(2,1)S(1)}, bf16[6,2048]{1,0:T(8,128)(2,1)S(1)}, u32[]{:S(2)}, u32[]{:S(2)}) collective-permute-start(bf16[6,2048]{1,0:T(8,128)(2,1)S(1)} %get-tuple-element.22), channel_id=1, source_target_pairs={{0,8},{8,16},{16,24},{24,32},{32,40},{40,48},{48,56},{56,64},{64,7... | collective-permute-start | bytes 73736 | tf_op jit(solution)/shard_map/ppermute | solution.py:13
  66.3 1.2 multiply_reduce_fusion.1
  67.5 4.9 %collective-permute-done.9 = bf16[6,2048]{1,0:T(8,128)(2,1)S(1)} collective-permute-done((bf16[6,2048]{1,0:T(8,128)(2,1)S(1)}, bf16[6,2048]{1,0:T(8,128)(2,1)S(1)}, u32[]{:S(2)}, u32[]{:S(2)}) %collective-permute-start.9) | collective-permute-done | bytes 24608 | tf_op jit(solution)/shard_map/ppermute | solution.py:13
  72.6 2.6 %convolution_convert_fusion.1 = bf16[12,3,256]{2,0,1:T(8,128)(2,1)S(1)} fusion(bf16[2048,3,256]{2,0,1:T(8,128)(2,1)} %all-gather.2.cloned.1.call-done, f32[2048]{0:T(1024)S(1)} %copy-done.8, f32[12]{0:T(128)S(1)} %add_rsqrt_fusion.1, bf16[6,2048]{1,0:T(8,128)(2,1)S(1)} %collective-permute-done.10, bf16[6,2048]{1,0:T(8,128)(2,1)S(1)} %collective-permute-done.9), kind=kOutput, calls=%fused_computation.57 | convolution fusion | flops 37929984 | bytes 3221552 | tf_op jit(solution)/shard_map/td,dsc->tsc/dot_general | solution.py:148
  75.4 5.7 %fusion.17 = bf16[1024,3,256]{2,0,1:T(8,128)(2,1)S(1)} fusion(bf16[2048,3,256]{2,0,1:T(8,128)(2,1)S(1)} %copy-done.5, bf16[1024,2048]{1,0:T(8,128)(2,1)} %copy-done.3, f32[2048]{0:T(1024)S(1)} %copy-done.8, f32[1024]{0:T(1024)S(1)} %rsqrt_bitcast_fusion), kind=kOutput, calls=%fused_computation.48 | convolution fusion | flops 3230400512 | bytes 8925184 | tf_op jit(solution)/shard_map/td,dsc->tsc/dot_general | solution.py:145
  81.5 2.6 %fusion.8 = f32[1024,3,256]{2,0,1:T(8,128)S(1)} fusion(f32[1030,3,256]{2,0,1:T(8,128)S(1)} %maximum_convert_fusion, f32[3,256]{1,0:T(4,128)S(1)} %get-tuple-element.50, f32[3,256]{1,0:T(4,128)S(1)} %get-tuple-element.51, f32[3,256]{1,0:T(4,128)S(1)} %get-tuple-element.52, f32[3,256]{1,0:T(4,128)S(1)} %get-tuple-element.53, ...), kind=kLoop, calls=%fused_computation.25 | loop fusion | flops 10223616 | bytes 25187328 | tf_op jit(solution)/shard_map/add | solution.py:154
  84.1 1.2 fusion.21
  85.6 3.8 %pad_maximum_fusion = (f32[1024,3,256]{2,0,1:T(8,128)}, bf16[1024,3,256]{2,0,1:T(8,128)(2,1)S(1)}) fusion(f32[1024,1,256]{2,0,1:T(8,128)S(1)} %get-tuple-element.25, f32[1024,1,256]{2,0,1:T(8,128)S(1)} %get-tuple-element.26, f32[1024,1,256]{2,0,1:T(8,128)S(1)} %get-tuple-element.24, f32[1030,3,256]{2,0,1:T(8,128)S(1)} %maximum_maximum_fusion, ...), kind=kLoop, calls=%fused_computation.37 | loop fusion | flops 12582912 | bytes 26760192 | tf_op jit(solution)/shard_map/stack | solution.py:157
  89.4 5.1 %multiply_reduce_fusion = (f32[2048]{0:T(1024)S(1)}, bf16[1024,2048]{1,0:T(8,128)(2,1)}) fusion(bf16[1024,2048]{1,0:T(8,128)(2,1)S(1)} %copy-done.4, f32[1024]{0:T(1024)S(1)} %rsqrt_bitcast_fusion, bf16[1024,3,256]{2,0,1:T(8,128)(2,1)S(1)} %get-tuple-element.28, bf16[2048,3,256]{2,0,1:T(8,128)(2,1)S(1)} %copy-done.5), kind=kOutput, calls=%fused_computation.3 | convolution fusion | flops 3233806336 | bytes 13119488 | tf_op jit(solution)/shard_map/tsc,dsc->td/dot_general | solution.py:184
  94.8 8.3 %convolution_convert_fusion = bf16[2048,3,256]{2,0,1:T(8,128)(2,1)} fusion(bf16[1024,3,256]{2,0,1:T(8,128)(2,1)} %copy-done.6, bf16[1024,2048]{1,0:T(8,128)(2,1)} %copy-done.3, f32[2048]{0:T(1024)S(1)} %copy-done.8, f32[1024]{0:T(1024)S(1)} %rsqrt_bitcast_fusion), kind=kOutput, calls=%fused_computation.9 | convolution fusion | flops 3231186944 | bytes 8925184 | tf_op jit(solution)/shard_map/td,tsc->dsc/dot_general | solution.py:199
  103.1 4.3 %gather_fusion.1 = bf16[32,64,3,256]{3,1,2,0:T(8,128)(2,1)} fusion(bf16[32,64,3,256]{3,1,0,2:T(8,128)(2,1)} %bitcast.165, s32[1024]{0:T(1024)S(1)} %pad_clamp_fusion), kind=kCustom, calls=%fused_computation.1 | custom fusion | bytes 6291584 | tf_op jit(solution)/shard_map/jit(_take)/gather | solution.py:203
  107.4 2.2 %broadcast_select_fusion = bf16[4,4,2,64,3,256]{5,3,4,2,1,0:T(8,128)(2,1)S(1)} fusion(bf16[4,4,2,64,3,256]{5,3,4,2,1,0:T(8,128)(2,1)} %bitcast.164, pred[4,4,2]{2,1,0:T(4,128)(4,1)S(1)} %compare_and_fusion), kind=kLoop, calls=%fused_computation.46 | loop fusion | flops 1572864 | bytes 6291488 | tf_op jit(solution)/shard_map/jit(_take)/select_n | solution.py:203
  109.8 3.2 %collective-permute-start.19 = (f32[2048]{0:T(1024)S(1)}, f32[2048]{0:T(1024)S(1)}, u32[]{:S(2)}, u32[]{:S(2)}) collective-permute-start(f32[2048]{0:T(1024)S(1)} %get-tuple-element.48), channel_id=1, source_target_pairs={{0,1},{1,0},{2,3},{3,2},{4,5},{5,4},{6,7},{7,6},{8,9},{9,8},{10,11... | collective-permute-start | bytes 24584 | tf_op jit(solution)/shard_map/ppermute | solution.py:21
  113.0 1.7 collective-permute-done.19
  114.8 1.2 collective-permute-start.20
  115.9 4.3 %collective-permute-done.20 = f32[2048]{0:T(1024)S(1)} collective-permute-done((f32[2048]{0:T(1024)S(1)}, f32[2048]{0:T(1024)S(1)}, u32[]{:S(2)}, u32[]{:S(2)}) %collective-permute-start.20) | collective-permute-done | bytes 8224 | tf_op jit(solution)/shard_map/ppermute | solution.py:21
  120.3 1.5 collective-permute-start.21
  121.7 2.4 %convert_add_fusion = (f32[4,4,64,3,256]{4,2,3,1,0:T(8,128)}, bf16[4,4,64,3,256]{4,2,3,1,0:T(8,128)(2,1)S(1)}) fusion(bf16[4,4,64,3,256]{4,2,3,1,0:T(8,128)(2,1)S(1)} %collective-permute-done.12, bf16[4,4,2,64,3,256]{5,3,4,2,1,0:T(8,128)(2,1)S(1)} %broadcast_select_fusion), kind=kLoop, calls=%fused_computation.38 | loop fusion | flops 3145728 | bytes 7864320 | tf_op jit(solution)/shard_map/add | solution.py:115
  124.2 1.0 slice_bitcast_fusion.8
  125.2 2.9 %collective-permute-start.14 = (bf16[4,64,3,256]{3,1,2,0:T(8,128)(2,1)}, bf16[4,64,3,256]{3,1,2,0:T(8,128)(2,1)}, u32[]{:S(2)}, u32[]{:S(2)}) collective-permute-start(bf16[4,64,3,256]{3,1,2,0:T(8,128)(2,1)} %get-tuple-element.32), channel_id=1, source_target_pairs={{0,128},{8,136},{16,144},{24,152},{32,160},{40,168},{48,176},{56,1... | collective-permute-start | bytes 1179656 | tf_op jit(solution)/shard_map/ppermute | solution.py:48
  128.2 2.0 %collective-permute-start.13 = (bf16[4,64,3,256]{3,1,2,0:T(8,128)(2,1)}, bf16[4,64,3,256]{3,1,2,0:T(8,128)(2,1)}, u32[]{:S(2)}, u32[]{:S(2)}) collective-permute-start(bf16[4,64,3,256]{3,1,2,0:T(8,128)(2,1)} %get-tuple-element.30), channel_id=1, source_target_pairs={{0,64},{8,72},{16,80},{24,88},{32,96},{40,104},{48,112},{56,120},{... | collective-permute-start | bytes 1179656 | tf_op jit(solution)/shard_map/ppermute | solution.py:48
  130.2 2.7 %multiply_reduce_fusion.2 = (f32[3,256]{1,0:T(4,128)S(1)}, f32[3,256]{1,0:T(4,128)S(1)}, f32[3,256]{1,0:T(4,128)S(1)}, f32[3,256]{1,0:T(4,128)S(1)}, f32[3,256]{...) fusion(f32[1024,3,256]{2,0,1:T(8,128)S(1)} %copy-done.1, f32[1030,3,256]{2,0,1:T(8,128)S(1)} %maximum_convert_fusion), kind=kLoop, calls=%fused_computation.39 | loop fusion | flops 11004672 | bytes 25187328 | tf_op jit(solution)/shard_map/reduce_sum | solution.py:190
  133.2 1.2 collective-permute-done.22
  134.6 2.1 %collective-permute-done.15 = bf16[4,64,3,256]{3,1,2,0:T(8,128)(2,1)} collective-permute-done((bf16[4,64,3,256]{3,1,2,0:T(8,128)(2,1)}, bf16[4,64,3,256]{3,1,2,0:T(8,128)(2,1)}, u32[]{:S(2)}, u32[]{:S(2)}) %collective-permute-start.15) | collective-permute-done | bytes 393248 | tf_op jit(solution)/shard_map/ppermute | solution.py:48
  136.6 7.9 %collective-permute-done.14 = bf16[4,64,3,256]{3,1,2,0:T(8,128)(2,1)} collective-permute-done((bf16[4,64,3,256]{3,1,2,0:T(8,128)(2,1)}, bf16[4,64,3,256]{3,1,2,0:T(8,128)(2,1)}, u32[]{:S(2)}, u32[]{:S(2)}) %collective-permute-start.14) | collective-permute-done | bytes 393248 | tf_op jit(solution)/shard_map/ppermute | solution.py:48
  144.6 0.9 collective-permute-done.13
  145.5 1.7 fusion.96
  147.2 1.7 collective-permute-start.18
  148.9 1.9 %collective-permute-start.17 = (bf16[64,3,256]{2,0,1:T(8,128)(2,1)S(1)}, bf16[64,3,256]{2,0,1:T(8,128)(2,1)S(1)}, u32[]{:S(2)}, u32[]{:S(2)}) collective-permute-start(bf16[64,3,256]{2,0,1:T(8,128)(2,1)S(1)} %get-tuple-element.35), channel_id=1, source_target_pairs={{0,32},{8,40},{16,48},{24,56},{32,0},{40,8},{48,16},{56,24},{64,96... | collective-permute-start | bytes 294920 | tf_op jit(solution)/shard_map/ppermute | solution.py:48
  150.9 2.8 %collective-permute-start.16 = (bf16[64,3,256]{2,0,1:T(8,128)(2,1)S(1)}, bf16[64,3,256]{2,0,1:T(8,128)(2,1)S(1)}, u32[]{:S(2)}, u32[]{:S(2)}) collective-permute-start(bf16[64,3,256]{2,0,1:T(8,128)(2,1)S(1)} %get-tuple-element.33), channel_id=1, source_target_pairs={{0,16},{8,24},{16,32},{24,40},{32,48},{40,56},{48,0},{56,8},{64,80... | collective-permute-start | bytes 294920 | tf_op jit(solution)/shard_map/ppermute | solution.py:48
  153.7 2.5 %collective-permute-start.24 = (f32[7424]{0:T(1024)S(1)}, f32[7424]{0:T(1024)S(1)}, u32[]{:S(2)}, u32[]{:S(2)}) collective-permute-start(f32[7424]{0:T(1024)S(1)} %add.575), channel_id=1, source_target_pairs={{0,32},{8,40},{16,48},{24,56},{32,0},{40,8},{48,16},{56,24},{64,96... | collective-permute-start | bytes 89096 | tf_op jit(solution)/shard_map/ppermute | solution.py:21
  156.3 5.7 %collective-permute-done.24 = f32[7424]{0:T(1024)S(1)} collective-permute-done((f32[7424]{0:T(1024)S(1)}, f32[7424]{0:T(1024)S(1)}, u32[]{:S(2)}, u32[]{:S(2)}) %collective-permute-start.24) | collective-permute-done | bytes 29728 | tf_op jit(solution)/shard_map/ppermute | solution.py:21
  162.0 2.8 %collective-permute-start.25 = (f32[7424]{0:T(1024)S(1)}, f32[7424]{0:T(1024)S(1)}, u32[]{:S(2)}, u32[]{:S(2)}) collective-permute-start(f32[7424]{0:T(1024)S(1)} %add.576), channel_id=1, source_target_pairs={{0,64},{8,72},{16,80},{24,88},{32,96},{40,104},{48,112},{56,120},{... | collective-permute-start | bytes 89096 | tf_op jit(solution)/shard_map/ppermute | solution.py:21
  164.9 1.9 %collective-permute-done.25 = f32[7424]{0:T(1024)S(1)} collective-permute-done((f32[7424]{0:T(1024)S(1)}, f32[7424]{0:T(1024)S(1)}, u32[]{:S(2)}, u32[]{:S(2)}) %collective-permute-start.25) | collective-permute-done | bytes 29728 | tf_op jit(solution)/shard_map/ppermute | solution.py:21
  166.8 1.8 collective-permute-start.26
  168.5 3.6 %collective-permute-done.26 = f32[7424]{0:T(1024)S(1)} collective-permute-done((f32[7424]{0:T(1024)S(1)}, f32[7424]{0:T(1024)S(1)}, u32[]{:S(2)}, u32[]{:S(2)}) %collective-permute-start.26) | collective-permute-done | bytes 29728 | tf_op jit(solution)/shard_map/ppermute | solution.py:21
  173.4 0.7 fusion.37
  174.1 1.4 fusion.22
  175.5 2.2 %fusion.27 = bf16[128,2048]{1,0:T(8,128)(2,1)} fusion(bf16[128,2048]{1,0:T(8,128)(2,1)S(1)} %copy-done.2, bf16[128,2048]{1,0:T(8,128)(2,1)} %reduce-scatter.2.cloned.1.call-done, f32[128]{0:T(128)S(1)} %broadcast_multiply_fusion, f32[2048]{0:T(1024)S(1)} %copy-done.8, f32[128]{0:T(128)S(1)} %add_rsqrt_fusion), kind=kLoop, calls=%fused_computation.65 | loop fusion | flops 2359296 | bytes 1582080 | tf_op jit(solution)/shard_map/convert_element_type | solution.py:215
  (94 shorter events, 4.8 us)
Async XLA Ops:
  7.2 65.4 %all-gather.2.cloned.1.call-start = ((), (), s32[]{:S(2)}) async-start(), calls=%async_computation.1 | async-start | bytes 3244032 | tf_op jit(solution)/shard_map/all_gather | solution.py:128
  7.2 14.0 %collective-permute-start = (bf16[128,2048]{1,0:T(8,128)(2,1)}, bf16[128,2048]{1,0:T(8,128)(2,1)S(1)}, u32[]{:S(2)}, u32[]{:S(2)}) collective-permute-start(bf16[128,2048]{1,0:T(8,128)(2,1)} %param.5), channel_id=1, source_target_pairs={{0,3},{1,0},{2,1},{3,2},{4,7},{5,4},{6,5},{7,6},{8,11},{9,8},{10,9... | collective-permute-start | bytes 1572872 | tf_op jit(solution)/shard_map/ppermute | solution.py:48
  7.8 14.7 %collective-permute-start.1 = (bf16[128,2048]{1,0:T(8,128)(2,1)}, bf16[128,2048]{1,0:T(8,128)(2,1)S(1)}, u32[]{:S(2)}, u32[]{:S(2)}) collective-permute-start(bf16[128,2048]{1,0:T(8,128)(2,1)} %param.5), channel_id=1, source_target_pairs={{0,1},{1,2},{2,3},{3,0},{4,5},{5,6},{6,7},{7,4},{8,9},{9,10},{10,1... | collective-permute-start | bytes 1572872 | tf_op jit(solution)/shard_map/ppermute | solution.py:48
  9.3 14.1 %collective-permute-start.4 = (bf16[128,2048]{1,0:T(8,128)(2,1)}, bf16[128,2048]{1,0:T(8,128)(2,1)S(1)}, u32[]{:S(2)}, u32[]{:S(2)}) collective-permute-start(bf16[128,2048]{1,0:T(8,128)(2,1)} %param.5), channel_id=1, source_target_pairs={{0,4},{1,5},{2,6},{3,7},{4,0},{5,1},{6,2},{7,3},{8,12},{9,13},{10,... | collective-permute-start | bytes 1572872 | tf_op jit(solution)/shard_map/ppermute | solution.py:48
  11.3 162.9 %reduce-scatter.2.cloned.1.call-start = ((), (), s32[]{:S(2)}) async-start(), calls=%async_computation.2 | async-start | bytes 4718592 | tf_op jit(solution)/shard_map/reduce_scatter | solution.py:196
  12.0 73.3 %collective-permute-start.11 = (bf16[6,256]{1,0:T(8,128)(2,1)S(1)}, bf16[6,256]{1,0:T(8,128)(2,1)S(1)}, u32[]{:S(2)}, u32[]{:S(2)}) collective-permute-start(bf16[6,256]{1,0:T(8,128)(2,1)S(1)} %slice.239), channel_id=1, source_target_pairs={{8,0},{16,8},{24,16},{32,24},{40,32},{48,40},{56,48},{64,56},{72,6... | collective-permute-start | bytes 9224 | tf_op jit(solution)/shard_map/ppermute | solution.py:13
  21.2 9.3 %collective-permute-start.3 = (bf16[64,2048]{1,0:T(8,128)(2,1)S(1)}, bf16[64,2048]{1,0:T(8,128)(2,1)S(1)}, u32[]{:S(2)}, u32[]{:S(2)}) collective-permute-start(bf16[64,2048]{1,0:T(8,128)(2,1)S(1)} %slice.282), channel_id=1, source_target_pairs={{0,3},{1,0},{2,1},{3,2},{4,7},{5,4},{6,5},{7,6},{8,11},{9,8},{10,9... | collective-permute-start | bytes 786440 | tf_op jit(solution)/shard_map/ppermute | solution.py:48
  22.6 10.5 %collective-permute-start.2 = (bf16[64,2048]{1,0:T(8,128)(2,1)S(1)}, bf16[64,2048]{1,0:T(8,128)(2,1)S(1)}, u32[]{:S(2)}, u32[]{:S(2)}) collective-permute-start(bf16[64,2048]{1,0:T(8,128)(2,1)S(1)} %slice.281), channel_id=1, source_target_pairs={{0,1},{1,2},{2,3},{3,0},{4,5},{5,6},{6,7},{7,4},{8,9},{9,10},{10,1... | collective-permute-start | bytes 786440 | tf_op jit(solution)/shard_map/ppermute | solution.py:48
  23.4 16.3 %collective-permute-start.5 = (bf16[128,2048]{1,0:T(8,128)(2,1)S(1)}, bf16[128,2048]{1,0:T(8,128)(2,1)S(1)}, u32[]{:S(2)}, u32[]{:S(2)}) collective-permute-start(bf16[128,2048]{1,0:T(8,128)(2,1)S(1)} %collective-permute-done.4), channel_id=1, source_target_pairs={{0,3},{1,0},{2,1},{3,2},{4,7},{5,4},{6,5},{7,6},{8,11},{9,8},{10,9... | collective-permute-start | bytes 1572872 | tf_op jit(solution)/shard_map/ppermute | solution.py:48
  26.0 16.3 %collective-permute-start.6 = (bf16[128,2048]{1,0:T(8,128)(2,1)S(1)}, bf16[128,2048]{1,0:T(8,128)(2,1)S(1)}, u32[]{:S(2)}, u32[]{:S(2)}) collective-permute-start(bf16[128,2048]{1,0:T(8,128)(2,1)S(1)} %collective-permute-done.4), channel_id=1, source_target_pairs={{0,1},{1,2},{2,3},{3,0},{4,5},{5,6},{6,7},{7,4},{8,9},{9,10},{10,1... | collective-permute-start | bytes 1572872 | tf_op jit(solution)/shard_map/ppermute | solution.py:48
  39.7 7.0 %collective-permute-start.8 = (bf16[64,2048]{1,0:T(8,128)(2,1)S(1)}, bf16[64,2048]{1,0:T(8,128)(2,1)S(1)}, u32[]{:S(2)}, u32[]{:S(2)}) collective-permute-start(bf16[64,2048]{1,0:T(8,128)(2,1)S(1)} %slice.284), channel_id=1, source_target_pairs={{0,3},{1,0},{2,1},{3,2},{4,7},{5,4},{6,5},{7,6},{8,11},{9,8},{10,9... | collective-permute-start | bytes 786440 | tf_op jit(solution)/shard_map/ppermute | solution.py:48
  42.3 7.7 %collective-permute-start.7 = (bf16[64,2048]{1,0:T(8,128)(2,1)S(1)}, bf16[64,2048]{1,0:T(8,128)(2,1)S(1)}, u32[]{:S(2)}, u32[]{:S(2)}) collective-permute-start(bf16[64,2048]{1,0:T(8,128)(2,1)S(1)} %slice.283), channel_id=1, source_target_pairs={{0,1},{1,2},{2,3},{3,0},{4,5},{5,6},{6,7},{7,4},{8,9},{9,10},{10,1... | collective-permute-start | bytes 786440 | tf_op jit(solution)/shard_map/ppermute | solution.py:48
  56.6 9.6 %copy-start = (bf16[8,128,2048]{2,1,0:T(8,128)(2,1)S(1)}, bf16[8,128,2048]{2,1,0:T(8,128)(2,1)}, u32[]{:S(2)}) copy-start(bf16[8,128,2048]{2,1,0:T(8,128)(2,1)} %gather_fusion) | copy-start | bytes 12582916
  59.5 8.0 %copy-start.3 = (bf16[1024,2048]{1,0:T(8,128)(2,1)}, bf16[1024,2048]{1,0:T(8,128)(2,1)S(1)}, u32[]{:S(2)}) copy-start(bf16[1024,2048]{1,0:T(8,128)(2,1)S(1)} %bitcast_select_fusion) | copy-start | bytes 12582916
  59.5 13.1 %copy-start.8 = (f32[2048]{0:T(1024)S(1)}, f32[2048]{0:T(1024)}, u32[]{:S(2)}) copy-start(f32[2048]{0:T(1024)} %param.6) | copy-start | bytes 24580
  59.5 8.0 %collective-permute-start.10 = (bf16[6,2048]{1,0:T(8,128)(2,1)S(1)}, bf16[6,2048]{1,0:T(8,128)(2,1)S(1)}, u32[]{:S(2)}, u32[]{:S(2)}) collective-permute-start(bf16[6,2048]{1,0:T(8,128)(2,1)S(1)} %get-tuple-element.23), channel_id=1, source_target_pairs={{8,0},{16,8},{24,16},{32,24},{40,32},{48,40},{56,48},{64,56},{72,6... | collective-permute-start | bytes 73736 | tf_op jit(solution)/shard_map/ppermute | solution.py:13
  64.1 8.3 %collective-permute-start.9 = (bf16[6,2048]{1,0:T(8,128)(2,1)S(1)}, bf16[6,2048]{1,0:T(8,128)(2,1)S(1)}, u32[]{:S(2)}, u32[]{:S(2)}) collective-permute-start(bf16[6,2048]{1,0:T(8,128)(2,1)S(1)} %get-tuple-element.22), channel_id=1, source_target_pairs={{0,8},{8,16},{16,24},{24,32},{32,40},{40,48},{48,56},{56,64},{64,7... | collective-permute-start | bytes 73736 | tf_op jit(solution)/shard_map/ppermute | solution.py:13
  72.6 2.8 %copy-start.5 = (bf16[2048,3,256]{2,0,1:T(8,128)(2,1)S(1)}, bf16[2048,3,256]{2,0,1:T(8,128)(2,1)}, u32[]{:S(2)}) copy-start(bf16[2048,3,256]{2,0,1:T(8,128)(2,1)} %all-gather.2.cloned.1.call-done) | copy-start | bytes 9437188
  81.5 2.6 %copy-start.7 = (bf16[1024,256]{1,0:T(8,128)(2,1)S(1)}, bf16[1024,256]{1,0:T(8,128)(2,1)}, u32[]{:S(2)}) copy-start(bf16[1024,256]{1,0:T(8,128)(2,1)} %param.9) | copy-start | bytes 1572868
  85.6 3.8 %copy-start.4 = (bf16[1024,2048]{1,0:T(8,128)(2,1)S(1)}, bf16[1024,2048]{1,0:T(8,128)(2,1)}, u32[]{:S(2)}) copy-start(bf16[1024,2048]{1,0:T(8,128)(2,1)} %copy-done.3) | copy-start | bytes 12582916
  89.4 5.1 %copy-start.6 = (bf16[1024,3,256]{2,0,1:T(8,128)(2,1)}, bf16[1024,3,256]{2,0,1:T(8,128)(2,1)S(1)}, u32[]{:S(2)}) copy-start(bf16[1024,3,256]{2,0,1:T(8,128)(2,1)S(1)} %get-tuple-element.28) | copy-start | bytes 4718596
  109.7 12.0 %collective-permute-start.12 = (bf16[4,4,64,3,256]{4,2,3,1,0:T(8,128)(2,1)S(1)}, bf16[4,4,64,3,256]{4,2,3,1,0:T(8,128)(2,1)S(1)}, u32[]{:S(2)}, u32[]{:S(2)}) collective-permute-start(bf16[4,4,64,3,256]{4,2,3,1,0:T(8,128)(2,1)S(1)} %slice_bitcast_fusion), channel_id=1, source_target_pairs={{0,8},{8,0},{16,24},{24,16},{32,40},{40,32},{48,56},{56,48},{64,72... | collective-permute-start | bytes 4718600 | tf_op jit(solution)/shard_map/ppermute | solution.py:48
  109.8 4.9 %collective-permute-start.19 = (f32[2048]{0:T(1024)S(1)}, f32[2048]{0:T(1024)S(1)}, u32[]{:S(2)}, u32[]{:S(2)}) collective-permute-start(f32[2048]{0:T(1024)S(1)} %get-tuple-element.48), channel_id=1, source_target_pairs={{0,1},{1,0},{2,3},{3,2},{4,5},{5,4},{6,7},{7,6},{8,9},{9,8},{10,11... | collective-permute-start | bytes 24584 | tf_op jit(solution)/shard_map/ppermute | solution.py:21
  114.8 5.5 %collective-permute-start.20 = (f32[2048]{0:T(1024)S(1)}, f32[2048]{0:T(1024)S(1)}, u32[]{:S(2)}, u32[]{:S(2)}) collective-permute-start(f32[2048]{0:T(1024)S(1)} %add.571), channel_id=1, source_target_pairs={{0,2},{1,3},{2,0},{3,1},{4,6},{5,7},{6,4},{7,5},{8,10},{9,11},{10,... | collective-permute-start | bytes 24584 | tf_op jit(solution)/shard_map/ppermute | solution.py:21
  120.3 12.8 %collective-permute-start.21 = (f32[2048]{0:T(1024)S(1)}, f32[2048]{0:T(1024)S(1)}, u32[]{:S(2)}, u32[]{:S(2)}) collective-permute-start(f32[2048]{0:T(1024)S(1)} %add.572), channel_id=1, source_target_pairs={{0,4},{1,5},{2,6},{3,7},{4,0},{5,1},{6,2},{7,3},{8,12},{9,13},{10,... | collective-permute-start | bytes 24584 | tf_op jit(solution)/shard_map/ppermute | solution.py:21
  121.7 8.5 %copy-start.1 = (f32[1024,3,256]{2,0,1:T(8,128)S(1)}, f32[1024,3,256]{2,0,1:T(8,128)}, u32[]{:S(2)}) copy-start(f32[1024,3,256]{2,0,1:T(8,128)} %get-tuple-element.7) | copy-start | bytes 9437188
  125.2 11.4 %collective-permute-start.15 = (bf16[4,64,3,256]{3,1,2,0:T(8,128)(2,1)}, bf16[4,64,3,256]{3,1,2,0:T(8,128)(2,1)}, u32[]{:S(2)}, u32[]{:S(2)}) collective-permute-start(bf16[4,64,3,256]{3,1,2,0:T(8,128)(2,1)} %get-tuple-element.31), channel_id=1, source_target_pairs={{0,192},{8,200},{16,208},{24,216},{32,224},{40,232},{48,240},{56,2... | collective-permute-start | bytes 1179656 | tf_op jit(solution)/shard_map/ppermute | solution.py:48
  125.2 19.3 %collective-permute-start.14 = (bf16[4,64,3,256]{3,1,2,0:T(8,128)(2,1)}, bf16[4,64,3,256]{3,1,2,0:T(8,128)(2,1)}, u32[]{:S(2)}, u32[]{:S(2)}) collective-permute-start(bf16[4,64,3,256]{3,1,2,0:T(8,128)(2,1)} %get-tuple-element.32), channel_id=1, source_target_pairs={{0,128},{8,136},{16,144},{24,152},{32,160},{40,168},{48,176},{56,1... | collective-permute-start | bytes 1179656 | tf_op jit(solution)/shard_map/ppermute | solution.py:48
  128.2 17.3 %collective-permute-start.13 = (bf16[4,64,3,256]{3,1,2,0:T(8,128)(2,1)}, bf16[4,64,3,256]{3,1,2,0:T(8,128)(2,1)}, u32[]{:S(2)}, u32[]{:S(2)}) collective-permute-start(bf16[4,64,3,256]{3,1,2,0:T(8,128)(2,1)} %get-tuple-element.30), channel_id=1, source_target_pairs={{0,64},{8,72},{16,80},{24,88},{32,96},{40,104},{48,112},{56,120},{... | collective-permute-start | bytes 1179656 | tf_op jit(solution)/shard_map/ppermute | solution.py:48
  132.9 41.2 %copy-start.2 = (bf16[128,2048]{1,0:T(8,128)(2,1)S(1)}, bf16[128,2048]{1,0:T(8,128)(2,1)}, u32[]{:S(2)}) copy-start(bf16[128,2048]{1,0:T(8,128)(2,1)} %param.5) | copy-start | bytes 1572868
  133.1 1.3 collective-permute-start.22
  134.4 19.3 %collective-permute-start.23 = (f32[7424]{0:T(1024)S(1)}, f32[7424]{0:T(1024)S(1)}, u32[]{:S(2)}, u32[]{:S(2)}) collective-permute-start(f32[7424]{0:T(1024)S(1)} %fusion.94), channel_id=1, source_target_pairs={{0,16},{8,24},{16,0},{24,8},{32,48},{40,56},{48,32},{56,40},{64,80... | collective-permute-start | bytes 89096 | tf_op jit(solution)/shard_map/ppermute | solution.py:21
  147.2 26.2 %collective-permute-start.18 = (bf16[64,3,256]{2,0,1:T(8,128)(2,1)S(1)}, bf16[64,3,256]{2,0,1:T(8,128)(2,1)S(1)}, u32[]{:S(2)}, u32[]{:S(2)}) collective-permute-start(bf16[64,3,256]{2,0,1:T(8,128)(2,1)S(1)} %get-tuple-element.34), channel_id=1, source_target_pairs={{0,48},{8,56},{16,0},{24,8},{32,16},{40,24},{48,32},{56,40},{64,11... | collective-permute-start | bytes 294920 | tf_op jit(solution)/shard_map/ppermute | solution.py:48
  148.9 24.5 %collective-permute-start.17 = (bf16[64,3,256]{2,0,1:T(8,128)(2,1)S(1)}, bf16[64,3,256]{2,0,1:T(8,128)(2,1)S(1)}, u32[]{:S(2)}, u32[]{:S(2)}) collective-permute-start(bf16[64,3,256]{2,0,1:T(8,128)(2,1)S(1)} %get-tuple-element.35), channel_id=1, source_target_pairs={{0,32},{8,40},{16,48},{24,56},{32,0},{40,8},{48,16},{56,24},{64,96... | collective-permute-start | bytes 294920 | tf_op jit(solution)/shard_map/ppermute | solution.py:48
  150.9 22.5 %collective-permute-start.16 = (bf16[64,3,256]{2,0,1:T(8,128)(2,1)S(1)}, bf16[64,3,256]{2,0,1:T(8,128)(2,1)S(1)}, u32[]{:S(2)}, u32[]{:S(2)}) collective-permute-start(bf16[64,3,256]{2,0,1:T(8,128)(2,1)S(1)} %get-tuple-element.33), channel_id=1, source_target_pairs={{0,16},{8,24},{16,32},{24,40},{32,48},{40,56},{48,0},{56,8},{64,80... | collective-permute-start | bytes 294920 | tf_op jit(solution)/shard_map/ppermute | solution.py:48
  153.7 8.3 %collective-permute-start.24 = (f32[7424]{0:T(1024)S(1)}, f32[7424]{0:T(1024)S(1)}, u32[]{:S(2)}, u32[]{:S(2)}) collective-permute-start(f32[7424]{0:T(1024)S(1)} %add.575), channel_id=1, source_target_pairs={{0,32},{8,40},{16,48},{24,56},{32,0},{40,8},{48,16},{56,24},{64,96... | collective-permute-start | bytes 89096 | tf_op jit(solution)/shard_map/ppermute | solution.py:21
  162.0 4.7 %collective-permute-start.25 = (f32[7424]{0:T(1024)S(1)}, f32[7424]{0:T(1024)S(1)}, u32[]{:S(2)}, u32[]{:S(2)}) collective-permute-start(f32[7424]{0:T(1024)S(1)} %add.576), channel_id=1, source_target_pairs={{0,64},{8,72},{16,80},{24,88},{32,96},{40,104},{48,112},{56,120},{... | collective-permute-start | bytes 89096 | tf_op jit(solution)/shard_map/ppermute | solution.py:21
  166.8 5.4 %collective-permute-start.26 = (f32[7424]{0:T(1024)S(1)}, f32[7424]{0:T(1024)S(1)}, u32[]{:S(2)}, u32[]{:S(2)}) collective-permute-start(f32[7424]{0:T(1024)S(1)} %add.577), channel_id=1, source_target_pairs={{0,128},{8,136},{16,144},{24,152},{32,160},{40,168},{48,176},{56,1... | collective-permute-start | bytes 89096 | tf_op jit(solution)/shard_map/ppermute | solution.py:21
Sparse Core Ops, SparseCore 0:
  11.4 59.0 all-gather.1
  94.7 53.9 reduce-scatter.1

commit v5 on v2

--- a/solution.py
+++ b/solution.py
@@ -181,8 +181,12 @@
     for tap in range(taps):
         grad_acc = grad_acc + filters[:, tap, :] * grad_extended[tap : tap + length]
     grad_streams = grad_acc.astype(jnp.bfloat16)
+    weight_terms = jnp.einsum(
+        "td,tsc->dsc", positions, grad_streams, preferred_element_type=jnp.float32
+    ).astype(jnp.bfloat16)
+    late_streams, _ = lax.optimization_barrier((grad_streams, weight_terms))
     normed_terms = jnp.einsum(
-        "tsc,dsc->td", grad_streams, weights, preferred_element_type=jnp.float32
+        "tsc,dsc->td", late_streams, weights, preferred_element_type=jnp.float32
     ).astype(jnp.bfloat16)
     late_conv, late_extended, _ = lax.optimization_barrier((grad_conv, extended, normed_terms))
     filter_local = jnp.stack(
@@ -196,9 +200,7 @@
     grad_normed = lax.psum_scatter(
         normed_terms, "tensor", scatter_dimension=0, tiled=True
     ).astype(jnp.float32)
-    weight_terms = jnp.einsum(
-        "td,tsc->dsc", positions, grad_streams, preferred_element_type=jnp.float32
-    ).astype(jnp.bfloat16)
+
     block = proj_weight.shape[0]
     weight_blocks = jnp.take(
         weight_terms.reshape((-1, block) + weight_terms.shape[1:]), d_absolute, axis=0

time: 181 us -> 178 us (0.983)
  matrix products: 21.7 us -> 18.7 us
  waiting for transfers between devices: 47 us -> 49.2 us
  starting transfers between devices: 47.3 us -> 45.2 us
    dot_general x1, matrix products: 8.31 us -> 5.34 us  [body(): jnp.einsum('td,tsc->dsc', positions, grad_streams, preferred_element_type...]
    ppermute x8, waiting for transfers between devices: 24.3 us -> 26.5 us  [butterfly_sum(): value = value + lax.ppermute(value, axis, pairs)]
    ppermute x8, starting transfers between devices: 12.1 us -> 10 us  [butterfly_sum(): value = value + lax.ppermute(value, axis, pairs)]
    unnamed x29 -> x27, local copies, waits for them, and re-layouts: 8.36 us -> 8.3 us
  transfers between devices with their start and end apart: 29 -> 29, of which waited for: 15 -> 15; matrix products, arithmetic and copies ran while one was open for 31% -> 27% of each run, Pallas kernels for 0% -> 0%
where the time goes in v5:
time: 178 us; the launch traced here: 177 us
  waiting for transfers between devices  49.2 us (28%)
  starting transfers between devices  45.2 us (25%)
  other arithmetic  27 us (15%)
  local copies, waits for them, and re-layouts  22.7 us (13%)
  matrix products  18.7 us (11%)
  between operations  14.6 us (8%)
    ppermute x8, waiting for transfers between devices, butterfly_sum(): value = value + lax.ppermute(value, axis, pairs)  26.5 us
    ppermute x16, starting transfers between devices, move(): return lax.ppermute(value, axis, pairs)  22.6 us
    ppermute x16, waiting for transfers between devices, move(): return lax.ppermute(value, axis, pairs)  17.8 us
    ppermute x3, starting transfers between devices, passed_along(): return lax.ppermute(shard, axis, pairs)  12.5 us
    ppermute x8, starting transfers between devices, butterfly_sum(): value = value + lax.ppermute(value, axis, pairs)  10 us
    unnamed x27, local copies, waits for them, and re-layouts  8.3 us
    dot_general x1, matrix products, body(): jnp.einsum('td,dsc->tsc', positions, weights, preferred_element_type=jnp....  5.68 us
    dot_general x1, matrix products, body(): jnp.einsum('td,tsc->dsc', positions, grad_streams, preferred_element_type...  5.34 us
  transfers between devices with their start and end apart: 29, of which 15 were waited for; matrix products, arithmetic and copies ran while one was open for 27% of the time, Pallas kernels for 0%

profile of v5, /device:TPU:10, one launch (start us, length us, event | category | flops | bytes accessed | tf_op | source)
XLA Modules:
  0.0 177.4 jit_solution(11468158030664895116)
XLA Ops:
  7.2 0.6 collective-permute-start
  7.8 1.5 collective-permute-start.1
  9.3 1.9 %collective-permute-start.4 = (bf16[128,2048]{1,0:T(8,128)(2,1)}, bf16[128,2048]{1,0:T(8,128)(2,1)S(1)}, u32[]{:S(2)}, u32[]{:S(2)}) collective-permute-start(bf16[128,2048]{1,0:T(8,128)(2,1)} %param.5), channel_id=1, source_target_pairs={{0,4},{1,5},{2,6},{3,7},{4,0},{5,1},{6,2},{7,3},{8,12},{9,13},{10,... | collective-permute-start | bytes 1572872 | tf_op jit(solution)/shard_map/ppermute | solution.py:48
  11.3 0.7 slice.239
  12.0 5.8 %collective-permute-start.11 = (bf16[6,256]{1,0:T(8,128)(2,1)S(1)}, bf16[6,256]{1,0:T(8,128)(2,1)S(1)}, u32[]{:S(2)}, u32[]{:S(2)}) collective-permute-start(bf16[6,256]{1,0:T(8,128)(2,1)S(1)} %slice.239), channel_id=1, source_target_pairs={{8,0},{16,8},{24,16},{32,24},{40,32},{48,40},{56,48},{64,56},{72,6... | collective-permute-start | bytes 9224 | tf_op jit(solution)/shard_map/ppermute | solution.py:13
  17.9 1.0 fusion.100
  19.0 1.9 %bitcast_dynamic-update-slice_fusion.5 = bf16[8,128,2048]{2,1,0:T(8,128)(2,1)} fusion(bf16[128,2048]{1,0:T(8,128)(2,1)} %param.5), kind=kLoop, calls=%fused_computation.87 | loop fusion | bytes 1048576
  21.2 1.4 collective-permute-start.3
  22.6 0.8 collective-permute-start.2
  23.4 2.6 %collective-permute-start.5 = (bf16[128,2048]{1,0:T(8,128)(2,1)S(1)}, bf16[128,2048]{1,0:T(8,128)(2,1)S(1)}, u32[]{:S(2)}, u32[]{:S(2)}) collective-permute-start(bf16[128,2048]{1,0:T(8,128)(2,1)S(1)} %collective-permute-done.4), channel_id=1, source_target_pairs={{0,3},{1,0},{2,1},{3,2},{4,7},{5,4},{6,5},{7,6},{8,11},{9,8},{10,9... | collective-permute-start | bytes 1572872 | tf_op jit(solution)/shard_map/ppermute | solution.py:48
  26.0 0.8 bitcast_dynamic-update-slice_fusion.4
  26.8 3.7 %collective-permute-done.3 = bf16[64,2048]{1,0:T(8,128)(2,1)S(1)} collective-permute-done((bf16[64,2048]{1,0:T(8,128)(2,1)S(1)}, bf16[64,2048]{1,0:T(8,128)(2,1)S(1)}, u32[]{:S(2)}, u32[]{:S(2)}) %collective-permute-start.3) | collective-permute-done | bytes 262176 | tf_op jit(solution)/shard_map/ppermute | solution.py:48
  30.5 2.6 %collective-permute-done.2 = bf16[64,2048]{1,0:T(8,128)(2,1)S(1)} collective-permute-done((bf16[64,2048]{1,0:T(8,128)(2,1)S(1)}, bf16[64,2048]{1,0:T(8,128)(2,1)S(1)}, u32[]{:S(2)}, u32[]{:S(2)}) %collective-permute-start.2) | collective-permute-done | bytes 262176 | tf_op jit(solution)/shard_map/ppermute | solution.py:48
  33.1 0.9 fusion.32
  34.0 0.9 bitcast_dynamic-update-slice_fusion.3
  34.8 0.8 bitcast_dynamic-update-slice_fusion.2
  35.7 4.0 %collective-permute-done.5 = bf16[128,2048]{1,0:T(8,128)(2,1)S(1)} collective-permute-done((bf16[128,2048]{1,0:T(8,128)(2,1)S(1)}, bf16[128,2048]{1,0:T(8,128)(2,1)S(1)}, u32[]{:S(2)}, u32[]{:S(2)}) %collective-permute-start.5) | collective-permute-done | bytes 524320 | tf_op jit(solution)/shard_map/ppermute | solution.py:48
  39.7 2.1 %collective-permute-start.8 = (bf16[64,2048]{1,0:T(8,128)(2,1)S(1)}, bf16[64,2048]{1,0:T(8,128)(2,1)S(1)}, u32[]{:S(2)}, u32[]{:S(2)}) collective-permute-start(bf16[64,2048]{1,0:T(8,128)(2,1)S(1)} %slice.284), channel_id=1, source_target_pairs={{0,3},{1,0},{2,1},{3,2},{4,7},{5,4},{6,5},{7,6},{8,11},{9,8},{10,9... | collective-permute-start | bytes 786440 | tf_op jit(solution)/shard_map/ppermute | solution.py:48
  42.4 0.8 bitcast_dynamic-update-slice_fusion.1
  43.2 3.5 %collective-permute-done.8 = bf16[64,2048]{1,0:T(8,128)(2,1)S(1)} collective-permute-done((bf16[64,2048]{1,0:T(8,128)(2,1)S(1)}, bf16[64,2048]{1,0:T(8,128)(2,1)S(1)}, u32[]{:S(2)}, u32[]{:S(2)}) %collective-permute-start.8) | collective-permute-done | bytes 262176 | tf_op jit(solution)/shard_map/ppermute | solution.py:48
  46.7 3.2 %collective-permute-done.7 = bf16[64,2048]{1,0:T(8,128)(2,1)S(1)} collective-permute-done((bf16[64,2048]{1,0:T(8,128)(2,1)S(1)}, bf16[64,2048]{1,0:T(8,128)(2,1)S(1)}, u32[]{:S(2)}, u32[]{:S(2)}) %collective-permute-start.7) | collective-permute-done | bytes 262176 | tf_op jit(solution)/shard_map/ppermute | solution.py:48
  49.9 0.8 fusion.33
  50.8 0.8 bitcast_dynamic-update-slice_fusion
  51.6 5.0 %gather_fusion = bf16[8,128,2048]{2,1,0:T(8,128)(2,1)} fusion(bf16[8,128,2048]{2,1,0:T(8,128)(2,1)} %bitcast_dynamic-update-slice_fusion, s32[1024]{0:T(1024)S(1)} %pad_clamp_fusion.1), kind=kCustom, calls=%fused_computation | custom fusion | bytes 8388640 | tf_op jit(solution)/shard_map/jit(_take)/gather | solution.py:129
  56.6 2.8 %bitcast_select_fusion = bf16[1024,2048]{1,0:T(8,128)(2,1)S(1)} fusion(bf16[8,128,2048]{2,1,0:T(8,128)(2,1)} %gather_fusion, pred[1024]{0:T(1024)(128)(4,1)S(1)} %broadcast_bitcast_fusion), kind=kLoop, calls=%fused_computation.8 | loop fusion | flops 2097152 | bytes 8389632 | tf_op jit(solution)/shard_map/jit(_take)/select_n | solution.py:129
  59.5 4.6 %collective-permute-start.10 = (bf16[6,2048]{1,0:T(8,128)(2,1)S(1)}, bf16[6,2048]{1,0:T(8,128)(2,1)S(1)}, u32[]{:S(2)}, u32[]{:S(2)}) collective-permute-start(bf16[6,2048]{1,0:T(8,128)(2,1)S(1)} %get-tuple-element.25), channel_id=1, source_target_pairs={{8,0},{16,8},{24,16},{32,24},{40,32},{48,40},{56,48},{64,56},{72,6... | collective-permute-start | bytes 73736 | tf_op jit(solution)/shard_map/ppermute | solution.py:13
  64.1 2.1 %collective-permute-start.9 = (bf16[6,2048]{1,0:T(8,128)(2,1)S(1)}, bf16[6,2048]{1,0:T(8,128)(2,1)S(1)}, u32[]{:S(2)}, u32[]{:S(2)}) collective-permute-start(bf16[6,2048]{1,0:T(8,128)(2,1)S(1)} %get-tuple-element.24), channel_id=1, source_target_pairs={{0,8},{8,16},{16,24},{24,32},{32,40},{40,48},{48,56},{56,64},{64,7... | collective-permute-start | bytes 73736 | tf_op jit(solution)/shard_map/ppermute | solution.py:13
  66.3 1.2 multiply_reduce_fusion.1
  67.5 4.9 %collective-permute-done.9 = bf16[6,2048]{1,0:T(8,128)(2,1)S(1)} collective-permute-done((bf16[6,2048]{1,0:T(8,128)(2,1)S(1)}, bf16[6,2048]{1,0:T(8,128)(2,1)S(1)}, u32[]{:S(2)}, u32[]{:S(2)}) %collective-permute-start.9) | collective-permute-done | bytes 24608 | tf_op jit(solution)/shard_map/ppermute | solution.py:13
  72.6 2.6 %convolution_convert_fusion.1 = bf16[12,3,256]{2,0,1:T(8,128)(2,1)S(1)} fusion(bf16[2048,3,256]{2,0,1:T(8,128)(2,1)} %all-gather.2.cloned.1.call-done, f32[2048]{0:T(1024)S(1)} %copy-done.8, f32[12]{0:T(128)S(1)} %add_rsqrt_fusion.1, bf16[6,2048]{1,0:T(8,128)(2,1)S(1)} %collective-permute-done.10, bf16[6,2048]{1,0:T(8,128)(2,1)S(1)} %collective-permute-done.9), kind=kOutput, calls=%fused_computation.57 | convolution fusion | flops 37929984 | bytes 3221552 | tf_op jit(solution)/shard_map/td,dsc->tsc/dot_general | solution.py:148
  75.4 5.7 %fusion.17 = bf16[1024,3,256]{2,0,1:T(8,128)(2,1)S(1)} fusion(bf16[2048,3,256]{2,0,1:T(8,128)(2,1)S(1)} %copy-done.6, bf16[1024,2048]{1,0:T(8,128)(2,1)} %copy-done.4, f32[2048]{0:T(1024)S(1)} %copy-done.8, f32[1024]{0:T(1024)S(1)} %rsqrt_bitcast_fusion), kind=kOutput, calls=%fused_computation.48 | convolution fusion | flops 3230400512 | bytes 8925184 | tf_op jit(solution)/shard_map/td,dsc->tsc/dot_general | solution.py:145
  81.5 2.6 %fusion.8 = f32[1024,3,256]{2,0,1:T(8,128)S(1)} fusion(f32[1030,3,256]{2,0,1:T(8,128)S(1)} %maximum_convert_fusion, f32[3,256]{1,0:T(4,128)S(1)} %get-tuple-element.52, f32[3,256]{1,0:T(4,128)S(1)} %get-tuple-element.53, f32[3,256]{1,0:T(4,128)S(1)} %get-tuple-element.54, f32[3,256]{1,0:T(4,128)S(1)} %get-tuple-element.55, ...), kind=kLoop, calls=%fused_computation.25 | loop fusion | flops 10223616 | bytes 25187328 | tf_op jit(solution)/shard_map/add | solution.py:154
  84.1 1.2 fusion.21
  85.6 3.8 %pad_maximum_fusion = (f32[1024,3,256]{2,0,1:T(8,128)}, bf16[1024,3,256]{2,0,1:T(8,128)(2,1)S(1)}) fusion(f32[1024,1,256]{2,0,1:T(8,128)S(1)} %get-tuple-element.27, f32[1024,1,256]{2,0,1:T(8,128)S(1)} %get-tuple-element.28, f32[1024,1,256]{2,0,1:T(8,128)S(1)} %get-tuple-element.26, f32[1030,3,256]{2,0,1:T(8,128)S(1)} %maximum_maximum_fusion, ...), kind=kLoop, calls=%fused_computation.37 | loop fusion | flops 12582912 | bytes 26760192 | tf_op jit(solution)/shard_map/stack | solution.py:157
  89.4 5.3 %convolution_convert_fusion = bf16[2048,3,256]{2,0,1:T(8,128)(2,1)} fusion(bf16[1024,3,256]{2,0,1:T(8,128)(2,1)S(1)} %get-tuple-element.8, bf16[1024,2048]{1,0:T(8,128)(2,1)S(1)} %copy-done.5, f32[2048]{0:T(1024)S(1)} %copy-done.8, f32[1024]{0:T(1024)S(1)} %rsqrt_bitcast_fusion), kind=kOutput, calls=%fused_computation.9 | convolution fusion | flops 3231186944 | bytes 8925184 | tf_op jit(solution)/shard_map/td,tsc->dsc/dot_general | solution.py:184
  94.7 5.1 %multiply_reduce_fusion = (f32[2048]{0:T(1024)S(1)}, bf16[1024,2048]{1,0:T(8,128)(2,1)}) fusion(bf16[1024,2048]{1,0:T(8,128)(2,1)S(1)} %copy-done.5, f32[1024]{0:T(1024)S(1)} %rsqrt_bitcast_fusion, bf16[1024,3,256]{2,0,1:T(8,128)(2,1)S(1)} %get-tuple-element.8, bf16[2048,3,256]{2,0,1:T(8,128)(2,1)S(1)} %copy-done.6), kind=kOutput, calls=%fused_computation.3 | convolution fusion | flops 3233806336 | bytes 13119488 | tf_op jit(solution)/shard_map/tsc,dsc->td/dot_general | solution.py:188
  100.1 4.4 %gather_fusion.1 = bf16[32,64,3,256]{3,1,2,0:T(8,128)(2,1)} fusion(bf16[32,64,3,256]{3,1,0,2:T(8,128)(2,1)} %bitcast.165, s32[1024]{0:T(1024)S(1)} %pad_clamp_fusion), kind=kCustom, calls=%fused_computation.1 | custom fusion | bytes 6291584 | tf_op jit(solution)/shard_map/jit(_take)/gather | solution.py:205
  104.5 2.2 %broadcast_select_fusion = bf16[4,4,2,64,3,256]{5,3,4,2,1,0:T(8,128)(2,1)S(1)} fusion(bf16[4,4,2,64,3,256]{5,3,4,2,1,0:T(8,128)(2,1)} %bitcast.164, pred[4,4,2]{2,1,0:T(4,128)(4,1)S(1)} %compare_and_fusion), kind=kLoop, calls=%fused_computation.46 | loop fusion | flops 1572864 | bytes 6291488 | tf_op jit(solution)/shard_map/jit(_take)/select_n | solution.py:205
  106.7 1.7 copy-done.2
  108.5 1.4 slice_bitcast_fusion
  109.9 1.1 copy-done.1
  110.9 2.7 %multiply_reduce_fusion.2 = (f32[3,256]{1,0:T(4,128)S(1)}, f32[3,256]{1,0:T(4,128)S(1)}, f32[3,256]{1,0:T(4,128)S(1)}, f32[3,256]{1,0:T(4,128)S(1)}, f32[3,256]{...) fusion(f32[1024,3,256]{2,0,1:T(8,128)S(1)} %copy-done.1, f32[1030,3,256]{2,0,1:T(8,128)S(1)} %maximum_convert_fusion), kind=kLoop, calls=%fused_computation.39 | loop fusion | flops 11004672 | bytes 25187328 | tf_op jit(solution)/shard_map/reduce_sum | solution.py:194
  113.8 2.7 %convert_add_fusion = (f32[4,4,64,3,256]{4,2,3,1,0:T(8,128)S(1)}, bf16[4,4,64,3,256]{4,2,3,1,0:T(8,128)(2,1)S(1)}) fusion(bf16[4,4,64,3,256]{4,2,3,1,0:T(8,128)(2,1)} %collective-permute-done.12, bf16[4,4,2,64,3,256]{5,3,4,2,1,0:T(8,128)(2,1)} %copy-done.2), kind=kLoop, calls=%fused_computation.38 | loop fusion | flops 3145728 | bytes 7864320 | tf_op jit(solution)/shard_map/add | solution.py:115
  116.7 3.1 %collective-permute-start.14 = (bf16[4,64,3,256]{3,1,2,0:T(8,128)(2,1)S(1)}, bf16[4,64,3,256]{3,1,2,0:T(8,128)(2,1)S(1)}, u32[]{:S(2)}, u32[]{:S(2)}) collective-permute-start(bf16[4,64,3,256]{3,1,2,0:T(8,128)(2,1)S(1)} %get-tuple-element.34), channel_id=1, source_target_pairs={{0,128},{8,136},{16,144},{24,152},{32,160},{40,168},{48,176},{56,1... | collective-permute-start | bytes 1179656 | tf_op jit(solution)/shard_map/ppermute | solution.py:48
  119.8 2.2 %collective-permute-start.13 = (bf16[4,64,3,256]{3,1,2,0:T(8,128)(2,1)S(1)}, bf16[4,64,3,256]{3,1,2,0:T(8,128)(2,1)S(1)}, u32[]{:S(2)}, u32[]{:S(2)}) collective-permute-start(bf16[4,64,3,256]{3,1,2,0:T(8,128)(2,1)S(1)} %get-tuple-element.32), channel_id=1, source_target_pairs={{0,64},{8,72},{16,80},{24,88},{32,96},{40,104},{48,112},{56,120},{... | collective-permute-start | bytes 1179656 | tf_op jit(solution)/shard_map/ppermute | solution.py:48
  122.0 1.2 collective-permute-done.19
  123.3 5.2 %collective-permute-done.20 = f32[7424]{0:T(1024)S(1)} collective-permute-done((f32[7424]{0:T(1024)S(1)}, f32[7424]{0:T(1024)S(1)}, u32[]{:S(2)}, u32[]{:S(2)}) %collective-permute-start.20) | collective-permute-done | bytes 29728 | tf_op jit(solution)/shard_map/ppermute | solution.py:21
  128.5 2.8 %collective-permute-start.21 = (f32[7424]{0:T(1024)S(1)}, f32[7424]{0:T(1024)S(1)}, u32[]{:S(2)}, u32[]{:S(2)}) collective-permute-start(f32[7424]{0:T(1024)S(1)} %add.572), channel_id=1, source_target_pairs={{0,32},{8,40},{16,48},{24,56},{32,0},{40,8},{48,16},{56,24},{64,96... | collective-permute-start | bytes 89096 | tf_op jit(solution)/shard_map/ppermute | solution.py:21
  131.3 5.1 %collective-permute-done.21 = f32[7424]{0:T(1024)S(1)} collective-permute-done((f32[7424]{0:T(1024)S(1)}, f32[7424]{0:T(1024)S(1)}, u32[]{:S(2)}, u32[]{:S(2)}) %collective-permute-start.21) | collective-permute-done | bytes 29728 | tf_op jit(solution)/shard_map/ppermute | solution.py:21
  136.5 3.9 %collective-permute-done.22 = f32[7424]{0:T(1024)S(1)} collective-permute-done((f32[7424]{0:T(1024)S(1)}, f32[7424]{0:T(1024)S(1)}, u32[]{:S(2)}, u32[]{:S(2)}) %collective-permute-start.22) | collective-permute-done | bytes 29728 | tf_op jit(solution)/shard_map/ppermute | solution.py:21
  140.4 1.1 collective-permute-start.23
  141.5 4.3 %collective-permute-done.23 = f32[7424]{0:T(1024)S(1)} collective-permute-done((f32[7424]{0:T(1024)S(1)}, f32[7424]{0:T(1024)S(1)}, u32[]{:S(2)}, u32[]{:S(2)}) %collective-permute-start.23) | collective-permute-done | bytes 29728 | tf_op jit(solution)/shard_map/ppermute | solution.py:21
  145.8 4.6 %collective-permute-start.24 = (f32[2048]{0:T(1024)S(1)}, f32[2048]{0:T(1024)S(1)}, u32[]{:S(2)}, u32[]{:S(2)}) collective-permute-start(f32[2048]{0:T(1024)S(1)} %slice.327), channel_id=1, source_target_pairs={{0,1},{1,0},{2,3},{3,2},{4,5},{5,4},{6,7},{7,6},{8,9},{9,8},{10,11... | collective-permute-start | bytes 24584 | tf_op jit(solution)/shard_map/ppermute | solution.py:21
  150.6 1.7 collective-permute-start.18
  152.3 2.2 %collective-permute-start.17 = (bf16[64,3,256]{2,0,1:T(8,128)(2,1)S(1)}, bf16[64,3,256]{2,0,1:T(8,128)(2,1)S(1)}, u32[]{:S(2)}, u32[]{:S(2)}) collective-permute-start(bf16[64,3,256]{2,0,1:T(8,128)(2,1)S(1)} %get-tuple-element.37), channel_id=1, source_target_pairs={{0,32},{8,40},{16,48},{24,56},{32,0},{40,8},{48,16},{56,24},{64,96... | collective-permute-start | bytes 294920 | tf_op jit(solution)/shard_map/ppermute | solution.py:48
  154.5 2.3 %collective-permute-start.16 = (bf16[64,3,256]{2,0,1:T(8,128)(2,1)S(1)}, bf16[64,3,256]{2,0,1:T(8,128)(2,1)S(1)}, u32[]{:S(2)}, u32[]{:S(2)}) collective-permute-start(bf16[64,3,256]{2,0,1:T(8,128)(2,1)S(1)} %get-tuple-element.35), channel_id=1, source_target_pairs={{0,16},{8,24},{16,32},{24,40},{32,48},{40,56},{48,0},{56,8},{64,80... | collective-permute-start | bytes 294920 | tf_op jit(solution)/shard_map/ppermute | solution.py:48
  156.9 5.1 %collective-permute-done.25 = f32[2048]{0:T(1024)S(1)} collective-permute-done((f32[2048]{0:T(1024)S(1)}, f32[2048]{0:T(1024)S(1)}, u32[]{:S(2)}, u32[]{:S(2)}) %collective-permute-start.25) | collective-permute-done | bytes 8224 | tf_op jit(solution)/shard_map/ppermute | solution.py:21
  162.1 1.3 collective-permute-start.26
  163.4 0.6 reshape.543
  164.1 1.7 collective-permute-done.26
  165.7 0.6 add.578
  166.4 0.7 fusion.37
  167.0 1.4 fusion.22
  168.4 2.2 %fusion.27 = bf16[128,2048]{1,0:T(8,128)(2,1)} fusion(bf16[128,2048]{1,0:T(8,128)(2,1)S(1)} %copy-done.3, bf16[128,2048]{1,0:T(8,128)(2,1)} %reduce-scatter.2.cloned.1.call-done, f32[128]{0:T(128)S(1)} %broadcast_multiply_fusion, f32[2048]{0:T(1024)S(1)} %copy-done.8, f32[128]{0:T(128)S(1)} %add_rsqrt_fusion), kind=kLoop, calls=%fused_computation.65 | loop fusion | flops 2359296 | bytes 1582080 | tf_op jit(solution)/shard_map/convert_element_type | solution.py:216
  (94 shorter events, 3.1 us)
Async XLA Ops:
  7.2 65.4 %all-gather.2.cloned.1.call-start = ((), (), s32[]{:S(2)}) async-start(), calls=%async_computation.1 | async-start | bytes 3244032 | tf_op jit(solution)/shard_map/all_gather | solution.py:128
  7.2 14.0 %collective-permute-start = (bf16[128,2048]{1,0:T(8,128)(2,1)}, bf16[128,2048]{1,0:T(8,128)(2,1)S(1)}, u32[]{:S(2)}, u32[]{:S(2)}) collective-permute-start(bf16[128,2048]{1,0:T(8,128)(2,1)} %param.5), channel_id=1, source_target_pairs={{0,3},{1,0},{2,1},{3,2},{4,7},{5,4},{6,5},{7,6},{8,11},{9,8},{10,9... | collective-permute-start | bytes 1572872 | tf_op jit(solution)/shard_map/ppermute | solution.py:48
  7.8 14.7 %collective-permute-start.1 = (bf16[128,2048]{1,0:T(8,128)(2,1)}, bf16[128,2048]{1,0:T(8,128)(2,1)S(1)}, u32[]{:S(2)}, u32[]{:S(2)}) collective-permute-start(bf16[128,2048]{1,0:T(8,128)(2,1)} %param.5), channel_id=1, source_target_pairs={{0,1},{1,2},{2,3},{3,0},{4,5},{5,6},{6,7},{7,4},{8,9},{9,10},{10,1... | collective-permute-start | bytes 1572872 | tf_op jit(solution)/shard_map/ppermute | solution.py:48
  9.3 14.1 %collective-permute-start.4 = (bf16[128,2048]{1,0:T(8,128)(2,1)}, bf16[128,2048]{1,0:T(8,128)(2,1)S(1)}, u32[]{:S(2)}, u32[]{:S(2)}) collective-permute-start(bf16[128,2048]{1,0:T(8,128)(2,1)} %param.5), channel_id=1, source_target_pairs={{0,4},{1,5},{2,6},{3,7},{4,0},{5,1},{6,2},{7,3},{8,12},{9,13},{10,... | collective-permute-start | bytes 1572872 | tf_op jit(solution)/shard_map/ppermute | solution.py:48
  11.3 155.8 %reduce-scatter.2.cloned.1.call-start = ((), (), s32[]{:S(2)}) async-start(), calls=%async_computation.2 | async-start | bytes 4718592 | tf_op jit(solution)/shard_map/reduce_scatter | solution.py:200
  12.0 73.3 %collective-permute-start.11 = (bf16[6,256]{1,0:T(8,128)(2,1)S(1)}, bf16[6,256]{1,0:T(8,128)(2,1)S(1)}, u32[]{:S(2)}, u32[]{:S(2)}) collective-permute-start(bf16[6,256]{1,0:T(8,128)(2,1)S(1)} %slice.239), channel_id=1, source_target_pairs={{8,0},{16,8},{24,16},{32,24},{40,32},{48,40},{56,48},{64,56},{72,6... | collective-permute-start | bytes 9224 | tf_op jit(solution)/shard_map/ppermute | solution.py:13
  21.2 9.3 %collective-permute-start.3 = (bf16[64,2048]{1,0:T(8,128)(2,1)S(1)}, bf16[64,2048]{1,0:T(8,128)(2,1)S(1)}, u32[]{:S(2)}, u32[]{:S(2)}) collective-permute-start(bf16[64,2048]{1,0:T(8,128)(2,1)S(1)} %slice.282), channel_id=1, source_target_pairs={{0,3},{1,0},{2,1},{3,2},{4,7},{5,4},{6,5},{7,6},{8,11},{9,8},{10,9... | collective-permute-start | bytes 786440 | tf_op jit(solution)/shard_map/ppermute | solution.py:48
  22.6 10.5 %collective-permute-start.2 = (bf16[64,2048]{1,0:T(8,128)(2,1)S(1)}, bf16[64,2048]{1,0:T(8,128)(2,1)S(1)}, u32[]{:S(2)}, u32[]{:S(2)}) collective-permute-start(bf16[64,2048]{1,0:T(8,128)(2,1)S(1)} %slice.281), channel_id=1, source_target_pairs={{0,1},{1,2},{2,3},{3,0},{4,5},{5,6},{6,7},{7,4},{8,9},{9,10},{10,1... | collective-permute-start | bytes 786440 | tf_op jit(solution)/shard_map/ppermute | solution.py:48
  23.4 16.3 %collective-permute-start.5 = (bf16[128,2048]{1,0:T(8,128)(2,1)S(1)}, bf16[128,2048]{1,0:T(8,128)(2,1)S(1)}, u32[]{:S(2)}, u32[]{:S(2)}) collective-permute-start(bf16[128,2048]{1,0:T(8,128)(2,1)S(1)} %collective-permute-done.4), channel_id=1, source_target_pairs={{0,3},{1,0},{2,1},{3,2},{4,7},{5,4},{6,5},{7,6},{8,11},{9,8},{10,9... | collective-permute-start | bytes 1572872 | tf_op jit(solution)/shard_map/ppermute | solution.py:48
  26.0 16.3 %collective-permute-start.6 = (bf16[128,2048]{1,0:T(8,128)(2,1)S(1)}, bf16[128,2048]{1,0:T(8,128)(2,1)S(1)}, u32[]{:S(2)}, u32[]{:S(2)}) collective-permute-start(bf16[128,2048]{1,0:T(8,128)(2,1)S(1)} %collective-permute-done.4), channel_id=1, source_target_pairs={{0,1},{1,2},{2,3},{3,0},{4,5},{5,6},{6,7},{7,4},{8,9},{9,10},{10,1... | collective-permute-start | bytes 1572872 | tf_op jit(solution)/shard_map/ppermute | solution.py:48
  39.7 7.0 %collective-permute-start.8 = (bf16[64,2048]{1,0:T(8,128)(2,1)S(1)}, bf16[64,2048]{1,0:T(8,128)(2,1)S(1)}, u32[]{:S(2)}, u32[]{:S(2)}) collective-permute-start(bf16[64,2048]{1,0:T(8,128)(2,1)S(1)} %slice.284), channel_id=1, source_target_pairs={{0,3},{1,0},{2,1},{3,2},{4,7},{5,4},{6,5},{7,6},{8,11},{9,8},{10,9... | collective-permute-start | bytes 786440 | tf_op jit(solution)/shard_map/ppermute | solution.py:48
  42.3 7.7 %collective-permute-start.7 = (bf16[64,2048]{1,0:T(8,128)(2,1)S(1)}, bf16[64,2048]{1,0:T(8,128)(2,1)S(1)}, u32[]{:S(2)}, u32[]{:S(2)}) collective-permute-start(bf16[64,2048]{1,0:T(8,128)(2,1)S(1)} %slice.283), channel_id=1, source_target_pairs={{0,1},{1,2},{2,3},{3,0},{4,5},{5,6},{6,7},{7,4},{8,9},{9,10},{10,1... | collective-permute-start | bytes 786440 | tf_op jit(solution)/shard_map/ppermute | solution.py:48
  56.6 9.6 %copy-start = (bf16[8,128,2048]{2,1,0:T(8,128)(2,1)S(1)}, bf16[8,128,2048]{2,1,0:T(8,128)(2,1)}, u32[]{:S(2)}) copy-start(bf16[8,128,2048]{2,1,0:T(8,128)(2,1)} %gather_fusion) | copy-start | bytes 12582916
  59.5 8.0 %copy-start.4 = (bf16[1024,2048]{1,0:T(8,128)(2,1)}, bf16[1024,2048]{1,0:T(8,128)(2,1)S(1)}, u32[]{:S(2)}) copy-start(bf16[1024,2048]{1,0:T(8,128)(2,1)S(1)} %bitcast_select_fusion) | copy-start | bytes 12582916
  59.5 13.1 %copy-start.8 = (f32[2048]{0:T(1024)S(1)}, f32[2048]{0:T(1024)}, u32[]{:S(2)}) copy-start(f32[2048]{0:T(1024)} %param.6) | copy-start | bytes 24580
  59.5 8.0 %collective-permute-start.10 = (bf16[6,2048]{1,0:T(8,128)(2,1)S(1)}, bf16[6,2048]{1,0:T(8,128)(2,1)S(1)}, u32[]{:S(2)}, u32[]{:S(2)}) collective-permute-start(bf16[6,2048]{1,0:T(8,128)(2,1)S(1)} %get-tuple-element.25), channel_id=1, source_target_pairs={{8,0},{16,8},{24,16},{32,24},{40,32},{48,40},{56,48},{64,56},{72,6... | collective-permute-start | bytes 73736 | tf_op jit(solution)/shard_map/ppermute | solution.py:13
  64.1 8.3 %collective-permute-start.9 = (bf16[6,2048]{1,0:T(8,128)(2,1)S(1)}, bf16[6,2048]{1,0:T(8,128)(2,1)S(1)}, u32[]{:S(2)}, u32[]{:S(2)}) collective-permute-start(bf16[6,2048]{1,0:T(8,128)(2,1)S(1)} %get-tuple-element.24), channel_id=1, source_target_pairs={{0,8},{8,16},{16,24},{24,32},{32,40},{40,48},{48,56},{56,64},{64,7... | collective-permute-start | bytes 73736 | tf_op jit(solution)/shard_map/ppermute | solution.py:13
  72.6 2.8 %copy-start.6 = (bf16[2048,3,256]{2,0,1:T(8,128)(2,1)S(1)}, bf16[2048,3,256]{2,0,1:T(8,128)(2,1)}, u32[]{:S(2)}) copy-start(bf16[2048,3,256]{2,0,1:T(8,128)(2,1)} %all-gather.2.cloned.1.call-done) | copy-start | bytes 9437188
  81.4 2.6 %copy-start.7 = (bf16[1024,256]{1,0:T(8,128)(2,1)S(1)}, bf16[1024,256]{1,0:T(8,128)(2,1)}, u32[]{:S(2)}) copy-start(bf16[1024,256]{1,0:T(8,128)(2,1)} %param.9) | copy-start | bytes 1572868
  85.6 3.8 %copy-start.5 = (bf16[1024,2048]{1,0:T(8,128)(2,1)S(1)}, bf16[1024,2048]{1,0:T(8,128)(2,1)}, u32[]{:S(2)}) copy-start(bf16[1024,2048]{1,0:T(8,128)(2,1)} %copy-done.4) | copy-start | bytes 12582916
  106.7 1.7 copy-start.2
  108.5 2.5 %copy-start.1 = (f32[1024,3,256]{2,0,1:T(8,128)S(1)}, f32[1024,3,256]{2,0,1:T(8,128)}, u32[]{:S(2)}) copy-start(f32[1024,3,256]{2,0,1:T(8,128)} %get-tuple-element.9) | copy-start | bytes 9437188
  109.9 3.9 %collective-permute-start.12 = (bf16[4,4,64,3,256]{4,2,3,1,0:T(8,128)(2,1)}, bf16[4,4,64,3,256]{4,2,3,1,0:T(8,128)(2,1)}, u32[]{:S(2)}, u32[]{:S(2)}) collective-permute-start(bf16[4,4,64,3,256]{4,2,3,1,0:T(8,128)(2,1)} %slice_bitcast_fusion), channel_id=1, source_target_pairs={{0,8},{8,0},{16,24},{24,16},{32,40},{40,32},{48,56},{56,48},{64,72... | collective-permute-start | bytes 4718600 | tf_op jit(solution)/shard_map/ppermute | solution.py:48
  116.5 50.6 %copy-start.3 = (bf16[128,2048]{1,0:T(8,128)(2,1)S(1)}, bf16[128,2048]{1,0:T(8,128)(2,1)}, u32[]{:S(2)}) copy-start(bf16[128,2048]{1,0:T(8,128)(2,1)} %param.5) | copy-start | bytes 1572868
  116.6 33.8 %collective-permute-start.15 = (bf16[4,64,3,256]{3,1,2,0:T(8,128)(2,1)S(1)}, bf16[4,64,3,256]{3,1,2,0:T(8,128)(2,1)S(1)}, u32[]{:S(2)}, u32[]{:S(2)}) collective-permute-start(bf16[4,64,3,256]{3,1,2,0:T(8,128)(2,1)S(1)} %get-tuple-element.33), channel_id=1, source_target_pairs={{0,192},{8,200},{16,208},{24,216},{32,224},{40,232},{48,240},{56,2... | collective-permute-start | bytes 1179656 | tf_op jit(solution)/shard_map/ppermute | solution.py:48
  116.7 33.7 %collective-permute-start.14 = (bf16[4,64,3,256]{3,1,2,0:T(8,128)(2,1)S(1)}, bf16[4,64,3,256]{3,1,2,0:T(8,128)(2,1)S(1)}, u32[]{:S(2)}, u32[]{:S(2)}) collective-permute-start(bf16[4,64,3,256]{3,1,2,0:T(8,128)(2,1)S(1)} %get-tuple-element.34), channel_id=1, source_target_pairs={{0,128},{8,136},{16,144},{24,152},{32,160},{40,168},{48,176},{56,1... | collective-permute-start | bytes 1179656 | tf_op jit(solution)/shard_map/ppermute | solution.py:48
  119.8 30.6 %collective-permute-start.13 = (bf16[4,64,3,256]{3,1,2,0:T(8,128)(2,1)S(1)}, bf16[4,64,3,256]{3,1,2,0:T(8,128)(2,1)S(1)}, u32[]{:S(2)}, u32[]{:S(2)}) collective-permute-start(bf16[4,64,3,256]{3,1,2,0:T(8,128)(2,1)S(1)} %get-tuple-element.32), channel_id=1, source_target_pairs={{0,64},{8,72},{16,80},{24,88},{32,96},{40,104},{48,112},{56,120},{... | collective-permute-start | bytes 1179656 | tf_op jit(solution)/shard_map/ppermute | solution.py:48
  122.0 1.2 collective-permute-start.19
  123.2 5.3 %collective-permute-start.20 = (f32[7424]{0:T(1024)S(1)}, f32[7424]{0:T(1024)S(1)}, u32[]{:S(2)}, u32[]{:S(2)}) collective-permute-start(f32[7424]{0:T(1024)S(1)} %fusion.94), channel_id=1, source_target_pairs={{0,16},{8,24},{16,0},{24,8},{32,48},{40,56},{48,32},{56,40},{64,80... | collective-permute-start | bytes 89096 | tf_op jit(solution)/shard_map/ppermute | solution.py:21
  128.5 7.9 %collective-permute-start.21 = (f32[7424]{0:T(1024)S(1)}, f32[7424]{0:T(1024)S(1)}, u32[]{:S(2)}, u32[]{:S(2)}) collective-permute-start(f32[7424]{0:T(1024)S(1)} %add.572), channel_id=1, source_target_pairs={{0,32},{8,40},{16,48},{24,56},{32,0},{40,8},{48,16},{56,24},{64,96... | collective-permute-start | bytes 89096 | tf_op jit(solution)/shard_map/ppermute | solution.py:21
  136.4 3.9 %collective-permute-start.22 = (f32[7424]{0:T(1024)S(1)}, f32[7424]{0:T(1024)S(1)}, u32[]{:S(2)}, u32[]{:S(2)}) collective-permute-start(f32[7424]{0:T(1024)S(1)} %add.573), channel_id=1, source_target_pairs={{0,64},{8,72},{16,80},{24,88},{32,96},{40,104},{48,112},{56,120},{... | collective-permute-start | bytes 89096 | tf_op jit(solution)/shard_map/ppermute | solution.py:21
  140.4 5.4 %collective-permute-start.23 = (f32[7424]{0:T(1024)S(1)}, f32[7424]{0:T(1024)S(1)}, u32[]{:S(2)}, u32[]{:S(2)}) collective-permute-start(f32[7424]{0:T(1024)S(1)} %add.574), channel_id=1, source_target_pairs={{0,128},{8,136},{16,144},{24,152},{32,160},{40,168},{48,176},{56,1... | collective-permute-start | bytes 89096 | tf_op jit(solution)/shard_map/ppermute | solution.py:21
  145.8 11.0 %collective-permute-start.24 = (f32[2048]{0:T(1024)S(1)}, f32[2048]{0:T(1024)S(1)}, u32[]{:S(2)}, u32[]{:S(2)}) collective-permute-start(f32[2048]{0:T(1024)S(1)} %slice.327), channel_id=1, source_target_pairs={{0,1},{1,0},{2,3},{3,2},{4,5},{5,4},{6,7},{7,6},{8,9},{9,8},{10,11... | collective-permute-start | bytes 24584 | tf_op jit(solution)/shard_map/ppermute | solution.py:21
  150.6 15.7 %collective-permute-start.18 = (bf16[64,3,256]{2,0,1:T(8,128)(2,1)S(1)}, bf16[64,3,256]{2,0,1:T(8,128)(2,1)S(1)}, u32[]{:S(2)}, u32[]{:S(2)}) collective-permute-start(bf16[64,3,256]{2,0,1:T(8,128)(2,1)S(1)} %get-tuple-element.36), channel_id=1, source_target_pairs={{0,48},{8,56},{16,0},{24,8},{32,16},{40,24},{48,32},{56,40},{64,11... | collective-permute-start | bytes 294920 | tf_op jit(solution)/shard_map/ppermute | solution.py:48
  152.3 14.1 %collective-permute-start.17 = (bf16[64,3,256]{2,0,1:T(8,128)(2,1)S(1)}, bf16[64,3,256]{2,0,1:T(8,128)(2,1)S(1)}, u32[]{:S(2)}, u32[]{:S(2)}) collective-permute-start(bf16[64,3,256]{2,0,1:T(8,128)(2,1)S(1)} %get-tuple-element.37), channel_id=1, source_target_pairs={{0,32},{8,40},{16,48},{24,56},{32,0},{40,8},{48,16},{56,24},{64,96... | collective-permute-start | bytes 294920 | tf_op jit(solution)/shard_map/ppermute | solution.py:48
  154.5 11.8 %collective-permute-start.16 = (bf16[64,3,256]{2,0,1:T(8,128)(2,1)S(1)}, bf16[64,3,256]{2,0,1:T(8,128)(2,1)S(1)}, u32[]{:S(2)}, u32[]{:S(2)}) collective-permute-start(bf16[64,3,256]{2,0,1:T(8,128)(2,1)S(1)} %get-tuple-element.35), channel_id=1, source_target_pairs={{0,16},{8,24},{16,32},{24,40},{32,48},{40,56},{48,0},{56,8},{64,80... | collective-permute-start | bytes 294920 | tf_op jit(solution)/shard_map/ppermute | solution.py:48
  156.8 5.2 %collective-permute-start.25 = (f32[2048]{0:T(1024)S(1)}, f32[2048]{0:T(1024)S(1)}, u32[]{:S(2)}, u32[]{:S(2)}) collective-permute-start(f32[2048]{0:T(1024)S(1)} %slice_add_fusion), channel_id=1, source_target_pairs={{0,2},{1,3},{2,0},{3,1},{4,6},{5,7},{6,4},{7,5},{8,10},{9,11},{10,... | collective-permute-start | bytes 24584 | tf_op jit(solution)/shard_map/ppermute | solution.py:21
  162.1 3.7 %collective-permute-start.26 = (f32[2048]{0:T(1024)S(1)}, f32[2048]{0:T(1024)S(1)}, u32[]{:S(2)}, u32[]{:S(2)}) collective-permute-start(f32[2048]{0:T(1024)S(1)} %add.577), channel_id=1, source_target_pairs={{0,4},{1,5},{2,6},{3,7},{4,0},{5,1},{6,2},{7,3},{8,12},{9,13},{10,... | collective-permute-start | bytes 24584 | tf_op jit(solution)/shard_map/ppermute | solution.py:21
Sparse Core Ops, SparseCore 0:
  11.4 59.0 all-gather.1
  100.0 56.9 reduce-scatter.1

commit v6 on v2

--- a/solution.py
+++ b/solution.py
@@ -107,14 +107,26 @@
     return jnp.stack(ring_gather(own, along_x, 0) + ring_gather(partner, along_x, 0))
 
 
+def ring_scatter_absolute(shard, move, place):
+    size = shard.shape[0]
+    total = lax.dynamic_index_in_dim(shard, place, axis=0, keepdims=False).astype(jnp.float32)
+    for k, by in ((1, 1), (2, 2), (3, -1)):
+        part = lax.dynamic_index_in_dim(shard, (place + k) % size, axis=0, keepdims=False)
+        total = total + move(part.astype(jnp.bfloat16), by).astype(jnp.float32)
+    return total
+
+
 def scatter_dp(blocks):
     along_y = mover("dp", DP_SPLIT, 0)
     along_h = mover("dp", DP_SPLIT, 1)
     across_core = mover("dp", DP_SPLIT, 2)
+    y, h, c = digits(lax.axis_index("dp"), DP_SPLIT)
     grid = blocks.reshape(DP_SPLIT + blocks.shape[1:])
-    summed = grid[:, :, 0].astype(jnp.float32) + across_core(grid[:, :, 1], 1).astype(jnp.float32)
-    column = ring_scatter_direct([summed[k] for k in range(DP_SPLIT[0])], along_y)
-    return ring_scatter_direct([column[k] for k in range(DP_SPLIT[1])], along_h)
+    keep = lax.dynamic_index_in_dim(grid, c, axis=2, keepdims=False)
+    send = lax.dynamic_index_in_dim(grid, 1 - c, axis=2, keepdims=False)
+    summed = keep.astype(jnp.float32) + across_core(send, 1).astype(jnp.float32)
+    column = ring_scatter_absolute(summed, along_y, y)
+    return ring_scatter_absolute(column, along_h, h)
 
 
 def body(inputs, norm_gain, proj_weight, filters, cotangent):
@@ -122,7 +134,6 @@
     width = taps - 1
     rows = inputs.shape[0]
     _, t_relative = slot_tables("tensor", TENSOR_SPLIT)
-    d_absolute, _ = slot_tables("dp", DP_SPLIT)
     wide = inputs.astype(jnp.float32)
     inv_rms = lax.rsqrt(jnp.mean(wide * wide, axis=1, keepdims=True) + 1e-05)
     weights = lax.all_gather(proj_weight, "dp", axis=0, tiled=True)
@@ -200,9 +211,7 @@
         "td,tsc->dsc", positions, grad_streams, preferred_element_type=jnp.float32
     ).astype(jnp.bfloat16)
     block = proj_weight.shape[0]
-    weight_blocks = jnp.take(
-        weight_terms.reshape((-1, block) + weight_terms.shape[1:]), d_absolute, axis=0
-    )
+    weight_blocks = weight_terms.reshape((-1, block) + weight_terms.shape[1:])
     grad_proj = scatter_dp(weight_blocks).astype(jnp.bfloat16)
     joined = butterfly_sum(jnp.concatenate([filter_local.reshape(-1), gain_local]), "dp")
     grad_filters = joined[: filter_local.size].reshape(filter_local.shape)

time: 181 us -> 179 us (0.989)
  other arithmetic: 27.1 us -> 29.8 us
  local copies, waits for them, and re-layouts: 22.5 us -> 20.1 us
    gather x1 -> x0, local copies, waits for them, and re-layouts: 4.32 us -> none  [body(): jnp.take(weight_terms.reshape((-1, block) + weight_terms.shape[1:]), d_ab...]
    dynamic_slice x0 -> x2, local copies, waits for them, and re-layouts: none -> 2.86 us  [the longest x1 1.43 us: scatter_dp(): keep = lax.dynamic_index_in_dim(grid, c, axis=2, keepdims=False)]
    select_n x2 -> x0, other arithmetic: 2.29 us -> none  [body(): jnp.take(weight_terms.reshape((-1, block) + weight_terms.shape[1:]), d_ab...]
    unnamed x29, local copies, waits for them, and re-layouts: 8.36 us -> 6.38 us
    add x1 -> x2, other arithmetic: 2.69 us -> 3.98 us  [the longest x1 2.54 us: scatter_dp(): summed = keep.astype(jnp.float32) + across_core(send, 1).astype(jnp.float32)]
where the time goes in v6:
time: 179 us; the launch traced here: 178 us
  starting transfers between devices  47 us (26%)
  waiting for transfers between devices  46.9 us (26%)
  other arithmetic  29.8 us (17%)
  local copies, waits for them, and re-layouts  20.1 us (11%)
  matrix products  19.9 us (11%)
  between operations  14.5 us (8%)
    ppermute x8, waiting for transfers between devices, butterfly_sum(): value = value + lax.ppermute(value, axis, pairs)  24.2 us
    ppermute x16, starting transfers between devices, move(): return lax.ppermute(value, axis, pairs)  22.8 us
    ppermute x16, waiting for transfers between devices, move(): return lax.ppermute(value, axis, pairs)  17.8 us
    ppermute x3, starting transfers between devices, passed_along(): return lax.ppermute(shard, axis, pairs)  12.5 us
    ppermute x8, starting transfers between devices, butterfly_sum(): value = value + lax.ppermute(value, axis, pairs)  11.6 us
    dot_general x1, matrix products, body(): jnp.einsum('td,tsc->dsc', positions, grad_streams, preferred_element_type...  6.54 us
    unnamed x29, local copies, waits for them, and re-layouts  6.38 us
    dot_general x1, matrix products, body(): jnp.einsum('td,dsc->tsc', positions, weights, preferred_element_type=jnp....  5.67 us
  transfers between devices with their start and end apart: 29, of which 15 were waited for; matrix products, arithmetic and copies ran while one was open for 31% of the time, Pallas kernels for 0%

profile of v6, /device:TPU:10, one launch (start us, length us, event | category | flops | bytes accessed | tf_op | source)
XLA Modules:
  0.0 178.3 jit_solution(10910939353602680047)
XLA Ops:
  7.8 1.5 collective-permute-start.1
  9.3 1.9 %collective-permute-start.4 = (bf16[128,2048]{1,0:T(8,128)(2,1)}, bf16[128,2048]{1,0:T(8,128)(2,1)S(1)}, u32[]{:S(2)}, u32[]{:S(2)}) collective-permute-start(bf16[128,2048]{1,0:T(8,128)(2,1)} %param.5), channel_id=1, source_target_pairs={{0,4},{1,5},{2,6},{3,7},{4,0},{5,1},{6,2},{7,3},{8,12},{9,13},{10,... | collective-permute-start | bytes 1572872 | tf_op jit(solution)/shard_map/ppermute | solution.py:48
  11.3 0.7 slice.203
  12.0 5.8 %collective-permute-start.11 = (bf16[6,256]{1,0:T(8,128)(2,1)S(1)}, bf16[6,256]{1,0:T(8,128)(2,1)S(1)}, u32[]{:S(2)}, u32[]{:S(2)}) collective-permute-start(bf16[6,256]{1,0:T(8,128)(2,1)S(1)} %slice.203), channel_id=1, source_target_pairs={{8,0},{16,8},{24,16},{32,24},{40,32},{48,40},{56,48},{64,56},{72,6... | collective-permute-start | bytes 9224 | tf_op jit(solution)/shard_map/ppermute | solution.py:13
  17.9 1.0 fusion.76
  19.0 1.9 %bitcast_dynamic-update-slice_fusion.5 = bf16[8,128,2048]{2,1,0:T(8,128)(2,1)} fusion(bf16[128,2048]{1,0:T(8,128)(2,1)} %param.5), kind=kLoop, calls=%fused_computation.87 | loop fusion | bytes 1048576
  21.2 1.4 collective-permute-start.3
  22.6 0.8 collective-permute-start.2
  23.4 2.6 %collective-permute-start.5 = (bf16[128,2048]{1,0:T(8,128)(2,1)S(1)}, bf16[128,2048]{1,0:T(8,128)(2,1)S(1)}, u32[]{:S(2)}, u32[]{:S(2)}) collective-permute-start(bf16[128,2048]{1,0:T(8,128)(2,1)S(1)} %collective-permute-done.4), channel_id=1, source_target_pairs={{0,3},{1,0},{2,1},{3,2},{4,7},{5,4},{6,5},{7,6},{8,11},{9,8},{10,9... | collective-permute-start | bytes 1572872 | tf_op jit(solution)/shard_map/ppermute | solution.py:48
  26.0 0.8 bitcast_dynamic-update-slice_fusion.4
  26.8 3.7 %collective-permute-done.3 = bf16[64,2048]{1,0:T(8,128)(2,1)S(1)} collective-permute-done((bf16[64,2048]{1,0:T(8,128)(2,1)S(1)}, bf16[64,2048]{1,0:T(8,128)(2,1)S(1)}, u32[]{:S(2)}, u32[]{:S(2)}) %collective-permute-start.3) | collective-permute-done | bytes 262176 | tf_op jit(solution)/shard_map/ppermute | solution.py:48
  30.5 2.6 %collective-permute-done.2 = bf16[64,2048]{1,0:T(8,128)(2,1)S(1)} collective-permute-done((bf16[64,2048]{1,0:T(8,128)(2,1)S(1)}, bf16[64,2048]{1,0:T(8,128)(2,1)S(1)}, u32[]{:S(2)}, u32[]{:S(2)}) %collective-permute-start.2) | collective-permute-done | bytes 262176 | tf_op jit(solution)/shard_map/ppermute | solution.py:48
  33.1 0.9 fusion.31
  34.0 0.8 bitcast_dynamic-update-slice_fusion.3
  34.8 0.8 bitcast_dynamic-update-slice_fusion.2
  35.7 4.0 %collective-permute-done.5 = bf16[128,2048]{1,0:T(8,128)(2,1)S(1)} collective-permute-done((bf16[128,2048]{1,0:T(8,128)(2,1)S(1)}, bf16[128,2048]{1,0:T(8,128)(2,1)S(1)}, u32[]{:S(2)}, u32[]{:S(2)}) %collective-permute-start.5) | collective-permute-done | bytes 524320 | tf_op jit(solution)/shard_map/ppermute | solution.py:48
  39.7 2.1 %collective-permute-start.8 = (bf16[64,2048]{1,0:T(8,128)(2,1)S(1)}, bf16[64,2048]{1,0:T(8,128)(2,1)S(1)}, u32[]{:S(2)}, u32[]{:S(2)}) collective-permute-start(bf16[64,2048]{1,0:T(8,128)(2,1)S(1)} %slice.236), channel_id=1, source_target_pairs={{0,3},{1,0},{2,1},{3,2},{4,7},{5,4},{6,5},{7,6},{8,11},{9,8},{10,9... | collective-permute-start | bytes 786440 | tf_op jit(solution)/shard_map/ppermute | solution.py:48
  42.4 0.8 bitcast_dynamic-update-slice_fusion.1
  43.2 3.5 %collective-permute-done.8 = bf16[64,2048]{1,0:T(8,128)(2,1)S(1)} collective-permute-done((bf16[64,2048]{1,0:T(8,128)(2,1)S(1)}, bf16[64,2048]{1,0:T(8,128)(2,1)S(1)}, u32[]{:S(2)}, u32[]{:S(2)}) %collective-permute-start.8) | collective-permute-done | bytes 262176 | tf_op jit(solution)/shard_map/ppermute | solution.py:48
  46.7 3.2 %collective-permute-done.7 = bf16[64,2048]{1,0:T(8,128)(2,1)S(1)} collective-permute-done((bf16[64,2048]{1,0:T(8,128)(2,1)S(1)}, bf16[64,2048]{1,0:T(8,128)(2,1)S(1)}, u32[]{:S(2)}, u32[]{:S(2)}) %collective-permute-start.7) | collective-permute-done | bytes 262176 | tf_op jit(solution)/shard_map/ppermute | solution.py:48
  49.9 0.8 fusion.32
  50.8 0.9 bitcast_dynamic-update-slice_fusion
  51.7 5.0 %gather_fusion = bf16[8,128,2048]{2,1,0:T(8,128)(2,1)} fusion(bf16[8,128,2048]{2,1,0:T(8,128)(2,1)} %bitcast_dynamic-update-slice_fusion, s32[1024]{0:T(1024)S(1)} %pad_clamp_fusion), kind=kCustom, calls=%fused_computation | custom fusion | bytes 8388640 | tf_op jit(solution)/shard_map/jit(_take)/gather | solution.py:140
  56.6 2.8 %bitcast_select_fusion = bf16[1024,2048]{1,0:T(8,128)(2,1)S(1)} fusion(bf16[8,128,2048]{2,1,0:T(8,128)(2,1)} %gather_fusion, pred[1024]{0:T(1024)(128)(4,1)S(1)} %broadcast_bitcast_fusion), kind=kLoop, calls=%fused_computation.7 | loop fusion | flops 2097152 | bytes 8389632 | tf_op jit(solution)/shard_map/jit(_take)/select_n | solution.py:140
  59.5 4.6 %collective-permute-start.10 = (bf16[6,2048]{1,0:T(8,128)(2,1)S(1)}, bf16[6,2048]{1,0:T(8,128)(2,1)S(1)}, u32[]{:S(2)}, u32[]{:S(2)}) collective-permute-start(bf16[6,2048]{1,0:T(8,128)(2,1)S(1)} %get-tuple-element.19), channel_id=1, source_target_pairs={{8,0},{16,8},{24,16},{32,24},{40,32},{48,40},{56,48},{64,56},{72,6... | collective-permute-start | bytes 73736 | tf_op jit(solution)/shard_map/ppermute | solution.py:13
  64.1 2.1 %collective-permute-start.9 = (bf16[6,2048]{1,0:T(8,128)(2,1)S(1)}, bf16[6,2048]{1,0:T(8,128)(2,1)S(1)}, u32[]{:S(2)}, u32[]{:S(2)}) collective-permute-start(bf16[6,2048]{1,0:T(8,128)(2,1)S(1)} %get-tuple-element.18), channel_id=1, source_target_pairs={{0,8},{8,16},{16,24},{24,32},{32,40},{40,48},{48,56},{56,64},{64,7... | collective-permute-start | bytes 73736 | tf_op jit(solution)/shard_map/ppermute | solution.py:13
  66.3 1.2 multiply_reduce_fusion.1
  67.5 4.9 %collective-permute-done.9 = bf16[6,2048]{1,0:T(8,128)(2,1)S(1)} collective-permute-done((bf16[6,2048]{1,0:T(8,128)(2,1)S(1)}, bf16[6,2048]{1,0:T(8,128)(2,1)S(1)}, u32[]{:S(2)}, u32[]{:S(2)}) %collective-permute-start.9) | collective-permute-done | bytes 24608 | tf_op jit(solution)/shard_map/ppermute | solution.py:13
  72.6 2.6 %convolution_convert_fusion.1 = bf16[12,3,256]{2,0,1:T(8,128)(2,1)S(1)} fusion(bf16[2048,3,256]{2,0,1:T(8,128)(2,1)} %all-gather.2.cloned.1.call-done, f32[2048]{0:T(1024)S(1)} %copy-done.9, f32[12]{0:T(128)S(1)} %add_rsqrt_fusion.1, bf16[6,2048]{1,0:T(8,128)(2,1)S(1)} %collective-permute-done.10, bf16[6,2048]{1,0:T(8,128)(2,1)S(1)} %collective-permute-done.9), kind=kOutput, calls=%fused_computation.55 | convolution fusion | flops 37929984 | bytes 3221552 | tf_op jit(solution)/shard_map/td,dsc->tsc/dot_general | solution.py:159
  75.4 5.7 %fusion.17 = bf16[1024,3,256]{2,0,1:T(8,128)(2,1)S(1)} fusion(bf16[2048,3,256]{2,0,1:T(8,128)(2,1)S(1)} %copy-done.3, bf16[1024,2048]{1,0:T(8,128)(2,1)} %copy-done.1, f32[2048]{0:T(1024)S(1)} %copy-done.9, f32[1024]{0:T(1024)S(1)} %rsqrt_bitcast_fusion), kind=kOutput, calls=%fused_computation.46 | convolution fusion | flops 3230400512 | bytes 8925184 | tf_op jit(solution)/shard_map/td,dsc->tsc/dot_general | solution.py:156
  81.5 2.6 %fusion.8 = f32[1024,3,256]{2,0,1:T(8,128)S(1)} fusion(f32[1030,3,256]{2,0,1:T(8,128)S(1)} %maximum_convert_fusion, f32[3,256]{1,0:T(4,128)S(1)} %get-tuple-element.48, f32[3,256]{1,0:T(4,128)S(1)} %get-tuple-element.49, f32[3,256]{1,0:T(4,128)S(1)} %get-tuple-element.50, f32[3,256]{1,0:T(4,128)S(1)} %get-tuple-element.51, ...), kind=kLoop, calls=%fused_computation.24 | loop fusion | flops 10223616 | bytes 25187328 | tf_op jit(solution)/shard_map/add | solution.py:165
  84.1 1.2 fusion.21
  85.6 3.8 %pad_maximum_fusion = (f32[1024,3,256]{2,0,1:T(8,128)}, bf16[1024,3,256]{2,0,1:T(8,128)(2,1)S(1)}) fusion(f32[1024,1,256]{2,0,1:T(8,128)S(1)} %get-tuple-element.21, f32[1024,1,256]{2,0,1:T(8,128)S(1)} %get-tuple-element.22, f32[1024,1,256]{2,0,1:T(8,128)S(1)} %get-tuple-element.20, f32[1030,3,256]{2,0,1:T(8,128)S(1)} %maximum_maximum_fusion, ...), kind=kLoop, calls=%fused_computation.36 | loop fusion | flops 12582912 | bytes 26760192 | tf_op jit(solution)/shard_map/stack | solution.py:168
  89.4 5.1 %multiply_reduce_fusion = (f32[2048]{0:T(1024)S(1)}, bf16[1024,2048]{1,0:T(8,128)(2,1)}) fusion(bf16[1024,2048]{1,0:T(8,128)(2,1)S(1)} %copy-done.2, f32[1024]{0:T(1024)S(1)} %rsqrt_bitcast_fusion, bf16[1024,3,256]{2,0,1:T(8,128)(2,1)S(1)} %get-tuple-element.24, bf16[2048,3,256]{2,0,1:T(8,128)(2,1)S(1)} %copy-done.3), kind=kOutput, calls=%fused_computation.2 | convolution fusion | flops 3233806336 | bytes 13119488 | tf_op jit(solution)/shard_map/tsc,dsc->td/dot_general | solution.py:195
  94.6 6.5 %convolution_convert_fusion = bf16[2048,3,256]{2,0,1:T(8,128)(2,1)S(1)} fusion(bf16[1024,3,256]{2,0,1:T(8,128)(2,1)} %copy-done.5, bf16[1024,2048]{1,0:T(8,128)(2,1)} %copy-done.1, f32[2048]{0:T(1024)S(1)} %copy-done.9, f32[1024]{0:T(1024)S(1)} %rsqrt_bitcast_fusion), kind=kOutput, calls=%fused_computation.8 | convolution fusion | flops 3231186944 | bytes 8925184 | tf_op jit(solution)/shard_map/td,tsc->dsc/dot_general | solution.py:210
  101.1 1.4 constant_dynamic-slice_fusion.1
  102.6 1.4 copy.37
  104.0 4.1 %multiply_reduce_fusion.2 = (f32[3,256]{1,0:T(4,128)S(1)}, f32[3,256]{1,0:T(4,128)S(1)}, f32[3,256]{1,0:T(4,128)S(1)}, f32[3,256]{1,0:T(4,128)S(1)}, f32[3,256]{...) fusion(f32[1024,3,256]{2,0,1:T(8,128)} %get-tuple-element.7, f32[1030,3,256]{2,0,1:T(8,128)S(1)} %maximum_convert_fusion), kind=kLoop, calls=%fused_computation.38 | loop fusion | flops 11004672 | bytes 25187328 | tf_op jit(solution)/shard_map/reduce_sum | solution.py:201
  108.9 2.5 %convert_add_fusion = f32[4,4,64,3,256]{4,2,3,1,0:T(8,128)S(1)} fusion(bf16[4,4,64,3,256]{4,2,3,1,0:T(8,128)(2,1)} %collective-permute-done.12, bf16[4,4,1,64,3,256]{5,3,2,1,0,4:T(8,128)(2,1)} %get-tuple-element.28), kind=kLoop, calls=%fused_computation.37 | loop fusion | flops 2359296 | bytes 6291456 | tf_op jit(solution)/shard_map/add | solution.py:127
  111.4 1.1 fusion.33
  112.5 3.0 %collective-permute-start.14 = (bf16[4,64,3,256]{3,1,2,0:T(8,128)(2,1)}, bf16[4,64,3,256]{3,1,2,0:T(8,128)(2,1)}, u32[]{:S(2)}, u32[]{:S(2)}) collective-permute-start(bf16[4,64,3,256]{3,1,2,0:T(8,128)(2,1)} %get-tuple-element.27), channel_id=1, source_target_pairs={{0,128},{8,136},{16,144},{24,152},{32,160},{40,168},{48,176},{56,1... | collective-permute-start | bytes 1179656 | tf_op jit(solution)/shard_map/ppermute | solution.py:48
  115.5 2.4 %collective-permute-start.13 = (bf16[4,64,3,256]{3,1,2,0:T(8,128)(2,1)S(1)}, bf16[4,64,3,256]{3,1,2,0:T(8,128)(2,1)}, u32[]{:S(2)}, u32[]{:S(2)}) collective-permute-start(bf16[4,64,3,256]{3,1,2,0:T(8,128)(2,1)S(1)} %get-tuple-element.25), channel_id=1, source_target_pairs={{0,64},{8,72},{16,80},{24,88},{32,96},{40,104},{48,112},{56,120},{... | collective-permute-start | bytes 1179656 | tf_op jit(solution)/shard_map/ppermute | solution.py:48
  118.0 1.2 collective-permute-done.19
  119.4 4.8 %collective-permute-done.20 = f32[7424]{0:T(1024)S(1)} collective-permute-done((f32[7424]{0:T(1024)S(1)}, f32[7424]{0:T(1024)S(1)}, u32[]{:S(2)}, u32[]{:S(2)}) %collective-permute-start.20) | collective-permute-done | bytes 29728 | tf_op jit(solution)/shard_map/ppermute | solution.py:21
  124.2 3.1 %collective-permute-start.21 = (f32[7424]{0:T(1024)S(1)}, f32[7424]{0:T(1024)S(1)}, u32[]{:S(2)}, u32[]{:S(2)}) collective-permute-start(f32[7424]{0:T(1024)S(1)} %add.392), channel_id=1, source_target_pairs={{0,32},{8,40},{16,48},{24,56},{32,0},{40,8},{48,16},{56,24},{64,96... | collective-permute-start | bytes 89096 | tf_op jit(solution)/shard_map/ppermute | solution.py:21
  127.2 4.8 %collective-permute-done.21 = f32[7424]{0:T(1024)S(1)} collective-permute-done((f32[7424]{0:T(1024)S(1)}, f32[7424]{0:T(1024)S(1)}, u32[]{:S(2)}, u32[]{:S(2)}) %collective-permute-start.21) | collective-permute-done | bytes 29728 | tf_op jit(solution)/shard_map/ppermute | solution.py:21
  132.0 3.9 %collective-permute-done.22 = f32[7424]{0:T(1024)S(1)} collective-permute-done((f32[7424]{0:T(1024)S(1)}, f32[7424]{0:T(1024)S(1)}, u32[]{:S(2)}, u32[]{:S(2)}) %collective-permute-start.22) | collective-permute-done | bytes 29728 | tf_op jit(solution)/shard_map/ppermute | solution.py:21
  135.9 0.6 add.394
  136.5 2.2 %collective-permute-start.23 = (f32[7424]{0:T(1024)}, f32[7424]{0:T(1024)}, u32[]{:S(2)}, u32[]{:S(2)}) collective-permute-start(f32[7424]{0:T(1024)} %add.394), channel_id=1, source_target_pairs={{0,128},{8,136},{16,144},{24,152},{32,160},{40,168},{48,176},{56,1... | collective-permute-start | bytes 89096 | tf_op jit(solution)/shard_map/ppermute | solution.py:21
  138.8 3.5 %collective-permute-done.23 = f32[7424]{0:T(1024)} collective-permute-done((f32[7424]{0:T(1024)}, f32[7424]{0:T(1024)}, u32[]{:S(2)}, u32[]{:S(2)}) %collective-permute-start.23) | collective-permute-done | bytes 29728 | tf_op jit(solution)/shard_map/ppermute | solution.py:21
  142.3 0.8 add.395
  143.1 4.6 %collective-permute-start.24 = (f32[2048]{0:T(1024)S(1)}, f32[2048]{0:T(1024)S(1)}, u32[]{:S(2)}, u32[]{:S(2)}) collective-permute-start(f32[2048]{0:T(1024)S(1)} %slice.269), channel_id=1, source_target_pairs={{0,1},{1,0},{2,3},{3,2},{4,5},{5,4},{6,7},{7,6},{8,9},{9,8},{10,11... | collective-permute-start | bytes 24584 | tf_op jit(solution)/shard_map/ppermute | solution.py:21
  147.7 1.4 fusion.30
  149.2 0.9 copy-done.4
  150.1 1.8 %collective-permute-start.18 = (bf16[64,3,256]{2,0,1:T(8,128)(2,1)S(1)}, bf16[64,3,256]{2,0,1:T(8,128)(2,1)S(1)}, u32[]{:S(2)}, u32[]{:S(2)}) collective-permute-start(bf16[64,3,256]{2,0,1:T(8,128)(2,1)S(1)} %get-tuple-element.32), channel_id=1, source_target_pairs={{0,48},{8,56},{16,0},{24,8},{32,16},{40,24},{48,32},{56,40},{64,11... | collective-permute-start | bytes 294920 | tf_op jit(solution)/shard_map/ppermute | solution.py:48
  151.9 2.4 %collective-permute-start.17 = (bf16[64,3,256]{2,0,1:T(8,128)(2,1)S(1)}, bf16[64,3,256]{2,0,1:T(8,128)(2,1)S(1)}, u32[]{:S(2)}, u32[]{:S(2)}) collective-permute-start(bf16[64,3,256]{2,0,1:T(8,128)(2,1)S(1)} %get-tuple-element.33), channel_id=1, source_target_pairs={{0,32},{8,40},{16,48},{24,56},{32,0},{40,8},{48,16},{56,24},{64,96... | collective-permute-start | bytes 294920 | tf_op jit(solution)/shard_map/ppermute | solution.py:48
  154.3 2.2 %collective-permute-start.16 = (bf16[64,3,256]{2,0,1:T(8,128)(2,1)S(1)}, bf16[64,3,256]{2,0,1:T(8,128)(2,1)S(1)}, u32[]{:S(2)}, u32[]{:S(2)}) collective-permute-start(bf16[64,3,256]{2,0,1:T(8,128)(2,1)S(1)} %get-tuple-element.31), channel_id=1, source_target_pairs={{0,16},{8,24},{16,32},{24,40},{32,48},{40,56},{48,0},{56,8},{64,80... | collective-permute-start | bytes 294920 | tf_op jit(solution)/shard_map/ppermute | solution.py:48
  156.6 5.1 %collective-permute-done.25 = f32[2048]{0:T(1024)S(1)} collective-permute-done((f32[2048]{0:T(1024)S(1)}, f32[2048]{0:T(1024)S(1)}, u32[]{:S(2)}, u32[]{:S(2)}) %collective-permute-start.25) | collective-permute-done | bytes 8224 | tf_op jit(solution)/shard_map/ppermute | solution.py:21
  161.7 1.4 collective-permute-start.26
  163.1 0.7 slice.268
  164.5 0.9 collective-permute-done.26
  166.0 1.6 fusion.38
  167.6 1.5 fusion.22
  169.1 2.3 %fusion.27 = bf16[128,2048]{1,0:T(8,128)(2,1)} fusion(bf16[128,2048]{1,0:T(8,128)(2,1)} %param.5, bf16[128,2048]{1,0:T(8,128)(2,1)} %reduce-scatter.2.cloned.1.call-done, f32[128]{0:T(128)S(1)} %broadcast_multiply_fusion, f32[2048]{0:T(1024)S(1)} %copy-done.9, f32[128]{0:T(128)S(1)} %add_rsqrt_fusion), kind=kLoop, calls=%fused_computation.63 | loop fusion | flops 2359296 | bytes 1582080 | tf_op jit(solution)/shard_map/convert_element_type | solution.py:223
  (92 shorter events, 5.1 us)
Async XLA Ops:
  7.2 65.4 %all-gather.2.cloned.1.call-start = ((), (), s32[]{:S(2)}) async-start(), calls=%async_computation.1 | async-start | bytes 3244032 | tf_op jit(solution)/shard_map/all_gather | solution.py:139
  7.2 14.0 %collective-permute-start = (bf16[128,2048]{1,0:T(8,128)(2,1)}, bf16[128,2048]{1,0:T(8,128)(2,1)S(1)}, u32[]{:S(2)}, u32[]{:S(2)}) collective-permute-start(bf16[128,2048]{1,0:T(8,128)(2,1)} %param.5), channel_id=1, source_target_pairs={{0,3},{1,0},{2,1},{3,2},{4,7},{5,4},{6,5},{7,6},{8,11},{9,8},{10,9... | collective-permute-start | bytes 1572872 | tf_op jit(solution)/shard_map/ppermute | solution.py:48
  7.8 14.7 %collective-permute-start.1 = (bf16[128,2048]{1,0:T(8,128)(2,1)}, bf16[128,2048]{1,0:T(8,128)(2,1)S(1)}, u32[]{:S(2)}, u32[]{:S(2)}) collective-permute-start(bf16[128,2048]{1,0:T(8,128)(2,1)} %param.5), channel_id=1, source_target_pairs={{0,1},{1,2},{2,3},{3,0},{4,5},{5,6},{6,7},{7,4},{8,9},{9,10},{10,1... | collective-permute-start | bytes 1572872 | tf_op jit(solution)/shard_map/ppermute | solution.py:48
  9.3 14.1 %collective-permute-start.4 = (bf16[128,2048]{1,0:T(8,128)(2,1)}, bf16[128,2048]{1,0:T(8,128)(2,1)S(1)}, u32[]{:S(2)}, u32[]{:S(2)}) collective-permute-start(bf16[128,2048]{1,0:T(8,128)(2,1)} %param.5), channel_id=1, source_target_pairs={{0,4},{1,5},{2,6},{3,7},{4,0},{5,1},{6,2},{7,3},{8,12},{9,13},{10,... | collective-permute-start | bytes 1572872 | tf_op jit(solution)/shard_map/ppermute | solution.py:48
  11.3 156.4 %reduce-scatter.2.cloned.1.call-start = ((), (), s32[]{:S(2)}) async-start(), calls=%async_computation.2 | async-start | bytes 4718592 | tf_op jit(solution)/shard_map/reduce_scatter | solution.py:207
  12.0 73.3 %collective-permute-start.11 = (bf16[6,256]{1,0:T(8,128)(2,1)S(1)}, bf16[6,256]{1,0:T(8,128)(2,1)S(1)}, u32[]{:S(2)}, u32[]{:S(2)}) collective-permute-start(bf16[6,256]{1,0:T(8,128)(2,1)S(1)} %slice.203), channel_id=1, source_target_pairs={{8,0},{16,8},{24,16},{32,24},{40,32},{48,40},{56,48},{64,56},{72,6... | collective-permute-start | bytes 9224 | tf_op jit(solution)/shard_map/ppermute | solution.py:13
  21.2 9.3 %collective-permute-start.3 = (bf16[64,2048]{1,0:T(8,128)(2,1)S(1)}, bf16[64,2048]{1,0:T(8,128)(2,1)S(1)}, u32[]{:S(2)}, u32[]{:S(2)}) collective-permute-start(bf16[64,2048]{1,0:T(8,128)(2,1)S(1)} %slice.234), channel_id=1, source_target_pairs={{0,3},{1,0},{2,1},{3,2},{4,7},{5,4},{6,5},{7,6},{8,11},{9,8},{10,9... | collective-permute-start | bytes 786440 | tf_op jit(solution)/shard_map/ppermute | solution.py:48
  22.6 10.5 %collective-permute-start.2 = (bf16[64,2048]{1,0:T(8,128)(2,1)S(1)}, bf16[64,2048]{1,0:T(8,128)(2,1)S(1)}, u32[]{:S(2)}, u32[]{:S(2)}) collective-permute-start(bf16[64,2048]{1,0:T(8,128)(2,1)S(1)} %slice.233), channel_id=1, source_target_pairs={{0,1},{1,2},{2,3},{3,0},{4,5},{5,6},{6,7},{7,4},{8,9},{9,10},{10,1... | collective-permute-start | bytes 786440 | tf_op jit(solution)/shard_map/ppermute | solution.py:48
  23.4 16.3 %collective-permute-start.5 = (bf16[128,2048]{1,0:T(8,128)(2,1)S(1)}, bf16[128,2048]{1,0:T(8,128)(2,1)S(1)}, u32[]{:S(2)}, u32[]{:S(2)}) collective-permute-start(bf16[128,2048]{1,0:T(8,128)(2,1)S(1)} %collective-permute-done.4), channel_id=1, source_target_pairs={{0,3},{1,0},{2,1},{3,2},{4,7},{5,4},{6,5},{7,6},{8,11},{9,8},{10,9... | collective-permute-start | bytes 1572872 | tf_op jit(solution)/shard_map/ppermute | solution.py:48
  26.0 16.3 %collective-permute-start.6 = (bf16[128,2048]{1,0:T(8,128)(2,1)S(1)}, bf16[128,2048]{1,0:T(8,128)(2,1)S(1)}, u32[]{:S(2)}, u32[]{:S(2)}) collective-permute-start(bf16[128,2048]{1,0:T(8,128)(2,1)S(1)} %collective-permute-done.4), channel_id=1, source_target_pairs={{0,1},{1,2},{2,3},{3,0},{4,5},{5,6},{6,7},{7,4},{8,9},{9,10},{10,1... | collective-permute-start | bytes 1572872 | tf_op jit(solution)/shard_map/ppermute | solution.py:48
  39.7 7.0 %collective-permute-start.8 = (bf16[64,2048]{1,0:T(8,128)(2,1)S(1)}, bf16[64,2048]{1,0:T(8,128)(2,1)S(1)}, u32[]{:S(2)}, u32[]{:S(2)}) collective-permute-start(bf16[64,2048]{1,0:T(8,128)(2,1)S(1)} %slice.236), channel_id=1, source_target_pairs={{0,3},{1,0},{2,1},{3,2},{4,7},{5,4},{6,5},{7,6},{8,11},{9,8},{10,9... | collective-permute-start | bytes 786440 | tf_op jit(solution)/shard_map/ppermute | solution.py:48
  42.3 7.7 %collective-permute-start.7 = (bf16[64,2048]{1,0:T(8,128)(2,1)S(1)}, bf16[64,2048]{1,0:T(8,128)(2,1)S(1)}, u32[]{:S(2)}, u32[]{:S(2)}) collective-permute-start(bf16[64,2048]{1,0:T(8,128)(2,1)S(1)} %slice.235), channel_id=1, source_target_pairs={{0,1},{1,2},{2,3},{3,0},{4,5},{5,6},{6,7},{7,4},{8,9},{9,10},{10,1... | collective-permute-start | bytes 786440 | tf_op jit(solution)/shard_map/ppermute | solution.py:48
  56.6 9.6 %copy-start = (bf16[8,128,2048]{2,1,0:T(8,128)(2,1)S(1)}, bf16[8,128,2048]{2,1,0:T(8,128)(2,1)}, u32[]{:S(2)}) copy-start(bf16[8,128,2048]{2,1,0:T(8,128)(2,1)} %gather_fusion) | copy-start | bytes 12582916
  59.5 8.0 %copy-start.1 = (bf16[1024,2048]{1,0:T(8,128)(2,1)}, bf16[1024,2048]{1,0:T(8,128)(2,1)S(1)}, u32[]{:S(2)}) copy-start(bf16[1024,2048]{1,0:T(8,128)(2,1)S(1)} %bitcast_select_fusion) | copy-start | bytes 12582916
  59.5 13.1 %copy-start.9 = (f32[2048]{0:T(1024)S(1)}, f32[2048]{0:T(1024)}, u32[]{:S(2)}) copy-start(f32[2048]{0:T(1024)} %param.6) | copy-start | bytes 24580
  59.5 8.0 %collective-permute-start.10 = (bf16[6,2048]{1,0:T(8,128)(2,1)S(1)}, bf16[6,2048]{1,0:T(8,128)(2,1)S(1)}, u32[]{:S(2)}, u32[]{:S(2)}) collective-permute-start(bf16[6,2048]{1,0:T(8,128)(2,1)S(1)} %get-tuple-element.19), channel_id=1, source_target_pairs={{8,0},{16,8},{24,16},{32,24},{40,32},{48,40},{56,48},{64,56},{72,6... | collective-permute-start | bytes 73736 | tf_op jit(solution)/shard_map/ppermute | solution.py:13
  64.1 8.3 %collective-permute-start.9 = (bf16[6,2048]{1,0:T(8,128)(2,1)S(1)}, bf16[6,2048]{1,0:T(8,128)(2,1)S(1)}, u32[]{:S(2)}, u32[]{:S(2)}) collective-permute-start(bf16[6,2048]{1,0:T(8,128)(2,1)S(1)} %get-tuple-element.18), channel_id=1, source_target_pairs={{0,8},{8,16},{16,24},{24,32},{32,40},{40,48},{48,56},{56,64},{64,7... | collective-permute-start | bytes 73736 | tf_op jit(solution)/shard_map/ppermute | solution.py:13
  72.6 2.8 %copy-start.3 = (bf16[2048,3,256]{2,0,1:T(8,128)(2,1)S(1)}, bf16[2048,3,256]{2,0,1:T(8,128)(2,1)}, u32[]{:S(2)}) copy-start(bf16[2048,3,256]{2,0,1:T(8,128)(2,1)} %all-gather.2.cloned.1.call-done) | copy-start | bytes 9437188
  81.5 2.6 %copy-start.6 = (bf16[1024,256]{1,0:T(8,128)(2,1)S(1)}, bf16[1024,256]{1,0:T(8,128)(2,1)}, u32[]{:S(2)}) copy-start(bf16[1024,256]{1,0:T(8,128)(2,1)} %param.9) | copy-start | bytes 1572868
  85.6 3.8 %copy-start.2 = (bf16[1024,2048]{1,0:T(8,128)(2,1)S(1)}, bf16[1024,2048]{1,0:T(8,128)(2,1)}, u32[]{:S(2)}) copy-start(bf16[1024,2048]{1,0:T(8,128)(2,1)} %copy-done.1) | copy-start | bytes 12582916
  89.4 5.1 %copy-start.5 = (bf16[1024,3,256]{2,0,1:T(8,128)(2,1)}, bf16[1024,3,256]{2,0,1:T(8,128)(2,1)S(1)}, u32[]{:S(2)}) copy-start(bf16[1024,3,256]{2,0,1:T(8,128)(2,1)S(1)} %get-tuple-element.24) | copy-start | bytes 4718596
  104.0 4.9 %collective-permute-start.12 = (bf16[4,4,64,3,256]{4,2,3,1,0:T(8,128)(2,1)}, bf16[4,4,64,3,256]{4,2,3,1,0:T(8,128)(2,1)}, u32[]{:S(2)}, u32[]{:S(2)}) collective-permute-start(bf16[4,4,64,3,256]{4,2,3,1,0:T(8,128)(2,1)} %bitcast.151), channel_id=1, source_target_pairs={{0,8},{8,0},{16,24},{24,16},{32,40},{40,32},{48,56},{56,48},{64,72... | collective-permute-start | bytes 4718600 | tf_op jit(solution)/shard_map/ppermute | solution.py:48
  108.9 9.1 %copy-start.7 = (f32[5376]{0:T(1024)S(1)}, f32[5376]{0:T(1024)}, u32[]{:S(2)}) copy-start(f32[5376]{0:T(1024)} %reshape.251) | copy-start | bytes 64516
  112.5 35.2 %collective-permute-start.15 = (bf16[4,64,3,256]{3,1,2,0:T(8,128)(2,1)}, bf16[4,64,3,256]{3,1,2,0:T(8,128)(2,1)}, u32[]{:S(2)}, u32[]{:S(2)}) collective-permute-start(bf16[4,64,3,256]{3,1,2,0:T(8,128)(2,1)} %get-tuple-element.26), channel_id=1, source_target_pairs={{0,192},{8,200},{16,208},{24,216},{32,224},{40,232},{48,240},{56,2... | collective-permute-start | bytes 1179656 | tf_op jit(solution)/shard_map/ppermute | solution.py:48
  112.5 35.2 %collective-permute-start.14 = (bf16[4,64,3,256]{3,1,2,0:T(8,128)(2,1)}, bf16[4,64,3,256]{3,1,2,0:T(8,128)(2,1)}, u32[]{:S(2)}, u32[]{:S(2)}) collective-permute-start(bf16[4,64,3,256]{3,1,2,0:T(8,128)(2,1)} %get-tuple-element.27), channel_id=1, source_target_pairs={{0,128},{8,136},{16,144},{24,152},{32,160},{40,168},{48,176},{56,1... | collective-permute-start | bytes 1179656 | tf_op jit(solution)/shard_map/ppermute | solution.py:48
  115.5 32.2 %collective-permute-start.13 = (bf16[4,64,3,256]{3,1,2,0:T(8,128)(2,1)S(1)}, bf16[4,64,3,256]{3,1,2,0:T(8,128)(2,1)}, u32[]{:S(2)}, u32[]{:S(2)}) collective-permute-start(bf16[4,64,3,256]{3,1,2,0:T(8,128)(2,1)S(1)} %get-tuple-element.25), channel_id=1, source_target_pairs={{0,64},{8,72},{16,80},{24,88},{32,96},{40,104},{48,112},{56,120},{... | collective-permute-start | bytes 1179656 | tf_op jit(solution)/shard_map/ppermute | solution.py:48
  117.9 1.3 collective-permute-start.19
  119.3 4.9 %collective-permute-start.20 = (f32[7424]{0:T(1024)S(1)}, f32[7424]{0:T(1024)S(1)}, u32[]{:S(2)}, u32[]{:S(2)}) collective-permute-start(f32[7424]{0:T(1024)S(1)} %fusion.73), channel_id=1, source_target_pairs={{0,16},{8,24},{16,0},{24,8},{32,48},{40,56},{48,32},{56,40},{64,80... | collective-permute-start | bytes 89096 | tf_op jit(solution)/shard_map/ppermute | solution.py:21
  124.2 7.8 %collective-permute-start.21 = (f32[7424]{0:T(1024)S(1)}, f32[7424]{0:T(1024)S(1)}, u32[]{:S(2)}, u32[]{:S(2)}) collective-permute-start(f32[7424]{0:T(1024)S(1)} %add.392), channel_id=1, source_target_pairs={{0,32},{8,40},{16,48},{24,56},{32,0},{40,8},{48,16},{56,24},{64,96... | collective-permute-start | bytes 89096 | tf_op jit(solution)/shard_map/ppermute | solution.py:21
  132.0 3.9 %collective-permute-start.22 = (f32[7424]{0:T(1024)S(1)}, f32[7424]{0:T(1024)S(1)}, u32[]{:S(2)}, u32[]{:S(2)}) collective-permute-start(f32[7424]{0:T(1024)S(1)} %add.393), channel_id=1, source_target_pairs={{0,64},{8,72},{16,80},{24,88},{32,96},{40,104},{48,112},{56,120},{... | collective-permute-start | bytes 89096 | tf_op jit(solution)/shard_map/ppermute | solution.py:21
  136.5 5.7 %collective-permute-start.23 = (f32[7424]{0:T(1024)}, f32[7424]{0:T(1024)}, u32[]{:S(2)}, u32[]{:S(2)}) collective-permute-start(f32[7424]{0:T(1024)} %add.394), channel_id=1, source_target_pairs={{0,128},{8,136},{16,144},{24,152},{32,160},{40,168},{48,176},{56,1... | collective-permute-start | bytes 89096 | tf_op jit(solution)/shard_map/ppermute | solution.py:21
  143.1 13.4 %copy-start.8 = (f32[7424]{0:T(1024)}, f32[7424]{0:T(1024)S(1)}, u32[]{:S(2)}) copy-start(f32[7424]{0:T(1024)S(1)} %add.395) | copy-start | bytes 89092
  143.1 13.4 %collective-permute-start.24 = (f32[2048]{0:T(1024)S(1)}, f32[2048]{0:T(1024)S(1)}, u32[]{:S(2)}, u32[]{:S(2)}) collective-permute-start(f32[2048]{0:T(1024)S(1)} %slice.269), channel_id=1, source_target_pairs={{0,1},{1,0},{2,3},{3,2},{4,5},{5,4},{6,7},{7,6},{8,9},{9,8},{10,11... | collective-permute-start | bytes 24584 | tf_op jit(solution)/shard_map/ppermute | solution.py:21
  149.1 0.9 copy-start.4
  150.1 15.9 %collective-permute-start.18 = (bf16[64,3,256]{2,0,1:T(8,128)(2,1)S(1)}, bf16[64,3,256]{2,0,1:T(8,128)(2,1)S(1)}, u32[]{:S(2)}, u32[]{:S(2)}) collective-permute-start(bf16[64,3,256]{2,0,1:T(8,128)(2,1)S(1)} %get-tuple-element.32), channel_id=1, source_target_pairs={{0,48},{8,56},{16,0},{24,8},{32,16},{40,24},{48,32},{56,40},{64,11... | collective-permute-start | bytes 294920 | tf_op jit(solution)/shard_map/ppermute | solution.py:48
  151.9 14.1 %collective-permute-start.17 = (bf16[64,3,256]{2,0,1:T(8,128)(2,1)S(1)}, bf16[64,3,256]{2,0,1:T(8,128)(2,1)S(1)}, u32[]{:S(2)}, u32[]{:S(2)}) collective-permute-start(bf16[64,3,256]{2,0,1:T(8,128)(2,1)S(1)} %get-tuple-element.33), channel_id=1, source_target_pairs={{0,32},{8,40},{16,48},{24,56},{32,0},{40,8},{48,16},{56,24},{64,96... | collective-permute-start | bytes 294920 | tf_op jit(solution)/shard_map/ppermute | solution.py:48
  154.3 11.7 %collective-permute-start.16 = (bf16[64,3,256]{2,0,1:T(8,128)(2,1)S(1)}, bf16[64,3,256]{2,0,1:T(8,128)(2,1)S(1)}, u32[]{:S(2)}, u32[]{:S(2)}) collective-permute-start(bf16[64,3,256]{2,0,1:T(8,128)(2,1)S(1)} %get-tuple-element.31), channel_id=1, source_target_pairs={{0,16},{8,24},{16,32},{24,40},{32,48},{40,56},{48,0},{56,8},{64,80... | collective-permute-start | bytes 294920 | tf_op jit(solution)/shard_map/ppermute | solution.py:48
  156.5 5.2 %collective-permute-start.25 = (f32[2048]{0:T(1024)S(1)}, f32[2048]{0:T(1024)S(1)}, u32[]{:S(2)}, u32[]{:S(2)}) collective-permute-start(f32[2048]{0:T(1024)S(1)} %slice_add_fusion), channel_id=1, source_target_pairs={{0,2},{1,3},{2,0},{3,1},{4,6},{5,7},{6,4},{7,5},{8,10},{9,11},{10,... | collective-permute-start | bytes 24584 | tf_op jit(solution)/shard_map/ppermute | solution.py:21
  161.7 3.7 %collective-permute-start.26 = (f32[2048]{0:T(1024)S(1)}, f32[2048]{0:T(1024)S(1)}, u32[]{:S(2)}, u32[]{:S(2)}) collective-permute-start(f32[2048]{0:T(1024)S(1)} %add.397), channel_id=1, source_target_pairs={{0,4},{1,5},{2,6},{3,7},{4,0},{5,1},{6,2},{7,3},{8,12},{9,13},{10,... | collective-permute-start | bytes 24584 | tf_op jit(solution)/shard_map/ppermute | solution.py:21
Sparse Core Ops, SparseCore 0:
  11.4 59.0 all-gather.1
  94.7 55.0 reduce-scatter.1

commit v7 on v6

--- a/solution.py
+++ b/solution.py
@@ -192,17 +192,17 @@
     for tap in range(taps):
         grad_acc = grad_acc + filters[:, tap, :] * grad_extended[tap : tap + length]
     grad_streams = grad_acc.astype(jnp.bfloat16)
+    filter_local = jnp.stack(
+        [
+            jnp.sum(grad_conv * extended[width - tap : width - tap + length], axis=0)
+            for tap in range(taps)
+        ],
+        axis=1,
+    )
+    early_streams, _ = lax.optimization_barrier((grad_streams, filter_local))
     normed_terms = jnp.einsum(
-        "tsc,dsc->td", grad_streams, weights, preferred_element_type=jnp.float32
-    ).astype(jnp.bfloat16)
-    late_conv, late_extended, _ = lax.optimization_barrier((grad_conv, extended, normed_terms))
-    filter_local = jnp.stack(
-        [
-            jnp.sum(late_conv * late_extended[width - tap : width - tap + length], axis=0)
-            for tap in range(taps)
-        ],
-        axis=1,
-    )
+        "tsc,dsc->td", early_streams, weights, preferred_element_type=jnp.float32
+    ).astype(jnp.bfloat16)
     gain_local = jnp.sum(normed_terms.astype(jnp.float32) * unit_all, axis=0)
     grad_normed = lax.psum_scatter(
         normed_terms, "tensor", scatter_dimension=0, tiled=True

time: 179 us -> 183 us (1.022); the launches traced: 178 us -> 180 us
  starting transfers between devices: 47 us -> 54.2 us
  waiting for transfers between devices: 46.9 us -> 39.8 us
    ppermute x3, waiting for transfers between devices: 4.9 us -> 0.13 us  [passed_along(): return lax.ppermute(shard, axis, pairs)]
    ppermute x8, starting transfers between devices: 11.6 us -> 15.7 us  [butterfly_sum(): value = value + lax.ppermute(value, axis, pairs)]
    another operation x2 -> x1, other arithmetic: 5 us -> 1.18 us  [body(): jnp.stack([grad_out * conv[:, 1] * conv[:, 2], grad_out * conv[:, 0] * co...]
    convert_element_type x0 -> x1, other arithmetic: none -> 3.65 us  [body(): grad_streams = grad_acc.astype(jnp.bfloat16)]
    ppermute x8, waiting for transfers between devices: 24.2 us -> 21 us  [butterfly_sum(): value = value + lax.ppermute(value, axis, pairs)]
    unnamed x29, local copies, waits for them, and re-layouts: 6.38 us -> 8.94 us
    ppermute x3, starting transfers between devices: 12.5 us -> 14.5 us  [passed_along(): return lax.ppermute(shard, axis, pairs)]
    dot_general x1, matrix products: 5.12 us -> 7.11 us  [body(): jnp.einsum('tsc,dsc->td', early_streams, weights, preferred_element_type=...]
  transfers between devices with their start and end apart: 29 -> 29, of which waited for: 15 -> 16; matrix products, arithmetic and copies ran while one was open for 31% -> 29% of each run, Pallas kernels for 0% -> 0%
where the time goes in v7:
time: 183 us; the launch traced here: 180 us
  starting transfers between devices  54.2 us (30%)
  waiting for transfers between devices  39.8 us (22%)
  other arithmetic  28.6 us (16%)
  local copies, waits for them, and re-layouts  21.5 us (12%)
  matrix products  21.4 us (12%)
  between operations  14.5 us (8%)
    ppermute x16, starting transfers between devices, move(): return lax.ppermute(value, axis, pairs)  23.8 us
    ppermute x8, waiting for transfers between devices, butterfly_sum(): value = value + lax.ppermute(value, axis, pairs)  21 us
    ppermute x16, waiting for transfers between devices, move(): return lax.ppermute(value, axis, pairs)  16.7 us
    ppermute x8, starting transfers between devices, butterfly_sum(): value = value + lax.ppermute(value, axis, pairs)  15.7 us
    ppermute x3, starting transfers between devices, passed_along(): return lax.ppermute(shard, axis, pairs)  14.5 us
    unnamed x29, local copies, waits for them, and re-layouts  8.94 us
    dot_general x1, matrix products, body(): jnp.einsum('tsc,dsc->td', early_streams, weights, preferred_element_type=...  7.11 us
    dot_general x1, matrix products, body(): jnp.einsum('td,tsc->dsc', positions, grad_streams, preferred_element_type...  6.06 us
  transfers between devices with their start and end apart: 29, of which 16 were waited for; matrix products, arithmetic and copies ran while one was open for 29% of the time, Pallas kernels for 0%

profile of v7, /device:TPU:10, one launch (start us, length us, event | category | flops | bytes accessed | tf_op | source)
XLA Modules:
  0.0 179.9 jit_solution(11887897741852540724)
XLA Ops:
  7.2 1.6 collective-permute-start.1
  9.3 1.9 %collective-permute-start.4 = (bf16[128,2048]{1,0:T(8,128)(2,1)}, bf16[128,2048]{1,0:T(8,128)(2,1)S(1)}, u32[]{:S(2)}, u32[]{:S(2)}) collective-permute-start(bf16[128,2048]{1,0:T(8,128)(2,1)} %param.5), channel_id=1, source_target_pairs={{0,4},{1,5},{2,6},{3,7},{4,0},{5,1},{6,2},{7,3},{8,12},{9,13},{10,... | collective-permute-start | bytes 1572872 | tf_op jit(solution)/shard_map/ppermute | solution.py:48
  12.0 5.8 %collective-permute-start.11 = (bf16[6,256]{1,0:T(8,128)(2,1)S(1)}, bf16[6,256]{1,0:T(8,128)(2,1)S(1)}, u32[]{:S(2)}, u32[]{:S(2)}) collective-permute-start(bf16[6,256]{1,0:T(8,128)(2,1)S(1)} %slice.189), channel_id=1, source_target_pairs={{8,0},{16,8},{24,16},{32,24},{40,32},{48,40},{56,48},{64,56},{72,6... | collective-permute-start | bytes 9224 | tf_op jit(solution)/shard_map/ppermute | solution.py:13
  17.9 1.1 fusion.70
  19.1 1.9 %bitcast_dynamic-update-slice_fusion.5 = bf16[8,128,2048]{2,1,0:T(8,128)(2,1)} fusion(bf16[128,2048]{1,0:T(8,128)(2,1)} %param.5), kind=kLoop, calls=%fused_computation.75 | loop fusion | bytes 1048576
  21.2 1.6 collective-permute-start.2
  23.4 1.5 collective-permute-start.6
  24.9 1.5 collective-permute-start.5
  26.4 0.8 bitcast_dynamic-update-slice_fusion.4
  27.2 3.3 %collective-permute-done.2 = bf16[64,2048]{1,0:T(8,128)(2,1)S(1)} collective-permute-done((bf16[64,2048]{1,0:T(8,128)(2,1)S(1)}, bf16[64,2048]{1,0:T(8,128)(2,1)S(1)}, u32[]{:S(2)}, u32[]{:S(2)}) %collective-permute-start.2) | collective-permute-done | bytes 262176 | tf_op jit(solution)/shard_map/ppermute | solution.py:48
  30.5 1.6 collective-permute-done.3
  32.1 0.9 fusion.25
  33.0 0.8 bitcast_dynamic-update-slice_fusion.3
  33.8 0.8 bitcast_dynamic-update-slice_fusion.2
  34.7 5.0 %collective-permute-done.6 = bf16[128,2048]{1,0:T(8,128)(2,1)S(1)} collective-permute-done((bf16[128,2048]{1,0:T(8,128)(2,1)S(1)}, bf16[128,2048]{1,0:T(8,128)(2,1)S(1)}, u32[]{:S(2)}, u32[]{:S(2)}) %collective-permute-start.6) | collective-permute-done | bytes 524320 | tf_op jit(solution)/shard_map/ppermute | solution.py:48
  39.7 1.6 collective-permute-start.7
  41.3 1.6 collective-permute-start.8
  42.9 0.8 bitcast_dynamic-update-slice_fusion.1
  43.7 3.6 %collective-permute-done.7 = bf16[64,2048]{1,0:T(8,128)(2,1)S(1)} collective-permute-done((bf16[64,2048]{1,0:T(8,128)(2,1)S(1)}, bf16[64,2048]{1,0:T(8,128)(2,1)S(1)}, u32[]{:S(2)}, u32[]{:S(2)}) %collective-permute-start.7) | collective-permute-done | bytes 262176 | tf_op jit(solution)/shard_map/ppermute | solution.py:48
  47.7 0.9 fusion.26
  48.6 0.9 bitcast_dynamic-update-slice_fusion
  49.5 5.0 %gather_fusion = bf16[8,128,2048]{2,1,0:T(8,128)(2,1)} fusion(bf16[8,128,2048]{2,1,0:T(8,128)(2,1)} %bitcast_dynamic-update-slice_fusion, s32[1024]{0:T(1024)S(1)} %pad_clamp_fusion), kind=kCustom, calls=%fused_computation | custom fusion | bytes 8388640 | tf_op jit(solution)/shard_map/jit(_take)/gather | solution.py:140
  54.5 2.8 %bitcast_select_fusion = bf16[1024,2048]{1,0:T(8,128)(2,1)S(1)} fusion(bf16[8,128,2048]{2,1,0:T(8,128)(2,1)} %gather_fusion, pred[1024]{0:T(1024)(128)(4,1)S(1)} %broadcast_bitcast_fusion), kind=kLoop, calls=%fused_computation.7 | loop fusion | flops 2097152 | bytes 8389632 | tf_op jit(solution)/shard_map/jit(_take)/select_n | solution.py:140
  57.4 1.9 %collective-permute-start.9 = (bf16[6,2048]{1,0:T(8,128)(2,1)S(1)}, bf16[6,2048]{1,0:T(8,128)(2,1)S(1)}, u32[]{:S(2)}, u32[]{:S(2)}) collective-permute-start(bf16[6,2048]{1,0:T(8,128)(2,1)S(1)} %get-tuple-element.19), channel_id=1, source_target_pairs={{0,8},{8,16},{16,24},{24,32},{32,40},{40,48},{48,56},{56,64},{64,7... | collective-permute-start | bytes 73736 | tf_op jit(solution)/shard_map/ppermute | solution.py:13
  59.3 6.8 %collective-permute-start.10 = (bf16[6,2048]{1,0:T(8,128)(2,1)S(1)}, bf16[6,2048]{1,0:T(8,128)(2,1)S(1)}, u32[]{:S(2)}, u32[]{:S(2)}) collective-permute-start(bf16[6,2048]{1,0:T(8,128)(2,1)S(1)} %get-tuple-element.20), channel_id=1, source_target_pairs={{8,0},{16,8},{24,16},{32,24},{40,32},{48,40},{56,48},{64,56},{72,6... | collective-permute-start | bytes 73736 | tf_op jit(solution)/shard_map/ppermute | solution.py:13
  66.2 1.2 multiply_reduce_fusion.1
  67.7 1.9 %all-gather.2.cloned.1.call-done = bf16[2048,3,256]{2,0,1:T(8,128)(2,1)} async-done(((bf16[64,3,256]{2,0,1:T(8,128)(2,1)}), bf16[2048,3,256]{2,0,1:T(8,128)(2,1)}) %all-gather.2.cloned.1.call-update) | async-done | bytes 3145744 | tf_op jit(solution)/shard_map/all_gather | solution.py:139
  69.6 2.6 %convolution_convert_fusion.1 = bf16[12,3,256]{2,0,1:T(8,128)(2,1)S(1)} fusion(bf16[2048,3,256]{2,0,1:T(8,128)(2,1)} %all-gather.2.cloned.1.call-done, f32[2048]{0:T(1024)S(1)} %copy-done.9, f32[12]{0:T(128)S(1)} %add_rsqrt_fusion.1, bf16[6,2048]{1,0:T(8,128)(2,1)S(1)} %collective-permute-done.10, bf16[6,2048]{1,0:T(8,128)(2,1)S(1)} %collective-permute-done.9), kind=kOutput, calls=%fused_computation.43 | convolution fusion | flops 37929984 | bytes 3221552 | tf_op jit(solution)/shard_map/td,dsc->tsc/dot_general | solution.py:159
  72.5 5.6 %fusion.11 = bf16[1024,3,256]{2,0,1:T(8,128)(2,1)S(1)} fusion(bf16[2048,3,256]{2,0,1:T(8,128)(2,1)S(1)} %copy-done.2, bf16[1024,2048]{1,0:T(8,128)(2,1)} %copy-done.1, f32[2048]{0:T(1024)S(1)} %copy-done.9, f32[1024]{0:T(1024)S(1)} %rsqrt_bitcast_fusion), kind=kOutput, calls=%fused_computation.34 | convolution fusion | flops 3230400512 | bytes 8925184 | tf_op jit(solution)/shard_map/td,dsc->tsc/dot_general | solution.py:156
  78.5 2.6 %multiply_add_fusion = f32[1024,3,256]{2,0,1:T(8,128)S(1)} fusion(f32[1030,3,256]{2,0,1:T(8,128)S(1)} %maximum_convert_fusion, f32[3,256]{1,0:T(4,128)S(1)} %get-tuple-element.47, f32[3,256]{1,0:T(4,128)S(1)} %get-tuple-element.48, f32[3,256]{1,0:T(4,128)S(1)} %get-tuple-element.49, f32[3,256]{1,0:T(4,128)S(1)} %get-tuple-element.50, ...), kind=kLoop, calls=%fused_computation.32 | loop fusion | flops 10223616 | bytes 25187328 | tf_op jit(solution)/shard_map/add | solution.py:165
  81.1 1.2 fusion.15
  82.3 2.7 %multiply_reduce_fusion.2 = (f32[3,256]{1,0:T(4,128)S(1)}, f32[3,256]{1,0:T(4,128)S(1)}, f32[3,256]{1,0:T(4,128)S(1)}, f32[3,256]{1,0:T(4,128)S(1)}, f32[3,256]{...) fusion(f32[1030,3,256]{2,0,1:T(8,128)S(1)} %maximum_convert_fusion, ...), kind=kLoop, calls=%fused_computation.25 | loop fusion | flops 12577536 | bytes 25187328 | tf_op jit(solution)/shard_map/reduce_sum | solution.py:197
  85.4 3.7 %fusion.2 = bf16[1024,3,256]{2,0,1:T(8,128)(2,1)} fusion(f32[1030,3,256]{2,0,1:T(8,128)S(1)} %maximum_maximum_fusion, f32[3,256]{1,0:T(4,128)S(1)} %get-tuple-element.47, f32[3,256]{1,0:T(4,128)S(1)} %get-tuple-element.48, f32[3,256]{1,0:T(4,128)S(1)} %get-tuple-element.49, f32[3,256]{1,0:T(4,128)S(1)} %get-tuple-element.50, ...), kind=kLoop, calls=%fused_computation.12 | loop fusion | flops 12582912 | bytes 23614464 | tf_op jit(solution)/shard_map/convert_element_type | solution.py:194
  89.1 7.1 %multiply_reduce_fusion = (f32[2048]{0:T(1024)S(1)}, bf16[1024,2048]{1,0:T(8,128)(2,1)}) fusion(bf16[1024,2048]{1,0:T(8,128)(2,1)} %copy-done.1, f32[1024]{0:T(1024)S(1)} %rsqrt_bitcast_fusion, bf16[1024,3,256]{2,0,1:T(8,128)(2,1)} %fusion.2, bf16[2048,3,256]{2,0,1:T(8,128)(2,1)S(1)} %copy-done.2), kind=kOutput, calls=%fused_computation.2 | convolution fusion | flops 3233806336 | bytes 13119488 | tf_op jit(solution)/shard_map/tsc,dsc->td/dot_general | solution.py:203
  96.2 1.4 copy-done.5
  97.6 6.1 %convolution_convert_fusion = bf16[2048,3,256]{2,0,1:T(8,128)(2,1)S(1)} fusion(bf16[1024,3,256]{2,0,1:T(8,128)(2,1)S(1)} %copy-done.5, bf16[1024,2048]{1,0:T(8,128)(2,1)} %copy-done.1, f32[2048]{0:T(1024)S(1)} %copy-done.9, f32[1024]{0:T(1024)S(1)} %rsqrt_bitcast_fusion), kind=kOutput, calls=%fused_computation.8 | convolution fusion | flops 3231186944 | bytes 8925184 | tf_op jit(solution)/shard_map/td,tsc->dsc/dot_general | solution.py:210
  103.7 1.4 constant_dynamic-slice_fusion.1
  106.2 2.5 %collective-permute-done.12 = bf16[4,4,64,3,256]{4,2,3,1,0:T(8,128)(2,1)S(1)} collective-permute-done((bf16[4,4,64,3,256]{4,2,3,1,0:T(8,128)(2,1)S(1)}, bf16[4,4,64,3,256]{4,2,3,1,0:T(8,128)(2,1)S(1)}, u32[]{:S(2)}, u32[]{:S(2)}) %collective-permute-start.12) | collective-permute-done | bytes 1572896 | tf_op jit(solution)/shard_map/ppermute | solution.py:48
  108.7 1.2 copy-done.4
  109.9 2.9 %convert_add_fusion = f32[4,4,64,3,256]{4,2,3,1,0:T(8,128)S(1)} fusion(bf16[4,4,64,3,256]{4,2,3,1,0:T(8,128)(2,1)} %copy-done.4, bf16[4,4,1,64,3,256]{5,3,2,1,0,4:T(8,128)(2,1)} %get-tuple-element.27), kind=kLoop, calls=%fused_computation.24 | loop fusion | flops 2359296 | bytes 6291456 | tf_op jit(solution)/shard_map/add | solution.py:127
  112.7 1.1 fusion.27
  113.8 1.5 collective-permute-start.13
  115.8 2.1 %collective-permute-start.14 = (bf16[4,64,3,256]{3,1,2,0:T(8,128)(2,1)S(1)}, bf16[4,64,3,256]{3,1,2,0:T(8,128)(2,1)}, u32[]{:S(2)}, u32[]{:S(2)}) collective-permute-start(bf16[4,64,3,256]{3,1,2,0:T(8,128)(2,1)S(1)} %get-tuple-element.26), channel_id=1, source_target_pairs={{0,128},{8,136},{16,144},{24,152},{32,160},{40,168},{48,176},{56,1... | collective-permute-start | bytes 1179656 | tf_op jit(solution)/shard_map/ppermute | solution.py:48
  118.1 1.2 collective-permute-done.19
  119.3 4.6 %collective-permute-start.20 = (f32[7424]{0:T(1024)S(1)}, f32[7424]{0:T(1024)S(1)}, u32[]{:S(2)}, u32[]{:S(2)}) collective-permute-start(f32[7424]{0:T(1024)S(1)} %fusion.67), channel_id=1, source_target_pairs={{0,16},{8,24},{16,0},{24,8},{32,48},{40,56},{48,32},{56,40},{64,80... | collective-permute-start | bytes 89096 | tf_op jit(solution)/shard_map/ppermute | solution.py:21
  123.9 2.4 %collective-permute-done.20 = f32[7424]{0:T(1024)S(1)} collective-permute-done((f32[7424]{0:T(1024)S(1)}, f32[7424]{0:T(1024)S(1)}, u32[]{:S(2)}, u32[]{:S(2)}) %collective-permute-start.20) | collective-permute-done | bytes 29728 | tf_op jit(solution)/shard_map/ppermute | solution.py:21
  126.3 2.1 %collective-permute-start.21 = (f32[7424]{0:T(1024)S(1)}, f32[7424]{0:T(1024)S(1)}, u32[]{:S(2)}, u32[]{:S(2)}) collective-permute-start(f32[7424]{0:T(1024)S(1)} %add.392), channel_id=1, source_target_pairs={{0,32},{8,40},{16,48},{24,56},{32,0},{40,8},{48,16},{56,24},{64,96... | collective-permute-start | bytes 89096 | tf_op jit(solution)/shard_map/ppermute | solution.py:21
  128.4 6.1 %collective-permute-done.21 = f32[7424]{0:T(1024)S(1)} collective-permute-done((f32[7424]{0:T(1024)S(1)}, f32[7424]{0:T(1024)S(1)}, u32[]{:S(2)}, u32[]{:S(2)}) %collective-permute-start.21) | collective-permute-done | bytes 29728 | tf_op jit(solution)/shard_map/ppermute | solution.py:21
  134.5 1.0 collective-permute-start.22
  135.5 2.9 %collective-permute-done.22 = f32[7424]{0:T(1024)S(1)} collective-permute-done((f32[7424]{0:T(1024)S(1)}, f32[7424]{0:T(1024)S(1)}, u32[]{:S(2)}, u32[]{:S(2)}) %collective-permute-start.22) | collective-permute-done | bytes 29728 | tf_op jit(solution)/shard_map/ppermute | solution.py:21
  139.0 0.9 collective-permute-start.23
  140.0 4.8 %collective-permute-done.23 = f32[7424]{0:T(1024)} collective-permute-done((f32[7424]{0:T(1024)}, f32[7424]{0:T(1024)}, u32[]{:S(2)}, u32[]{:S(2)}) %collective-permute-start.23) | collective-permute-done | bytes 29728 | tf_op jit(solution)/shard_map/ppermute | solution.py:21
  145.6 3.1 %collective-permute-start.24 = (f32[2048]{0:T(1024)S(1)}, f32[2048]{0:T(1024)S(1)}, u32[]{:S(2)}, u32[]{:S(2)}) collective-permute-start(f32[2048]{0:T(1024)S(1)} %slice.248), channel_id=1, source_target_pairs={{0,1},{1,0},{2,3},{3,2},{4,5},{5,4},{6,7},{7,6},{8,9},{9,8},{10,11... | collective-permute-start | bytes 24584 | tf_op jit(solution)/shard_map/ppermute | solution.py:21
  148.7 1.4 fusion.24
  150.1 0.9 copy-done.3
  151.1 3.4 %collective-permute-start.16 = (bf16[64,3,256]{2,0,1:T(8,128)(2,1)S(1)}, bf16[64,3,256]{2,0,1:T(8,128)(2,1)S(1)}, u32[]{:S(2)}, u32[]{:S(2)}) collective-permute-start(bf16[64,3,256]{2,0,1:T(8,128)(2,1)S(1)} %get-tuple-element.30), channel_id=1, source_target_pairs={{0,16},{8,24},{16,32},{24,40},{32,48},{40,56},{48,0},{56,8},{64,80... | collective-permute-start | bytes 294920 | tf_op jit(solution)/shard_map/ppermute | solution.py:48
  154.4 0.9 collective-permute-start.18
  155.3 2.8 %collective-permute-start.17 = (bf16[64,3,256]{2,0,1:T(8,128)(2,1)S(1)}, bf16[64,3,256]{2,0,1:T(8,128)(2,1)S(1)}, u32[]{:S(2)}, u32[]{:S(2)}) collective-permute-start(bf16[64,3,256]{2,0,1:T(8,128)(2,1)S(1)} %get-tuple-element.32), channel_id=1, source_target_pairs={{0,32},{8,40},{16,48},{24,56},{32,0},{40,8},{48,16},{56,24},{64,96... | collective-permute-start | bytes 294920 | tf_op jit(solution)/shard_map/ppermute | solution.py:48
  158.1 2.4 %collective-permute-start.25 = (f32[2048]{0:T(1024)S(1)}, f32[2048]{0:T(1024)S(1)}, u32[]{:S(2)}, u32[]{:S(2)}) collective-permute-start(f32[2048]{0:T(1024)S(1)} %slice_add_fusion), channel_id=1, source_target_pairs={{0,2},{1,3},{2,0},{3,1},{4,6},{5,7},{6,4},{7,5},{8,10},{9,11},{10,... | collective-permute-start | bytes 24584 | tf_op jit(solution)/shard_map/ppermute | solution.py:21
  160.5 2.8 %collective-permute-done.25 = f32[2048]{0:T(1024)S(1)} collective-permute-done((f32[2048]{0:T(1024)S(1)}, f32[2048]{0:T(1024)S(1)}, u32[]{:S(2)}, u32[]{:S(2)}) %collective-permute-start.25) | collective-permute-done | bytes 8224 | tf_op jit(solution)/shard_map/ppermute | solution.py:21
  163.3 1.5 collective-permute-start.26
  167.6 1.6 fusion.32
  169.2 1.5 fusion.16
  170.8 2.3 %fusion.21 = bf16[128,2048]{1,0:T(8,128)(2,1)} fusion(bf16[128,2048]{1,0:T(8,128)(2,1)} %param.5, bf16[128,2048]{1,0:T(8,128)(2,1)} %reduce-scatter.2.cloned.1.call-done, f32[128]{0:T(128)S(1)} %broadcast_multiply_fusion, f32[2048]{0:T(1024)S(1)} %copy-done.9, f32[128]{0:T(128)S(1)} %add_rsqrt_fusion), kind=kLoop, calls=%fused_computation.51 | loop fusion | flops 2359296 | bytes 1582080 | tf_op jit(solution)/shard_map/convert_element_type | solution.py:223
  (92 shorter events, 10.0 us)
Async XLA Ops:
  7.2 62.5 %all-gather.2.cloned.1.call-start = ((), (), s32[]{:S(2)}) async-start(), calls=%async_computation.1 | async-start | bytes 3244032 | tf_op jit(solution)/shard_map/all_gather | solution.py:139
  7.2 14.0 %collective-permute-start.1 = (bf16[128,2048]{1,0:T(8,128)(2,1)}, bf16[128,2048]{1,0:T(8,128)(2,1)S(1)}, u32[]{:S(2)}, u32[]{:S(2)}) collective-permute-start(bf16[128,2048]{1,0:T(8,128)(2,1)} %param.5), channel_id=1, source_target_pairs={{0,1},{1,2},{2,3},{3,0},{4,5},{5,6},{6,7},{7,4},{8,9},{9,10},{10,1... | collective-permute-start | bytes 1572872 | tf_op jit(solution)/shard_map/ppermute | solution.py:48
  8.8 14.0 %collective-permute-start = (bf16[128,2048]{1,0:T(8,128)(2,1)}, bf16[128,2048]{1,0:T(8,128)(2,1)S(1)}, u32[]{:S(2)}, u32[]{:S(2)}) collective-permute-start(bf16[128,2048]{1,0:T(8,128)(2,1)} %param.5), channel_id=1, source_target_pairs={{0,3},{1,0},{2,1},{3,2},{4,7},{5,4},{6,5},{7,6},{8,11},{9,8},{10,9... | collective-permute-start | bytes 1572872 | tf_op jit(solution)/shard_map/ppermute | solution.py:48
  9.3 14.1 %collective-permute-start.4 = (bf16[128,2048]{1,0:T(8,128)(2,1)}, bf16[128,2048]{1,0:T(8,128)(2,1)S(1)}, u32[]{:S(2)}, u32[]{:S(2)}) collective-permute-start(bf16[128,2048]{1,0:T(8,128)(2,1)} %param.5), channel_id=1, source_target_pairs={{0,4},{1,5},{2,6},{3,7},{4,0},{5,1},{6,2},{7,3},{8,12},{9,13},{10,... | collective-permute-start | bytes 1572872 | tf_op jit(solution)/shard_map/ppermute | solution.py:48
  11.3 158.0 %reduce-scatter.2.cloned.1.call-start = ((), (), s32[]{:S(2)}) async-start(), calls=%async_computation.2 | async-start | bytes 4718592 | tf_op jit(solution)/shard_map/reduce_scatter | solution.py:207
  12.0 73.1 %collective-permute-start.11 = (bf16[6,256]{1,0:T(8,128)(2,1)S(1)}, bf16[6,256]{1,0:T(8,128)(2,1)S(1)}, u32[]{:S(2)}, u32[]{:S(2)}) collective-permute-start(bf16[6,256]{1,0:T(8,128)(2,1)S(1)} %slice.189), channel_id=1, source_target_pairs={{8,0},{16,8},{24,16},{32,24},{40,32},{48,40},{56,48},{64,56},{72,6... | collective-permute-start | bytes 9224 | tf_op jit(solution)/shard_map/ppermute | solution.py:13
  21.2 9.3 %collective-permute-start.2 = (bf16[64,2048]{1,0:T(8,128)(2,1)S(1)}, bf16[64,2048]{1,0:T(8,128)(2,1)S(1)}, u32[]{:S(2)}, u32[]{:S(2)}) collective-permute-start(bf16[64,2048]{1,0:T(8,128)(2,1)S(1)} %slice.212), channel_id=1, source_target_pairs={{0,1},{1,2},{2,3},{3,0},{4,5},{5,6},{6,7},{7,4},{8,9},{9,10},{10,1... | collective-permute-start | bytes 786440 | tf_op jit(solution)/shard_map/ppermute | solution.py:48
  22.8 9.3 %collective-permute-start.3 = (bf16[64,2048]{1,0:T(8,128)(2,1)S(1)}, bf16[64,2048]{1,0:T(8,128)(2,1)S(1)}, u32[]{:S(2)}, u32[]{:S(2)}) collective-permute-start(bf16[64,2048]{1,0:T(8,128)(2,1)S(1)} %slice.213), channel_id=1, source_target_pairs={{0,3},{1,0},{2,1},{3,2},{4,7},{5,4},{6,5},{7,6},{8,11},{9,8},{10,9... | collective-permute-start | bytes 786440 | tf_op jit(solution)/shard_map/ppermute | solution.py:48
  23.4 16.3 %collective-permute-start.6 = (bf16[128,2048]{1,0:T(8,128)(2,1)S(1)}, bf16[128,2048]{1,0:T(8,128)(2,1)S(1)}, u32[]{:S(2)}, u32[]{:S(2)}) collective-permute-start(bf16[128,2048]{1,0:T(8,128)(2,1)S(1)} %collective-permute-done.4), channel_id=1, source_target_pairs={{0,1},{1,2},{2,3},{3,0},{4,5},{5,6},{6,7},{7,4},{8,9},{9,10},{10,1... | collective-permute-start | bytes 1572872 | tf_op jit(solution)/shard_map/ppermute | solution.py:48
  24.9 16.4 %collective-permute-start.5 = (bf16[128,2048]{1,0:T(8,128)(2,1)S(1)}, bf16[128,2048]{1,0:T(8,128)(2,1)S(1)}, u32[]{:S(2)}, u32[]{:S(2)}) collective-permute-start(bf16[128,2048]{1,0:T(8,128)(2,1)S(1)} %collective-permute-done.4), channel_id=1, source_target_pairs={{0,3},{1,0},{2,1},{3,2},{4,7},{5,4},{6,5},{7,6},{8,11},{9,8},{10,9... | collective-permute-start | bytes 1572872 | tf_op jit(solution)/shard_map/ppermute | solution.py:48
  39.7 7.6 %collective-permute-start.7 = (bf16[64,2048]{1,0:T(8,128)(2,1)S(1)}, bf16[64,2048]{1,0:T(8,128)(2,1)S(1)}, u32[]{:S(2)}, u32[]{:S(2)}) collective-permute-start(bf16[64,2048]{1,0:T(8,128)(2,1)S(1)} %slice.214), channel_id=1, source_target_pairs={{0,1},{1,2},{2,3},{3,0},{4,5},{5,6},{6,7},{7,4},{8,9},{9,10},{10,1... | collective-permute-start | bytes 786440 | tf_op jit(solution)/shard_map/ppermute | solution.py:48
  41.3 6.4 %collective-permute-start.8 = (bf16[64,2048]{1,0:T(8,128)(2,1)S(1)}, bf16[64,2048]{1,0:T(8,128)(2,1)S(1)}, u32[]{:S(2)}, u32[]{:S(2)}) collective-permute-start(bf16[64,2048]{1,0:T(8,128)(2,1)S(1)} %slice.215), channel_id=1, source_target_pairs={{0,3},{1,0},{2,1},{3,2},{4,7},{5,4},{6,5},{7,6},{8,11},{9,8},{10,9... | collective-permute-start | bytes 786440 | tf_op jit(solution)/shard_map/ppermute | solution.py:48
  54.5 11.7 %copy-start = (bf16[8,128,2048]{2,1,0:T(8,128)(2,1)S(1)}, bf16[8,128,2048]{2,1,0:T(8,128)(2,1)}, u32[]{:S(2)}) copy-start(bf16[8,128,2048]{2,1,0:T(8,128)(2,1)} %gather_fusion) | copy-start | bytes 12582916
  57.4 10.0 %copy-start.1 = (bf16[1024,2048]{1,0:T(8,128)(2,1)}, bf16[1024,2048]{1,0:T(8,128)(2,1)S(1)}, u32[]{:S(2)}) copy-start(bf16[1024,2048]{1,0:T(8,128)(2,1)S(1)} %bitcast_select_fusion) | copy-start | bytes 12582916
  57.4 12.3 %copy-start.9 = (f32[2048]{0:T(1024)S(1)}, f32[2048]{0:T(1024)}, u32[]{:S(2)}) copy-start(f32[2048]{0:T(1024)} %param.6) | copy-start | bytes 24580
  57.4 10.0 %collective-permute-start.9 = (bf16[6,2048]{1,0:T(8,128)(2,1)S(1)}, bf16[6,2048]{1,0:T(8,128)(2,1)S(1)}, u32[]{:S(2)}, u32[]{:S(2)}) collective-permute-start(bf16[6,2048]{1,0:T(8,128)(2,1)S(1)} %get-tuple-element.19), channel_id=1, source_target_pairs={{0,8},{8,16},{16,24},{24,32},{32,40},{40,48},{48,56},{56,64},{64,7... | collective-permute-start | bytes 73736 | tf_op jit(solution)/shard_map/ppermute | solution.py:13
  59.3 8.2 %collective-permute-start.10 = (bf16[6,2048]{1,0:T(8,128)(2,1)S(1)}, bf16[6,2048]{1,0:T(8,128)(2,1)S(1)}, u32[]{:S(2)}, u32[]{:S(2)}) collective-permute-start(bf16[6,2048]{1,0:T(8,128)(2,1)S(1)} %get-tuple-element.20), channel_id=1, source_target_pairs={{8,0},{16,8},{24,16},{32,24},{40,32},{48,40},{56,48},{64,56},{72,6... | collective-permute-start | bytes 73736 | tf_op jit(solution)/shard_map/ppermute | solution.py:13
  69.6 2.8 %copy-start.2 = (bf16[2048,3,256]{2,0,1:T(8,128)(2,1)S(1)}, bf16[2048,3,256]{2,0,1:T(8,128)(2,1)}, u32[]{:S(2)}) copy-start(bf16[2048,3,256]{2,0,1:T(8,128)(2,1)} %all-gather.2.cloned.1.call-done) | copy-start | bytes 9437188
  78.5 2.6 %copy-start.6 = (bf16[1024,256]{1,0:T(8,128)(2,1)S(1)}, bf16[1024,256]{1,0:T(8,128)(2,1)}, u32[]{:S(2)}) copy-start(bf16[1024,256]{1,0:T(8,128)(2,1)} %param.9) | copy-start | bytes 1572868
  96.2 1.4 copy-start.5
  105.2 3.5 %collective-permute-start.12 = (bf16[4,4,64,3,256]{4,2,3,1,0:T(8,128)(2,1)S(1)}, bf16[4,4,64,3,256]{4,2,3,1,0:T(8,128)(2,1)S(1)}, u32[]{:S(2)}, u32[]{:S(2)}) collective-permute-start(bf16[4,4,64,3,256]{4,2,3,1,0:T(8,128)(2,1)S(1)} %bitcast.154), channel_id=1, source_target_pairs={{0,8},{8,0},{16,24},{24,16},{32,40},{40,32},{48,56},{56,48},{64,72... | collective-permute-start | bytes 4718600 | tf_op jit(solution)/shard_map/ppermute | solution.py:48
  108.7 1.2 copy-start.4
  109.9 8.1 %copy-start.7 = (f32[5376]{0:T(1024)S(1)}, f32[5376]{0:T(1024)}, u32[]{:S(2)}) copy-start(f32[5376]{0:T(1024)} %reshape.251) | copy-start | bytes 64516
  113.8 34.8 %collective-permute-start.13 = (bf16[4,64,3,256]{3,1,2,0:T(8,128)(2,1)}, bf16[4,64,3,256]{3,1,2,0:T(8,128)(2,1)}, u32[]{:S(2)}, u32[]{:S(2)}) collective-permute-start(bf16[4,64,3,256]{3,1,2,0:T(8,128)(2,1)} %get-tuple-element.24), channel_id=1, source_target_pairs={{0,64},{8,72},{16,80},{24,88},{32,96},{40,104},{48,112},{56,120},{... | collective-permute-start | bytes 1179656 | tf_op jit(solution)/shard_map/ppermute | solution.py:48
  115.3 33.4 %collective-permute-start.15 = (bf16[4,64,3,256]{3,1,2,0:T(8,128)(2,1)}, bf16[4,64,3,256]{3,1,2,0:T(8,128)(2,1)}, u32[]{:S(2)}, u32[]{:S(2)}) collective-permute-start(bf16[4,64,3,256]{3,1,2,0:T(8,128)(2,1)} %get-tuple-element.25), channel_id=1, source_target_pairs={{0,192},{8,200},{16,208},{24,216},{32,224},{40,232},{48,240},{56,2... | collective-permute-start | bytes 1179656 | tf_op jit(solution)/shard_map/ppermute | solution.py:48
  115.8 32.8 %collective-permute-start.14 = (bf16[4,64,3,256]{3,1,2,0:T(8,128)(2,1)S(1)}, bf16[4,64,3,256]{3,1,2,0:T(8,128)(2,1)}, u32[]{:S(2)}, u32[]{:S(2)}) collective-permute-start(bf16[4,64,3,256]{3,1,2,0:T(8,128)(2,1)S(1)} %get-tuple-element.26), channel_id=1, source_target_pairs={{0,128},{8,136},{16,144},{24,152},{32,160},{40,168},{48,176},{56,1... | collective-permute-start | bytes 1179656 | tf_op jit(solution)/shard_map/ppermute | solution.py:48
  118.0 1.3 collective-permute-start.19
  119.3 7.0 %collective-permute-start.20 = (f32[7424]{0:T(1024)S(1)}, f32[7424]{0:T(1024)S(1)}, u32[]{:S(2)}, u32[]{:S(2)}) collective-permute-start(f32[7424]{0:T(1024)S(1)} %fusion.67), channel_id=1, source_target_pairs={{0,16},{8,24},{16,0},{24,8},{32,48},{40,56},{48,32},{56,40},{64,80... | collective-permute-start | bytes 89096 | tf_op jit(solution)/shard_map/ppermute | solution.py:21
  126.3 8.2 %collective-permute-start.21 = (f32[7424]{0:T(1024)S(1)}, f32[7424]{0:T(1024)S(1)}, u32[]{:S(2)}, u32[]{:S(2)}) collective-permute-start(f32[7424]{0:T(1024)S(1)} %add.392), channel_id=1, source_target_pairs={{0,32},{8,40},{16,48},{24,56},{32,0},{40,8},{48,16},{56,24},{64,96... | collective-permute-start | bytes 89096 | tf_op jit(solution)/shard_map/ppermute | solution.py:21
  134.5 3.9 %collective-permute-start.22 = (f32[7424]{0:T(1024)S(1)}, f32[7424]{0:T(1024)S(1)}, u32[]{:S(2)}, u32[]{:S(2)}) collective-permute-start(f32[7424]{0:T(1024)S(1)} %add.393), channel_id=1, source_target_pairs={{0,64},{8,72},{16,80},{24,88},{32,96},{40,104},{48,112},{56,120},{... | collective-permute-start | bytes 89096 | tf_op jit(solution)/shard_map/ppermute | solution.py:21
  139.0 5.7 %collective-permute-start.23 = (f32[7424]{0:T(1024)}, f32[7424]{0:T(1024)}, u32[]{:S(2)}, u32[]{:S(2)}) collective-permute-start(f32[7424]{0:T(1024)} %add.394), channel_id=1, source_target_pairs={{0,128},{8,136},{16,144},{24,152},{32,160},{40,168},{48,176},{56,1... | collective-permute-start | bytes 89096 | tf_op jit(solution)/shard_map/ppermute | solution.py:21
  145.6 12.5 %copy-start.8 = (f32[7424]{0:T(1024)}, f32[7424]{0:T(1024)S(1)}, u32[]{:S(2)}) copy-start(f32[7424]{0:T(1024)S(1)} %add.395) | copy-start | bytes 89092
  145.6 12.5 %collective-permute-start.24 = (f32[2048]{0:T(1024)S(1)}, f32[2048]{0:T(1024)S(1)}, u32[]{:S(2)}, u32[]{:S(2)}) collective-permute-start(f32[2048]{0:T(1024)S(1)} %slice.248), channel_id=1, source_target_pairs={{0,1},{1,0},{2,3},{3,2},{4,5},{5,4},{6,7},{7,6},{8,9},{9,8},{10,11... | collective-permute-start | bytes 24584 | tf_op jit(solution)/shard_map/ppermute | solution.py:21
  150.1 0.9 copy-start.3
  151.1 16.5 %collective-permute-start.16 = (bf16[64,3,256]{2,0,1:T(8,128)(2,1)S(1)}, bf16[64,3,256]{2,0,1:T(8,128)(2,1)S(1)}, u32[]{:S(2)}, u32[]{:S(2)}) collective-permute-start(bf16[64,3,256]{2,0,1:T(8,128)(2,1)S(1)} %get-tuple-element.30), channel_id=1, source_target_pairs={{0,16},{8,24},{16,32},{24,40},{32,48},{40,56},{48,0},{56,8},{64,80... | collective-permute-start | bytes 294920 | tf_op jit(solution)/shard_map/ppermute | solution.py:48
  154.4 13.2 %collective-permute-start.18 = (bf16[64,3,256]{2,0,1:T(8,128)(2,1)S(1)}, bf16[64,3,256]{2,0,1:T(8,128)(2,1)S(1)}, u32[]{:S(2)}, u32[]{:S(2)}) collective-permute-start(bf16[64,3,256]{2,0,1:T(8,128)(2,1)S(1)} %get-tuple-element.31), channel_id=1, source_target_pairs={{0,48},{8,56},{16,0},{24,8},{32,16},{40,24},{48,32},{56,40},{64,11... | collective-permute-start | bytes 294920 | tf_op jit(solution)/shard_map/ppermute | solution.py:48
  155.3 12.3 %collective-permute-start.17 = (bf16[64,3,256]{2,0,1:T(8,128)(2,1)S(1)}, bf16[64,3,256]{2,0,1:T(8,128)(2,1)S(1)}, u32[]{:S(2)}, u32[]{:S(2)}) collective-permute-start(bf16[64,3,256]{2,0,1:T(8,128)(2,1)S(1)} %get-tuple-element.32), channel_id=1, source_target_pairs={{0,32},{8,40},{16,48},{24,56},{32,0},{40,8},{48,16},{56,24},{64,96... | collective-permute-start | bytes 294920 | tf_op jit(solution)/shard_map/ppermute | solution.py:48
  158.1 5.2 %collective-permute-start.25 = (f32[2048]{0:T(1024)S(1)}, f32[2048]{0:T(1024)S(1)}, u32[]{:S(2)}, u32[]{:S(2)}) collective-permute-start(f32[2048]{0:T(1024)S(1)} %slice_add_fusion), channel_id=1, source_target_pairs={{0,2},{1,3},{2,0},{3,1},{4,6},{5,7},{6,4},{7,5},{8,10},{9,11},{10,... | collective-permute-start | bytes 24584 | tf_op jit(solution)/shard_map/ppermute | solution.py:21
  163.3 3.7 %collective-permute-start.26 = (f32[2048]{0:T(1024)S(1)}, f32[2048]{0:T(1024)S(1)}, u32[]{:S(2)}, u32[]{:S(2)}) collective-permute-start(f32[2048]{0:T(1024)S(1)} %add.397), channel_id=1, source_target_pairs={{0,4},{1,5},{2,6},{3,7},{4,0},{5,1},{6,2},{7,3},{8,12},{9,13},{10,... | collective-permute-start | bytes 24584 | tf_op jit(solution)/shard_map/ppermute | solution.py:21
Sparse Core Ops, SparseCore 0:
  11.4 58.2 all-gather.1
  96.3 58.8 reduce-scatter.1

commit v8 on v6

--- a/solution.py
+++ b/solution.py
@@ -192,8 +192,12 @@
     for tap in range(taps):
         grad_acc = grad_acc + filters[:, tap, :] * grad_extended[tap : tap + length]
     grad_streams = grad_acc.astype(jnp.bfloat16)
+    weight_terms = jnp.einsum(
+        "td,tsc->dsc", positions, grad_streams, preferred_element_type=jnp.float32
+    ).astype(jnp.bfloat16)
+    late_streams, _ = lax.optimization_barrier((grad_streams, weight_terms))
     normed_terms = jnp.einsum(
-        "tsc,dsc->td", grad_streams, weights, preferred_element_type=jnp.float32
+        "tsc,dsc->td", late_streams, weights, preferred_element_type=jnp.float32
     ).astype(jnp.bfloat16)
     late_conv, late_extended, _ = lax.optimization_barrier((grad_conv, extended, normed_terms))
     filter_local = jnp.stack(
@@ -207,9 +211,7 @@
     grad_normed = lax.psum_scatter(
         normed_terms, "tensor", scatter_dimension=0, tiled=True
     ).astype(jnp.float32)
-    weight_terms = jnp.einsum(
-        "td,tsc->dsc", positions, grad_streams, preferred_element_type=jnp.float32
-    ).astype(jnp.bfloat16)
+
     block = proj_weight.shape[0]
     weight_blocks = weight_terms.reshape((-1, block) + weight_terms.shape[1:])
     grad_proj = scatter_dp(weight_blocks).astype(jnp.bfloat16)

time: 179 us -> 180 us (level)
  local copies, waits for them, and re-layouts: 20.1 us -> 22 us
    dynamic_slice x1, local copies, waits for them, and re-layouts: 1.43 us -> 3.43 us  [scatter_dp(): keep = lax.dynamic_index_in_dim(grid, c, axis=2, keepdims=False)]
    ppermute x8, starting transfers between devices: 11.6 us -> 9.73 us  [butterfly_sum(): value = value + lax.ppermute(value, axis, pairs)]
    unnamed x29 -> x27, local copies, waits for them, and re-layouts: 6.38 us -> 6.42 us
  transfers between devices with their start and end apart: 29 -> 29, of which waited for: 15 -> 15; matrix products, arithmetic and copies ran while one was open for 31% -> 29% of each run, Pallas kernels for 0% -> 0%
where the time goes in v8:
time: 180 us; the launch traced here: 179 us
  waiting for transfers between devices  48.6 us (27%)
  starting transfers between devices  45.3 us (25%)
  other arithmetic  30 us (17%)
  local copies, waits for them, and re-layouts  22 us (12%)
  matrix products  18.7 us (10%)
  between operations  14.5 us (8%)
    ppermute x8, waiting for transfers between devices, butterfly_sum(): value = value + lax.ppermute(value, axis, pairs)  25.9 us
    ppermute x16, starting transfers between devices, move(): return lax.ppermute(value, axis, pairs)  23 us
    ppermute x16, waiting for transfers between devices, move(): return lax.ppermute(value, axis, pairs)  17.8 us
    ppermute x3, starting transfers between devices, passed_along(): return lax.ppermute(shard, axis, pairs)  12.5 us
    ppermute x8, starting transfers between devices, butterfly_sum(): value = value + lax.ppermute(value, axis, pairs)  9.73 us
    unnamed x27, local copies, waits for them, and re-layouts  6.42 us
    dot_general x1, matrix products, body(): jnp.einsum('td,dsc->tsc', positions, weights, preferred_element_type=jnp....  5.67 us
    dot_general x1, matrix products, body(): jnp.einsum('td,tsc->dsc', positions, grad_streams, preferred_element_type...  5.34 us
  transfers between devices with their start and end apart: 29, of which 15 were waited for; matrix products, arithmetic and copies ran while one was open for 29% of the time, Pallas kernels for 0%

profile of v8, /device:TPU:10, one launch (start us, length us, event | category | flops | bytes accessed | tf_op | source)
XLA Modules:
  0.0 179.1 jit_solution(10962823493095655421)
XLA Ops:
  7.8 1.5 collective-permute-start.1
  9.3 1.9 %collective-permute-start.4 = (bf16[128,2048]{1,0:T(8,128)(2,1)}, bf16[128,2048]{1,0:T(8,128)(2,1)S(1)}, u32[]{:S(2)}, u32[]{:S(2)}) collective-permute-start(bf16[128,2048]{1,0:T(8,128)(2,1)} %param.5), channel_id=1, source_target_pairs={{0,4},{1,5},{2,6},{3,7},{4,0},{5,1},{6,2},{7,3},{8,12},{9,13},{10,... | collective-permute-start | bytes 1572872 | tf_op jit(solution)/shard_map/ppermute | solution.py:48
  11.3 0.7 slice.203
  12.0 5.8 %collective-permute-start.11 = (bf16[6,256]{1,0:T(8,128)(2,1)S(1)}, bf16[6,256]{1,0:T(8,128)(2,1)S(1)}, u32[]{:S(2)}, u32[]{:S(2)}) collective-permute-start(bf16[6,256]{1,0:T(8,128)(2,1)S(1)} %slice.203), channel_id=1, source_target_pairs={{8,0},{16,8},{24,16},{32,24},{40,32},{48,40},{56,48},{64,56},{72,6... | collective-permute-start | bytes 9224 | tf_op jit(solution)/shard_map/ppermute | solution.py:13
  17.9 1.0 fusion.76
  19.0 1.9 %bitcast_dynamic-update-slice_fusion.5 = bf16[8,128,2048]{2,1,0:T(8,128)(2,1)} fusion(bf16[128,2048]{1,0:T(8,128)(2,1)} %param.5), kind=kLoop, calls=%fused_computation.87 | loop fusion | bytes 1048576
  21.2 1.4 collective-permute-start.3
  22.6 0.8 collective-permute-start.2
  23.4 2.6 %collective-permute-start.5 = (bf16[128,2048]{1,0:T(8,128)(2,1)S(1)}, bf16[128,2048]{1,0:T(8,128)(2,1)S(1)}, u32[]{:S(2)}, u32[]{:S(2)}) collective-permute-start(bf16[128,2048]{1,0:T(8,128)(2,1)S(1)} %collective-permute-done.4), channel_id=1, source_target_pairs={{0,3},{1,0},{2,1},{3,2},{4,7},{5,4},{6,5},{7,6},{8,11},{9,8},{10,9... | collective-permute-start | bytes 1572872 | tf_op jit(solution)/shard_map/ppermute | solution.py:48
  26.0 0.8 bitcast_dynamic-update-slice_fusion.4
  26.8 3.7 %collective-permute-done.3 = bf16[64,2048]{1,0:T(8,128)(2,1)S(1)} collective-permute-done((bf16[64,2048]{1,0:T(8,128)(2,1)S(1)}, bf16[64,2048]{1,0:T(8,128)(2,1)S(1)}, u32[]{:S(2)}, u32[]{:S(2)}) %collective-permute-start.3) | collective-permute-done | bytes 262176 | tf_op jit(solution)/shard_map/ppermute | solution.py:48
  30.5 2.6 %collective-permute-done.2 = bf16[64,2048]{1,0:T(8,128)(2,1)S(1)} collective-permute-done((bf16[64,2048]{1,0:T(8,128)(2,1)S(1)}, bf16[64,2048]{1,0:T(8,128)(2,1)S(1)}, u32[]{:S(2)}, u32[]{:S(2)}) %collective-permute-start.2) | collective-permute-done | bytes 262176 | tf_op jit(solution)/shard_map/ppermute | solution.py:48
  33.1 0.9 fusion.31
  34.0 0.9 bitcast_dynamic-update-slice_fusion.3
  34.8 0.8 bitcast_dynamic-update-slice_fusion.2
  35.7 4.0 %collective-permute-done.5 = bf16[128,2048]{1,0:T(8,128)(2,1)S(1)} collective-permute-done((bf16[128,2048]{1,0:T(8,128)(2,1)S(1)}, bf16[128,2048]{1,0:T(8,128)(2,1)S(1)}, u32[]{:S(2)}, u32[]{:S(2)}) %collective-permute-start.5) | collective-permute-done | bytes 524320 | tf_op jit(solution)/shard_map/ppermute | solution.py:48
  39.7 2.1 %collective-permute-start.8 = (bf16[64,2048]{1,0:T(8,128)(2,1)S(1)}, bf16[64,2048]{1,0:T(8,128)(2,1)S(1)}, u32[]{:S(2)}, u32[]{:S(2)}) collective-permute-start(bf16[64,2048]{1,0:T(8,128)(2,1)S(1)} %slice.236), channel_id=1, source_target_pairs={{0,3},{1,0},{2,1},{3,2},{4,7},{5,4},{6,5},{7,6},{8,11},{9,8},{10,9... | collective-permute-start | bytes 786440 | tf_op jit(solution)/shard_map/ppermute | solution.py:48
  42.4 0.8 bitcast_dynamic-update-slice_fusion.1
  43.2 3.5 %collective-permute-done.8 = bf16[64,2048]{1,0:T(8,128)(2,1)S(1)} collective-permute-done((bf16[64,2048]{1,0:T(8,128)(2,1)S(1)}, bf16[64,2048]{1,0:T(8,128)(2,1)S(1)}, u32[]{:S(2)}, u32[]{:S(2)}) %collective-permute-start.8) | collective-permute-done | bytes 262176 | tf_op jit(solution)/shard_map/ppermute | solution.py:48
  46.7 3.2 %collective-permute-done.7 = bf16[64,2048]{1,0:T(8,128)(2,1)S(1)} collective-permute-done((bf16[64,2048]{1,0:T(8,128)(2,1)S(1)}, bf16[64,2048]{1,0:T(8,128)(2,1)S(1)}, u32[]{:S(2)}, u32[]{:S(2)}) %collective-permute-start.7) | collective-permute-done | bytes 262176 | tf_op jit(solution)/shard_map/ppermute | solution.py:48
  49.9 0.8 fusion.32
  50.8 0.8 bitcast_dynamic-update-slice_fusion
  51.6 5.0 %gather_fusion = bf16[8,128,2048]{2,1,0:T(8,128)(2,1)} fusion(bf16[8,128,2048]{2,1,0:T(8,128)(2,1)} %bitcast_dynamic-update-slice_fusion, s32[1024]{0:T(1024)S(1)} %pad_clamp_fusion), kind=kCustom, calls=%fused_computation | custom fusion | bytes 8388640 | tf_op jit(solution)/shard_map/jit(_take)/gather | solution.py:140
  56.6 2.8 %bitcast_select_fusion = bf16[1024,2048]{1,0:T(8,128)(2,1)S(1)} fusion(bf16[8,128,2048]{2,1,0:T(8,128)(2,1)} %gather_fusion, pred[1024]{0:T(1024)(128)(4,1)S(1)} %broadcast_bitcast_fusion), kind=kLoop, calls=%fused_computation.7 | loop fusion | flops 2097152 | bytes 8389632 | tf_op jit(solution)/shard_map/jit(_take)/select_n | solution.py:140
  59.5 4.6 %collective-permute-start.10 = (bf16[6,2048]{1,0:T(8,128)(2,1)S(1)}, bf16[6,2048]{1,0:T(8,128)(2,1)S(1)}, u32[]{:S(2)}, u32[]{:S(2)}) collective-permute-start(bf16[6,2048]{1,0:T(8,128)(2,1)S(1)} %get-tuple-element.21), channel_id=1, source_target_pairs={{8,0},{16,8},{24,16},{32,24},{40,32},{48,40},{56,48},{64,56},{72,6... | collective-permute-start | bytes 73736 | tf_op jit(solution)/shard_map/ppermute | solution.py:13
  64.1 2.1 %collective-permute-start.9 = (bf16[6,2048]{1,0:T(8,128)(2,1)S(1)}, bf16[6,2048]{1,0:T(8,128)(2,1)S(1)}, u32[]{:S(2)}, u32[]{:S(2)}) collective-permute-start(bf16[6,2048]{1,0:T(8,128)(2,1)S(1)} %get-tuple-element.20), channel_id=1, source_target_pairs={{0,8},{8,16},{16,24},{24,32},{32,40},{40,48},{48,56},{56,64},{64,7... | collective-permute-start | bytes 73736 | tf_op jit(solution)/shard_map/ppermute | solution.py:13
  66.3 1.2 multiply_reduce_fusion.1
  67.5 4.9 %collective-permute-done.9 = bf16[6,2048]{1,0:T(8,128)(2,1)S(1)} collective-permute-done((bf16[6,2048]{1,0:T(8,128)(2,1)S(1)}, bf16[6,2048]{1,0:T(8,128)(2,1)S(1)}, u32[]{:S(2)}, u32[]{:S(2)}) %collective-permute-start.9) | collective-permute-done | bytes 24608 | tf_op jit(solution)/shard_map/ppermute | solution.py:13
  72.6 2.6 %convolution_convert_fusion.1 = bf16[12,3,256]{2,0,1:T(8,128)(2,1)S(1)} fusion(bf16[2048,3,256]{2,0,1:T(8,128)(2,1)} %all-gather.2.cloned.1.call-done, f32[2048]{0:T(1024)S(1)} %copy-done.8, f32[12]{0:T(128)S(1)} %add_rsqrt_fusion.1, bf16[6,2048]{1,0:T(8,128)(2,1)S(1)} %collective-permute-done.10, bf16[6,2048]{1,0:T(8,128)(2,1)S(1)} %collective-permute-done.9), kind=kOutput, calls=%fused_computation.55 | convolution fusion | flops 37929984 | bytes 3221552 | tf_op jit(solution)/shard_map/td,dsc->tsc/dot_general | solution.py:159
  75.4 5.7 %fusion.17 = bf16[1024,3,256]{2,0,1:T(8,128)(2,1)S(1)} fusion(bf16[2048,3,256]{2,0,1:T(8,128)(2,1)S(1)} %copy-done.3, bf16[1024,2048]{1,0:T(8,128)(2,1)} %copy-done.1, f32[2048]{0:T(1024)S(1)} %copy-done.8, f32[1024]{0:T(1024)S(1)} %rsqrt_bitcast_fusion), kind=kOutput, calls=%fused_computation.46 | convolution fusion | flops 3230400512 | bytes 8925184 | tf_op jit(solution)/shard_map/td,dsc->tsc/dot_general | solution.py:156
  81.4 2.6 %fusion.8 = f32[1024,3,256]{2,0,1:T(8,128)S(1)} fusion(f32[1030,3,256]{2,0,1:T(8,128)S(1)} %maximum_convert_fusion, f32[3,256]{1,0:T(4,128)S(1)} %get-tuple-element.50, f32[3,256]{1,0:T(4,128)S(1)} %get-tuple-element.51, f32[3,256]{1,0:T(4,128)S(1)} %get-tuple-element.52, f32[3,256]{1,0:T(4,128)S(1)} %get-tuple-element.53, ...), kind=kLoop, calls=%fused_computation.24 | loop fusion | flops 10223616 | bytes 25187328 | tf_op jit(solution)/shard_map/add | solution.py:165
  84.0 1.2 fusion.21
  85.5 3.8 %pad_maximum_fusion = (f32[1024,3,256]{2,0,1:T(8,128)}, bf16[1024,3,256]{2,0,1:T(8,128)(2,1)S(1)}) fusion(f32[1024,1,256]{2,0,1:T(8,128)S(1)} %get-tuple-element.23, f32[1024,1,256]{2,0,1:T(8,128)S(1)} %get-tuple-element.24, f32[1024,1,256]{2,0,1:T(8,128)S(1)} %get-tuple-element.22, f32[1030,3,256]{2,0,1:T(8,128)S(1)} %maximum_maximum_fusion, ...), kind=kLoop, calls=%fused_computation.36 | loop fusion | flops 12582912 | bytes 26760192 | tf_op jit(solution)/shard_map/stack | solution.py:168
  89.4 5.3 %convolution_convert_fusion = bf16[2048,3,256]{2,0,1:T(8,128)(2,1)} fusion(bf16[1024,3,256]{2,0,1:T(8,128)(2,1)S(1)} %get-tuple-element.8, bf16[1024,2048]{1,0:T(8,128)(2,1)S(1)} %copy-done.2, f32[2048]{0:T(1024)S(1)} %copy-done.8, f32[1024]{0:T(1024)S(1)} %rsqrt_bitcast_fusion), kind=kOutput, calls=%fused_computation.8 | convolution fusion | flops 3231186944 | bytes 8925184 | tf_op jit(solution)/shard_map/td,tsc->dsc/dot_general | solution.py:195
  94.7 5.1 %multiply_reduce_fusion = (f32[2048]{0:T(1024)S(1)}, bf16[1024,2048]{1,0:T(8,128)(2,1)}) fusion(bf16[1024,2048]{1,0:T(8,128)(2,1)S(1)} %copy-done.2, f32[1024]{0:T(1024)S(1)} %rsqrt_bitcast_fusion, bf16[1024,3,256]{2,0,1:T(8,128)(2,1)S(1)} %get-tuple-element.8, bf16[2048,3,256]{2,0,1:T(8,128)(2,1)S(1)} %copy-done.3), kind=kOutput, calls=%fused_computation.2 | convolution fusion | flops 3233806336 | bytes 13119488 | tf_op jit(solution)/shard_map/tsc,dsc->td/dot_general | solution.py:199
  99.8 3.4 %constant_dynamic-slice_fusion.1 = (bf16[4,4,1,64,3,256]{5,3,2,1,0,4:T(8,128)(2,1)}, bf16[4,4,1,64,3,256]{5,3,2,1,0,4:T(8,128)(2,1)S(1)}) fusion(bf16[4,4,2,64,3,256]{5,3,2,1,0,4:T(8,128)(2,1)} %bitcast.153, s32[]{:T(128)S(6)} %select_n.209, s32[]{:T(128)S(6)} %select_n.210), kind=kLoop, calls=%fused_computation.146 | loop fusion | bytes 6291464 | tf_op jit(solution)/shard_map/jit(dynamic_index_in_dim)/dynamic_slice | solution.py:125
  103.3 1.3 copy.37
  104.6 4.1 %multiply_reduce_fusion.2 = (f32[3,256]{1,0:T(4,128)S(1)}, f32[3,256]{1,0:T(4,128)S(1)}, f32[3,256]{1,0:T(4,128)S(1)}, f32[3,256]{1,0:T(4,128)S(1)}, f32[3,256]{...) fusion(f32[1024,3,256]{2,0,1:T(8,128)} %get-tuple-element.9, f32[1030,3,256]{2,0,1:T(8,128)S(1)} %maximum_convert_fusion), kind=kLoop, calls=%fused_computation.38 | loop fusion | flops 11004672 | bytes 25187328 | tf_op jit(solution)/shard_map/reduce_sum | solution.py:205
  109.5 2.7 %convert_add_fusion = f32[4,4,64,3,256]{4,2,3,1,0:T(8,128)S(1)} fusion(bf16[4,4,64,3,256]{4,2,3,1,0:T(8,128)(2,1)} %collective-permute-done.12, bf16[4,4,1,64,3,256]{5,3,2,1,0,4:T(8,128)(2,1)} %get-tuple-element.30), kind=kLoop, calls=%fused_computation.37 | loop fusion | flops 2359296 | bytes 6291456 | tf_op jit(solution)/shard_map/add | solution.py:127
  112.2 1.1 fusion.33
  113.3 3.3 %collective-permute-start.14 = (bf16[4,64,3,256]{3,1,2,0:T(8,128)(2,1)}, bf16[4,64,3,256]{3,1,2,0:T(8,128)(2,1)}, u32[]{:S(2)}, u32[]{:S(2)}) collective-permute-start(bf16[4,64,3,256]{3,1,2,0:T(8,128)(2,1)} %get-tuple-element.29), channel_id=1, source_target_pairs={{0,128},{8,136},{16,144},{24,152},{32,160},{40,168},{48,176},{56,1... | collective-permute-start | bytes 1179656 | tf_op jit(solution)/shard_map/ppermute | solution.py:48
  116.5 2.2 %collective-permute-start.13 = (bf16[4,64,3,256]{3,1,2,0:T(8,128)(2,1)S(1)}, bf16[4,64,3,256]{3,1,2,0:T(8,128)(2,1)}, u32[]{:S(2)}, u32[]{:S(2)}) collective-permute-start(bf16[4,64,3,256]{3,1,2,0:T(8,128)(2,1)S(1)} %get-tuple-element.27), channel_id=1, source_target_pairs={{0,64},{8,72},{16,80},{24,88},{32,96},{40,104},{48,112},{56,120},{... | collective-permute-start | bytes 1179656 | tf_op jit(solution)/shard_map/ppermute | solution.py:48
  118.8 1.2 collective-permute-done.19
  120.1 5.2 %collective-permute-done.20 = f32[7424]{0:T(1024)S(1)} collective-permute-done((f32[7424]{0:T(1024)S(1)}, f32[7424]{0:T(1024)S(1)}, u32[]{:S(2)}, u32[]{:S(2)}) %collective-permute-start.20) | collective-permute-done | bytes 29728 | tf_op jit(solution)/shard_map/ppermute | solution.py:21
  125.3 2.6 %collective-permute-start.21 = (f32[7424]{0:T(1024)S(1)}, f32[7424]{0:T(1024)S(1)}, u32[]{:S(2)}, u32[]{:S(2)}) collective-permute-start(f32[7424]{0:T(1024)S(1)} %add.392), channel_id=1, source_target_pairs={{0,32},{8,40},{16,48},{24,56},{32,0},{40,8},{48,16},{56,24},{64,96... | collective-permute-start | bytes 89096 | tf_op jit(solution)/shard_map/ppermute | solution.py:21
  127.9 5.3 %collective-permute-done.21 = f32[7424]{0:T(1024)S(1)} collective-permute-done((f32[7424]{0:T(1024)S(1)}, f32[7424]{0:T(1024)S(1)}, u32[]{:S(2)}, u32[]{:S(2)}) %collective-permute-start.21) | collective-permute-done | bytes 29728 | tf_op jit(solution)/shard_map/ppermute | solution.py:21
  133.2 3.9 %collective-permute-done.22 = f32[7424]{0:T(1024)S(1)} collective-permute-done((f32[7424]{0:T(1024)S(1)}, f32[7424]{0:T(1024)S(1)}, u32[]{:S(2)}, u32[]{:S(2)}) %collective-permute-start.22) | collective-permute-done | bytes 29728 | tf_op jit(solution)/shard_map/ppermute | solution.py:21
  137.1 0.6 add.394
  137.8 1.6 collective-permute-start.23
  139.3 4.1 %collective-permute-done.23 = f32[7424]{0:T(1024)} collective-permute-done((f32[7424]{0:T(1024)}, f32[7424]{0:T(1024)}, u32[]{:S(2)}, u32[]{:S(2)}) %collective-permute-start.23) | collective-permute-done | bytes 29728 | tf_op jit(solution)/shard_map/ppermute | solution.py:21
  143.5 0.8 add.395
  144.3 4.0 %collective-permute-start.24 = (f32[2048]{0:T(1024)S(1)}, f32[2048]{0:T(1024)S(1)}, u32[]{:S(2)}, u32[]{:S(2)}) collective-permute-start(f32[2048]{0:T(1024)S(1)} %slice.269), channel_id=1, source_target_pairs={{0,1},{1,0},{2,3},{3,2},{4,5},{5,4},{6,7},{7,6},{8,9},{9,8},{10,11... | collective-permute-start | bytes 24584 | tf_op jit(solution)/shard_map/ppermute | solution.py:21
  148.3 1.5 fusion.30
  149.8 0.9 copy-done.4
  150.7 2.0 %collective-permute-start.18 = (bf16[64,3,256]{2,0,1:T(8,128)(2,1)S(1)}, bf16[64,3,256]{2,0,1:T(8,128)(2,1)S(1)}, u32[]{:S(2)}, u32[]{:S(2)}) collective-permute-start(bf16[64,3,256]{2,0,1:T(8,128)(2,1)S(1)} %get-tuple-element.34), channel_id=1, source_target_pairs={{0,48},{8,56},{16,0},{24,8},{32,16},{40,24},{48,32},{56,40},{64,11... | collective-permute-start | bytes 294920 | tf_op jit(solution)/shard_map/ppermute | solution.py:48
  152.7 2.4 %collective-permute-start.17 = (bf16[64,3,256]{2,0,1:T(8,128)(2,1)S(1)}, bf16[64,3,256]{2,0,1:T(8,128)(2,1)S(1)}, u32[]{:S(2)}, u32[]{:S(2)}) collective-permute-start(bf16[64,3,256]{2,0,1:T(8,128)(2,1)S(1)} %get-tuple-element.35), channel_id=1, source_target_pairs={{0,32},{8,40},{16,48},{24,56},{32,0},{40,8},{48,16},{56,24},{64,96... | collective-permute-start | bytes 294920 | tf_op jit(solution)/shard_map/ppermute | solution.py:48
  155.1 2.2 %collective-permute-start.16 = (bf16[64,3,256]{2,0,1:T(8,128)(2,1)S(1)}, bf16[64,3,256]{2,0,1:T(8,128)(2,1)S(1)}, u32[]{:S(2)}, u32[]{:S(2)}) collective-permute-start(bf16[64,3,256]{2,0,1:T(8,128)(2,1)S(1)} %get-tuple-element.33), channel_id=1, source_target_pairs={{0,16},{8,24},{16,32},{24,40},{32,48},{40,56},{48,0},{56,8},{64,80... | collective-permute-start | bytes 294920 | tf_op jit(solution)/shard_map/ppermute | solution.py:48
  157.4 5.1 %collective-permute-done.25 = f32[2048]{0:T(1024)S(1)} collective-permute-done((f32[2048]{0:T(1024)S(1)}, f32[2048]{0:T(1024)S(1)}, u32[]{:S(2)}, u32[]{:S(2)}) %collective-permute-start.25) | collective-permute-done | bytes 8224 | tf_op jit(solution)/shard_map/ppermute | solution.py:21
  162.5 1.3 collective-permute-start.26
  163.8 0.7 slice.268
  165.2 1.0 collective-permute-done.26
  166.8 1.6 fusion.38
  168.4 1.5 fusion.22
  170.0 2.3 %fusion.27 = bf16[128,2048]{1,0:T(8,128)(2,1)} fusion(bf16[128,2048]{1,0:T(8,128)(2,1)} %param.5, bf16[128,2048]{1,0:T(8,128)(2,1)} %reduce-scatter.2.cloned.1.call-done, f32[128]{0:T(128)S(1)} %broadcast_multiply_fusion, f32[2048]{0:T(1024)S(1)} %copy-done.8, f32[128]{0:T(128)S(1)} %add_rsqrt_fusion), kind=kLoop, calls=%fused_computation.63 | loop fusion | flops 2359296 | bytes 1582080 | tf_op jit(solution)/shard_map/convert_element_type | solution.py:225
  (90 shorter events, 5.1 us)
Async XLA Ops:
  7.2 65.4 %all-gather.2.cloned.1.call-start = ((), (), s32[]{:S(2)}) async-start(), calls=%async_computation.1 | async-start | bytes 3244032 | tf_op jit(solution)/shard_map/all_gather | solution.py:139
  7.2 14.0 %collective-permute-start = (bf16[128,2048]{1,0:T(8,128)(2,1)}, bf16[128,2048]{1,0:T(8,128)(2,1)S(1)}, u32[]{:S(2)}, u32[]{:S(2)}) collective-permute-start(bf16[128,2048]{1,0:T(8,128)(2,1)} %param.5), channel_id=1, source_target_pairs={{0,3},{1,0},{2,1},{3,2},{4,7},{5,4},{6,5},{7,6},{8,11},{9,8},{10,9... | collective-permute-start | bytes 1572872 | tf_op jit(solution)/shard_map/ppermute | solution.py:48
  7.8 14.7 %collective-permute-start.1 = (bf16[128,2048]{1,0:T(8,128)(2,1)}, bf16[128,2048]{1,0:T(8,128)(2,1)S(1)}, u32[]{:S(2)}, u32[]{:S(2)}) collective-permute-start(bf16[128,2048]{1,0:T(8,128)(2,1)} %param.5), channel_id=1, source_target_pairs={{0,1},{1,2},{2,3},{3,0},{4,5},{5,6},{6,7},{7,4},{8,9},{9,10},{10,1... | collective-permute-start | bytes 1572872 | tf_op jit(solution)/shard_map/ppermute | solution.py:48
  9.3 14.1 %collective-permute-start.4 = (bf16[128,2048]{1,0:T(8,128)(2,1)}, bf16[128,2048]{1,0:T(8,128)(2,1)S(1)}, u32[]{:S(2)}, u32[]{:S(2)}) collective-permute-start(bf16[128,2048]{1,0:T(8,128)(2,1)} %param.5), channel_id=1, source_target_pairs={{0,4},{1,5},{2,6},{3,7},{4,0},{5,1},{6,2},{7,3},{8,12},{9,13},{10,... | collective-permute-start | bytes 1572872 | tf_op jit(solution)/shard_map/ppermute | solution.py:48
  11.3 157.2 %reduce-scatter.2.cloned.1.call-start = ((), (), s32[]{:S(2)}) async-start(), calls=%async_computation.2 | async-start | bytes 4718592 | tf_op jit(solution)/shard_map/reduce_scatter | solution.py:211
  12.0 73.3 %collective-permute-start.11 = (bf16[6,256]{1,0:T(8,128)(2,1)S(1)}, bf16[6,256]{1,0:T(8,128)(2,1)S(1)}, u32[]{:S(2)}, u32[]{:S(2)}) collective-permute-start(bf16[6,256]{1,0:T(8,128)(2,1)S(1)} %slice.203), channel_id=1, source_target_pairs={{8,0},{16,8},{24,16},{32,24},{40,32},{48,40},{56,48},{64,56},{72,6... | collective-permute-start | bytes 9224 | tf_op jit(solution)/shard_map/ppermute | solution.py:13
  21.2 9.3 %collective-permute-start.3 = (bf16[64,2048]{1,0:T(8,128)(2,1)S(1)}, bf16[64,2048]{1,0:T(8,128)(2,1)S(1)}, u32[]{:S(2)}, u32[]{:S(2)}) collective-permute-start(bf16[64,2048]{1,0:T(8,128)(2,1)S(1)} %slice.234), channel_id=1, source_target_pairs={{0,3},{1,0},{2,1},{3,2},{4,7},{5,4},{6,5},{7,6},{8,11},{9,8},{10,9... | collective-permute-start | bytes 786440 | tf_op jit(solution)/shard_map/ppermute | solution.py:48
  22.6 10.5 %collective-permute-start.2 = (bf16[64,2048]{1,0:T(8,128)(2,1)S(1)}, bf16[64,2048]{1,0:T(8,128)(2,1)S(1)}, u32[]{:S(2)}, u32[]{:S(2)}) collective-permute-start(bf16[64,2048]{1,0:T(8,128)(2,1)S(1)} %slice.233), channel_id=1, source_target_pairs={{0,1},{1,2},{2,3},{3,0},{4,5},{5,6},{6,7},{7,4},{8,9},{9,10},{10,1... | collective-permute-start | bytes 786440 | tf_op jit(solution)/shard_map/ppermute | solution.py:48
  23.4 16.3 %collective-permute-start.5 = (bf16[128,2048]{1,0:T(8,128)(2,1)S(1)}, bf16[128,2048]{1,0:T(8,128)(2,1)S(1)}, u32[]{:S(2)}, u32[]{:S(2)}) collective-permute-start(bf16[128,2048]{1,0:T(8,128)(2,1)S(1)} %collective-permute-done.4), channel_id=1, source_target_pairs={{0,3},{1,0},{2,1},{3,2},{4,7},{5,4},{6,5},{7,6},{8,11},{9,8},{10,9... | collective-permute-start | bytes 1572872 | tf_op jit(solution)/shard_map/ppermute | solution.py:48
  26.0 16.3 %collective-permute-start.6 = (bf16[128,2048]{1,0:T(8,128)(2,1)S(1)}, bf16[128,2048]{1,0:T(8,128)(2,1)S(1)}, u32[]{:S(2)}, u32[]{:S(2)}) collective-permute-start(bf16[128,2048]{1,0:T(8,128)(2,1)S(1)} %collective-permute-done.4), channel_id=1, source_target_pairs={{0,1},{1,2},{2,3},{3,0},{4,5},{5,6},{6,7},{7,4},{8,9},{9,10},{10,1... | collective-permute-start | bytes 1572872 | tf_op jit(solution)/shard_map/ppermute | solution.py:48
  39.7 7.0 %collective-permute-start.8 = (bf16[64,2048]{1,0:T(8,128)(2,1)S(1)}, bf16[64,2048]{1,0:T(8,128)(2,1)S(1)}, u32[]{:S(2)}, u32[]{:S(2)}) collective-permute-start(bf16[64,2048]{1,0:T(8,128)(2,1)S(1)} %slice.236), channel_id=1, source_target_pairs={{0,3},{1,0},{2,1},{3,2},{4,7},{5,4},{6,5},{7,6},{8,11},{9,8},{10,9... | collective-permute-start | bytes 786440 | tf_op jit(solution)/shard_map/ppermute | solution.py:48
  42.3 7.7 %collective-permute-start.7 = (bf16[64,2048]{1,0:T(8,128)(2,1)S(1)}, bf16[64,2048]{1,0:T(8,128)(2,1)S(1)}, u32[]{:S(2)}, u32[]{:S(2)}) collective-permute-start(bf16[64,2048]{1,0:T(8,128)(2,1)S(1)} %slice.235), channel_id=1, source_target_pairs={{0,1},{1,2},{2,3},{3,0},{4,5},{5,6},{6,7},{7,4},{8,9},{9,10},{10,1... | collective-permute-start | bytes 786440 | tf_op jit(solution)/shard_map/ppermute | solution.py:48
  56.6 9.6 %copy-start = (bf16[8,128,2048]{2,1,0:T(8,128)(2,1)S(1)}, bf16[8,128,2048]{2,1,0:T(8,128)(2,1)}, u32[]{:S(2)}) copy-start(bf16[8,128,2048]{2,1,0:T(8,128)(2,1)} %gather_fusion) | copy-start | bytes 12582916
  59.5 8.0 %copy-start.1 = (bf16[1024,2048]{1,0:T(8,128)(2,1)}, bf16[1024,2048]{1,0:T(8,128)(2,1)S(1)}, u32[]{:S(2)}) copy-start(bf16[1024,2048]{1,0:T(8,128)(2,1)S(1)} %bitcast_select_fusion) | copy-start | bytes 12582916
  59.5 13.1 %copy-start.8 = (f32[2048]{0:T(1024)S(1)}, f32[2048]{0:T(1024)}, u32[]{:S(2)}) copy-start(f32[2048]{0:T(1024)} %param.6) | copy-start | bytes 24580
  59.5 8.0 %collective-permute-start.10 = (bf16[6,2048]{1,0:T(8,128)(2,1)S(1)}, bf16[6,2048]{1,0:T(8,128)(2,1)S(1)}, u32[]{:S(2)}, u32[]{:S(2)}) collective-permute-start(bf16[6,2048]{1,0:T(8,128)(2,1)S(1)} %get-tuple-element.21), channel_id=1, source_target_pairs={{8,0},{16,8},{24,16},{32,24},{40,32},{48,40},{56,48},{64,56},{72,6... | collective-permute-start | bytes 73736 | tf_op jit(solution)/shard_map/ppermute | solution.py:13
  64.1 8.2 %collective-permute-start.9 = (bf16[6,2048]{1,0:T(8,128)(2,1)S(1)}, bf16[6,2048]{1,0:T(8,128)(2,1)S(1)}, u32[]{:S(2)}, u32[]{:S(2)}) collective-permute-start(bf16[6,2048]{1,0:T(8,128)(2,1)S(1)} %get-tuple-element.20), channel_id=1, source_target_pairs={{0,8},{8,16},{16,24},{24,32},{32,40},{40,48},{48,56},{56,64},{64,7... | collective-permute-start | bytes 73736 | tf_op jit(solution)/shard_map/ppermute | solution.py:13
  72.6 2.8 %copy-start.3 = (bf16[2048,3,256]{2,0,1:T(8,128)(2,1)S(1)}, bf16[2048,3,256]{2,0,1:T(8,128)(2,1)}, u32[]{:S(2)}) copy-start(bf16[2048,3,256]{2,0,1:T(8,128)(2,1)} %all-gather.2.cloned.1.call-done) | copy-start | bytes 9437188
  81.4 2.6 %copy-start.5 = (bf16[1024,256]{1,0:T(8,128)(2,1)S(1)}, bf16[1024,256]{1,0:T(8,128)(2,1)}, u32[]{:S(2)}) copy-start(bf16[1024,256]{1,0:T(8,128)(2,1)} %param.9) | copy-start | bytes 1572868
  85.5 3.8 %copy-start.2 = (bf16[1024,2048]{1,0:T(8,128)(2,1)S(1)}, bf16[1024,2048]{1,0:T(8,128)(2,1)}, u32[]{:S(2)}) copy-start(bf16[1024,2048]{1,0:T(8,128)(2,1)} %copy-done.1) | copy-start | bytes 12582916
  104.6 4.9 %collective-permute-start.12 = (bf16[4,4,64,3,256]{4,2,3,1,0:T(8,128)(2,1)}, bf16[4,4,64,3,256]{4,2,3,1,0:T(8,128)(2,1)}, u32[]{:S(2)}, u32[]{:S(2)}) collective-permute-start(bf16[4,4,64,3,256]{4,2,3,1,0:T(8,128)(2,1)} %bitcast.151), channel_id=1, source_target_pairs={{0,8},{8,0},{16,24},{24,16},{32,40},{40,32},{48,56},{56,48},{64,72... | collective-permute-start | bytes 4718600 | tf_op jit(solution)/shard_map/ppermute | solution.py:48
  109.5 9.3 %copy-start.6 = (f32[5376]{0:T(1024)S(1)}, f32[5376]{0:T(1024)}, u32[]{:S(2)}) copy-start(f32[5376]{0:T(1024)} %reshape.251) | copy-start | bytes 64516
  113.3 35.0 %collective-permute-start.15 = (bf16[4,64,3,256]{3,1,2,0:T(8,128)(2,1)}, bf16[4,64,3,256]{3,1,2,0:T(8,128)(2,1)}, u32[]{:S(2)}, u32[]{:S(2)}) collective-permute-start(bf16[4,64,3,256]{3,1,2,0:T(8,128)(2,1)} %get-tuple-element.28), channel_id=1, source_target_pairs={{0,192},{8,200},{16,208},{24,216},{32,224},{40,232},{48,240},{56,2... | collective-permute-start | bytes 1179656 | tf_op jit(solution)/shard_map/ppermute | solution.py:48
  113.3 35.0 %collective-permute-start.14 = (bf16[4,64,3,256]{3,1,2,0:T(8,128)(2,1)}, bf16[4,64,3,256]{3,1,2,0:T(8,128)(2,1)}, u32[]{:S(2)}, u32[]{:S(2)}) collective-permute-start(bf16[4,64,3,256]{3,1,2,0:T(8,128)(2,1)} %get-tuple-element.29), channel_id=1, source_target_pairs={{0,128},{8,136},{16,144},{24,152},{32,160},{40,168},{48,176},{56,1... | collective-permute-start | bytes 1179656 | tf_op jit(solution)/shard_map/ppermute | solution.py:48
  116.5 31.8 %collective-permute-start.13 = (bf16[4,64,3,256]{3,1,2,0:T(8,128)(2,1)S(1)}, bf16[4,64,3,256]{3,1,2,0:T(8,128)(2,1)}, u32[]{:S(2)}, u32[]{:S(2)}) collective-permute-start(bf16[4,64,3,256]{3,1,2,0:T(8,128)(2,1)S(1)} %get-tuple-element.27), channel_id=1, source_target_pairs={{0,64},{8,72},{16,80},{24,88},{32,96},{40,104},{48,112},{56,120},{... | collective-permute-start | bytes 1179656 | tf_op jit(solution)/shard_map/ppermute | solution.py:48
  118.7 1.3 collective-permute-start.19
  120.0 5.3 %collective-permute-start.20 = (f32[7424]{0:T(1024)S(1)}, f32[7424]{0:T(1024)S(1)}, u32[]{:S(2)}, u32[]{:S(2)}) collective-permute-start(f32[7424]{0:T(1024)S(1)} %fusion.73), channel_id=1, source_target_pairs={{0,16},{8,24},{16,0},{24,8},{32,48},{40,56},{48,32},{56,40},{64,80... | collective-permute-start | bytes 89096 | tf_op jit(solution)/shard_map/ppermute | solution.py:21
  125.3 7.9 %collective-permute-start.21 = (f32[7424]{0:T(1024)S(1)}, f32[7424]{0:T(1024)S(1)}, u32[]{:S(2)}, u32[]{:S(2)}) collective-permute-start(f32[7424]{0:T(1024)S(1)} %add.392), channel_id=1, source_target_pairs={{0,32},{8,40},{16,48},{24,56},{32,0},{40,8},{48,16},{56,24},{64,96... | collective-permute-start | bytes 89096 | tf_op jit(solution)/shard_map/ppermute | solution.py:21
  133.2 3.9 %collective-permute-start.22 = (f32[7424]{0:T(1024)S(1)}, f32[7424]{0:T(1024)S(1)}, u32[]{:S(2)}, u32[]{:S(2)}) collective-permute-start(f32[7424]{0:T(1024)S(1)} %add.393), channel_id=1, source_target_pairs={{0,64},{8,72},{16,80},{24,88},{32,96},{40,104},{48,112},{56,120},{... | collective-permute-start | bytes 89096 | tf_op jit(solution)/shard_map/ppermute | solution.py:21
  137.8 5.7 %collective-permute-start.23 = (f32[7424]{0:T(1024)}, f32[7424]{0:T(1024)}, u32[]{:S(2)}, u32[]{:S(2)}) collective-permute-start(f32[7424]{0:T(1024)} %add.394), channel_id=1, source_target_pairs={{0,128},{8,136},{16,144},{24,152},{32,160},{40,168},{48,176},{56,1... | collective-permute-start | bytes 89096 | tf_op jit(solution)/shard_map/ppermute | solution.py:21
  144.3 13.0 %copy-start.7 = (f32[7424]{0:T(1024)}, f32[7424]{0:T(1024)S(1)}, u32[]{:S(2)}) copy-start(f32[7424]{0:T(1024)S(1)} %add.395) | copy-start | bytes 89092
  144.3 13.0 %collective-permute-start.24 = (f32[2048]{0:T(1024)S(1)}, f32[2048]{0:T(1024)S(1)}, u32[]{:S(2)}, u32[]{:S(2)}) collective-permute-start(f32[2048]{0:T(1024)S(1)} %slice.269), channel_id=1, source_target_pairs={{0,1},{1,0},{2,3},{3,2},{4,5},{5,4},{6,7},{7,6},{8,9},{9,8},{10,11... | collective-permute-start | bytes 24584 | tf_op jit(solution)/shard_map/ppermute | solution.py:21
  149.8 0.9 copy-start.4
  150.7 16.1 %collective-permute-start.18 = (bf16[64,3,256]{2,0,1:T(8,128)(2,1)S(1)}, bf16[64,3,256]{2,0,1:T(8,128)(2,1)S(1)}, u32[]{:S(2)}, u32[]{:S(2)}) collective-permute-start(bf16[64,3,256]{2,0,1:T(8,128)(2,1)S(1)} %get-tuple-element.34), channel_id=1, source_target_pairs={{0,48},{8,56},{16,0},{24,8},{32,16},{40,24},{48,32},{56,40},{64,11... | collective-permute-start | bytes 294920 | tf_op jit(solution)/shard_map/ppermute | solution.py:48
  152.7 14.1 %collective-permute-start.17 = (bf16[64,3,256]{2,0,1:T(8,128)(2,1)S(1)}, bf16[64,3,256]{2,0,1:T(8,128)(2,1)S(1)}, u32[]{:S(2)}, u32[]{:S(2)}) collective-permute-start(bf16[64,3,256]{2,0,1:T(8,128)(2,1)S(1)} %get-tuple-element.35), channel_id=1, source_target_pairs={{0,32},{8,40},{16,48},{24,56},{32,0},{40,8},{48,16},{56,24},{64,96... | collective-permute-start | bytes 294920 | tf_op jit(solution)/shard_map/ppermute | solution.py:48
  155.1 11.7 %collective-permute-start.16 = (bf16[64,3,256]{2,0,1:T(8,128)(2,1)S(1)}, bf16[64,3,256]{2,0,1:T(8,128)(2,1)S(1)}, u32[]{:S(2)}, u32[]{:S(2)}) collective-permute-start(bf16[64,3,256]{2,0,1:T(8,128)(2,1)S(1)} %get-tuple-element.33), channel_id=1, source_target_pairs={{0,16},{8,24},{16,32},{24,40},{32,48},{40,56},{48,0},{56,8},{64,80... | collective-permute-start | bytes 294920 | tf_op jit(solution)/shard_map/ppermute | solution.py:48
  157.3 5.2 %collective-permute-start.25 = (f32[2048]{0:T(1024)S(1)}, f32[2048]{0:T(1024)S(1)}, u32[]{:S(2)}, u32[]{:S(2)}) collective-permute-start(f32[2048]{0:T(1024)S(1)} %slice_add_fusion), channel_id=1, source_target_pairs={{0,2},{1,3},{2,0},{3,1},{4,6},{5,7},{6,4},{7,5},{8,10},{9,11},{10,... | collective-permute-start | bytes 24584 | tf_op jit(solution)/shard_map/ppermute | solution.py:21
  162.5 3.7 %collective-permute-start.26 = (f32[2048]{0:T(1024)S(1)}, f32[2048]{0:T(1024)S(1)}, u32[]{:S(2)}, u32[]{:S(2)}) collective-permute-start(f32[2048]{0:T(1024)S(1)} %add.397), channel_id=1, source_target_pairs={{0,4},{1,5},{2,6},{3,7},{4,0},{5,1},{6,2},{7,3},{8,12},{9,13},{10,... | collective-permute-start | bytes 24584 | tf_op jit(solution)/shard_map/ppermute | solution.py:21
Sparse Core Ops, SparseCore 0:
  11.4 59.0 all-gather.1
  99.9 56.8 reduce-scatter.1
